TPU v7x, 32 devices: a whole 2x2x4 slice. The times are simulated.
32 devices in a mesh: groups: 2 (over y), dp: 4 (over z), task: 4 (over x, core).
Axes of the slice: x: 2, y: 2, z: 4, core: 2. Of those that a mesh axis runs over, the one named last changes fastest.
Arguments:
- coords: bfloat16 [3, 6144], P(None, ('groups', 'dp')), parts along dimension 1, may hold values from 0 to 1
- lengthscales: float32 [6], P('groups'), parts along dimension 0, may hold values from 0.15 to 0.5
- vectors: bfloat16 [2, 6144, 256], P(None, ('groups', 'dp'), 'task'), parts along dimension 1, may hold values from -6 to 6
- mixing: bfloat16 [512, 256], P('groups'), parts along dimension 0, may hold values from -0.078125 to 0.078125
- noise: float32 [512], P(('groups', 'task')), parts along dimension 0, may hold values from 0.1 to 1
Outputs:
- product: bfloat16 [2, 6144, 256], P(None, ('groups', 'dp'), 'task'), parts along dimension 1
- gradient: float32 [512, 256], P(('groups', 'task')), parts along dimension 0
There are 2 independent parts, one for each index of `groups`. A program takes and returns all parts, laid end to end along the dimension named above; each array names one. Nothing has to cross between parts.
All inputs are finite; a program needn't handle non-finite values.
Results may differ from a plain program's by a relative error of at most 0.0056.
Values may be sent and summed in bfloat16 or wider, within the bound.
No kernel may reach another device: no remote copies, remote signals or barrier semaphores. Data moves between devices by JAX's collectives and lax.ppermute only.
A program may use at most 64 MiB of HBM per device.

v0:
```python
import math

import jax
import jax.numpy as jnp
from jax import lax
from jax.sharding import PartitionSpec as P


def kernel_tile(left, right):
    diff = left[:, :, None] - right[:, None, :]
    return jnp.exp(0.1 - jnp.sqrt(jnp.sum(diff * diff, axis=0) + 0.01))


def per_device(coords, lengthscales, vectors, mixing, noise):
    n_rows = coords.shape[1]
    local_tasks = vectors.shape[2]
    inverse = 1.0 / lengthscales
    own_scaled = coords.astype(jnp.float32) * inverse[:, None]
    whole_vectors = lax.all_gather(vectors, "task", axis=2, tiled=True)
    task_start = lax.axis_index("task") * local_tasks
    empty = jnp.zeros((2, n_rows, local_tasks), jnp.float32)
    point_piece = lax.all_gather(coords, "dp", axis=1, tiled=True)
    vector_piece = lax.all_gather(vectors, "dp", axis=1, tiled=True)
    width = point_piece.shape[1]
    block = math.gcd(width, 512)
    piece_scaled = point_piece.astype(jnp.float32) * inverse[:, None]

    def inner(index, accum):
        right = lax.dynamic_slice_in_dim(piece_scaled, index * block, block, 1)
        values = lax.dynamic_slice_in_dim(vector_piece, index * block, block, 1)
        tile = kernel_tile(own_scaled, right).astype(jnp.bfloat16)
        return accum + jnp.einsum("nr,srm->snm", tile, values, preferred_element_type=jnp.float32)

    summed = lax.fori_loop(0, width // block, inner, empty)
    images = summed.astype(jnp.bfloat16)
    whole_images = lax.all_gather(images, "task", axis=2, tiled=True)
    own_rows = lax.dynamic_slice_in_dim(mixing, task_start, local_tasks, 0)
    mixed = jnp.einsum("sna,ca->snc", whole_images, own_rows, preferred_element_type=jnp.float32)
    product = (mixed + noise[None, None, :] * vectors.astype(jnp.float32)).astype(jnp.bfloat16)
    signs = jnp.array([1.0, -1.0], jnp.bfloat16)
    signed = images * signs[:, None, None]
    partial_grad = jnp.einsum(
        "sna,snb->ab", signed, whole_vectors, preferred_element_type=jnp.float32
    )
    total = lax.psum(partial_grad, "dp")
    gradient = total / (2.0 * n_rows * lax.axis_size("dp"))
    return (product, gradient)


def solution(mesh):
    in_specs = (
        P(None, ("groups", "dp")),
        P("groups"),
        P(None, ("groups", "dp"), "task"),
        P("groups", None),
        P(("groups", "task")),
    )
    out_specs = (P(None, ("groups", "dp"), "task"), P(("groups", "task"), None))
    return jax.shard_map(
        per_device, mesh=mesh, in_specs=in_specs, out_specs=out_specs, check_vma=False
    )
```

profile of v0, /device:TPU:0, one launch (start us, length us, event | category | flops | bytes accessed | tf_op | source)
XLA Modules:
  0.0 107.4 jit_solution(3715109820188452420)
XLA Ops:
  7.2 0.0 all-reduce.2.cloned.1.call-start
  7.3 21.9 %all_gather.12 = bf16[2,3072,64]{1,2,0:T(8,128)(2,1)} all-gather(bf16[2,768,64]{1,2,0:T(8,128)(2,1)} %param.10), channel_id=1, replica_groups=mesh['groups'=2,'dp'=4,'task'=4] {'dp'}, dimensions={1}, use_global_device_ids=true | all-gather | bytes 983040 | tf_op jit(solution)/shard_map/all_gather | solution.py:23
  29.1 8.8 %all_gather.15 = bf16[2,768,256]{1,2,0:T(8,128)(2,1)S(1)} all-gather(bf16[2,768,64]{1,2,0:T(8,128)(2,1)} %param.10), channel_id=1, replica_groups=mesh['groups'=2,'dp'=4,'task'=4] {'task'}, dimensions={2}, use_global_device_ids=true | all-gather | bytes 983040 | tf_op jit(solution)/shard_map/all_gather | solution.py:19
  37.9 13.1 %all_gather.13 = bf16[3,3072]{1,0:T(4,128)(2,1)S(1)} all-gather(bf16[3,768]{1,0:T(4,128)(2,1)S(1)} %copy-done.2), channel_id=1, replica_groups=mesh['groups'=2,'dp'=4,'task'=4] {'dp'}, dimensions={1}, use_global_device_ids=true | all-gather | bytes 23040 | tf_op jit(solution)/shard_map/all_gather | solution.py:22
  51.0 0.1 convert_multiply_fusion.1
  51.1 0.1 convert_multiply_fusion
  51.2 13.9 %while.14 = (s32[]{:T(128)}, f32[2,768,64]{1,2,0:T(8,128)S(1)}, bf16[2,3072,64]{1,2,0:T(8,128)(2,1)}, f32[3,768]{1,0:T(4,128)S(1)}, f32[3,3072]{1,0:T(4,128)S(1)...) while((s32[]{:T(128)}, f32[2,768,64]{1,2,0:T(8,128)S(1)}, bf16[2,3072,64]{1,2,0:T(8,128)(2,1)}, ...), condition=%wide.region_2.0_spmd.clone, body=%wide.region_0.0_spmd.clone.sunk | while | flops 105185288 | bytes 4091045 | solution.py:34
  51.2 0.5 multiply_reduce_fusion.2
  51.7 1.8 %fusion.22 = f32[2,768,64]{1,2,0:T(8,128)S(1)} fusion(f32[768,512]{1,0:T(8,128)S(1)} %multiply_reduce_fusion.2, f32[2,768,64]{1,2,0:T(8,128)S(1)} %get-tuple-element.166, pred[]{:T(512)S(6)} %compare.3, bf16[2,3072,64]{1,2,0:T(8,128)(2,1)} %get-tuple-element.176, s32[]{:T(128)S(6)} %select_n.14), kind=kOutput, calls=%fused_computation.3.clone.1 | convolution fusion | flops 102039552 | bytes 2490373 | tf_op jit(solution)/shard_map/while/body/eval_jaxpr/nr,srm->snm/dot_general | solution.py:32
  53.5 0.5 multiply_reduce_fusion.2
  54.1 1.8 %fusion.22 = f32[2,768,64]{1,2,0:T(8,128)S(1)} fusion(f32[768,512]{1,0:T(8,128)S(1)} %multiply_reduce_fusion.2, f32[2,768,64]{1,2,0:T(8,128)S(1)} %get-tuple-element.166, pred[]{:T(512)S(6)} %compare.3, bf16[2,3072,64]{1,2,0:T(8,128)(2,1)} %get-tuple-element.176, s32[]{:T(128)S(6)} %select_n.14), kind=kOutput, calls=%fused_computation.3.clone.1 | convolution fusion | flops 102039552 | bytes 2490373 | tf_op jit(solution)/shard_map/while/body/eval_jaxpr/nr,srm->snm/dot_general | solution.py:32
  55.9 0.5 multiply_reduce_fusion.2
  56.4 1.8 %fusion.22 = f32[2,768,64]{1,2,0:T(8,128)S(1)} fusion(f32[768,512]{1,0:T(8,128)S(1)} %multiply_reduce_fusion.2, f32[2,768,64]{1,2,0:T(8,128)S(1)} %get-tuple-element.166, pred[]{:T(512)S(6)} %compare.3, bf16[2,3072,64]{1,2,0:T(8,128)(2,1)} %get-tuple-element.176, s32[]{:T(128)S(6)} %select_n.14), kind=kOutput, calls=%fused_computation.3.clone.1 | convolution fusion | flops 102039552 | bytes 2490373 | tf_op jit(solution)/shard_map/while/body/eval_jaxpr/nr,srm->snm/dot_general | solution.py:32
  58.2 0.5 multiply_reduce_fusion.2
  58.7 1.8 %fusion.22 = f32[2,768,64]{1,2,0:T(8,128)S(1)} fusion(f32[768,512]{1,0:T(8,128)S(1)} %multiply_reduce_fusion.2, f32[2,768,64]{1,2,0:T(8,128)S(1)} %get-tuple-element.166, pred[]{:T(512)S(6)} %compare.3, bf16[2,3072,64]{1,2,0:T(8,128)(2,1)} %get-tuple-element.176, s32[]{:T(128)S(6)} %select_n.14), kind=kOutput, calls=%fused_computation.3.clone.1 | convolution fusion | flops 102039552 | bytes 2490373 | tf_op jit(solution)/shard_map/while/body/eval_jaxpr/nr,srm->snm/dot_general | solution.py:32
  60.5 0.5 multiply_reduce_fusion.2
  61.0 1.8 %fusion.22 = f32[2,768,64]{1,2,0:T(8,128)S(1)} fusion(f32[768,512]{1,0:T(8,128)S(1)} %multiply_reduce_fusion.2, f32[2,768,64]{1,2,0:T(8,128)S(1)} %get-tuple-element.166, pred[]{:T(512)S(6)} %compare.3, bf16[2,3072,64]{1,2,0:T(8,128)(2,1)} %get-tuple-element.176, s32[]{:T(128)S(6)} %select_n.14), kind=kOutput, calls=%fused_computation.3.clone.1 | convolution fusion | flops 102039552 | bytes 2490373 | tf_op jit(solution)/shard_map/while/body/eval_jaxpr/nr,srm->snm/dot_general | solution.py:32
  62.8 0.5 multiply_reduce_fusion.2
  63.3 1.8 %fusion.22 = f32[2,768,64]{1,2,0:T(8,128)S(1)} fusion(f32[768,512]{1,0:T(8,128)S(1)} %multiply_reduce_fusion.2, f32[2,768,64]{1,2,0:T(8,128)S(1)} %get-tuple-element.166, pred[]{:T(512)S(6)} %compare.3, bf16[2,3072,64]{1,2,0:T(8,128)(2,1)} %get-tuple-element.176, s32[]{:T(128)S(6)} %select_n.14), kind=kOutput, calls=%fused_computation.3.clone.1 | convolution fusion | flops 102039552 | bytes 2490373 | tf_op jit(solution)/shard_map/while/body/eval_jaxpr/nr,srm->snm/dot_general | solution.py:32
  65.2 1.0 convolution_bitcast_fusion.1
  66.2 7.6 %all_gather.14 = bf16[2,768,256]{1,2,0:T(8,128)(2,1)S(1)} all-gather(bf16[2,768,64]{1,2,0:T(8,128)(2,1)S(1)} %convert_element_type.24), channel_id=1, replica_groups=mesh['groups'=2,'dp'=4,'task'=4] {'task'}, dimensions={2}, use_global_device_ids=true | all-gather | bytes 983040 | tf_op jit(solution)/shard_map/all_gather | solution.py:36
  73.8 0.9 fusion.9
  74.8 24.3 %all-reduce.2.cloned.1.call-done = f32[64,256]{1,0:T(8,128)} async-done(((f32[64,256]{1,0:T(8,128)}), f32[64,256]{1,0:T(8,128)}) %all-reduce.2.cloned.1.call-update) | async-done | bytes 65552 | tf_op jit(solution)/shard_map/psum | solution.py:45
  99.1 1.5 %broadcast_multiply_fusion = f32[64,256]{1,0:T(8,128)} fusion(f32[64,256]{1,0:T(8,128)} %all-reduce.2.cloned.1.call-done), kind=kLoop, calls=%fused_computation.19 | loop fusion | flops 16384 | bytes 131072 | tf_op jit(solution)/shard_map/div | solution.py:46
  (22 shorter events, 0.1 us)
Async XLA Ops:
  7.2 66.7 %copy-start = (bf16[256,256]{1,0:T(8,128)(2,1)S(1)}, bf16[256,256]{1,0:T(8,128)(2,1)}, u32[]{:S(2)}) copy-start(bf16[256,256]{1,0:T(8,128)(2,1)} %param.11) | copy-start | bytes 393220
  7.2 30.7 %copy-start.5 = (f32[3]{0:T(128)S(1)}, f32[3]{0:T(128)}, u32[]{:S(2)}) copy-start(f32[3]{0:T(128)} %param.9) | copy-start | bytes 40
  7.2 30.7 %copy-start.2 = (bf16[3,768]{1,0:T(4,128)(2,1)S(1)}, bf16[3,768]{1,0:T(4,128)(2,1)}, u32[]{:S(2)}) copy-start(bf16[3,768]{1,0:T(4,128)(2,1)} %param.8) | copy-start | bytes 13828
  7.2 91.9 %all-reduce.2.cloned.1.call-start = ((), (), s32[]{:S(2)}) async-start(), calls=%async_computation | async-start | bytes 131072 | tf_op jit(solution)/shard_map/psum | solution.py:45
  51.2 14.0 %copy-start.4 = (bf16[2]{0:T(256)(128)(2,1)S(1)}, bf16[2]{0:T(256)(128)(2,1)}, u32[]{:S(2)}) copy-start(bf16[2]{0:T(256)(128)(2,1)} %constant.65.clone) | copy-start | bytes 16
  65.1 8.7 %copy-start.1 = (bf16[2,768,64]{1,2,0:T(8,128)(2,1)S(1)}, bf16[2,768,64]{1,2,0:T(8,128)(2,1)}, u32[]{:S(2)}) copy-start(bf16[2,768,64]{1,2,0:T(8,128)(2,1)} %param.10) | copy-start | bytes 589828
  65.1 8.7 %copy-start.3 = (f32[64]{0:T(128)S(1)}, f32[64]{0:T(128)}, u32[]{:S(2)}) copy-start(f32[64]{0:T(128)} %param.12) | copy-start | bytes 772
Sparse Core Ops, SparseCore 0:
  66.3 32.7 all-reduce.1
where the time goes:
time: 108 us; the launch traced here: 107 us
  blocking collectives  51.4 us (48%)
  waiting for transfers between devices  24.4 us (23%)
  between operations  14.1 us (13%)
  matrix products  12.4 us (11%)
  other arithmetic  4.7 us (4%)
    psum x1, waiting for transfers between devices, per_device(): total = lax.psum(partial_grad, 'dp')  24.3 us
    all_gather x1, blocking collectives, per_device(): vector_piece = lax.all_gather(vectors, 'dp', axis=1, tiled=True)  21.9 us
    all_gather x1, blocking collectives, per_device(): point_piece = lax.all_gather(coords, 'dp', axis=1, tiled=True)  13.1 us
    dot_general x6, matrix products, inner(): jnp.einsum('nr,srm->snm', tile, values, preferred_element_type=jnp.float32)  10.5 us
    all_gather x1, blocking collectives, per_device(): whole_vectors = lax.all_gather(vectors, 'task', axis=2, tiled=True)  8.79 us
    all_gather x1, blocking collectives, per_device(): whole_images = lax.all_gather(images, 'task', axis=2, tiled=True)  7.64 us
    reduce_sum x6, other arithmetic, kernel_tile(): return jnp.exp(0.1 - jnp.sqrt(jnp.sum(diff * diff, axis=0) + 0.01))  3.05 us
  transfers between devices with their start and end apart: 1, of which 1 were waited for; matrix products, arithmetic and copies ran while one was open for 1% of the time, Pallas kernels for 0%

commit v1 on v0

v1 whole, which is shorter than its diff:
```python
import jax
import jax.numpy as jnp
from jax import lax
from jax.sharding import PartitionSpec as P


def kernel_tile(left, right):
    diff = left[:, :, None] - right[:, None, :]
    return jnp.exp(0.1 - jnp.sqrt(jnp.sum(diff * diff, axis=0) + 0.01))


def shift(x, axis, k, n):
    return lax.ppermute(x, axis, [(i, (i + k) % n) for i in range(n)])


def butterfly_sum(x, axis, n):
    if n & (n - 1):
        return lax.psum(x, axis)
    step = 1
    while step < n:
        x = x + lax.ppermute(x, axis, [(i, i ^ step) for i in range(n)])
        step *= 2
    return x


def per_device(coords, lengthscales, vectors, mixing, noise):
    n_rows = coords.shape[1]
    local_tasks = vectors.shape[2]
    n_dp = lax.axis_size("dp")
    inverse = 1.0 / lengthscales
    own_scaled = coords.astype(jnp.float32) * inverse[:, None]
    task_start = lax.axis_index("task") * local_tasks

    def block(right_coords, values):
        right = right_coords.astype(jnp.float32) * inverse[:, None]
        tile = kernel_tile(own_scaled, right).astype(jnp.bfloat16)
        return jnp.einsum("nr,srm->snm", tile, values, preferred_element_type=jnp.float32)

    summed = block(coords, vectors)
    if n_dp <= 4:
        for k in range(1, n_dp):
            summed = summed + block(shift(coords, "dp", k, n_dp), shift(vectors, "dp", k, n_dp))
    else:

        def ring(_, carry):
            accum, right_coords, values = carry
            right_coords = shift(right_coords, "dp", 1, n_dp)
            values = shift(values, "dp", 1, n_dp)
            return accum + block(right_coords, values), right_coords, values

        summed = lax.fori_loop(0, n_dp - 1, ring, (summed, coords, vectors))[0]
    whole_vectors = lax.all_gather(vectors, "task", axis=2, tiled=True)
    images = summed.astype(jnp.bfloat16)
    whole_images = lax.all_gather(images, "task", axis=2, tiled=True)
    own_rows = lax.dynamic_slice_in_dim(mixing, task_start, local_tasks, 0)
    mixed = jnp.einsum("sna,ca->snc", whole_images, own_rows, preferred_element_type=jnp.float32)
    product = (mixed + noise[None, None, :] * vectors.astype(jnp.float32)).astype(jnp.bfloat16)
    signs = jnp.array([1.0, -1.0], jnp.bfloat16)
    signed = images * signs[:, None, None]
    partial_grad = jnp.einsum(
        "sna,snb->ab", signed, whole_vectors, preferred_element_type=jnp.float32
    )
    total = butterfly_sum(partial_grad, "dp", n_dp)
    gradient = total / (2.0 * n_rows * n_dp)
    return (product, gradient)


def solution(mesh):
    in_specs = (
        P(None, ("groups", "dp")),
        P("groups"),
        P(None, ("groups", "dp"), "task"),
        P("groups", None),
        P(("groups", "task")),
    )
    out_specs = (P(None, ("groups", "dp"), "task"), P(("groups", "task"), None))
    return jax.shard_map(
        per_device, mesh=mesh, in_specs=in_specs, out_specs=out_specs, check_vma=False
    )
```

time: 108 us -> 47.9 us (0.44)
  blocking collectives: 51.4 us -> 17.2 us
  waiting for transfers between devices: 24.4 us -> 4.25 us
  between operations: 14.1 us -> 0.71 us
  starting transfers between devices: 0.04 us -> 13 us
  matrix products: 12.4 us -> 5.69 us
  other arithmetic: 4.7 us -> 6.81 us
    all_gather x2 -> x0, blocking collectives: 35 us -> none  [the longest x1 21.9 us: per_device(): vector_piece = lax.all_gather(vectors, 'dp', axis=1, tiled=True)]
    psum x1 -> x0, waiting for transfers between devices: 24.3 us -> none  [per_device(): total = lax.psum(partial_grad, 'dp')]
    ppermute x0 -> x8, starting transfers between devices: none -> 13 us  [the longest x6 10.8 us: shift(): return lax.ppermute(x, axis, [(i, (i + k) % n) for i in range(n)])]
    dot_general x6 -> x0, matrix products: 10.5 us -> none  [inner(): jnp.einsum('nr,srm->snm', tile, values, preferred_element_type=jnp.float32)]
    unnamed x0 -> x4, matrix products: none -> 4.38 us
    ppermute x0 -> x8, waiting for transfers between devices: none -> 4.25 us  [the longest x2 4.23 us: butterfly_sum(): x = x + lax.ppermute(x, axis, [(i, i ^ step) for i in range(n)])]
    reduce_sum x6 -> x1, other arithmetic: 3.05 us -> 4.65 us  [kernel_tile(): return jnp.exp(0.1 - jnp.sqrt(jnp.sum(diff * diff, axis=0) + 0.01))]
  transfers between devices with their start and end apart: 1 -> 8, of which waited for: 1 -> 1; matrix products, arithmetic and copies ran while one was open for 1% -> 22% of each run, Pallas kernels for 0% -> 0%
where the time goes in v1:
time: 47.9 us; the launch traced here: 47.7 us
  blocking collectives  17.2 us (36%)
  starting transfers between devices  13 us (27%)
  other arithmetic  6.81 us (14%)
  matrix products  5.69 us (12%)
  waiting for transfers between devices  4.25 us (9%)
  between operations  0.71 us (1%)
    ppermute x6, starting transfers between devices, shift(): return lax.ppermute(x, axis, [(i, (i + k) % n) for i in range(n)])  10.8 us
    all_gather x1, blocking collectives, per_device(): whole_vectors = lax.all_gather(vectors, 'task', axis=2, tiled=True)  8.79 us
    all_gather x1, blocking collectives, per_device(): whole_images = lax.all_gather(images, 'task', axis=2, tiled=True)  8.43 us
    reduce_sum x1, other arithmetic, kernel_tile(): return jnp.exp(0.1 - jnp.sqrt(jnp.sum(diff * diff, axis=0) + 0.01))  4.65 us
    unnamed x4, matrix products  4.38 us
    ppermute x2, waiting for transfers between devices, butterfly_sum(): x = x + lax.ppermute(x, axis, [(i, i ^ step) for i in range(n)])  4.23 us
    ppermute x2, starting transfers between devices, butterfly_sum(): x = x + lax.ppermute(x, axis, [(i, i ^ step) for i in range(n)])  2.18 us
  transfers between devices with their start and end apart: 8, of which 1 were waited for; matrix products, arithmetic and copies ran while one was open for 22% of the time, Pallas kernels for 0%

profile of v1, /device:TPU:0, one launch (start us, length us, event | category | flops | bytes accessed | tf_op | source)
XLA Modules:
  0.0 47.7 jit_solution(16076304417554878309)
XLA Ops:
  0.6 0.0 copy-start
  0.6 3.1 %collective-permute-start = (bf16[3,768]{1,0:T(4,128)(2,1)}, bf16[3,768]{1,0:T(4,128)(2,1)S(1)}, u32[]{:S(2)}, u32[]{:S(2)}) collective-permute-start(bf16[3,768]{1,0:T(4,128)(2,1)} %param.6), channel_id=1, source_target_pairs={{0,4},{4,8},{8,12},{12,0},{1,5},{5,9},{9,13},{13,1},{2,6},{6,10},{... | collective-permute-start | bytes 13832 | tf_op jit(solution)/shard_map/ppermute | solution.py:13
  3.7 2.6 %collective-permute-start.2 = (bf16[3,768]{1,0:T(4,128)(2,1)}, bf16[3,768]{1,0:T(4,128)(2,1)S(1)}, u32[]{:S(2)}, u32[]{:S(2)}) collective-permute-start(bf16[3,768]{1,0:T(4,128)(2,1)} %param.6), channel_id=1, source_target_pairs={{0,8},{4,12},{8,0},{12,4},{1,9},{5,13},{9,1},{13,5},{2,10},{6,14},... | collective-permute-start | bytes 13832 | tf_op jit(solution)/shard_map/ppermute | solution.py:13
  6.3 1.3 %collective-permute-start.4 = (bf16[3,768]{1,0:T(4,128)(2,1)}, bf16[3,768]{1,0:T(4,128)(2,1)S(1)}, u32[]{:S(2)}, u32[]{:S(2)}) collective-permute-start(bf16[3,768]{1,0:T(4,128)(2,1)} %param.6), channel_id=1, source_target_pairs={{0,12},{4,0},{8,4},{12,8},{1,13},{5,1},{9,5},{13,9},{2,14},{6,2},{... | collective-permute-start | bytes 13832 | tf_op jit(solution)/shard_map/ppermute | solution.py:13
  7.7 0.7 %collective-permute-start.1 = (bf16[2,768,64]{1,2,0:T(8,128)(2,1)}, bf16[2,768,64]{1,2,0:T(8,128)(2,1)S(1)}, u32[]{:S(2)}, u32[]{:S(2)}) collective-permute-start(bf16[2,768,64]{1,2,0:T(8,128)(2,1)} %param.8), channel_id=1, source_target_pairs={{0,4},{4,8},{8,12},{12,0},{1,5},{5,9},{9,13},{13,1},{2,6},{6,10},{... | collective-permute-start | bytes 589832 | tf_op jit(solution)/shard_map/ppermute | solution.py:13
  8.3 0.3 collective-permute-start.3
  8.7 8.8 %all_gather.7 = bf16[2,768,256]{1,2,0:T(8,128)(2,1)S(1)} all-gather(bf16[2,768,64]{1,2,0:T(8,128)(2,1)} %param.8), channel_id=1, replica_groups=mesh['groups'=2,'dp'=4,'task'=4] {'task'}, dimensions={2}, use_global_device_ids=true | all-gather | bytes 983040 | tf_op jit(solution)/shard_map/all_gather | solution.py:52
  17.5 0.7 %broadcast_divide_fusion = f32[3]{0:T(128)S(1)} fusion(f32[3]{0:T(128)} %param.7), kind=kLoop, calls=%fused_computation.27 | loop fusion | flops 3 | bytes 24 | tf_op jit(solution)/shard_map/div | solution.py:30
  18.1 2.8 %collective-permute-start.5 = (bf16[2,768,64]{1,2,0:T(8,128)(2,1)}, bf16[2,768,64]{1,2,0:T(8,128)(2,1)S(1)}, u32[]{:S(2)}, u32[]{:S(2)}) collective-permute-start(bf16[2,768,64]{1,2,0:T(8,128)(2,1)} %param.8), channel_id=1, source_target_pairs={{0,12},{4,0},{8,4},{12,8},{1,13},{5,1},{9,5},{13,9},{2,14},{6,2},{... | collective-permute-start | bytes 589832 | tf_op jit(solution)/shard_map/ppermute | solution.py:13
  21.0 0.8 %convert_multiply_fusion = (f32[3,768]{1,0:T(4,128)S(1)}, f32[3,768]{1,0:T(4,128)S(1)}, f32[3,768]{1,0:T(4,128)S(1)}, f32[3,768]{1,0:T(4,128)S(1)}) fusion(bf16[3,768]{1,0:T(4,128)(2,1)S(1)} %collective-permute-done.4, f32[3]{0:T(128)S(1)} %broadcast_divide_fusion, bf16[3,768]{1,0:T(4,128)(2,1)S(1)} %collective-permute-done, ...), kind=kLoop, calls=%fused_computation.22 | loop fusion | flops 18432 | bytes 55308 | tf_op jit(solution)/shard_map/mul | solution.py:35
  21.7 4.7 %multiply_reduce_fusion.2 = (f32[768,768]{1,0:T(8,128)S(1)}, f32[768,768]{1,0:T(8,128)S(1)}, f32[768,768]{1,0:T(8,128)S(1)}, f32[768,768]{1,0:T(8,128)S(1)}) fusion(f32[3,768]{1,0:T(4,128)S(1)} %get-tuple-element.7, f32[3,768]{1,0:T(4,128)S(1)} %get-tuple-element.9, f32[3,768]{1,0:T(4,128)S(1)} %get-tuple-element.8, f32[3,768]{1,0:T(4,128)S(1)} %get-tuple-element.6), kind=kLoop, calls=%fused_computation.2 | loop fusion | flops 18874368 | bytes 9474048 | tf_op jit(solution)/shard_map/reduce_sum | solution.py:9
  26.4 1.1 %fusion = f32[768,128]{0,1:S(1)} fusion(bf16[768,128]{0,1:T(8,128)(2,1)S(1)} %bitcast.29, f32[768,768]{1,0:T(8,128)S(1)} %get-tuple-element.5), kind=kOutput, calls=%fused_computation.9 | convolution fusion | flops 152764416 | bytes 2949120
  27.5 1.1 %fusion.1 = f32[768,128]{0,1:S(1)} fusion(bf16[768,128]{0,1:T(8,128)(2,1)S(1)} %bitcast.35, f32[768,768]{1,0:T(8,128)S(1)} %get-tuple-element.2), kind=kOutput, calls=%fused_computation.10 | convolution fusion | flops 152764416 | bytes 2949120
  28.6 1.1 %fusion.2 = f32[768,128]{0,1:S(1)} fusion(bf16[768,128]{0,1:T(8,128)(2,1)S(1)} %bitcast.34, f32[768,768]{1,0:T(8,128)S(1)} %get-tuple-element.3), kind=kOutput, calls=%fused_computation.11 | convolution fusion | flops 152764416 | bytes 2949120
  29.7 0.0 copy-start.3
  29.7 1.1 %fusion.3 = f32[768,128]{0,1:S(1)} fusion(bf16[768,128]{0,1:T(8,128)(2,1)S(1)} %bitcast.36, f32[768,768]{1,0:T(8,128)S(1)} %get-tuple-element.4), kind=kOutput, calls=%fused_computation.12 | convolution fusion | flops 152764416 | bytes 2949120
  30.8 0.1 fusion.5
  30.9 0.4 convolution_bitcast_fusion
  31.3 0.6 %collective-permute-start.6 = (f32[64,256]{1,0:T(8,128)S(1)}, f32[64,256]{1,0:T(8,128)S(1)}, u32[]{:S(2)}, u32[]{:S(2)}) collective-permute-start(f32[64,256]{1,0:T(8,128)S(1)} %convolution_bitcast_fusion), channel_id=1, source_target_pairs={{0,4},{4,0},{8,12},{12,8},{1,5},{5,1},{9,13},{13,9},{2,6},{6,2},{1... | collective-permute-start | bytes 196616 | tf_op jit(solution)/shard_map/ppermute | solution.py:21
  31.9 8.4 %all_gather.6 = bf16[2,768,256]{1,2,0:T(8,128)(2,1)S(1)} all-gather(bf16[2,768,64]{1,2,0:T(8,128)(2,1)S(1)} %fusion.5), channel_id=1, replica_groups=mesh['groups'=2,'dp'=4,'task'=4] {'task'}, dimensions={2}, use_global_device_ids=true | all-gather | bytes 983040 | tf_op jit(solution)/shard_map/all_gather | solution.py:54
  40.4 1.5 %collective-permute-start.7 = (f32[64,256]{1,0:T(8,128)S(1)}, f32[64,256]{1,0:T(8,128)S(1)}, u32[]{:S(2)}, u32[]{:S(2)}) collective-permute-start(f32[64,256]{1,0:T(8,128)S(1)} %add.45), channel_id=1, source_target_pairs={{0,8},{4,12},{8,0},{12,4},{1,9},{5,13},{9,1},{13,5},{2,10},{6,14},... | collective-permute-start | bytes 196616 | tf_op jit(solution)/shard_map/ppermute | solution.py:21
  41.9 0.9 %fusion.4 = bf16[2,768,64]{1,2,0:T(8,128)(2,1)} fusion(bf16[2,768,256]{1,2,0:T(8,128)(2,1)S(1)} %all_gather.6, bf16[2,768,64]{1,2,0:T(8,128)(2,1)S(1)} %copy-done.1, f32[64]{0:T(128)S(1)} %copy-done.2, bf16[256,256]{1,0:T(8,128)(2,1)S(1)} %copy-done, s32[]{:T(128)S(6)} %select_n.3), kind=kOutput, calls=%fused_computation.13 | convolution fusion | flops 50724864 | bytes 1212932 | tf_op jit(solution)/shard_map/sna,ca->snc/dot_general | solution.py:56
  42.9 4.2 %collective-permute-done.7 = f32[64,256]{1,0:T(8,128)S(1)} collective-permute-done((f32[64,256]{1,0:T(8,128)S(1)}, f32[64,256]{1,0:T(8,128)S(1)}, u32[]{:S(2)}, u32[]{:S(2)}) %collective-permute-start.7) | collective-permute-done | bytes 65568 | tf_op jit(solution)/shard_map/ppermute | solution.py:21
  47.1 0.6 %add_multiply_fusion = f32[64,256]{1,0:T(8,128)} fusion(f32[64,256]{1,0:T(8,128)S(1)} %add.45, f32[64,256]{1,0:T(8,128)S(1)} %collective-permute-done.7), kind=kLoop, calls=%fused_computation.19 | loop fusion | flops 32768 | bytes 196608 | tf_op jit(solution)/shard_map/div | solution.py:64
  (14 shorter events, 0.0 us)
Async XLA Ops:
  0.6 41.3 %copy-start = (bf16[256,256]{1,0:T(8,128)(2,1)S(1)}, bf16[256,256]{1,0:T(8,128)(2,1)}, u32[]{:S(2)}) copy-start(bf16[256,256]{1,0:T(8,128)(2,1)} %param.9) | copy-start | bytes 393220
  0.6 17.5 %collective-permute-start = (bf16[3,768]{1,0:T(4,128)(2,1)}, bf16[3,768]{1,0:T(4,128)(2,1)S(1)}, u32[]{:S(2)}, u32[]{:S(2)}) collective-permute-start(bf16[3,768]{1,0:T(4,128)(2,1)} %param.6), channel_id=1, source_target_pairs={{0,4},{4,8},{8,12},{12,0},{1,5},{5,9},{9,13},{13,1},{2,6},{6,10},{... | collective-permute-start | bytes 13832 | tf_op jit(solution)/shard_map/ppermute | solution.py:13
  3.7 17.2 %collective-permute-start.2 = (bf16[3,768]{1,0:T(4,128)(2,1)}, bf16[3,768]{1,0:T(4,128)(2,1)S(1)}, u32[]{:S(2)}, u32[]{:S(2)}) collective-permute-start(bf16[3,768]{1,0:T(4,128)(2,1)} %param.6), channel_id=1, source_target_pairs={{0,8},{4,12},{8,0},{12,4},{1,9},{5,13},{9,1},{13,5},{2,10},{6,14},... | collective-permute-start | bytes 13832 | tf_op jit(solution)/shard_map/ppermute | solution.py:13
  6.3 14.6 %collective-permute-start.4 = (bf16[3,768]{1,0:T(4,128)(2,1)}, bf16[3,768]{1,0:T(4,128)(2,1)S(1)}, u32[]{:S(2)}, u32[]{:S(2)}) collective-permute-start(bf16[3,768]{1,0:T(4,128)(2,1)} %param.6), channel_id=1, source_target_pairs={{0,12},{4,0},{8,4},{12,8},{1,13},{5,1},{9,5},{13,9},{2,14},{6,2},{... | collective-permute-start | bytes 13832 | tf_op jit(solution)/shard_map/ppermute | solution.py:13
  7.7 19.8 %collective-permute-start.1 = (bf16[2,768,64]{1,2,0:T(8,128)(2,1)}, bf16[2,768,64]{1,2,0:T(8,128)(2,1)S(1)}, u32[]{:S(2)}, u32[]{:S(2)}) collective-permute-start(bf16[2,768,64]{1,2,0:T(8,128)(2,1)} %param.8), channel_id=1, source_target_pairs={{0,4},{4,8},{8,12},{12,0},{1,5},{5,9},{9,13},{13,1},{2,6},{6,10},{... | collective-permute-start | bytes 589832 | tf_op jit(solution)/shard_map/ppermute | solution.py:13
  8.3 20.3 %collective-permute-start.3 = (bf16[2,768,64]{1,2,0:T(8,128)(2,1)}, bf16[2,768,64]{1,2,0:T(8,128)(2,1)S(1)}, u32[]{:S(2)}, u32[]{:S(2)}) collective-permute-start(bf16[2,768,64]{1,2,0:T(8,128)(2,1)} %param.8), channel_id=1, source_target_pairs={{0,8},{4,12},{8,0},{12,4},{1,9},{5,13},{9,1},{13,5},{2,10},{6,14},... | collective-permute-start | bytes 589832 | tf_op jit(solution)/shard_map/ppermute | solution.py:13
  18.1 11.6 %collective-permute-start.5 = (bf16[2,768,64]{1,2,0:T(8,128)(2,1)}, bf16[2,768,64]{1,2,0:T(8,128)(2,1)S(1)}, u32[]{:S(2)}, u32[]{:S(2)}) collective-permute-start(bf16[2,768,64]{1,2,0:T(8,128)(2,1)} %param.8), channel_id=1, source_target_pairs={{0,12},{4,0},{8,4},{12,8},{1,13},{5,1},{9,5},{13,9},{2,14},{6,2},{... | collective-permute-start | bytes 589832 | tf_op jit(solution)/shard_map/ppermute | solution.py:13
  21.7 4.7 %copy-start.1 = (bf16[2,768,64]{1,2,0:T(8,128)(2,1)S(1)}, bf16[2,768,64]{1,2,0:T(8,128)(2,1)}, u32[]{:S(2)}) copy-start(bf16[2,768,64]{1,2,0:T(8,128)(2,1)} %param.8) | copy-start | bytes 589828
  29.7 1.2 %copy-start.3 = (bf16[2]{0:T(256)(128)(2,1)S(1)}, bf16[2]{0:T(256)(128)(2,1)}, u32[]{:S(2)}) copy-start(bf16[2]{0:T(256)(128)(2,1)} %constant.23.clone) | copy-start | bytes 16
  30.8 11.1 %copy-start.2 = (f32[64]{0:T(128)S(1)}, f32[64]{0:T(128)}, u32[]{:S(2)}) copy-start(f32[64]{0:T(128)} %param.10) | copy-start | bytes 772
  31.3 9.1 %collective-permute-start.6 = (f32[64,256]{1,0:T(8,128)S(1)}, f32[64,256]{1,0:T(8,128)S(1)}, u32[]{:S(2)}, u32[]{:S(2)}) collective-permute-start(f32[64,256]{1,0:T(8,128)S(1)} %convolution_bitcast_fusion), channel_id=1, source_target_pairs={{0,4},{4,0},{8,12},{12,8},{1,5},{5,1},{9,13},{13,9},{2,6},{6,2},{1... | collective-permute-start | bytes 196616 | tf_op jit(solution)/shard_map/ppermute | solution.py:21
  40.4 6.7 %collective-permute-start.7 = (f32[64,256]{1,0:T(8,128)S(1)}, f32[64,256]{1,0:T(8,128)S(1)}, u32[]{:S(2)}, u32[]{:S(2)}) collective-permute-start(f32[64,256]{1,0:T(8,128)S(1)} %add.45), channel_id=1, source_target_pairs={{0,8},{4,12},{8,0},{12,4},{1,9},{5,13},{9,1},{13,5},{2,10},{6,14},... | collective-permute-start | bytes 196616 | tf_op jit(solution)/shard_map/ppermute | solution.py:21

commit v2 on v1

--- a/solution.py
+++ b/solution.py
@@ -13,7 +13,13 @@
     return lax.ppermute(x, axis, [(i, (i + k) % n) for i in range(n)])
 
 
-def butterfly_sum(x, axis, n):
+def sum_over(x, axis, n):
+    if n == 4:
+        got = [shift(x, axis, k, n) for k in range(1, n)]
+        even = lax.axis_index(axis) % 2 == 0
+        first = x + jnp.where(even, got[2], got[0])
+        second = got[1] + jnp.where(even, got[0], got[2])
+        return first + second
     if n & (n - 1):
         return lax.psum(x, axis)
     step = 1
@@ -27,9 +33,11 @@
     n_rows = coords.shape[1]
     local_tasks = vectors.shape[2]
     n_dp = lax.axis_size("dp")
+    n_task = lax.axis_size("task")
+    task_index = lax.axis_index("task")
     inverse = 1.0 / lengthscales
     own_scaled = coords.astype(jnp.float32) * inverse[:, None]
-    task_start = lax.axis_index("task") * local_tasks
+    task_start = task_index * local_tasks
 
     def block(right_coords, values):
         right = right_coords.astype(jnp.float32) * inverse[:, None]
@@ -49,7 +57,10 @@
             return accum + block(right_coords, values), right_coords, values
 
         summed = lax.fori_loop(0, n_dp - 1, ring, (summed, coords, vectors))[0]
-    whole_vectors = lax.all_gather(vectors, "task", axis=2, tiled=True)
+
+    task_blocks = [(task_index, vectors)]
+    for k in range(1, n_task):
+        task_blocks.append(((task_index - k) % n_task, shift(vectors, "task", k, n_task)))
     images = summed.astype(jnp.bfloat16)
     whole_images = lax.all_gather(images, "task", axis=2, tiled=True)
     own_rows = lax.dynamic_slice_in_dim(mixing, task_start, local_tasks, 0)
@@ -57,10 +68,13 @@
     product = (mixed + noise[None, None, :] * vectors.astype(jnp.float32)).astype(jnp.bfloat16)
     signs = jnp.array([1.0, -1.0], jnp.bfloat16)
     signed = images * signs[:, None, None]
-    partial_grad = jnp.einsum(
-        "sna,snb->ab", signed, whole_vectors, preferred_element_type=jnp.float32
-    )
-    total = butterfly_sum(partial_grad, "dp", n_dp)
+    partial_grad = jnp.zeros((local_tasks, n_task * local_tasks), jnp.float32)
+    for source, values in task_blocks:
+        piece = jnp.einsum("sna,snb->ab", signed, values, preferred_element_type=jnp.float32)
+        partial_grad = lax.dynamic_update_slice_in_dim(
+            partial_grad, piece, source * local_tasks, 1
+        )
+    total = sum_over(partial_grad, "dp", n_dp)
     gradient = total / (2.0 * n_rows * n_dp)
     return (product, gradient)
 

time: 47.9 us -> 51.7 us (1.079)
  blocking collectives: 17.2 us -> 8.74 us
  starting transfers between devices: 13 us -> 17.9 us
  waiting for transfers between devices: 4.25 us -> 9.04 us
  local copies, waits for them, and re-layouts: 0.02 us -> 1.83 us
  matrix products: 5.69 us -> 6.33 us
    ppermute x6 -> x12, waiting for transfers between devices: 0.02 us -> 9.04 us  [shift(): return lax.ppermute(x, axis, [(i, (i + k) % n) for i in range(n)])]
    all_gather x1 -> x0, blocking collectives: 8.79 us -> none  [per_device(): whole_vectors = lax.all_gather(vectors, 'task', axis=2, tiled=True)]
    ppermute x6 -> x12, starting transfers between devices: 10.8 us -> 17.9 us  [shift(): return lax.ppermute(x, axis, [(i, (i + k) % n) for i in range(n)])]
    ppermute x2 -> x0, waiting for transfers between devices: 4.23 us -> none  [butterfly_sum(): x = x + lax.ppermute(x, axis, [(i, i ^ step) for i in range(n)])]
    ppermute x2 -> x0, starting transfers between devices: 2.18 us -> none  [butterfly_sum(): x = x + lax.ppermute(x, axis, [(i, i ^ step) for i in range(n)])]
    dynamic_update_slice x0 -> x4, local copies, waits for them, and re-layouts: none -> 1.8 us  [per_device(): lax.dynamic_update_slice_in_dim(partial_grad, piece, source * local_tasks...]
    dot_general x1 -> x4, matrix products: 0.36 us -> 1.02 us  [per_device(): jnp.einsum('sna,snb->ab', signed, values, preferred_element_type=jnp.floa...]
  transfers between devices with their start and end apart: 8 -> 12, of which waited for: 1 -> 3; matrix products, arithmetic and copies ran while one was open for 22% -> 26% of each run, Pallas kernels for 0% -> 0%
where the time goes in v2:
time: 51.7 us; the launch traced here: 51.5 us
  starting transfers between devices  17.9 us (35%)
  waiting for transfers between devices  9.04 us (17%)
  blocking collectives  8.74 us (17%)
  other arithmetic  6.81 us (13%)
  matrix products  6.33 us (12%)
  local copies, waits for them, and re-layouts  1.83 us (4%)
  between operations  0.82 us (2%)
    ppermute x12, starting transfers between devices, shift(): return lax.ppermute(x, axis, [(i, (i + k) % n) for i in range(n)])  17.9 us
    ppermute x12, waiting for transfers between devices, shift(): return lax.ppermute(x, axis, [(i, (i + k) % n) for i in range(n)])  9.04 us
    all_gather x1, blocking collectives, per_device(): whole_images = lax.all_gather(images, 'task', axis=2, tiled=True)  8.74 us
    reduce_sum x1, other arithmetic, kernel_tile(): return jnp.exp(0.1 - jnp.sqrt(jnp.sum(diff * diff, axis=0) + 0.01))  4.65 us
    unnamed x4, matrix products  4.37 us
    dynamic_update_slice x4, local copies, waits for them, and re-layouts, per_device(): lax.dynamic_update_slice_in_dim(partial_grad, piece, source * local_tasks...  1.8 us
  transfers between devices with their start and end apart: 12, of which 3 were waited for; matrix products, arithmetic and copies ran while one was open for 26% of the time, Pallas kernels for 0%

profile of v2, /device:TPU:0, one launch (start us, length us, event | category | flops | bytes accessed | tf_op | source)
XLA Modules:
  0.0 51.5 jit_solution(7300909522001316579)
XLA Ops:
  0.6 5.1 %collective-permute-start.4 = (bf16[3,768]{1,0:T(4,128)(2,1)}, bf16[3,768]{1,0:T(4,128)(2,1)S(1)}, u32[]{:S(2)}, u32[]{:S(2)}) collective-permute-start(bf16[3,768]{1,0:T(4,128)(2,1)} %param.6), channel_id=1, source_target_pairs={{0,12},{4,0},{8,4},{12,8},{1,13},{5,1},{9,5},{13,9},{2,14},{6,2},{... | collective-permute-start | bytes 13832 | tf_op jit(solution)/shard_map/ppermute | solution.py:13
  5.8 1.0 %collective-permute-start.2 = (bf16[3,768]{1,0:T(4,128)(2,1)}, bf16[3,768]{1,0:T(4,128)(2,1)S(1)}, u32[]{:S(2)}, u32[]{:S(2)}) collective-permute-start(bf16[3,768]{1,0:T(4,128)(2,1)} %param.6), channel_id=1, source_target_pairs={{0,8},{4,12},{8,0},{12,4},{1,9},{5,13},{9,1},{13,5},{2,10},{6,14},... | collective-permute-start | bytes 13832 | tf_op jit(solution)/shard_map/ppermute | solution.py:13
  6.8 2.8 %collective-permute-start.5 = (bf16[2,768,64]{1,2,0:T(8,128)(2,1)}, bf16[2,768,64]{1,2,0:T(8,128)(2,1)S(1)}, u32[]{:S(2)}, u32[]{:S(2)}) collective-permute-start(bf16[2,768,64]{1,2,0:T(8,128)(2,1)} %param.8), channel_id=1, source_target_pairs={{0,12},{4,0},{8,4},{12,8},{1,13},{5,1},{9,5},{13,9},{2,14},{6,2},{... | collective-permute-start | bytes 589832 | tf_op jit(solution)/shard_map/ppermute | solution.py:13
  9.6 2.0 %collective-permute-start.3 = (bf16[2,768,64]{1,2,0:T(8,128)(2,1)}, bf16[2,768,64]{1,2,0:T(8,128)(2,1)S(1)}, u32[]{:S(2)}, u32[]{:S(2)}) collective-permute-start(bf16[2,768,64]{1,2,0:T(8,128)(2,1)} %param.8), channel_id=1, source_target_pairs={{0,8},{4,12},{8,0},{12,4},{1,9},{5,13},{9,1},{13,5},{2,10},{6,14},... | collective-permute-start | bytes 589832 | tf_op jit(solution)/shard_map/ppermute | solution.py:13
  11.6 0.7 %broadcast_divide_fusion = f32[3]{0:T(128)S(1)} fusion(f32[3]{0:T(128)} %param.7), kind=kLoop, calls=%fused_computation.36 | loop fusion | flops 3 | bytes 24 | tf_op jit(solution)/shard_map/div | solution.py:38
  12.3 1.6 %collective-permute-start.7 = (bf16[2,768,64]{1,2,0:T(8,128)(2,1)}, bf16[2,768,64]{1,2,0:T(8,128)(2,1)S(1)}, u32[]{:S(2)}, u32[]{:S(2)}) collective-permute-start(bf16[2,768,64]{1,2,0:T(8,128)(2,1)} %param.8), channel_id=1, source_target_pairs={{0,2},{1,3},{2,0},{3,1},{4,6},{5,7},{6,4},{7,5},{8,10},{9,11},{10,... | collective-permute-start | bytes 589832 | tf_op jit(solution)/shard_map/ppermute | solution.py:13
  13.9 0.8 %convert_multiply_fusion = (f32[3,768]{1,0:T(4,128)S(1)}, f32[3,768]{1,0:T(4,128)S(1)}, f32[3,768]{1,0:T(4,128)S(1)}, f32[3,768]{1,0:T(4,128)S(1)}) fusion(bf16[3,768]{1,0:T(4,128)(2,1)S(1)} %collective-permute-done.4, f32[3]{0:T(128)S(1)} %broadcast_divide_fusion, bf16[3,768]{1,0:T(4,128)(2,1)S(1)} %collective-permute-done, ...), kind=kLoop, calls=%fused_computation.31 | loop fusion | flops 18432 | bytes 55308 | tf_op jit(solution)/shard_map/mul | solution.py:43
  14.7 4.7 %multiply_reduce_fusion.2 = (f32[768,768]{1,0:T(8,128)S(1)}, f32[768,768]{1,0:T(8,128)S(1)}, f32[768,768]{1,0:T(8,128)S(1)}, f32[768,768]{1,0:T(8,128)S(1)}) fusion(f32[3,768]{1,0:T(4,128)S(1)} %get-tuple-element.7, f32[3,768]{1,0:T(4,128)S(1)} %get-tuple-element.9, f32[3,768]{1,0:T(4,128)S(1)} %get-tuple-element.8, f32[3,768]{1,0:T(4,128)S(1)} %get-tuple-element.6), kind=kLoop, calls=%fused_computation.2 | loop fusion | flops 18874368 | bytes 9474048 | tf_op jit(solution)/shard_map/reduce_sum | solution.py:9
  19.3 1.1 %fusion = f32[768,128]{0,1:S(1)} fusion(bf16[768,128]{0,1:T(8,128)(2,1)S(1)} %bitcast.38, f32[768,768]{1,0:T(8,128)S(1)} %get-tuple-element.5), kind=kOutput, calls=%fused_computation.9 | convolution fusion | flops 152764416 | bytes 2949120
  20.4 1.4 %collective-permute-start.8 = (bf16[2,768,64]{1,2,0:T(8,128)(2,1)S(1)}, bf16[2,768,64]{1,2,0:T(8,128)(2,1)S(1)}, u32[]{:S(2)}, u32[]{:S(2)}) collective-permute-start(bf16[2,768,64]{1,2,0:T(8,128)(2,1)S(1)} %copy-done.1), channel_id=1, source_target_pairs={{0,3},{1,0},{2,1},{3,2},{4,7},{5,4},{6,5},{7,6},{8,11},{9,8},{10,9... | collective-permute-start | bytes 589832 | tf_op jit(solution)/shard_map/ppermute | solution.py:13
  21.9 1.1 %fusion.3 = f32[768,128]{0,1:S(1)} fusion(bf16[768,128]{0,1:T(8,128)(2,1)S(1)} %bitcast.44, f32[768,768]{1,0:T(8,128)S(1)} %get-tuple-element.4), kind=kOutput, calls=%fused_computation.12 | convolution fusion | flops 152764416 | bytes 2949120
  23.0 5.4 %collective-permute-done.3 = bf16[2,768,64]{1,2,0:T(8,128)(2,1)S(1)} collective-permute-done((bf16[2,768,64]{1,2,0:T(8,128)(2,1)}, bf16[2,768,64]{1,2,0:T(8,128)(2,1)S(1)}, u32[]{:S(2)}, u32[]{:S(2)}) %collective-permute-start.3) | collective-permute-done | bytes 196640 | tf_op jit(solution)/shard_map/ppermute | solution.py:13
  28.3 1.1 %fusion.2 = f32[768,128]{0,1:S(1)} fusion(bf16[768,128]{0,1:T(8,128)(2,1)S(1)} %bitcast.43, f32[768,768]{1,0:T(8,128)S(1)} %get-tuple-element.3), kind=kOutput, calls=%fused_computation.11 | convolution fusion | flops 152764416 | bytes 2949120
  29.4 1.1 %fusion.1 = f32[768,128]{0,1:S(1)} fusion(bf16[768,128]{0,1:T(8,128)(2,1)S(1)} %bitcast.45, f32[768,768]{1,0:T(8,128)S(1)} %get-tuple-element.2), kind=kOutput, calls=%fused_computation.10 | convolution fusion | flops 152764416 | bytes 2949120
  30.9 0.4 dynamic_update_slice.12
  31.7 0.5 dynamic_update_slice.13
  32.7 8.7 %all_gather.3 = bf16[2,768,256]{1,2,0:T(8,128)(2,1)S(1)} all-gather(bf16[2,768,64]{1,2,0:T(8,128)(2,1)S(1)} %fusion.5), channel_id=1, replica_groups=mesh['groups'=2,'dp'=4,'task'=4] {'task'}, dimensions={2}, use_global_device_ids=true | all-gather | bytes 983040 | tf_op jit(solution)/shard_map/all_gather | solution.py:65
  41.7 0.6 %dynamic_update_slice.15 = f32[64,256]{1,0:T(8,128)S(1)} dynamic-update-slice(f32[64,256]{1,0:T(8,128)S(1)} %dynamic_update_slice.14, f32[64,64]{1,0:T(8,128)S(1)} %convolution_bitcast_fusion, s32[]{:T(128)} %constant.54.clone.1, s32[]{:T(128)S(6)} %select_n.50) | dynamic-update-slice | bytes 32772 | tf_op jit(solution)/shard_map/dynamic_update_slice | solution.py:74
  42.4 2.5 %collective-permute-start.10 = (f32[64,256]{1,0:T(8,128)S(1)}, f32[64,256]{1,0:T(8,128)S(1)}, u32[]{:S(2)}, u32[]{:S(2)}) collective-permute-start(f32[64,256]{1,0:T(8,128)S(1)} %dynamic_update_slice.15), channel_id=1, source_target_pairs={{0,4},{4,8},{8,12},{12,0},{1,5},{5,9},{9,13},{13,1},{2,6},{6,10},{... | collective-permute-start | bytes 196616 | tf_op jit(solution)/shard_map/ppermute | solution.py:13
  44.9 1.4 %collective-permute-start.9 = (f32[64,256]{1,0:T(8,128)S(1)}, f32[64,256]{1,0:T(8,128)S(1)}, u32[]{:S(2)}, u32[]{:S(2)}) collective-permute-start(f32[64,256]{1,0:T(8,128)S(1)} %dynamic_update_slice.15), channel_id=1, source_target_pairs={{0,12},{4,0},{8,4},{12,8},{1,13},{5,1},{9,5},{13,9},{2,14},{6,2},{... | collective-permute-start | bytes 196616 | tf_op jit(solution)/shard_map/ppermute | solution.py:13
  46.3 0.9 %fusion.4 = bf16[2,768,64]{1,2,0:T(8,128)(2,1)} fusion(bf16[2,768,256]{1,2,0:T(8,128)(2,1)S(1)} %all_gather.3, bf16[2,768,64]{1,2,0:T(8,128)(2,1)S(1)} %copy-done.1, f32[64]{0:T(128)S(1)} %copy-done.3, bf16[256,256]{1,0:T(8,128)(2,1)S(1)} %copy-done, s32[]{:T(128)S(6)} %select_n.44), kind=kOutput, calls=%fused_computation.13 | convolution fusion | flops 50724864 | bytes 1212932 | tf_op jit(solution)/shard_map/sna,ca->snc/dot_general | solution.py:67
  47.2 2.5 %collective-permute-done.11 = f32[64,256]{1,0:T(8,128)S(1)} collective-permute-done((f32[64,256]{1,0:T(8,128)S(1)}, f32[64,256]{1,0:T(8,128)S(1)}, u32[]{:S(2)}, u32[]{:S(2)}) %collective-permute-start.11) | collective-permute-done | bytes 65568 | tf_op jit(solution)/shard_map/ppermute | solution.py:13
  49.7 1.2 %collective-permute-done.9 = f32[64,256]{1,0:T(8,128)S(1)} collective-permute-done((f32[64,256]{1,0:T(8,128)S(1)}, f32[64,256]{1,0:T(8,128)S(1)}, u32[]{:S(2)}, u32[]{:S(2)}) %collective-permute-start.9) | collective-permute-done | bytes 65568 | tf_op jit(solution)/shard_map/ppermute | solution.py:13
  50.9 0.6 %add_multiply_fusion = f32[64,256]{1,0:T(8,128)} fusion(f32[64,256]{1,0:T(8,128)S(1)} %collective-permute-done.11, f32[64,256]{1,0:T(8,128)S(1)} %collective-permute-done.10, f32[64,256]{1,0:T(8,128)S(1)} %collective-permute-done.9, f32[64,256]{1,0:T(8,128)S(1)} %dynamic_update_slice.15, pred[]{:T(512)S(6)} %eq.8), kind=kLoop, calls=%fused_computation.28 | loop fusion | flops 98304 | bytes 327681 | tf_op jit(solution)/shard_map/div | solution.py:78
  (28 shorter events, 1.6 us)
Async XLA Ops:
  0.6 45.6 %copy-start = (bf16[256,256]{1,0:T(8,128)(2,1)S(1)}, bf16[256,256]{1,0:T(8,128)(2,1)}, u32[]{:S(2)}) copy-start(bf16[256,256]{1,0:T(8,128)(2,1)} %param.9) | copy-start | bytes 393220
  0.6 11.6 %collective-permute-start.4 = (bf16[3,768]{1,0:T(4,128)(2,1)}, bf16[3,768]{1,0:T(4,128)(2,1)S(1)}, u32[]{:S(2)}, u32[]{:S(2)}) collective-permute-start(bf16[3,768]{1,0:T(4,128)(2,1)} %param.6), channel_id=1, source_target_pairs={{0,12},{4,0},{8,4},{12,8},{1,13},{5,1},{9,5},{13,9},{2,14},{6,2},{... | collective-permute-start | bytes 13832 | tf_op jit(solution)/shard_map/ppermute | solution.py:13
  5.7 6.5 %collective-permute-start = (bf16[3,768]{1,0:T(4,128)(2,1)}, bf16[3,768]{1,0:T(4,128)(2,1)S(1)}, u32[]{:S(2)}, u32[]{:S(2)}) collective-permute-start(bf16[3,768]{1,0:T(4,128)(2,1)} %param.6), channel_id=1, source_target_pairs={{0,4},{4,8},{8,12},{12,0},{1,5},{5,9},{9,13},{13,1},{2,6},{6,10},{... | collective-permute-start | bytes 13832 | tf_op jit(solution)/shard_map/ppermute | solution.py:13
  5.8 6.6 %collective-permute-start.2 = (bf16[3,768]{1,0:T(4,128)(2,1)}, bf16[3,768]{1,0:T(4,128)(2,1)S(1)}, u32[]{:S(2)}, u32[]{:S(2)}) collective-permute-start(bf16[3,768]{1,0:T(4,128)(2,1)} %param.6), channel_id=1, source_target_pairs={{0,8},{4,12},{8,0},{12,4},{1,9},{5,13},{9,1},{13,5},{2,10},{6,14},... | collective-permute-start | bytes 13832 | tf_op jit(solution)/shard_map/ppermute | solution.py:13
  6.8 13.7 %collective-permute-start.5 = (bf16[2,768,64]{1,2,0:T(8,128)(2,1)}, bf16[2,768,64]{1,2,0:T(8,128)(2,1)S(1)}, u32[]{:S(2)}, u32[]{:S(2)}) collective-permute-start(bf16[2,768,64]{1,2,0:T(8,128)(2,1)} %param.8), channel_id=1, source_target_pairs={{0,12},{4,0},{8,4},{12,8},{1,13},{5,1},{9,5},{13,9},{2,14},{6,2},{... | collective-permute-start | bytes 589832 | tf_op jit(solution)/shard_map/ppermute | solution.py:13
  9.6 18.8 %collective-permute-start.3 = (bf16[2,768,64]{1,2,0:T(8,128)(2,1)}, bf16[2,768,64]{1,2,0:T(8,128)(2,1)S(1)}, u32[]{:S(2)}, u32[]{:S(2)}) collective-permute-start(bf16[2,768,64]{1,2,0:T(8,128)(2,1)} %param.8), channel_id=1, source_target_pairs={{0,8},{4,12},{8,0},{12,4},{1,9},{5,13},{9,1},{13,5},{2,10},{6,14},... | collective-permute-start | bytes 589832 | tf_op jit(solution)/shard_map/ppermute | solution.py:13
  12.3 17.2 %collective-permute-start.1 = (bf16[2,768,64]{1,2,0:T(8,128)(2,1)}, bf16[2,768,64]{1,2,0:T(8,128)(2,1)S(1)}, u32[]{:S(2)}, u32[]{:S(2)}) collective-permute-start(bf16[2,768,64]{1,2,0:T(8,128)(2,1)} %param.8), channel_id=1, source_target_pairs={{0,4},{4,8},{8,12},{12,0},{1,5},{5,9},{9,13},{13,1},{2,6},{6,10},{... | collective-permute-start | bytes 589832 | tf_op jit(solution)/shard_map/ppermute | solution.py:13
  12.3 19.1 %collective-permute-start.6 = (bf16[2,768,64]{1,2,0:T(8,128)(2,1)}, bf16[2,768,64]{1,2,0:T(8,128)(2,1)S(1)}, u32[]{:S(2)}, u32[]{:S(2)}) collective-permute-start(bf16[2,768,64]{1,2,0:T(8,128)(2,1)} %param.8), channel_id=1, source_target_pairs={{0,1},{1,2},{2,3},{3,0},{4,5},{5,6},{6,7},{7,4},{8,9},{9,10},{10,1... | collective-permute-start | bytes 589832 | tf_op jit(solution)/shard_map/ppermute | solution.py:13
  12.3 19.8 %collective-permute-start.7 = (bf16[2,768,64]{1,2,0:T(8,128)(2,1)}, bf16[2,768,64]{1,2,0:T(8,128)(2,1)S(1)}, u32[]{:S(2)}, u32[]{:S(2)}) collective-permute-start(bf16[2,768,64]{1,2,0:T(8,128)(2,1)} %param.8), channel_id=1, source_target_pairs={{0,2},{1,3},{2,0},{3,1},{4,6},{5,7},{6,4},{7,5},{8,10},{9,11},{10,... | collective-permute-start | bytes 589832 | tf_op jit(solution)/shard_map/ppermute | solution.py:13
  14.7 4.7 %copy-start.1 = (bf16[2,768,64]{1,2,0:T(8,128)(2,1)S(1)}, bf16[2,768,64]{1,2,0:T(8,128)(2,1)}, u32[]{:S(2)}) copy-start(bf16[2,768,64]{1,2,0:T(8,128)(2,1)} %param.8) | copy-start | bytes 589828
  20.4 21.0 %collective-permute-start.8 = (bf16[2,768,64]{1,2,0:T(8,128)(2,1)S(1)}, bf16[2,768,64]{1,2,0:T(8,128)(2,1)S(1)}, u32[]{:S(2)}, u32[]{:S(2)}) collective-permute-start(bf16[2,768,64]{1,2,0:T(8,128)(2,1)S(1)} %copy-done.1), channel_id=1, source_target_pairs={{0,3},{1,0},{2,1},{3,2},{4,7},{5,4},{6,5},{7,6},{8,11},{9,8},{10,9... | collective-permute-start | bytes 589832 | tf_op jit(solution)/shard_map/ppermute | solution.py:13
  29.4 1.2 %copy-start.2 = (bf16[2]{0:T(256)(128)(2,1)S(1)}, bf16[2]{0:T(256)(128)(2,1)}, u32[]{:S(2)}) copy-start(bf16[2]{0:T(256)(128)(2,1)} %constant.65.clone) | copy-start | bytes 16
  30.5 15.7 %copy-start.3 = (f32[64]{0:T(128)S(1)}, f32[64]{0:T(128)}, u32[]{:S(2)}) copy-start(f32[64]{0:T(128)} %param.10) | copy-start | bytes 772
  42.3 7.4 %collective-permute-start.11 = (f32[64,256]{1,0:T(8,128)S(1)}, f32[64,256]{1,0:T(8,128)S(1)}, u32[]{:S(2)}, u32[]{:S(2)}) collective-permute-start(f32[64,256]{1,0:T(8,128)S(1)} %dynamic_update_slice.15), channel_id=1, source_target_pairs={{0,8},{4,12},{8,0},{12,4},{1,9},{5,13},{9,1},{13,5},{2,10},{6,14},... | collective-permute-start | bytes 196616 | tf_op jit(solution)/shard_map/ppermute | solution.py:13
  42.4 7.3 %collective-permute-start.10 = (f32[64,256]{1,0:T(8,128)S(1)}, f32[64,256]{1,0:T(8,128)S(1)}, u32[]{:S(2)}, u32[]{:S(2)}) collective-permute-start(f32[64,256]{1,0:T(8,128)S(1)} %dynamic_update_slice.15), channel_id=1, source_target_pairs={{0,4},{4,8},{8,12},{12,0},{1,5},{5,9},{9,13},{13,1},{2,6},{6,10},{... | collective-permute-start | bytes 196616 | tf_op jit(solution)/shard_map/ppermute | solution.py:13
  44.9 6.0 %collective-permute-start.9 = (f32[64,256]{1,0:T(8,128)S(1)}, f32[64,256]{1,0:T(8,128)S(1)}, u32[]{:S(2)}, u32[]{:S(2)}) collective-permute-start(f32[64,256]{1,0:T(8,128)S(1)} %dynamic_update_slice.15), channel_id=1, source_target_pairs={{0,12},{4,0},{8,4},{12,8},{1,13},{5,1},{9,5},{13,9},{2,14},{6,2},{... | collective-permute-start | bytes 196616 | tf_op jit(solution)/shard_map/ppermute | solution.py:13

commit v3 on v2

--- a/solution.py
+++ b/solution.py
@@ -29,15 +29,24 @@
     return x
 
 
+def rows_to_owner(columns, axis, n, width):
+    me = lax.axis_index(axis)
+    pieces = []
+    for k in range(n):
+        rows = lax.dynamic_slice_in_dim(columns, ((me - k) % n) * width, width, 0)
+        pieces.append(rows if k == 0 else shift(rows, axis, -k, n))
+    ordered = jnp.concatenate(pieces + pieces, axis=1)
+    return lax.dynamic_slice_in_dim(ordered, ((n - me) % n) * width, n * width, 1)
+
+
 def per_device(coords, lengthscales, vectors, mixing, noise):
     n_rows = coords.shape[1]
     local_tasks = vectors.shape[2]
     n_dp = lax.axis_size("dp")
     n_task = lax.axis_size("task")
-    task_index = lax.axis_index("task")
+    task_start = lax.axis_index("task") * local_tasks
     inverse = 1.0 / lengthscales
     own_scaled = coords.astype(jnp.float32) * inverse[:, None]
-    task_start = task_index * local_tasks
 
     def block(right_coords, values):
         right = right_coords.astype(jnp.float32) * inverse[:, None]
@@ -46,8 +55,9 @@
 
     summed = block(coords, vectors)
     if n_dp <= 4:
+        moved = [shift(vectors, "dp", k, n_dp) for k in range(1, n_dp)]
         for k in range(1, n_dp):
-            summed = summed + block(shift(coords, "dp", k, n_dp), shift(vectors, "dp", k, n_dp))
+            summed = summed + block(shift(coords, "dp", k, n_dp), moved[k - 1])
     else:
 
         def ring(_, carry):
@@ -58,23 +68,18 @@
 
         summed = lax.fori_loop(0, n_dp - 1, ring, (summed, coords, vectors))[0]
 
-    task_blocks = [(task_index, vectors)]
-    for k in range(1, n_task):
-        task_blocks.append(((task_index - k) % n_task, shift(vectors, "task", k, n_task)))
     images = summed.astype(jnp.bfloat16)
     whole_images = lax.all_gather(images, "task", axis=2, tiled=True)
     own_rows = lax.dynamic_slice_in_dim(mixing, task_start, local_tasks, 0)
     mixed = jnp.einsum("sna,ca->snc", whole_images, own_rows, preferred_element_type=jnp.float32)
     product = (mixed + noise[None, None, :] * vectors.astype(jnp.float32)).astype(jnp.bfloat16)
     signs = jnp.array([1.0, -1.0], jnp.bfloat16)
-    signed = images * signs[:, None, None]
-    partial_grad = jnp.zeros((local_tasks, n_task * local_tasks), jnp.float32)
-    for source, values in task_blocks:
-        piece = jnp.einsum("sna,snb->ab", signed, values, preferred_element_type=jnp.float32)
-        partial_grad = lax.dynamic_update_slice_in_dim(
-            partial_grad, piece, source * local_tasks, 1
-        )
-    total = sum_over(partial_grad, "dp", n_dp)
+    signed = vectors * signs[:, None, None]
+    columns = jnp.einsum(
+        "sna,snb->ab", whole_images, signed, preferred_element_type=jnp.float32
+    )
+    columns = sum_over(columns, "dp", n_dp)
+    total = rows_to_owner(columns, "task", n_task, local_tasks)
     gradient = total / (2.0 * n_rows * n_dp)
     return (product, gradient)
 

time: 51.7 us -> 54.9 us (1.062)
  waiting for transfers between devices: 9.04 us -> 15.9 us
  starting transfers between devices: 17.9 us -> 16.6 us
  local copies, waits for them, and re-layouts: 1.83 us -> 0.95 us
  matrix products: 6.33 us -> 5.68 us
  other arithmetic: 6.81 us -> 6.21 us
    ppermute x12, waiting for transfers between devices: 9.04 us -> 15.9 us  [shift(): return lax.ppermute(x, axis, [(i, (i + k) % n) for i in range(n)])]
    dynamic_update_slice x4 -> x0, local copies, waits for them, and re-layouts: 1.8 us -> none  [per_device(): lax.dynamic_update_slice_in_dim(partial_grad, piece, source * local_tasks...]
    ppermute x12, starting transfers between devices: 17.9 us -> 16.6 us  [shift(): return lax.ppermute(x, axis, [(i, (i + k) % n) for i in range(n)])]
    unnamed x8 -> x15, local copies, waits for them, and re-layouts: 0.02 us -> 0.83 us
    dot_general x4 -> x1, matrix products: 1.02 us -> 0.36 us  [per_device(): jnp.einsum('sna,snb->ab', whole_images, signed, preferred_element_type=jn...]
    div x1, other arithmetic: 0.65 us -> 0.02 us  [per_device(): gradient = total / (2.0 * n_rows * n_dp)]
  transfers between devices with their start and end apart: 12 -> 12, of which waited for: 3 -> 5; matrix products, arithmetic and copies ran while one was open for 26% -> 19% of each run, Pallas kernels for 0% -> 0%
where the time goes in v3:
time: 54.9 us; the launch traced here: 54.7 us
  starting transfers between devices  16.6 us (30%)
  waiting for transfers between devices  15.9 us (29%)
  blocking collectives  8.6 us (16%)
  other arithmetic  6.21 us (11%)
  matrix products  5.68 us (10%)
  local copies, waits for them, and re-layouts  0.95 us (2%)
  between operations  0.77 us (1%)
    ppermute x12, starting transfers between devices, shift(): return lax.ppermute(x, axis, [(i, (i + k) % n) for i in range(n)])  16.6 us
    ppermute x12, waiting for transfers between devices, shift(): return lax.ppermute(x, axis, [(i, (i + k) % n) for i in range(n)])  15.9 us
    all_gather x1, blocking collectives, per_device(): whole_images = lax.all_gather(images, 'task', axis=2, tiled=True)  8.6 us
    reduce_sum x1, other arithmetic, kernel_tile(): return jnp.exp(0.1 - jnp.sqrt(jnp.sum(diff * diff, axis=0) + 0.01))  4.65 us
    unnamed x4, matrix products  4.38 us
  transfers between devices with their start and end apart: 12, of which 5 were waited for; matrix products, arithmetic and copies ran while one was open for 19% of the time, Pallas kernels for 0%

profile of v3, /device:TPU:0, one launch (start us, length us, event | category | flops | bytes accessed | tf_op | source)
XLA Modules:
  0.0 54.7 jit_solution(9136951681818556676)
XLA Ops:
  0.6 5.1 %collective-permute-start.4 = (bf16[3,768]{1,0:T(4,128)(2,1)}, bf16[3,768]{1,0:T(4,128)(2,1)S(1)}, u32[]{:S(2)}, u32[]{:S(2)}) collective-permute-start(bf16[3,768]{1,0:T(4,128)(2,1)} %param.6), channel_id=1, source_target_pairs={{0,12},{4,0},{8,4},{12,8},{1,13},{5,1},{9,5},{13,9},{2,14},{6,2},{... | collective-permute-start | bytes 13832 | tf_op jit(solution)/shard_map/ppermute | solution.py:13
  5.8 1.0 %collective-permute-start.2 = (bf16[3,768]{1,0:T(4,128)(2,1)}, bf16[3,768]{1,0:T(4,128)(2,1)S(1)}, u32[]{:S(2)}, u32[]{:S(2)}) collective-permute-start(bf16[3,768]{1,0:T(4,128)(2,1)} %param.6), channel_id=1, source_target_pairs={{0,8},{4,12},{8,0},{12,4},{1,9},{5,13},{9,1},{13,5},{2,10},{6,14},... | collective-permute-start | bytes 13832 | tf_op jit(solution)/shard_map/ppermute | solution.py:13
  6.8 2.8 %collective-permute-start.5 = (bf16[2,768,64]{1,2,0:T(8,128)(2,1)}, bf16[2,768,64]{1,2,0:T(8,128)(2,1)S(1)}, u32[]{:S(2)}, u32[]{:S(2)}) collective-permute-start(bf16[2,768,64]{1,2,0:T(8,128)(2,1)} %param.8), channel_id=1, source_target_pairs={{0,12},{4,0},{8,4},{12,8},{1,13},{5,1},{9,5},{13,9},{2,14},{6,2},{... | collective-permute-start | bytes 589832 | tf_op jit(solution)/shard_map/ppermute | solution.py:13
  9.6 2.0 %collective-permute-start.3 = (bf16[2,768,64]{1,2,0:T(8,128)(2,1)}, bf16[2,768,64]{1,2,0:T(8,128)(2,1)S(1)}, u32[]{:S(2)}, u32[]{:S(2)}) collective-permute-start(bf16[2,768,64]{1,2,0:T(8,128)(2,1)} %param.8), channel_id=1, source_target_pairs={{0,8},{4,12},{8,0},{12,4},{1,9},{5,13},{9,1},{13,5},{2,10},{6,14},... | collective-permute-start | bytes 589832 | tf_op jit(solution)/shard_map/ppermute | solution.py:13
  11.6 0.7 %broadcast_divide_fusion = f32[3]{0:T(128)S(1)} fusion(f32[3]{0:T(128)} %param.7), kind=kLoop, calls=%fused_computation.39 | loop fusion | flops 3 | bytes 24 | tf_op jit(solution)/shard_map/div | solution.py:48
  12.3 0.8 %convert_multiply_fusion = (f32[3,768]{1,0:T(4,128)S(1)}, f32[3,768]{1,0:T(4,128)S(1)}, f32[3,768]{1,0:T(4,128)S(1)}, f32[3,768]{1,0:T(4,128)S(1)}) fusion(bf16[3,768]{1,0:T(4,128)(2,1)S(1)} %collective-permute-done.4, f32[3]{0:T(128)S(1)} %broadcast_divide_fusion, bf16[3,768]{1,0:T(4,128)(2,1)S(1)} %collective-permute-done, ...), kind=kLoop, calls=%fused_computation.31 | loop fusion | flops 18432 | bytes 55308 | tf_op jit(solution)/shard_map/mul | solution.py:52
  13.1 4.7 %multiply_reduce_fusion.2 = (f32[768,768]{1,0:T(8,128)S(1)}, f32[768,768]{1,0:T(8,128)S(1)}, f32[768,768]{1,0:T(8,128)S(1)}, f32[768,768]{1,0:T(8,128)S(1)}) fusion(f32[3,768]{1,0:T(4,128)S(1)} %get-tuple-element.15, f32[3,768]{1,0:T(4,128)S(1)} %get-tuple-element.17, f32[3,768]{1,0:T(4,128)S(1)} %get-tuple-element.16, f32[3,768]{1,0:T(4,128)S(1)} %get-tuple-element.14), kind=kLoop, calls=%fused_computation.2 | loop fusion | flops 18874368 | bytes 9474048 | tf_op jit(solution)/shard_map/reduce_sum | solution.py:9
  17.7 1.1 %fusion = f32[768,128]{0,1:S(1)} fusion(bf16[768,128]{0,1:T(8,128)(2,1)S(1)} %bitcast.29, f32[768,768]{1,0:T(8,128)S(1)} %get-tuple-element.9), kind=kOutput, calls=%fused_computation.9 | convolution fusion | flops 152764416 | bytes 2949120
  18.8 1.1 %fusion.3 = f32[768,128]{0,1:S(1)} fusion(bf16[768,128]{0,1:T(8,128)(2,1)S(1)} %bitcast.36, f32[768,768]{1,0:T(8,128)S(1)} %get-tuple-element.8), kind=kOutput, calls=%fused_computation.12 | convolution fusion | flops 152764416 | bytes 2949120
  19.9 8.4 %collective-permute-done.3 = bf16[2,768,64]{1,2,0:T(8,128)(2,1)S(1)} collective-permute-done((bf16[2,768,64]{1,2,0:T(8,128)(2,1)}, bf16[2,768,64]{1,2,0:T(8,128)(2,1)S(1)}, u32[]{:S(2)}, u32[]{:S(2)}) %collective-permute-start.3) | collective-permute-done | bytes 196640 | tf_op jit(solution)/shard_map/ppermute | solution.py:13
  28.3 1.1 %fusion.2 = f32[768,128]{0,1:S(1)} fusion(bf16[768,128]{0,1:T(8,128)(2,1)S(1)} %bitcast.34, f32[768,768]{1,0:T(8,128)S(1)} %get-tuple-element.7), kind=kOutput, calls=%fused_computation.11 | convolution fusion | flops 152764416 | bytes 2949120
  29.4 1.1 %fusion.1 = f32[768,128]{0,1:S(1)} fusion(bf16[768,128]{0,1:T(8,128)(2,1)S(1)} %bitcast.35, f32[768,768]{1,0:T(8,128)S(1)} %get-tuple-element.6), kind=kOutput, calls=%fused_computation.10 | convolution fusion | flops 152764416 | bytes 2949120
  30.6 8.6 %all_gather.3 = bf16[2,768,256]{1,2,0:T(8,128)(2,1)S(1)} all-gather(bf16[2,768,64]{1,2,0:T(8,128)(2,1)S(1)} %fusion.5), channel_id=1, replica_groups=mesh['groups'=2,'dp'=4,'task'=4] {'task'}, dimensions={2}, use_global_device_ids=true | all-gather | bytes 983040 | tf_op jit(solution)/shard_map/all_gather | solution.py:72
  39.2 0.4 convolution_bitcast_fusion
  39.7 0.5 collective-permute-start.7
  40.2 3.3 %collective-permute-start.6 = (f32[256,64]{0,1:T(8,128)S(1)}, f32[256,64]{0,1:T(8,128)S(1)}, u32[]{:S(2)}, u32[]{:S(2)}) collective-permute-start(f32[256,64]{0,1:T(8,128)S(1)} %convolution_bitcast_fusion), channel_id=1, source_target_pairs={{0,12},{4,0},{8,4},{12,8},{1,13},{5,1},{9,5},{13,9},{2,14},{6,2},{... | collective-permute-start | bytes 196616 | tf_op jit(solution)/shard_map/ppermute | solution.py:13
  43.6 3.1 %collective-permute-done.8 = f32[256,64]{0,1:T(8,128)S(1)} collective-permute-done((f32[256,64]{0,1:T(8,128)S(1)}, f32[256,64]{0,1:T(8,128)S(1)}, u32[]{:S(2)}, u32[]{:S(2)}) %collective-permute-start.8) | collective-permute-done | bytes 65568 | tf_op jit(solution)/shard_map/ppermute | solution.py:13
  46.7 1.0 %collective-permute-done.6 = f32[256,64]{0,1:T(8,128)S(1)} collective-permute-done((f32[256,64]{0,1:T(8,128)S(1)}, f32[256,64]{0,1:T(8,128)S(1)}, u32[]{:S(2)}, u32[]{:S(2)}) %collective-permute-start.6) | collective-permute-done | bytes 65568 | tf_op jit(solution)/shard_map/ppermute | solution.py:13
  47.9 0.2 collective-permute-start.9
  48.1 0.9 %fusion.4 = bf16[2,768,64]{1,2,0:T(8,128)(2,1)} fusion(bf16[2,768,256]{1,2,0:T(8,128)(2,1)S(1)} %all_gather.3, bf16[2,768,64]{1,2,0:T(8,128)(2,1)S(1)} %copy-done.1, f32[64]{0:T(128)S(1)} %copy-done.2, bf16[256,256]{1,0:T(8,128)(2,1)S(1)} %copy-done, s32[]{:T(128)S(6)} %select_n.57), kind=kOutput, calls=%fused_computation.13 | convolution fusion | flops 50724864 | bytes 1212932 | tf_op jit(solution)/shard_map/sna,ca->snc/dot_general | solution.py:74
  49.0 1.5 %collective-permute-start.10 = (f32[64,64]{0,1:T(8,128)S(1)}, f32[64,64]{0,1:T(8,128)S(1)}, u32[]{:S(2)}, u32[]{:S(2)}) collective-permute-start(f32[64,64]{0,1:T(8,128)S(1)} %get-tuple-element.12), channel_id=1, source_target_pairs={{0,2},{1,3},{2,0},{3,1},{4,6},{5,7},{6,4},{7,5},{8,10},{9,11},{10,... | collective-permute-start | bytes 49160 | tf_op jit(solution)/shard_map/ppermute | solution.py:13
  50.5 2.4 %collective-permute-done.10 = f32[64,64]{0,1:T(8,128)S(1)} collective-permute-done((f32[64,64]{0,1:T(8,128)S(1)}, f32[64,64]{0,1:T(8,128)S(1)}, u32[]{:S(2)}, u32[]{:S(2)}) %collective-permute-start.10) | collective-permute-done | bytes 16416 | tf_op jit(solution)/shard_map/ppermute | solution.py:13
  53.0 0.9 %collective-permute-done.11 = f32[64,64]{0,1:T(8,128)S(1)} collective-permute-done((f32[64,64]{0,1:T(8,128)S(1)}, f32[64,64]{0,1:T(8,128)S(1)}, u32[]{:S(2)}, u32[]{:S(2)}) %collective-permute-start.11) | collective-permute-done | bytes 16416 | tf_op jit(solution)/shard_map/ppermute | solution.py:13
  54.0 0.7 %copy.9 = f32[64,256]{1,0:T(8,128)} copy(f32[64,256]{0,1:T(8,128)S(1)} %dynamic-slice_multiply_fusion) | data formatting | bytes 131072
  (30 shorter events, 0.5 us)
Async XLA Ops:
  0.6 47.5 %copy-start = (bf16[256,256]{1,0:T(8,128)(2,1)S(1)}, bf16[256,256]{1,0:T(8,128)(2,1)}, u32[]{:S(2)}) copy-start(bf16[256,256]{1,0:T(8,128)(2,1)} %param.9) | copy-start | bytes 393220
  0.6 11.6 %collective-permute-start.4 = (bf16[3,768]{1,0:T(4,128)(2,1)}, bf16[3,768]{1,0:T(4,128)(2,1)S(1)}, u32[]{:S(2)}, u32[]{:S(2)}) collective-permute-start(bf16[3,768]{1,0:T(4,128)(2,1)} %param.6), channel_id=1, source_target_pairs={{0,12},{4,0},{8,4},{12,8},{1,13},{5,1},{9,5},{13,9},{2,14},{6,2},{... | collective-permute-start | bytes 13832 | tf_op jit(solution)/shard_map/ppermute | solution.py:13
  5.7 6.5 %collective-permute-start = (bf16[3,768]{1,0:T(4,128)(2,1)}, bf16[3,768]{1,0:T(4,128)(2,1)S(1)}, u32[]{:S(2)}, u32[]{:S(2)}) collective-permute-start(bf16[3,768]{1,0:T(4,128)(2,1)} %param.6), channel_id=1, source_target_pairs={{0,4},{4,8},{8,12},{12,0},{1,5},{5,9},{9,13},{13,1},{2,6},{6,10},{... | collective-permute-start | bytes 13832 | tf_op jit(solution)/shard_map/ppermute | solution.py:13
  5.8 6.5 %collective-permute-start.2 = (bf16[3,768]{1,0:T(4,128)(2,1)}, bf16[3,768]{1,0:T(4,128)(2,1)S(1)}, u32[]{:S(2)}, u32[]{:S(2)}) collective-permute-start(bf16[3,768]{1,0:T(4,128)(2,1)} %param.6), channel_id=1, source_target_pairs={{0,8},{4,12},{8,0},{12,4},{1,9},{5,13},{9,1},{13,5},{2,10},{6,14},... | collective-permute-start | bytes 13832 | tf_op jit(solution)/shard_map/ppermute | solution.py:13
  6.8 12.1 %collective-permute-start.5 = (bf16[2,768,64]{1,2,0:T(8,128)(2,1)}, bf16[2,768,64]{1,2,0:T(8,128)(2,1)S(1)}, u32[]{:S(2)}, u32[]{:S(2)}) collective-permute-start(bf16[2,768,64]{1,2,0:T(8,128)(2,1)} %param.8), channel_id=1, source_target_pairs={{0,12},{4,0},{8,4},{12,8},{1,13},{5,1},{9,5},{13,9},{2,14},{6,2},{... | collective-permute-start | bytes 589832 | tf_op jit(solution)/shard_map/ppermute | solution.py:13
  9.6 18.8 %collective-permute-start.3 = (bf16[2,768,64]{1,2,0:T(8,128)(2,1)}, bf16[2,768,64]{1,2,0:T(8,128)(2,1)S(1)}, u32[]{:S(2)}, u32[]{:S(2)}) collective-permute-start(bf16[2,768,64]{1,2,0:T(8,128)(2,1)} %param.8), channel_id=1, source_target_pairs={{0,8},{4,12},{8,0},{12,4},{1,9},{5,13},{9,1},{13,5},{2,10},{6,14},... | collective-permute-start | bytes 589832 | tf_op jit(solution)/shard_map/ppermute | solution.py:13
  12.3 17.2 %collective-permute-start.1 = (bf16[2,768,64]{1,2,0:T(8,128)(2,1)}, bf16[2,768,64]{1,2,0:T(8,128)(2,1)S(1)}, u32[]{:S(2)}, u32[]{:S(2)}) collective-permute-start(bf16[2,768,64]{1,2,0:T(8,128)(2,1)} %param.8), channel_id=1, source_target_pairs={{0,4},{4,8},{8,12},{12,0},{1,5},{5,9},{9,13},{13,1},{2,6},{6,10},{... | collective-permute-start | bytes 589832 | tf_op jit(solution)/shard_map/ppermute | solution.py:13
  13.1 4.7 %copy-start.1 = (bf16[2,768,64]{1,2,0:T(8,128)(2,1)S(1)}, bf16[2,768,64]{1,2,0:T(8,128)(2,1)}, u32[]{:S(2)}) copy-start(bf16[2,768,64]{1,2,0:T(8,128)(2,1)} %param.8) | copy-start | bytes 589828
  29.4 9.8 %copy-start.3 = (bf16[2]{0:T(256)(128)(2,1)S(1)}, bf16[2]{0:T(256)(128)(2,1)}, u32[]{:S(2)}) copy-start(bf16[2]{0:T(256)(128)(2,1)} %constant.74.clone) | copy-start | bytes 16
  30.5 17.6 %copy-start.2 = (f32[64]{0:T(128)S(1)}, f32[64]{0:T(128)}, u32[]{:S(2)}) copy-start(f32[64]{0:T(128)} %param.10) | copy-start | bytes 772
  39.6 7.1 %collective-permute-start.8 = (f32[256,64]{0,1:T(8,128)S(1)}, f32[256,64]{0,1:T(8,128)S(1)}, u32[]{:S(2)}, u32[]{:S(2)}) collective-permute-start(f32[256,64]{0,1:T(8,128)S(1)} %convolution_bitcast_fusion), channel_id=1, source_target_pairs={{0,8},{4,12},{8,0},{12,4},{1,9},{5,13},{9,1},{13,5},{2,10},{6,14},... | collective-permute-start | bytes 196616 | tf_op jit(solution)/shard_map/ppermute | solution.py:13
  39.7 7.0 %collective-permute-start.7 = (f32[256,64]{0,1:T(8,128)S(1)}, f32[256,64]{0,1:T(8,128)S(1)}, u32[]{:S(2)}, u32[]{:S(2)}) collective-permute-start(f32[256,64]{0,1:T(8,128)S(1)} %convolution_bitcast_fusion), channel_id=1, source_target_pairs={{0,4},{4,8},{8,12},{12,0},{1,5},{5,9},{9,13},{13,1},{2,6},{6,10},{... | collective-permute-start | bytes 196616 | tf_op jit(solution)/shard_map/ppermute | solution.py:13
  40.2 7.5 %collective-permute-start.6 = (f32[256,64]{0,1:T(8,128)S(1)}, f32[256,64]{0,1:T(8,128)S(1)}, u32[]{:S(2)}, u32[]{:S(2)}) collective-permute-start(f32[256,64]{0,1:T(8,128)S(1)} %convolution_bitcast_fusion), channel_id=1, source_target_pairs={{0,12},{4,0},{8,4},{12,8},{1,13},{5,1},{9,5},{13,9},{2,14},{6,2},{... | collective-permute-start | bytes 196616 | tf_op jit(solution)/shard_map/ppermute | solution.py:13
  47.9 2.7 %collective-permute-start.9 = (f32[64,64]{0,1:T(8,128)S(1)}, f32[64,64]{0,1:T(8,128)S(1)}, u32[]{:S(2)}, u32[]{:S(2)}) collective-permute-start(f32[64,64]{0,1:T(8,128)S(1)} %get-tuple-element.13), channel_id=1, source_target_pairs={{0,3},{1,0},{2,1},{3,2},{4,7},{5,4},{6,5},{7,6},{8,11},{9,8},{10,9... | collective-permute-start | bytes 49160 | tf_op jit(solution)/shard_map/ppermute | solution.py:13
  49.0 3.9 %collective-permute-start.10 = (f32[64,64]{0,1:T(8,128)S(1)}, f32[64,64]{0,1:T(8,128)S(1)}, u32[]{:S(2)}, u32[]{:S(2)}) collective-permute-start(f32[64,64]{0,1:T(8,128)S(1)} %get-tuple-element.12), channel_id=1, source_target_pairs={{0,2},{1,3},{2,0},{3,1},{4,6},{5,7},{6,4},{7,5},{8,10},{9,11},{10,... | collective-permute-start | bytes 49160 | tf_op jit(solution)/shard_map/ppermute | solution.py:13
  50.5 3.3 %collective-permute-start.11 = (f32[64,64]{0,1:T(8,128)S(1)}, f32[64,64]{0,1:T(8,128)S(1)}, u32[]{:S(2)}, u32[]{:S(2)}) collective-permute-start(f32[64,64]{0,1:T(8,128)S(1)} %get-tuple-element.10), channel_id=1, source_target_pairs={{0,1},{1,2},{2,3},{3,0},{4,5},{5,6},{6,7},{7,4},{8,9},{9,10},{10,1... | collective-permute-start | bytes 49160 | tf_op jit(solution)/shard_map/ppermute | solution.py:13

commit v4 on v1

--- a/solution.py
+++ b/solution.py
@@ -13,7 +13,13 @@
     return lax.ppermute(x, axis, [(i, (i + k) % n) for i in range(n)])
 
 
-def butterfly_sum(x, axis, n):
+def sum_over(x, axis, n):
+    if n == 4:
+        got = [shift(x, axis, k, n) for k in range(1, n)]
+        even = lax.axis_index(axis) % 2 == 0
+        first = x + jnp.where(even, got[2], got[0])
+        second = got[1] + jnp.where(even, got[0], got[2])
+        return first + second
     if n & (n - 1):
         return lax.psum(x, axis)
     step = 1
@@ -27,19 +33,20 @@
     n_rows = coords.shape[1]
     local_tasks = vectors.shape[2]
     n_dp = lax.axis_size("dp")
+    task_start = lax.axis_index("task") * local_tasks
     inverse = 1.0 / lengthscales
     own_scaled = coords.astype(jnp.float32) * inverse[:, None]
-    task_start = lax.axis_index("task") * local_tasks
 
     def block(right_coords, values):
         right = right_coords.astype(jnp.float32) * inverse[:, None]
         tile = kernel_tile(own_scaled, right).astype(jnp.bfloat16)
         return jnp.einsum("nr,srm->snm", tile, values, preferred_element_type=jnp.float32)
 
-    summed = block(coords, vectors)
     if n_dp <= 4:
+        moved = [shift(vectors, "dp", k, n_dp) for k in range(1, n_dp)]
+        summed = block(coords, vectors)
         for k in range(1, n_dp):
-            summed = summed + block(shift(coords, "dp", k, n_dp), shift(vectors, "dp", k, n_dp))
+            summed = summed + block(shift(coords, "dp", k, n_dp), moved[k - 1])
     else:
 
         def ring(_, carry):
@@ -48,19 +55,21 @@
             values = shift(values, "dp", 1, n_dp)
             return accum + block(right_coords, values), right_coords, values
 
+        summed = block(coords, vectors)
         summed = lax.fori_loop(0, n_dp - 1, ring, (summed, coords, vectors))[0]
+
     whole_vectors = lax.all_gather(vectors, "task", axis=2, tiled=True)
     images = summed.astype(jnp.bfloat16)
-    whole_images = lax.all_gather(images, "task", axis=2, tiled=True)
-    own_rows = lax.dynamic_slice_in_dim(mixing, task_start, local_tasks, 0)
-    mixed = jnp.einsum("sna,ca->snc", whole_images, own_rows, preferred_element_type=jnp.float32)
-    product = (mixed + noise[None, None, :] * vectors.astype(jnp.float32)).astype(jnp.bfloat16)
     signs = jnp.array([1.0, -1.0], jnp.bfloat16)
     signed = images * signs[:, None, None]
     partial_grad = jnp.einsum(
         "sna,snb->ab", signed, whole_vectors, preferred_element_type=jnp.float32
     )
-    total = butterfly_sum(partial_grad, "dp", n_dp)
+    total = sum_over(partial_grad, "dp", n_dp)
+    whole_images = lax.all_gather(jnp.transpose(images, (2, 0, 1)), "task", axis=0, tiled=True)
+    own_rows = lax.dynamic_slice_in_dim(mixing, task_start, local_tasks, 0)
+    mixed = jnp.einsum("asn,ca->snc", whole_images, own_rows, preferred_element_type=jnp.float32)
+    product = (mixed + noise[None, None, :] * vectors.astype(jnp.float32)).astype(jnp.bfloat16)
     gradient = total / (2.0 * n_rows * n_dp)
     return (product, gradient)
 

time: 47.9 us -> 46.2 us (0.965)
  waiting for transfers between devices: 4.25 us -> 0.42 us
  starting transfers between devices: 13 us -> 15.9 us
  blocking collectives: 17.2 us -> 16.4 us
    ppermute x6 -> x9, starting transfers between devices: 10.8 us -> 15.9 us  [shift(): return lax.ppermute(x, axis, [(i, (i + k) % n) for i in range(n)])]
    ppermute x2 -> x0, waiting for transfers between devices: 4.23 us -> none  [butterfly_sum(): x = x + lax.ppermute(x, axis, [(i, i ^ step) for i in range(n)])]
    ppermute x2 -> x0, starting transfers between devices: 2.18 us -> none  [butterfly_sum(): x = x + lax.ppermute(x, axis, [(i, i ^ step) for i in range(n)])]
    all_gather x1, blocking collectives: 8.43 us -> 7.62 us  [per_device(): lax.all_gather(jnp.transpose(images, (2, 0, 1)), 'task', axis=0, tiled=True)]
  transfers between devices with their start and end apart: 8 -> 9, of which waited for: 1 -> 1; matrix products, arithmetic and copies ran while one was open for 22% -> 22% of each run, Pallas kernels for 0% -> 0%
where the time goes in v4:
time: 46.2 us; the launch traced here: 46 us
  blocking collectives  16.4 us (35%)
  starting transfers between devices  15.9 us (34%)
  other arithmetic  6.82 us (15%)
  matrix products  5.69 us (12%)
  between operations  0.71 us (2%)
    ppermute x9, starting transfers between devices, shift(): return lax.ppermute(x, axis, [(i, (i + k) % n) for i in range(n)])  15.9 us
    all_gather x1, blocking collectives, per_device(): whole_vectors = lax.all_gather(vectors, 'task', axis=2, tiled=True)  8.79 us
    all_gather x1, blocking collectives, per_device(): lax.all_gather(jnp.transpose(images, (2, 0, 1)), 'task', axis=0, tiled=True)  7.62 us
    reduce_sum x1, other arithmetic, kernel_tile(): return jnp.exp(0.1 - jnp.sqrt(jnp.sum(diff * diff, axis=0) + 0.01))  4.65 us
    unnamed x4, matrix products  4.38 us
    dot_general x1, matrix products, per_device(): jnp.einsum('asn,ca->snc', whole_images, own_rows, preferred_element_type=...  0.94 us
  transfers between devices with their start and end apart: 9, of which 1 were waited for; matrix products, arithmetic and copies ran while one was open for 22% of the time, Pallas kernels for 0%

profile of v4, /device:TPU:0, one launch (start us, length us, event | category | flops | bytes accessed | tf_op | source)
XLA Modules:
  0.0 46.0 jit_solution(16352547767321226601)
XLA Ops:
  0.6 0.0 copy-start
  0.6 5.1 %collective-permute-start.4 = (bf16[3,768]{1,0:T(4,128)(2,1)}, bf16[3,768]{1,0:T(4,128)(2,1)S(1)}, u32[]{:S(2)}, u32[]{:S(2)}) collective-permute-start(bf16[3,768]{1,0:T(4,128)(2,1)} %param.6), channel_id=1, source_target_pairs={{0,12},{4,0},{8,4},{12,8},{1,13},{5,1},{9,5},{13,9},{2,14},{6,2},{... | collective-permute-start | bytes 13832 | tf_op jit(solution)/shard_map/ppermute | solution.py:13
  5.7 1.0 %collective-permute-start.2 = (bf16[3,768]{1,0:T(4,128)(2,1)}, bf16[3,768]{1,0:T(4,128)(2,1)S(1)}, u32[]{:S(2)}, u32[]{:S(2)}) collective-permute-start(bf16[3,768]{1,0:T(4,128)(2,1)} %param.6), channel_id=1, source_target_pairs={{0,8},{4,12},{8,0},{12,4},{1,9},{5,13},{9,1},{13,5},{2,10},{6,14},... | collective-permute-start | bytes 13832 | tf_op jit(solution)/shard_map/ppermute | solution.py:13
  6.8 2.8 %collective-permute-start.5 = (bf16[2,768,64]{1,2,0:T(8,128)(2,1)}, bf16[2,768,64]{1,2,0:T(8,128)(2,1)S(1)}, u32[]{:S(2)}, u32[]{:S(2)}) collective-permute-start(bf16[2,768,64]{1,2,0:T(8,128)(2,1)} %param.8), channel_id=1, source_target_pairs={{0,12},{4,0},{8,4},{12,8},{1,13},{5,1},{9,5},{13,9},{2,14},{6,2},{... | collective-permute-start | bytes 589832 | tf_op jit(solution)/shard_map/ppermute | solution.py:13
  9.6 2.0 %collective-permute-start.3 = (bf16[2,768,64]{1,2,0:T(8,128)(2,1)}, bf16[2,768,64]{1,2,0:T(8,128)(2,1)S(1)}, u32[]{:S(2)}, u32[]{:S(2)}) collective-permute-start(bf16[2,768,64]{1,2,0:T(8,128)(2,1)} %param.8), channel_id=1, source_target_pairs={{0,8},{4,12},{8,0},{12,4},{1,9},{5,13},{9,1},{13,5},{2,10},{6,14},... | collective-permute-start | bytes 589832 | tf_op jit(solution)/shard_map/ppermute | solution.py:13
  11.6 8.8 %all_gather.7 = bf16[2,768,256]{1,2,0:T(8,128)(2,1)S(1)} all-gather(bf16[2,768,64]{1,2,0:T(8,128)(2,1)} %param.8), channel_id=1, replica_groups=mesh['groups'=2,'dp'=4,'task'=4] {'task'}, dimensions={2}, use_global_device_ids=true | all-gather | bytes 983040 | tf_op jit(solution)/shard_map/all_gather | solution.py:61
  20.4 0.7 %broadcast_divide_fusion = f32[3]{0:T(128)S(1)} fusion(f32[3]{0:T(128)} %param.7), kind=kLoop, calls=%fused_computation.27 | loop fusion | flops 3 | bytes 24 | tf_op jit(solution)/shard_map/div | solution.py:37
  21.1 0.0 collective-permute-done.4
  21.1 0.0 collective-permute-done.2
  21.1 0.8 %convert_multiply_fusion = (f32[3,768]{1,0:T(4,128)S(1)}, f32[3,768]{1,0:T(4,128)S(1)}, f32[3,768]{1,0:T(4,128)S(1)}, f32[3,768]{1,0:T(4,128)S(1)}) fusion(bf16[3,768]{1,0:T(4,128)(2,1)S(1)} %collective-permute-done.4, f32[3]{0:T(128)S(1)} %broadcast_divide_fusion, bf16[3,768]{1,0:T(4,128)(2,1)S(1)} %collective-permute-done, ...), kind=kLoop, calls=%fused_computation.22 | loop fusion | flops 18432 | bytes 55308 | tf_op jit(solution)/shard_map/mul | solution.py:41
  21.9 4.7 %multiply_reduce_fusion.2 = (f32[768,768]{1,0:T(8,128)S(1)}, f32[768,768]{1,0:T(8,128)S(1)}, f32[768,768]{1,0:T(8,128)S(1)}, f32[768,768]{1,0:T(8,128)S(1)}) fusion(f32[3,768]{1,0:T(4,128)S(1)} %get-tuple-element.7, f32[3,768]{1,0:T(4,128)S(1)} %get-tuple-element.9, f32[3,768]{1,0:T(4,128)S(1)} %get-tuple-element.8, f32[3,768]{1,0:T(4,128)S(1)} %get-tuple-element.6), kind=kLoop, calls=%fused_computation.2 | loop fusion | flops 18874368 | bytes 9474048 | tf_op jit(solution)/shard_map/reduce_sum | solution.py:9
  26.5 1.1 %fusion = f32[768,128]{0,1:S(1)} fusion(bf16[768,128]{0,1:T(8,128)(2,1)S(1)} %bitcast.32, f32[768,768]{1,0:T(8,128)S(1)} %get-tuple-element.5), kind=kOutput, calls=%fused_computation.9 | convolution fusion | flops 152764416 | bytes 2949120
  27.6 1.1 %fusion.3 = f32[768,128]{0,1:S(1)} fusion(bf16[768,128]{0,1:T(8,128)(2,1)S(1)} %bitcast.38, f32[768,768]{1,0:T(8,128)S(1)} %get-tuple-element.4), kind=kOutput, calls=%fused_computation.12 | convolution fusion | flops 152764416 | bytes 2949120
  28.7 1.1 %fusion.2 = f32[768,128]{0,1:S(1)} fusion(bf16[768,128]{0,1:T(8,128)(2,1)S(1)} %bitcast.37, f32[768,768]{1,0:T(8,128)S(1)} %get-tuple-element.3), kind=kOutput, calls=%fused_computation.11 | convolution fusion | flops 152764416 | bytes 2949120
  29.8 0.4 collective-permute-done.1
  30.2 1.1 %fusion.1 = f32[768,128]{0,1:S(1)} fusion(bf16[768,128]{0,1:T(8,128)(2,1)S(1)} %bitcast.39, f32[768,768]{1,0:T(8,128)S(1)} %get-tuple-element.2), kind=kOutput, calls=%fused_computation.10 | convolution fusion | flops 152764416 | bytes 2949120
  31.3 0.1 add_convert_fusion
  31.4 0.4 convolution_bitcast_fusion
  31.8 1.1 %collective-permute-start.8 = (f32[64,256]{1,0:T(8,128)S(1)}, f32[64,256]{1,0:T(8,128)S(1)}, u32[]{:S(2)}, u32[]{:S(2)}) collective-permute-start(f32[64,256]{1,0:T(8,128)S(1)} %convolution_bitcast_fusion), channel_id=1, source_target_pairs={{0,8},{4,12},{8,0},{12,4},{1,9},{5,13},{9,1},{13,5},{2,10},{6,14},... | collective-permute-start | bytes 196616 | tf_op jit(solution)/shard_map/ppermute | solution.py:13
  32.9 2.9 %collective-permute-start.7 = (f32[64,256]{1,0:T(8,128)S(1)}, f32[64,256]{1,0:T(8,128)S(1)}, u32[]{:S(2)}, u32[]{:S(2)}) collective-permute-start(f32[64,256]{1,0:T(8,128)S(1)} %convolution_bitcast_fusion), channel_id=1, source_target_pairs={{0,4},{4,8},{8,12},{12,0},{1,5},{5,9},{9,13},{13,1},{2,6},{6,10},{... | collective-permute-start | bytes 196616 | tf_op jit(solution)/shard_map/ppermute | solution.py:13
  35.8 0.9 %collective-permute-start.6 = (f32[64,256]{1,0:T(8,128)S(1)}, f32[64,256]{1,0:T(8,128)S(1)}, u32[]{:S(2)}, u32[]{:S(2)}) collective-permute-start(f32[64,256]{1,0:T(8,128)S(1)} %convolution_bitcast_fusion), channel_id=1, source_target_pairs={{0,12},{4,0},{8,4},{12,8},{1,13},{5,1},{9,5},{13,9},{2,14},{6,2},{... | collective-permute-start | bytes 196616 | tf_op jit(solution)/shard_map/ppermute | solution.py:13
  36.8 7.6 %all_gather.6 = bf16[256,2,768]{2,0,1:T(8,128)(2,1)S(1)} all-gather(bf16[64,2,768]{2,0,1:T(8,128)(2,1)S(1)} %bitcast.31), channel_id=1, replica_groups=mesh['groups'=2,'dp'=4,'task'=4] {'task'}, dimensions={0}, use_global_device_ids=true | all-gather | bytes 983040 | tf_op jit(solution)/shard_map/all_gather | solution.py:69
  44.4 0.9 %fusion.4 = bf16[2,768,64]{1,2,0:T(8,128)(2,1)} fusion(bf16[256,2,768]{2,0,1:T(8,128)(2,1)S(1)} %all_gather.6, bf16[2,768,64]{1,2,0:T(8,128)(2,1)S(1)} %copy-done.1, f32[64]{0:T(128)S(1)} %copy-done.2, bf16[256,256]{1,0:T(8,128)(2,1)S(1)} %copy-done, s32[]{:T(128)S(6)} %select_n.22), kind=kOutput, calls=%fused_computation.13 | convolution fusion | flops 50724864 | bytes 1212932 | tf_op jit(solution)/shard_map/asn,ca->snc/dot_general | solution.py:71
  45.3 0.7 %add_multiply_fusion = f32[64,256]{1,0:T(8,128)} fusion(f32[64,256]{1,0:T(8,128)S(1)} %collective-permute-done.8, f32[64,256]{1,0:T(8,128)S(1)} %collective-permute-done.7, f32[64,256]{1,0:T(8,128)S(1)} %collective-permute-done.6, f32[64,256]{1,0:T(8,128)S(1)} %convolution_bitcast_fusion, pred[]{:T(512)S(6)} %eq.5), kind=kLoop, calls=%fused_computation.19 | loop fusion | flops 98304 | bytes 327681 | tf_op jit(solution)/shard_map/div | solution.py:73
  (15 shorter events, 0.0 us)
Async XLA Ops:
  0.6 43.7 %copy-start = (bf16[256,256]{1,0:T(8,128)(2,1)S(1)}, bf16[256,256]{1,0:T(8,128)(2,1)}, u32[]{:S(2)}) copy-start(bf16[256,256]{1,0:T(8,128)(2,1)} %param.9) | copy-start | bytes 393220
  0.6 20.4 %collective-permute-start.4 = (bf16[3,768]{1,0:T(4,128)(2,1)}, bf16[3,768]{1,0:T(4,128)(2,1)S(1)}, u32[]{:S(2)}, u32[]{:S(2)}) collective-permute-start(bf16[3,768]{1,0:T(4,128)(2,1)} %param.6), channel_id=1, source_target_pairs={{0,12},{4,0},{8,4},{12,8},{1,13},{5,1},{9,5},{13,9},{2,14},{6,2},{... | collective-permute-start | bytes 13832 | tf_op jit(solution)/shard_map/ppermute | solution.py:13
  5.7 15.3 %collective-permute-start = (bf16[3,768]{1,0:T(4,128)(2,1)}, bf16[3,768]{1,0:T(4,128)(2,1)S(1)}, u32[]{:S(2)}, u32[]{:S(2)}) collective-permute-start(bf16[3,768]{1,0:T(4,128)(2,1)} %param.6), channel_id=1, source_target_pairs={{0,4},{4,8},{8,12},{12,0},{1,5},{5,9},{9,13},{13,1},{2,6},{6,10},{... | collective-permute-start | bytes 13832 | tf_op jit(solution)/shard_map/ppermute | solution.py:13
  5.7 15.3 %collective-permute-start.2 = (bf16[3,768]{1,0:T(4,128)(2,1)}, bf16[3,768]{1,0:T(4,128)(2,1)S(1)}, u32[]{:S(2)}, u32[]{:S(2)}) collective-permute-start(bf16[3,768]{1,0:T(4,128)(2,1)} %param.6), channel_id=1, source_target_pairs={{0,8},{4,12},{8,0},{12,4},{1,9},{5,13},{9,1},{13,5},{2,10},{6,14},... | collective-permute-start | bytes 13832 | tf_op jit(solution)/shard_map/ppermute | solution.py:13
  6.8 20.9 %collective-permute-start.5 = (bf16[2,768,64]{1,2,0:T(8,128)(2,1)}, bf16[2,768,64]{1,2,0:T(8,128)(2,1)S(1)}, u32[]{:S(2)}, u32[]{:S(2)}) collective-permute-start(bf16[2,768,64]{1,2,0:T(8,128)(2,1)} %param.8), channel_id=1, source_target_pairs={{0,12},{4,0},{8,4},{12,8},{1,13},{5,1},{9,5},{13,9},{2,14},{6,2},{... | collective-permute-start | bytes 589832 | tf_op jit(solution)/shard_map/ppermute | solution.py:13
  9.6 19.1 %collective-permute-start.3 = (bf16[2,768,64]{1,2,0:T(8,128)(2,1)}, bf16[2,768,64]{1,2,0:T(8,128)(2,1)S(1)}, u32[]{:S(2)}, u32[]{:S(2)}) collective-permute-start(bf16[2,768,64]{1,2,0:T(8,128)(2,1)} %param.8), channel_id=1, source_target_pairs={{0,8},{4,12},{8,0},{12,4},{1,9},{5,13},{9,1},{13,5},{2,10},{6,14},... | collective-permute-start | bytes 589832 | tf_op jit(solution)/shard_map/ppermute | solution.py:13
  21.1 9.2 %collective-permute-start.1 = (bf16[2,768,64]{1,2,0:T(8,128)(2,1)}, bf16[2,768,64]{1,2,0:T(8,128)(2,1)S(1)}, u32[]{:S(2)}, u32[]{:S(2)}) collective-permute-start(bf16[2,768,64]{1,2,0:T(8,128)(2,1)} %param.8), channel_id=1, source_target_pairs={{0,4},{4,8},{8,12},{12,0},{1,5},{5,9},{9,13},{13,1},{2,6},{6,10},{... | collective-permute-start | bytes 589832 | tf_op jit(solution)/shard_map/ppermute | solution.py:13
  21.8 4.7 %copy-start.1 = (bf16[2,768,64]{1,2,0:T(8,128)(2,1)S(1)}, bf16[2,768,64]{1,2,0:T(8,128)(2,1)}, u32[]{:S(2)}) copy-start(bf16[2,768,64]{1,2,0:T(8,128)(2,1)} %param.8) | copy-start | bytes 589828
  30.2 1.2 %copy-start.3 = (bf16[2]{0:T(256)(128)(2,1)S(1)}, bf16[2]{0:T(256)(128)(2,1)}, u32[]{:S(2)}) copy-start(bf16[2]{0:T(256)(128)(2,1)} %constant.38.clone) | copy-start | bytes 16
  31.3 13.1 %copy-start.2 = (f32[64]{0:T(128)S(1)}, f32[64]{0:T(128)}, u32[]{:S(2)}) copy-start(f32[64]{0:T(128)} %param.10) | copy-start | bytes 772
  31.8 13.5 %collective-permute-start.8 = (f32[64,256]{1,0:T(8,128)S(1)}, f32[64,256]{1,0:T(8,128)S(1)}, u32[]{:S(2)}, u32[]{:S(2)}) collective-permute-start(f32[64,256]{1,0:T(8,128)S(1)} %convolution_bitcast_fusion), channel_id=1, source_target_pairs={{0,8},{4,12},{8,0},{12,4},{1,9},{5,13},{9,1},{13,5},{2,10},{6,14},... | collective-permute-start | bytes 196616 | tf_op jit(solution)/shard_map/ppermute | solution.py:13
  32.9 12.4 %collective-permute-start.7 = (f32[64,256]{1,0:T(8,128)S(1)}, f32[64,256]{1,0:T(8,128)S(1)}, u32[]{:S(2)}, u32[]{:S(2)}) collective-permute-start(f32[64,256]{1,0:T(8,128)S(1)} %convolution_bitcast_fusion), channel_id=1, source_target_pairs={{0,4},{4,8},{8,12},{12,0},{1,5},{5,9},{9,13},{13,1},{2,6},{6,10},{... | collective-permute-start | bytes 196616 | tf_op jit(solution)/shard_map/ppermute | solution.py:13
  35.8 9.5 %collective-permute-start.6 = (f32[64,256]{1,0:T(8,128)S(1)}, f32[64,256]{1,0:T(8,128)S(1)}, u32[]{:S(2)}, u32[]{:S(2)}) collective-permute-start(f32[64,256]{1,0:T(8,128)S(1)} %convolution_bitcast_fusion), channel_id=1, source_target_pairs={{0,12},{4,0},{8,4},{12,8},{1,13},{5,1},{9,5},{13,9},{2,14},{6,2},{... | collective-permute-start | bytes 196616 | tf_op jit(solution)/shard_map/ppermute | solution.py:13

commit v5 on v4

--- a/solution.py
+++ b/solution.py
@@ -1,12 +1,43 @@
 import jax
 import jax.numpy as jnp
 from jax import lax
+from jax.experimental import pallas as pl
+from jax.experimental.pallas import tpu as pltpu
 from jax.sharding import PartitionSpec as P
 
 
-def kernel_tile(left, right):
-    diff = left[:, :, None] - right[:, None, :]
-    return jnp.exp(0.1 - jnp.sqrt(jnp.sum(diff * diff, axis=0) + 0.01))
+def _block_kernel(rt_ref, l_ref, vt_ref, acc_ref, out_ref):
+    n_cols = l_ref.shape[1]
+    chunk = 256 if n_cols % 256 == 0 else n_cols
+    for start in range(0, n_cols, chunk):
+        cols = slice(start, start + chunk)
+        d2 = None
+        for c in range(rt_ref.shape[1]):
+            diff = rt_ref[:, c : c + 1] - l_ref[c : c + 1, cols]
+            d2 = diff * diff if d2 is None else d2 + diff * diff
+        kt = jnp.exp(0.1 - jnp.sqrt(d2 + 0.01)).astype(jnp.bfloat16)
+        for s in range(vt_ref.shape[0]):
+            out_ref[s, :, cols] = acc_ref[s, :, cols] + jnp.dot(
+                vt_ref[s], kt, preferred_element_type=jnp.float32
+            )
+
+
+def kernel_block(right_t, left, values_t, accum):
+    r, n = right_t.shape[0], left.shape[1]
+    s, t = values_t.shape[0], values_t.shape[1]
+    vmem = pltpu.MemorySpace.VMEM if hasattr(pltpu, "MemorySpace") else pltpu.TPUMemorySpace.VMEM
+    return pl.pallas_call(
+        _block_kernel,
+        out_shape=jax.ShapeDtypeStruct(accum.shape, jnp.float32),
+        in_specs=[pl.BlockSpec(memory_space=vmem)] * 4,
+        out_specs=pl.BlockSpec(memory_space=vmem),
+        input_output_aliases={3: 0},
+        cost_estimate=pl.CostEstimate(
+            flops=2 * s * t * r * n + 10 * r * n,
+            transcendentals=2 * r * n,
+            bytes_accessed=4 * (r * 3 + 3 * n) + 2 * s * t * r + 8 * s * t * n,
+        ),
+    )(right_t, left, values_t, accum)
 
 
 def shift(x, axis, k, n):
@@ -37,26 +68,27 @@
     inverse = 1.0 / lengthscales
     own_scaled = coords.astype(jnp.float32) * inverse[:, None]
 
-    def block(right_coords, values):
-        right = right_coords.astype(jnp.float32) * inverse[:, None]
-        tile = kernel_tile(own_scaled, right).astype(jnp.bfloat16)
-        return jnp.einsum("nr,srm->snm", tile, values, preferred_element_type=jnp.float32)
+    def block(accum, right_coords, values):
+        right_t = (right_coords.astype(jnp.float32) * inverse[:, None]).T
+        return kernel_block(right_t, own_scaled, jnp.swapaxes(values, 1, 2), accum)
 
+    empty = jnp.zeros((vectors.shape[0], local_tasks, n_rows), jnp.float32)
     if n_dp <= 4:
         moved = [shift(vectors, "dp", k, n_dp) for k in range(1, n_dp)]
-        summed = block(coords, vectors)
+        summed = block(empty, coords, vectors)
         for k in range(1, n_dp):
-            summed = summed + block(shift(coords, "dp", k, n_dp), moved[k - 1])
+            summed = block(summed, shift(coords, "dp", k, n_dp), moved[k - 1])
     else:
 
         def ring(_, carry):
             accum, right_coords, values = carry
             right_coords = shift(right_coords, "dp", 1, n_dp)
             values = shift(values, "dp", 1, n_dp)
-            return accum + block(right_coords, values), right_coords, values
+            return block(accum, right_coords, values), right_coords, values
 
-        summed = block(coords, vectors)
+        summed = block(empty, coords, vectors)
         summed = lax.fori_loop(0, n_dp - 1, ring, (summed, coords, vectors))[0]
+    summed = jnp.swapaxes(summed, 1, 2)
 
     whole_vectors = lax.all_gather(vectors, "task", axis=2, tiled=True)
     images = summed.astype(jnp.bfloat16)

time: 46.2 us -> 60.2 us (1.30)
  Pallas kernels: 0 us -> 17.3 us
  local copies, waits for them, and re-layouts: 0.02 us -> 6.65 us
  other arithmetic: 6.82 us -> 1.35 us
  matrix products: 5.69 us -> 2.37 us
  starting transfers between devices: 15.9 us -> 14.2 us
    pallas_call x0 -> x4, Pallas kernels: none -> 17.3 us  [kernel_block(): pl.pallas_call(_block_kernel, out_shape=jax.ShapeDtypeStruct(accum.shape,...]
    reduce_sum x1 -> x0, other arithmetic: 4.65 us -> none  [kernel_tile(): return jnp.exp(0.1 - jnp.sqrt(jnp.sum(diff * diff, axis=0) + 0.01))]
    unnamed x4 -> x0, matrix products: 4.38 us -> none
    transpose x0 -> x4, local copies, waits for them, and re-layouts: none -> 3.78 us  [block(): right_t = (right_coords.astype(jnp.float32) * inverse[:, None]).T]
    unnamed x8 -> x22, local copies, waits for them, and re-layouts: 0.02 us -> 2.07 us
    ppermute x9, starting transfers between devices: 15.9 us -> 14.2 us  [shift(): return lax.ppermute(x, axis, [(i, (i + k) % n) for i in range(n)])]
    dot_general x1, matrix products: 0.36 us -> 1.43 us  [per_device(): jnp.einsum('sna,snb->ab', signed, whole_vectors, preferred_element_type=j...]
    broadcast_in_dim x0 -> x1, local copies, waits for them, and re-layouts: none -> 0.79 us  [per_device(): empty = jnp.zeros((vectors.shape[0], local_tasks, n_rows), jnp.float32)]
  transfers between devices with their start and end apart: 9 -> 9, of which waited for: 1 -> 0; matrix products, arithmetic and copies ran while one was open for 22% -> 10% of each run, Pallas kernels for 0% -> 22%
where the time goes in v5:
time: 60.2 us; the launch traced here: 59.5 us
  Pallas kernels  17.3 us (29%)
  blocking collectives  16.8 us (28%)
  starting transfers between devices  14.2 us (24%)
  local copies, waits for them, and re-layouts  6.65 us (11%)
  matrix products  2.37 us (4%)
  other arithmetic  1.35 us (2%)
  between operations  0.73 us (1%)
    pallas_call x4, Pallas kernels, kernel_block(): pl.pallas_call(_block_kernel, out_shape=jax.ShapeDtypeStruct(accum.shape,...  17.3 us
    ppermute x9, starting transfers between devices, shift(): return lax.ppermute(x, axis, [(i, (i + k) % n) for i in range(n)])  14.2 us
    all_gather x1, blocking collectives, per_device(): whole_vectors = lax.all_gather(vectors, 'task', axis=2, tiled=True)  8.79 us
    all_gather x1, blocking collectives, per_device(): lax.all_gather(jnp.transpose(images, (2, 0, 1)), 'task', axis=0, tiled=True)  8.01 us
    transpose x4, local copies, waits for them, and re-layouts, block(): right_t = (right_coords.astype(jnp.float32) * inverse[:, None]).T  3.78 us
    unnamed x22, local copies, waits for them, and re-layouts  2.07 us
    dot_general x1, matrix products, per_device(): jnp.einsum('sna,snb->ab', signed, whole_vectors, preferred_element_type=j...  1.43 us
  transfers between devices with their start and end apart: 9, of which 0 were waited for; matrix products, arithmetic and copies ran while one was open for 10% of the time, Pallas kernels for 22%

profile of v5, /device:TPU:0, one launch (start us, length us, event | category | flops | bytes accessed | tf_op | source)
XLA Modules:
  0.0 59.5 jit_solution(10226080772603372766)
XLA Ops:
  0.7 5.1 %collective-permute-start = (bf16[3,768]{1,0:T(4,128)(2,1)}, bf16[3,768]{1,0:T(4,128)(2,1)S(1)}, u32[]{:S(2)}, u32[]{:S(2)}) collective-permute-start(bf16[3,768]{1,0:T(4,128)(2,1)} %param.6), channel_id=1, source_target_pairs={{0,12},{4,0},{8,4},{12,8},{1,13},{5,1},{9,5},{13,9},{2,14},{6,2},{... | collective-permute-start | bytes 13832 | tf_op jit(solution)/shard_map/ppermute | solution.py:44
  5.8 1.0 %collective-permute-start.4 = (bf16[3,768]{1,0:T(4,128)(2,1)}, bf16[3,768]{1,0:T(4,128)(2,1)S(1)}, u32[]{:S(2)}, u32[]{:S(2)}) collective-permute-start(bf16[3,768]{1,0:T(4,128)(2,1)} %param.6), channel_id=1, source_target_pairs={{0,4},{4,8},{8,12},{12,0},{1,5},{5,9},{9,13},{13,1},{2,6},{6,10},{... | collective-permute-start | bytes 13832 | tf_op jit(solution)/shard_map/ppermute | solution.py:44
  6.8 2.5 %collective-permute-start.5 = (bf16[2,768,64]{1,2,0:T(8,128)(2,1)}, bf16[2,768,64]{1,2,0:T(8,128)(2,1)S(1)}, u32[]{:S(2)}, u32[]{:S(2)}) collective-permute-start(bf16[2,768,64]{1,2,0:T(8,128)(2,1)} %param.8), channel_id=1, source_target_pairs={{0,4},{4,8},{8,12},{12,0},{1,5},{5,9},{9,13},{13,1},{2,6},{6,10},{... | collective-permute-start | bytes 589832 | tf_op jit(solution)/shard_map/ppermute | solution.py:44
  9.3 0.9 %collective-permute-start.3 = (bf16[2,768,64]{1,2,0:T(8,128)(2,1)}, bf16[2,768,64]{1,2,0:T(8,128)(2,1)S(1)}, u32[]{:S(2)}, u32[]{:S(2)}) collective-permute-start(bf16[2,768,64]{1,2,0:T(8,128)(2,1)} %param.8), channel_id=1, source_target_pairs={{0,8},{4,12},{8,0},{12,4},{1,9},{5,13},{9,1},{13,5},{2,10},{6,14},... | collective-permute-start | bytes 589832 | tf_op jit(solution)/shard_map/ppermute | solution.py:44
  10.2 8.8 %all_gather.7 = bf16[2,768,256]{1,2,0:T(8,128)(2,1)S(1)} all-gather(bf16[2,768,64]{1,2,0:T(8,128)(2,1)} %param.8), channel_id=1, replica_groups=mesh['groups'=2,'dp'=4,'task'=4] {'task'}, dimensions={2}, use_global_device_ids=true | all-gather | bytes 983040 | tf_op jit(solution)/shard_map/all_gather | solution.py:93
  19.0 1.5 %collective-permute-start.1 = (bf16[2,768,64]{1,2,0:T(8,128)(2,1)S(1)}, bf16[2,768,64]{1,2,0:T(8,128)(2,1)S(1)}, u32[]{:S(2)}, u32[]{:S(2)}) collective-permute-start(bf16[2,768,64]{1,2,0:T(8,128)(2,1)S(1)} %copy-done.2), channel_id=1, source_target_pairs={{0,12},{4,0},{8,4},{12,8},{1,13},{5,1},{9,5},{13,9},{2,14},{6,2},{... | collective-permute-start | bytes 589832 | tf_op jit(solution)/shard_map/ppermute | solution.py:44
  20.5 0.7 %fusion.8 = (f32[768,3]{0,1:T(4,128)S(1)}, f32[3,768]{1,0:T(4,128)}, f32[768,3]{0,1:T(4,128)S(1)}, f32[768,3]{0,1:T(4,128)S(1)}, f32[768,3]{0,1:T(4,128)S(1)}) fusion(f32[3]{0:T(128)S(1)} %broadcast_divide_fusion, bf16[3,768]{1,0:T(4,128)(2,1)S(1)} %copy-done.4, bf16[3,768]{1,0:T(4,128)(2,1)S(1)} %collective-permute-done.2, ...), kind=kLoop, calls=%fused_computation.17 | loop fusion | flops 18432 | bytes 64524 | tf_op jit(solution)/shard_map/transpose | solution.py:72
  21.2 0.9 %copy.12.rt_ref = f32[768,3]{1,0:T(8,128)} copy(f32[768,3]{0,1:T(4,128)S(1)} %get-tuple-element.2) | data formatting | bytes 18432 | tf_op jit(solution)/shard_map/transpose | solution.py:72
  22.2 1.0 %copy.13.rt_ref = f32[768,3]{1,0:T(8,128)} copy(f32[768,3]{0,1:T(4,128)S(1)} %get-tuple-element.5) | data formatting | bytes 18432 | tf_op jit(solution)/shard_map/transpose | solution.py:72
  23.1 0.9 %copy.14.rt_ref = f32[768,3]{1,0:T(8,128)} copy(f32[768,3]{0,1:T(4,128)S(1)} %get-tuple-element.4) | data formatting | bytes 18432 | tf_op jit(solution)/shard_map/transpose | solution.py:72
  24.1 0.9 %copy.15.rt_ref = f32[768,3]{1,0:T(8,128)} copy(f32[768,3]{0,1:T(4,128)S(1)} %get-tuple-element.6) | data formatting | bytes 18432 | tf_op jit(solution)/shard_map/transpose | solution.py:72
  25.0 0.8 %broadcast_in_dim.2.acc_ref = f32[2,64,768]{2,1,0:T(8,128)} broadcast(f32[]{:T(128)} %constant.25.clone.1), dimensions={} | broadcast | bytes 393220 | tf_op jit(solution)/shard_map/broadcast_in_dim | solution.py:75
  25.8 4.3 %shard_map.77.acc_ref = f32[2,64,768]{2,1,0:T(8,128)} custom-call(f32[768,3]{1,0:T(8,128)} %copy.12.rt_ref, f32[3,768]{1,0:T(4,128)} %get-tuple-element.3.l_ref, bf16[2,64,768]{2,1,0:T(8,128)(2,1)} %bitcast.24, f32[2,64,768]{2,1,0:T(8,128)} %broadcast_in_dim.2.acc_ref), custom_call_target="tpu_custom_call", output_to_operand_aliasing={{}: (3, {})} | custom-call | flops 156893184 | bytes 1001472 | tf_op jit(solution)/shard_map/pallas_call | solution.py:29
  30.1 0.7 %copy-done.8 = bf16[2,768,64]{1,2,0:T(8,128)(2,1)} copy-done((bf16[2,768,64]{1,2,0:T(8,128)(2,1)}, bf16[2,768,64]{1,2,0:T(8,128)(2,1)S(1)}, u32[]{:S(2)}) %copy-start.8) | copy-done | bytes 196632
  30.8 4.3 %shard_map.78.acc_ref = f32[2,64,768]{2,1,0:T(8,128)} custom-call(f32[768,3]{1,0:T(8,128)} %copy.13.rt_ref, f32[3,768]{1,0:T(4,128)} %get-tuple-element.3.l_ref, bf16[2,64,768]{2,1,0:T(8,128)(2,1)} %bitcast.26, f32[2,64,768]{2,1,0:T(8,128)} %shard_map.77.acc_ref), custom_call_target="tpu_custom_call", output_to_operand_aliasing={{}: (3, {})} | custom-call | flops 156893184 | bytes 1001472 | tf_op jit(solution)/shard_map/pallas_call | solution.py:29
  35.1 0.7 %copy-done.7 = bf16[2,768,64]{1,2,0:T(8,128)(2,1)} copy-done((bf16[2,768,64]{1,2,0:T(8,128)(2,1)}, bf16[2,768,64]{1,2,0:T(8,128)(2,1)S(1)}, u32[]{:S(2)}) %copy-start.7) | copy-done | bytes 196632
  35.8 4.3 %shard_map.79.acc_ref = f32[2,64,768]{2,1,0:T(8,128)} custom-call(f32[768,3]{1,0:T(8,128)} %copy.14.rt_ref, f32[3,768]{1,0:T(4,128)} %get-tuple-element.3.l_ref, bf16[2,64,768]{2,1,0:T(8,128)(2,1)} %bitcast.25, f32[2,64,768]{2,1,0:T(8,128)} %shard_map.78.acc_ref), custom_call_target="tpu_custom_call", output_to_operand_aliasing={{}: (3, {})} | custom-call | flops 156893184 | bytes 1001472 | tf_op jit(solution)/shard_map/pallas_call | solution.py:29
  40.1 0.7 %copy-done.9 = bf16[2,768,64]{1,2,0:T(8,128)(2,1)} copy-done((bf16[2,768,64]{1,2,0:T(8,128)(2,1)}, bf16[2,768,64]{1,2,0:T(8,128)(2,1)S(1)}, u32[]{:S(2)}) %copy-start.9) | copy-done | bytes 196632
  40.8 4.3 %shard_map.80 = f32[2,64,768]{2,1,0:T(8,128)} custom-call(f32[768,3]{1,0:T(8,128)} %copy.15.rt_ref, f32[3,768]{1,0:T(4,128)} %get-tuple-element.3.l_ref, bf16[2,64,768]{2,1,0:T(8,128)(2,1)} %bitcast.27, f32[2,64,768]{2,1,0:T(8,128)} %shard_map.79.acc_ref), custom_call_target="tpu_custom_call", output_to_operand_aliasing={{}: (3, {})} | custom-call | flops 156893184 | bytes 1001472 | tf_op jit(solution)/shard_map/pallas_call | solution.py:29
  45.2 1.4 %convolution_bitcast_fusion = f32[64,256]{1,0:T(8,128)S(1)} fusion(bf16[2,768,256]{1,2,0:T(8,128)(2,1)S(1)} %all_gather.7, bf16[2]{0:T(256)(128)(2,1)S(1)} %copy-done.6, f32[2,64,768]{2,1,0:T(8,128)} %shard_map.80), kind=kOutput, calls=%fused_computation.2 | convolution fusion | flops 50528256 | bytes 1245188 | tf_op jit(solution)/shard_map/sna,snb->ab/dot_general | solution.py:97
  46.6 2.0 %collective-permute-start.6 = (f32[64,256]{1,0:T(8,128)S(1)}, f32[64,256]{1,0:T(8,128)S(1)}, u32[]{:S(2)}, u32[]{:S(2)}) collective-permute-start(f32[64,256]{1,0:T(8,128)S(1)} %convolution_bitcast_fusion), channel_id=1, source_target_pairs={{0,12},{4,0},{8,4},{12,8},{1,13},{5,1},{9,5},{13,9},{2,14},{6,2},{... | collective-permute-start | bytes 196616 | tf_op jit(solution)/shard_map/ppermute | solution.py:44
  48.7 1.1 %collective-permute-start.8 = (f32[64,256]{1,0:T(8,128)S(1)}, f32[64,256]{1,0:T(8,128)S(1)}, u32[]{:S(2)}, u32[]{:S(2)}) collective-permute-start(f32[64,256]{1,0:T(8,128)S(1)} %convolution_bitcast_fusion), channel_id=1, source_target_pairs={{0,8},{4,12},{8,0},{12,4},{1,9},{5,13},{9,1},{13,5},{2,10},{6,14},... | collective-permute-start | bytes 196616 | tf_op jit(solution)/shard_map/ppermute | solution.py:44
  49.8 8.0 %all_gather.6 = bf16[256,2,768]{2,0,1:T(8,128)(2,1)S(1)} all-gather(bf16[64,2,768]{2,0,1:T(8,128)(2,1)S(1)} %convert_bitcast_fusion), channel_id=1, replica_groups=mesh['groups'=2,'dp'=4,'task'=4] {'task'}, dimensions={0}, use_global_device_ids=true | all-gather | bytes 983040 | tf_op jit(solution)/shard_map/all_gather | solution.py:101
  57.9 0.9 %fusion = bf16[2,768,64]{1,2,0:T(8,128)(2,1)} fusion(bf16[256,2,768]{2,0,1:T(8,128)(2,1)S(1)} %all_gather.6, bf16[2,768,64]{1,2,0:T(8,128)(2,1)S(1)} %copy-done.3, f32[64]{0:T(128)S(1)} %copy-done.5, bf16[256,256]{1,0:T(8,128)(2,1)S(1)} %copy-done, s32[]{:T(128)S(6)} %select_n.22), kind=kOutput, calls=%fused_computation.1 | convolution fusion | flops 50724864 | bytes 1212932 | tf_op jit(solution)/shard_map/asn,ca->snc/dot_general | solution.py:103
  (33 shorter events, 0.8 us)
Async XLA Ops:
  0.6 57.2 %copy-start = (bf16[256,256]{1,0:T(8,128)(2,1)S(1)}, bf16[256,256]{1,0:T(8,128)(2,1)}, u32[]{:S(2)}) copy-start(bf16[256,256]{1,0:T(8,128)(2,1)} %param.9) | copy-start | bytes 393220
  0.6 18.3 %copy-start.2 = (bf16[2,768,64]{1,2,0:T(8,128)(2,1)S(1)}, bf16[2,768,64]{1,2,0:T(8,128)(2,1)}, u32[]{:S(2)}) copy-start(bf16[2,768,64]{1,2,0:T(8,128)(2,1)} %param.8) | copy-start | bytes 589828
  0.7 18.3 %copy-start.10 = (f32[3]{0:T(128)S(1)}, f32[3]{0:T(128)}, u32[]{:S(2)}) copy-start(f32[3]{0:T(128)} %param.7) | copy-start | bytes 40
  0.7 18.3 %collective-permute-start = (bf16[3,768]{1,0:T(4,128)(2,1)}, bf16[3,768]{1,0:T(4,128)(2,1)S(1)}, u32[]{:S(2)}, u32[]{:S(2)}) collective-permute-start(bf16[3,768]{1,0:T(4,128)(2,1)} %param.6), channel_id=1, source_target_pairs={{0,12},{4,0},{8,4},{12,8},{1,13},{5,1},{9,5},{13,9},{2,14},{6,2},{... | collective-permute-start | bytes 13832 | tf_op jit(solution)/shard_map/ppermute | solution.py:44
  5.8 14.8 %collective-permute-start.2 = (bf16[3,768]{1,0:T(4,128)(2,1)}, bf16[3,768]{1,0:T(4,128)(2,1)S(1)}, u32[]{:S(2)}, u32[]{:S(2)}) collective-permute-start(bf16[3,768]{1,0:T(4,128)(2,1)} %param.6), channel_id=1, source_target_pairs={{0,8},{4,12},{8,0},{12,4},{1,9},{5,13},{9,1},{13,5},{2,10},{6,14},... | collective-permute-start | bytes 13832 | tf_op jit(solution)/shard_map/ppermute | solution.py:44
  5.8 14.8 %collective-permute-start.4 = (bf16[3,768]{1,0:T(4,128)(2,1)}, bf16[3,768]{1,0:T(4,128)(2,1)S(1)}, u32[]{:S(2)}, u32[]{:S(2)}) collective-permute-start(bf16[3,768]{1,0:T(4,128)(2,1)} %param.6), channel_id=1, source_target_pairs={{0,4},{4,8},{8,12},{12,0},{1,5},{5,9},{9,13},{13,1},{2,6},{6,10},{... | collective-permute-start | bytes 13832 | tf_op jit(solution)/shard_map/ppermute | solution.py:44
  6.8 23.3 %collective-permute-start.5 = (bf16[2,768,64]{1,2,0:T(8,128)(2,1)}, bf16[2,768,64]{1,2,0:T(8,128)(2,1)S(1)}, u32[]{:S(2)}, u32[]{:S(2)}) collective-permute-start(bf16[2,768,64]{1,2,0:T(8,128)(2,1)} %param.8), channel_id=1, source_target_pairs={{0,4},{4,8},{8,12},{12,0},{1,5},{5,9},{9,13},{13,1},{2,6},{6,10},{... | collective-permute-start | bytes 589832 | tf_op jit(solution)/shard_map/ppermute | solution.py:44
  9.3 25.9 %collective-permute-start.3 = (bf16[2,768,64]{1,2,0:T(8,128)(2,1)}, bf16[2,768,64]{1,2,0:T(8,128)(2,1)S(1)}, u32[]{:S(2)}, u32[]{:S(2)}) collective-permute-start(bf16[2,768,64]{1,2,0:T(8,128)(2,1)} %param.8), channel_id=1, source_target_pairs={{0,8},{4,12},{8,0},{12,4},{1,9},{5,13},{9,1},{13,5},{2,10},{6,14},... | collective-permute-start | bytes 589832 | tf_op jit(solution)/shard_map/ppermute | solution.py:44
  19.0 1.6 %copy-start.4 = (bf16[3,768]{1,0:T(4,128)(2,1)S(1)}, bf16[3,768]{1,0:T(4,128)(2,1)}, u32[]{:S(2)}) copy-start(bf16[3,768]{1,0:T(4,128)(2,1)} %param.6) | copy-start | bytes 13828
  19.0 21.1 %collective-permute-start.1 = (bf16[2,768,64]{1,2,0:T(8,128)(2,1)S(1)}, bf16[2,768,64]{1,2,0:T(8,128)(2,1)S(1)}, u32[]{:S(2)}, u32[]{:S(2)}) collective-permute-start(bf16[2,768,64]{1,2,0:T(8,128)(2,1)S(1)} %copy-done.2), channel_id=1, source_target_pairs={{0,12},{4,0},{8,4},{12,8},{1,13},{5,1},{9,5},{13,9},{2,14},{6,2},{... | collective-permute-start | bytes 589832 | tf_op jit(solution)/shard_map/ppermute | solution.py:44
  30.1 0.7 %copy-start.8 = (bf16[2,768,64]{1,2,0:T(8,128)(2,1)}, bf16[2,768,64]{1,2,0:T(8,128)(2,1)S(1)}, u32[]{:S(2)}) copy-start(bf16[2,768,64]{1,2,0:T(8,128)(2,1)S(1)} %collective-permute-done.5) | copy-start | bytes 589828
  35.1 0.7 %copy-start.7 = (bf16[2,768,64]{1,2,0:T(8,128)(2,1)}, bf16[2,768,64]{1,2,0:T(8,128)(2,1)S(1)}, u32[]{:S(2)}) copy-start(bf16[2,768,64]{1,2,0:T(8,128)(2,1)S(1)} %collective-permute-done.3) | copy-start | bytes 589828
  40.1 0.7 %copy-start.9 = (bf16[2,768,64]{1,2,0:T(8,128)(2,1)}, bf16[2,768,64]{1,2,0:T(8,128)(2,1)S(1)}, u32[]{:S(2)}) copy-start(bf16[2,768,64]{1,2,0:T(8,128)(2,1)S(1)} %collective-permute-done.1) | copy-start | bytes 589828
  40.8 4.3 %copy-start.6 = (bf16[2]{0:T(256)(128)(2,1)S(1)}, bf16[2]{0:T(256)(128)(2,1)}, u32[]{:S(2)}) copy-start(bf16[2]{0:T(256)(128)(2,1)} %constant.34.clone) | copy-start | bytes 16
  45.2 4.6 %copy-start.1 = (f32[2,64,768]{2,1,0:T(8,128)S(1)}, f32[2,64,768]{2,1,0:T(8,128)}, u32[]{:S(2)}) copy-start(f32[2,64,768]{2,1,0:T(8,128)} %shard_map.80) | copy-start | bytes 1179652
  46.6 12.2 %collective-permute-start.6 = (f32[64,256]{1,0:T(8,128)S(1)}, f32[64,256]{1,0:T(8,128)S(1)}, u32[]{:S(2)}, u32[]{:S(2)}) collective-permute-start(f32[64,256]{1,0:T(8,128)S(1)} %convolution_bitcast_fusion), channel_id=1, source_target_pairs={{0,12},{4,0},{8,4},{12,8},{1,13},{5,1},{9,5},{13,9},{2,14},{6,2},{... | collective-permute-start | bytes 196616 | tf_op jit(solution)/shard_map/ppermute | solution.py:44
  48.6 10.2 %collective-permute-start.7 = (f32[64,256]{1,0:T(8,128)S(1)}, f32[64,256]{1,0:T(8,128)S(1)}, u32[]{:S(2)}, u32[]{:S(2)}) collective-permute-start(f32[64,256]{1,0:T(8,128)S(1)} %convolution_bitcast_fusion), channel_id=1, source_target_pairs={{0,4},{4,8},{8,12},{12,0},{1,5},{5,9},{9,13},{13,1},{2,6},{6,10},{... | collective-permute-start | bytes 196616 | tf_op jit(solution)/shard_map/ppermute | solution.py:44
  48.7 10.2 %collective-permute-start.8 = (f32[64,256]{1,0:T(8,128)S(1)}, f32[64,256]{1,0:T(8,128)S(1)}, u32[]{:S(2)}, u32[]{:S(2)}) collective-permute-start(f32[64,256]{1,0:T(8,128)S(1)} %convolution_bitcast_fusion), channel_id=1, source_target_pairs={{0,8},{4,12},{8,0},{12,4},{1,9},{5,13},{9,1},{13,5},{2,10},{6,14},... | collective-permute-start | bytes 196616 | tf_op jit(solution)/shard_map/ppermute | solution.py:44
  49.8 8.0 %copy-start.3 = (bf16[2,768,64]{1,2,0:T(8,128)(2,1)S(1)}, bf16[2,768,64]{1,2,0:T(8,128)(2,1)}, u32[]{:S(2)}) copy-start(bf16[2,768,64]{1,2,0:T(8,128)(2,1)} %param.8) | copy-start | bytes 589828
  49.8 8.0 %copy-start.5 = (f32[64]{0:T(128)S(1)}, f32[64]{0:T(128)}, u32[]{:S(2)}) copy-start(f32[64]{0:T(128)} %param.10) | copy-start | bytes 772

commit v6 on v4

--- a/solution.py
+++ b/solution.py
@@ -58,7 +58,10 @@
         summed = block(coords, vectors)
         summed = lax.fori_loop(0, n_dp - 1, ring, (summed, coords, vectors))[0]
 
-    whole_vectors = lax.all_gather(vectors, "task", axis=2, tiled=True)
+    n_task = lax.axis_size("task")
+    task_index = lax.axis_index("task")
+    rotated = [vectors] + [shift(vectors, "task", -k, n_task) for k in range(1, n_task)]
+    whole_vectors = jnp.concatenate(rotated, axis=2)
     images = summed.astype(jnp.bfloat16)
     signs = jnp.array([1.0, -1.0], jnp.bfloat16)
     signed = images * signs[:, None, None]
@@ -70,6 +73,9 @@
     own_rows = lax.dynamic_slice_in_dim(mixing, task_start, local_tasks, 0)
     mixed = jnp.einsum("asn,ca->snc", whole_images, own_rows, preferred_element_type=jnp.float32)
     product = (mixed + noise[None, None, :] * vectors.astype(jnp.float32)).astype(jnp.bfloat16)
+    doubled = jnp.concatenate([total, total], axis=1)
+    start = ((n_task - task_index) % n_task) * local_tasks
+    total = lax.dynamic_slice_in_dim(doubled, start, n_task * local_tasks, 1)
     gradient = total / (2.0 * n_rows * n_dp)
     return (product, gradient)
 

time: 46.2 us -> 48.6 us (1.052)
  blocking collectives: 16.4 us -> 8.33 us
  waiting for transfers between devices: 0.42 us -> 5.87 us
  starting transfers between devices: 15.9 us -> 19.4 us
  local copies, waits for them, and re-layouts: 0.02 us -> 1.18 us
    all_gather x1 -> x0, blocking collectives: 8.79 us -> none  [per_device(): whole_vectors = lax.all_gather(vectors, 'task', axis=2, tiled=True)]
    ppermute x9 -> x12, waiting for transfers between devices: 0.42 us -> 5.87 us  [shift(): return lax.ppermute(x, axis, [(i, (i + k) % n) for i in range(n)])]
    ppermute x9 -> x12, starting transfers between devices: 15.9 us -> 19.4 us  [shift(): return lax.ppermute(x, axis, [(i, (i + k) % n) for i in range(n)])]
    unnamed x8 -> x9, local copies, waits for them, and re-layouts: 0.02 us -> 1.18 us
    all_gather x1, blocking collectives: 7.62 us -> 8.33 us  [per_device(): lax.all_gather(jnp.transpose(images, (2, 0, 1)), 'task', axis=0, tiled=True)]
  transfers between devices with their start and end apart: 9 -> 12, of which waited for: 1 -> 2; matrix products, arithmetic and copies ran while one was open for 22% -> 26% of each run, Pallas kernels for 0% -> 0%
where the time goes in v6:
time: 48.6 us; the launch traced here: 48.4 us
  starting transfers between devices  19.4 us (40%)
  blocking collectives  8.33 us (17%)
  other arithmetic  6.94 us (14%)
  matrix products  5.97 us (12%)
  waiting for transfers between devices  5.87 us (12%)
  local copies, waits for them, and re-layouts  1.18 us (2%)
  between operations  0.81 us (2%)
    ppermute x12, starting transfers between devices, shift(): return lax.ppermute(x, axis, [(i, (i + k) % n) for i in range(n)])  19.4 us
    all_gather x1, blocking collectives, per_device(): lax.all_gather(jnp.transpose(images, (2, 0, 1)), 'task', axis=0, tiled=True)  8.33 us
    ppermute x12, waiting for transfers between devices, shift(): return lax.ppermute(x, axis, [(i, (i + k) % n) for i in range(n)])  5.87 us
    reduce_sum x1, other arithmetic, kernel_tile(): return jnp.exp(0.1 - jnp.sqrt(jnp.sum(diff * diff, axis=0) + 0.01))  4.66 us
    unnamed x4, matrix products  4.38 us
    unnamed x9, local copies, waits for them, and re-layouts  1.18 us
  transfers between devices with their start and end apart: 12, of which 2 were waited for; matrix products, arithmetic and copies ran while one was open for 26% of the time, Pallas kernels for 0%

profile of v6, /device:TPU:0, one launch (start us, length us, event | category | flops | bytes accessed | tf_op | source)
XLA Modules:
  0.0 48.4 jit_solution(2035574846493108648)
XLA Ops:
  0.6 5.1 %collective-permute-start.4 = (bf16[3,768]{1,0:T(4,128)(2,1)}, bf16[3,768]{1,0:T(4,128)(2,1)S(1)}, u32[]{:S(2)}, u32[]{:S(2)}) collective-permute-start(bf16[3,768]{1,0:T(4,128)(2,1)} %param.6), channel_id=1, source_target_pairs={{0,12},{4,0},{8,4},{12,8},{1,13},{5,1},{9,5},{13,9},{2,14},{6,2},{... | collective-permute-start | bytes 13832 | tf_op jit(solution)/shard_map/ppermute | solution.py:13
  5.8 1.0 %collective-permute-start.2 = (bf16[3,768]{1,0:T(4,128)(2,1)}, bf16[3,768]{1,0:T(4,128)(2,1)S(1)}, u32[]{:S(2)}, u32[]{:S(2)}) collective-permute-start(bf16[3,768]{1,0:T(4,128)(2,1)} %param.6), channel_id=1, source_target_pairs={{0,8},{4,12},{8,0},{12,4},{1,9},{5,13},{9,1},{13,5},{2,10},{6,14},... | collective-permute-start | bytes 13832 | tf_op jit(solution)/shard_map/ppermute | solution.py:13
  6.8 2.8 %collective-permute-start.5 = (bf16[2,768,64]{1,2,0:T(8,128)(2,1)}, bf16[2,768,64]{1,2,0:T(8,128)(2,1)S(1)}, u32[]{:S(2)}, u32[]{:S(2)}) collective-permute-start(bf16[2,768,64]{1,2,0:T(8,128)(2,1)} %param.8), channel_id=1, source_target_pairs={{0,12},{4,0},{8,4},{12,8},{1,13},{5,1},{9,5},{13,9},{2,14},{6,2},{... | collective-permute-start | bytes 589832 | tf_op jit(solution)/shard_map/ppermute | solution.py:13
  9.6 2.0 %collective-permute-start.3 = (bf16[2,768,64]{1,2,0:T(8,128)(2,1)}, bf16[2,768,64]{1,2,0:T(8,128)(2,1)S(1)}, u32[]{:S(2)}, u32[]{:S(2)}) collective-permute-start(bf16[2,768,64]{1,2,0:T(8,128)(2,1)} %param.8), channel_id=1, source_target_pairs={{0,8},{4,12},{8,0},{12,4},{1,9},{5,13},{9,1},{13,5},{2,10},{6,14},... | collective-permute-start | bytes 589832 | tf_op jit(solution)/shard_map/ppermute | solution.py:13
  11.6 0.7 %broadcast_divide_fusion = f32[3]{0:T(128)S(1)} fusion(f32[3]{0:T(128)} %param.7), kind=kLoop, calls=%fused_computation.38 | loop fusion | flops 3 | bytes 24 | tf_op jit(solution)/shard_map/div | solution.py:37
  12.3 1.2 %copy.15 = bf16[2,768,64]{2,1,0:T(8,128)(2,1)S(1)} copy(bf16[2,768,64]{1,2,0:T(8,128)(2,1)} %param.8) | data formatting | bytes 393216 | tf_op args[2]
  13.6 1.6 %collective-permute-start.7 = (bf16[2,768,64]{2,1,0:T(8,128)(2,1)S(1)}, bf16[2,768,64]{2,1,0:T(8,128)(2,1)S(1)}, u32[]{:S(2)}, u32[]{:S(2)}) collective-permute-start(bf16[2,768,64]{2,1,0:T(8,128)(2,1)S(1)} %copy.15), channel_id=1, source_target_pairs={{0,2},{1,3},{2,0},{3,1},{4,6},{5,7},{6,4},{7,5},{8,10},{9,11},{10,... | collective-permute-start | bytes 589832 | tf_op jit(solution)/shard_map/ppermute | solution.py:13
  15.2 0.8 %convert_multiply_fusion = (f32[3,768]{1,0:T(4,128)S(1)}, f32[3,768]{1,0:T(4,128)S(1)}, f32[3,768]{1,0:T(4,128)S(1)}, f32[3,768]{1,0:T(4,128)S(1)}) fusion(bf16[3,768]{1,0:T(4,128)(2,1)S(1)} %collective-permute-done.4, f32[3]{0:T(128)S(1)} %broadcast_divide_fusion, bf16[3,768]{1,0:T(4,128)(2,1)S(1)} %collective-permute-done, ...), kind=kLoop, calls=%fused_computation.33 | loop fusion | flops 18432 | bytes 55308 | tf_op jit(solution)/shard_map/mul | solution.py:41
  15.9 4.7 %multiply_reduce_fusion.2 = (f32[768,768]{1,0:T(8,128)S(1)}, f32[768,768]{1,0:T(8,128)S(1)}, f32[768,768]{1,0:T(8,128)S(1)}, f32[768,768]{1,0:T(8,128)S(1)}) fusion(f32[3,768]{1,0:T(4,128)S(1)} %get-tuple-element.7, f32[3,768]{1,0:T(4,128)S(1)} %get-tuple-element.9, f32[3,768]{1,0:T(4,128)S(1)} %get-tuple-element.8, f32[3,768]{1,0:T(4,128)S(1)} %get-tuple-element.6), kind=kLoop, calls=%fused_computation.2 | loop fusion | flops 18874368 | bytes 9474048 | tf_op jit(solution)/shard_map/reduce_sum | solution.py:9
  20.6 1.1 %fusion = f32[768,128]{0,1:S(1)} fusion(bf16[768,128]{0,1:T(8,128)(2,1)S(1)} %bitcast.31, f32[768,768]{1,0:T(8,128)S(1)} %get-tuple-element.5), kind=kOutput, calls=%fused_computation.9 | convolution fusion | flops 152764416 | bytes 2949120
  21.7 1.4 %collective-permute-start.6 = (bf16[2,768,64]{2,1,0:T(8,128)(2,1)S(1)}, bf16[2,768,64]{2,1,0:T(8,128)(2,1)S(1)}, u32[]{:S(2)}, u32[]{:S(2)}) collective-permute-start(bf16[2,768,64]{2,1,0:T(8,128)(2,1)S(1)} %copy.15), channel_id=1, source_target_pairs={{0,3},{1,0},{2,1},{3,2},{4,7},{5,4},{6,5},{7,6},{8,11},{9,8},{10,9... | collective-permute-start | bytes 589832 | tf_op jit(solution)/shard_map/ppermute | solution.py:13
  23.2 1.1 %fusion.3 = f32[768,128]{0,1:S(1)} fusion(bf16[768,128]{0,1:T(8,128)(2,1)S(1)} %bitcast.37, f32[768,768]{1,0:T(8,128)S(1)} %get-tuple-element.4), kind=kOutput, calls=%fused_computation.12 | convolution fusion | flops 152764416 | bytes 2949120
  24.3 4.1 %collective-permute-done.3 = bf16[2,768,64]{1,2,0:T(8,128)(2,1)S(1)} collective-permute-done((bf16[2,768,64]{1,2,0:T(8,128)(2,1)}, bf16[2,768,64]{1,2,0:T(8,128)(2,1)S(1)}, u32[]{:S(2)}, u32[]{:S(2)}) %collective-permute-start.3) | collective-permute-done | bytes 196640 | tf_op jit(solution)/shard_map/ppermute | solution.py:13
  28.3 1.1 %fusion.2 = f32[768,128]{0,1:S(1)} fusion(bf16[768,128]{0,1:T(8,128)(2,1)S(1)} %bitcast.36, f32[768,768]{1,0:T(8,128)S(1)} %get-tuple-element.3), kind=kOutput, calls=%fused_computation.11 | convolution fusion | flops 152764416 | bytes 2949120
  29.5 1.1 %fusion.1 = f32[768,128]{0,1:S(1)} fusion(bf16[768,128]{0,1:T(8,128)(2,1)S(1)} %bitcast.38, f32[768,768]{1,0:T(8,128)S(1)} %get-tuple-element.2), kind=kOutput, calls=%fused_computation.10 | convolution fusion | flops 152764416 | bytes 2949120
  30.5 0.1 add_convert_fusion
  30.7 1.8 %collective-permute-done.6 = bf16[2,768,64]{2,1,0:T(8,128)(2,1)S(1)} collective-permute-done((bf16[2,768,64]{2,1,0:T(8,128)(2,1)S(1)}, bf16[2,768,64]{2,1,0:T(8,128)(2,1)S(1)}, u32[]{:S(2)}, u32[]{:S(2)}) %collective-permute-start.6) | collective-permute-done | bytes 196640 | tf_op jit(solution)/shard_map/ppermute | solution.py:13
  32.4 0.6 %convolution_bitcast_fusion = f32[64,256]{1,0:T(8,128)S(1)} fusion(bf16[2,768,64]{2,1,0:T(8,128)(2,1)S(1)} %collective-permute-done.8, bf16[2,768,64]{2,1,0:T(8,128)(2,1)S(1)} %collective-permute-done.7, bf16[2,768,64]{2,1,0:T(8,128)(2,1)S(1)} %collective-permute-done.6, bf16[2,768,64]{2,1,0:T(8,128)(2,1)S(1)} %copy.15, ...), kind=kOutput, calls=%fused_computation.14 | convolution fusion | flops 53575680 | bytes 1048580 | tf_op jit(solution)/shard_map/sna,snb->ab/dot_general | solution.py:68
  33.1 1.5 %collective-permute-start.11 = (f32[64,256]{1,0:T(8,128)S(1)}, f32[64,256]{1,0:T(8,128)S(1)}, u32[]{:S(2)}, u32[]{:S(2)}) collective-permute-start(f32[64,256]{1,0:T(8,128)S(1)} %convolution_bitcast_fusion), channel_id=1, source_target_pairs={{0,8},{4,12},{8,0},{12,4},{1,9},{5,13},{9,1},{13,5},{2,10},{6,14},... | collective-permute-start | bytes 196616 | tf_op jit(solution)/shard_map/ppermute | solution.py:13
  34.5 2.9 %collective-permute-start.10 = (f32[64,256]{1,0:T(8,128)S(1)}, f32[64,256]{1,0:T(8,128)S(1)}, u32[]{:S(2)}, u32[]{:S(2)}) collective-permute-start(f32[64,256]{1,0:T(8,128)S(1)} %convolution_bitcast_fusion), channel_id=1, source_target_pairs={{0,4},{4,8},{8,12},{12,0},{1,5},{5,9},{9,13},{13,1},{2,6},{6,10},{... | collective-permute-start | bytes 196616 | tf_op jit(solution)/shard_map/ppermute | solution.py:13
  37.5 0.9 %collective-permute-start.9 = (f32[64,256]{1,0:T(8,128)S(1)}, f32[64,256]{1,0:T(8,128)S(1)}, u32[]{:S(2)}, u32[]{:S(2)}) collective-permute-start(f32[64,256]{1,0:T(8,128)S(1)} %convolution_bitcast_fusion), channel_id=1, source_target_pairs={{0,12},{4,0},{8,4},{12,8},{1,13},{5,1},{9,5},{13,9},{2,14},{6,2},{... | collective-permute-start | bytes 196616 | tf_op jit(solution)/shard_map/ppermute | solution.py:13
  38.4 8.3 %all_gather.3 = bf16[256,2,768]{2,0,1:T(8,128)(2,1)S(1)} all-gather(bf16[64,2,768]{2,0,1:T(8,128)(2,1)S(1)} %bitcast.30), channel_id=1, replica_groups=mesh['groups'=2,'dp'=4,'task'=4] {'task'}, dimensions={0}, use_global_device_ids=true | all-gather | bytes 983040 | tf_op jit(solution)/shard_map/all_gather | solution.py:72
  46.7 0.9 %fusion.4 = bf16[2,768,64]{1,2,0:T(8,128)(2,1)} fusion(bf16[256,2,768]{2,0,1:T(8,128)(2,1)S(1)} %all_gather.3, bf16[2,768,64]{1,2,0:T(8,128)(2,1)S(1)} %copy-done.1, f32[64]{0:T(128)S(1)} %copy-done.2, bf16[256,256]{1,0:T(8,128)(2,1)S(1)} %copy-done, s32[]{:T(128)S(6)} %select_n.29), kind=kOutput, calls=%fused_computation.13 | convolution fusion | flops 50724864 | bytes 1212932 | tf_op jit(solution)/shard_map/asn,ca->snc/dot_general | solution.py:74
  47.7 0.7 %fusion.16 = f32[64,256]{1,0:T(8,128)} fusion(s32[]{:T(128)S(6)} %select_n.35, f32[64,256]{1,0:T(8,128)S(1)} %add_add_fusion), kind=kLoop, calls=%fused_computation.29 | loop fusion | flops 32768 | bytes 131076 | tf_op jit(solution)/shard_map/div | solution.py:79
  (22 shorter events, 0.2 us)
Async XLA Ops:
  0.6 46.1 %copy-start = (bf16[256,256]{1,0:T(8,128)(2,1)S(1)}, bf16[256,256]{1,0:T(8,128)(2,1)}, u32[]{:S(2)}) copy-start(bf16[256,256]{1,0:T(8,128)(2,1)} %param.9) | copy-start | bytes 393220
  0.6 12.8 %collective-permute-start.4 = (bf16[3,768]{1,0:T(4,128)(2,1)}, bf16[3,768]{1,0:T(4,128)(2,1)S(1)}, u32[]{:S(2)}, u32[]{:S(2)}) collective-permute-start(bf16[3,768]{1,0:T(4,128)(2,1)} %param.6), channel_id=1, source_target_pairs={{0,12},{4,0},{8,4},{12,8},{1,13},{5,1},{9,5},{13,9},{2,14},{6,2},{... | collective-permute-start | bytes 13832 | tf_op jit(solution)/shard_map/ppermute | solution.py:13
  5.7 7.8 %collective-permute-start = (bf16[3,768]{1,0:T(4,128)(2,1)}, bf16[3,768]{1,0:T(4,128)(2,1)S(1)}, u32[]{:S(2)}, u32[]{:S(2)}) collective-permute-start(bf16[3,768]{1,0:T(4,128)(2,1)} %param.6), channel_id=1, source_target_pairs={{0,4},{4,8},{8,12},{12,0},{1,5},{5,9},{9,13},{13,1},{2,6},{6,10},{... | collective-permute-start | bytes 13832 | tf_op jit(solution)/shard_map/ppermute | solution.py:13
  5.8 7.8 %collective-permute-start.2 = (bf16[3,768]{1,0:T(4,128)(2,1)}, bf16[3,768]{1,0:T(4,128)(2,1)S(1)}, u32[]{:S(2)}, u32[]{:S(2)}) collective-permute-start(bf16[3,768]{1,0:T(4,128)(2,1)} %param.6), channel_id=1, source_target_pairs={{0,8},{4,12},{8,0},{12,4},{1,9},{5,13},{9,1},{13,5},{2,10},{6,14},... | collective-permute-start | bytes 13832 | tf_op jit(solution)/shard_map/ppermute | solution.py:13
  6.8 15.0 %collective-permute-start.5 = (bf16[2,768,64]{1,2,0:T(8,128)(2,1)}, bf16[2,768,64]{1,2,0:T(8,128)(2,1)S(1)}, u32[]{:S(2)}, u32[]{:S(2)}) collective-permute-start(bf16[2,768,64]{1,2,0:T(8,128)(2,1)} %param.8), channel_id=1, source_target_pairs={{0,12},{4,0},{8,4},{12,8},{1,13},{5,1},{9,5},{13,9},{2,14},{6,2},{... | collective-permute-start | bytes 589832 | tf_op jit(solution)/shard_map/ppermute | solution.py:13
  9.6 18.8 %collective-permute-start.3 = (bf16[2,768,64]{1,2,0:T(8,128)(2,1)}, bf16[2,768,64]{1,2,0:T(8,128)(2,1)S(1)}, u32[]{:S(2)}, u32[]{:S(2)}) collective-permute-start(bf16[2,768,64]{1,2,0:T(8,128)(2,1)} %param.8), channel_id=1, source_target_pairs={{0,8},{4,12},{8,0},{12,4},{1,9},{5,13},{9,1},{13,5},{2,10},{6,14},... | collective-permute-start | bytes 589832 | tf_op jit(solution)/shard_map/ppermute | solution.py:13
  13.5 16.0 %collective-permute-start.1 = (bf16[2,768,64]{1,2,0:T(8,128)(2,1)}, bf16[2,768,64]{1,2,0:T(8,128)(2,1)S(1)}, u32[]{:S(2)}, u32[]{:S(2)}) collective-permute-start(bf16[2,768,64]{1,2,0:T(8,128)(2,1)} %param.8), channel_id=1, source_target_pairs={{0,4},{4,8},{8,12},{12,0},{1,5},{5,9},{9,13},{13,1},{2,6},{6,10},{... | collective-permute-start | bytes 589832 | tf_op jit(solution)/shard_map/ppermute | solution.py:13
  13.5 17.1 %collective-permute-start.8 = (bf16[2,768,64]{2,1,0:T(8,128)(2,1)S(1)}, bf16[2,768,64]{2,1,0:T(8,128)(2,1)S(1)}, u32[]{:S(2)}, u32[]{:S(2)}) collective-permute-start(bf16[2,768,64]{2,1,0:T(8,128)(2,1)S(1)} %copy.15), channel_id=1, source_target_pairs={{0,1},{1,2},{2,3},{3,0},{4,5},{5,6},{6,7},{7,4},{8,9},{9,10},{10,1... | collective-permute-start | bytes 589832 | tf_op jit(solution)/shard_map/ppermute | solution.py:13
  13.6 17.1 %collective-permute-start.7 = (bf16[2,768,64]{2,1,0:T(8,128)(2,1)S(1)}, bf16[2,768,64]{2,1,0:T(8,128)(2,1)S(1)}, u32[]{:S(2)}, u32[]{:S(2)}) collective-permute-start(bf16[2,768,64]{2,1,0:T(8,128)(2,1)S(1)} %copy.15), channel_id=1, source_target_pairs={{0,2},{1,3},{2,0},{3,1},{4,6},{5,7},{6,4},{7,5},{8,10},{9,11},{10,... | collective-permute-start | bytes 589832 | tf_op jit(solution)/shard_map/ppermute | solution.py:13
  15.9 4.7 %copy-start.1 = (bf16[2,768,64]{1,2,0:T(8,128)(2,1)S(1)}, bf16[2,768,64]{1,2,0:T(8,128)(2,1)}, u32[]{:S(2)}) copy-start(bf16[2,768,64]{1,2,0:T(8,128)(2,1)} %param.8) | copy-start | bytes 589828
  21.7 10.7 %collective-permute-start.6 = (bf16[2,768,64]{2,1,0:T(8,128)(2,1)S(1)}, bf16[2,768,64]{2,1,0:T(8,128)(2,1)S(1)}, u32[]{:S(2)}, u32[]{:S(2)}) collective-permute-start(bf16[2,768,64]{2,1,0:T(8,128)(2,1)S(1)} %copy.15), channel_id=1, source_target_pairs={{0,3},{1,0},{2,1},{3,2},{4,7},{5,4},{6,5},{7,6},{8,11},{9,8},{10,9... | collective-permute-start | bytes 589832 | tf_op jit(solution)/shard_map/ppermute | solution.py:13
  29.4 3.0 %copy-start.3 = (bf16[2]{0:T(256)(128)(2,1)S(1)}, bf16[2]{0:T(256)(128)(2,1)}, u32[]{:S(2)}) copy-start(bf16[2]{0:T(256)(128)(2,1)} %constant.50.clone) | copy-start | bytes 16
  30.6 16.1 %copy-start.2 = (f32[64]{0:T(128)S(1)}, f32[64]{0:T(128)}, u32[]{:S(2)}) copy-start(f32[64]{0:T(128)} %param.10) | copy-start | bytes 772
  33.1 14.6 %collective-permute-start.11 = (f32[64,256]{1,0:T(8,128)S(1)}, f32[64,256]{1,0:T(8,128)S(1)}, u32[]{:S(2)}, u32[]{:S(2)}) collective-permute-start(f32[64,256]{1,0:T(8,128)S(1)} %convolution_bitcast_fusion), channel_id=1, source_target_pairs={{0,8},{4,12},{8,0},{12,4},{1,9},{5,13},{9,1},{13,5},{2,10},{6,14},... | collective-permute-start | bytes 196616 | tf_op jit(solution)/shard_map/ppermute | solution.py:13
  34.5 13.1 %collective-permute-start.10 = (f32[64,256]{1,0:T(8,128)S(1)}, f32[64,256]{1,0:T(8,128)S(1)}, u32[]{:S(2)}, u32[]{:S(2)}) collective-permute-start(f32[64,256]{1,0:T(8,128)S(1)} %convolution_bitcast_fusion), channel_id=1, source_target_pairs={{0,4},{4,8},{8,12},{12,0},{1,5},{5,9},{9,13},{13,1},{2,6},{6,10},{... | collective-permute-start | bytes 196616 | tf_op jit(solution)/shard_map/ppermute | solution.py:13
  37.5 10.2 %collective-permute-start.9 = (f32[64,256]{1,0:T(8,128)S(1)}, f32[64,256]{1,0:T(8,128)S(1)}, u32[]{:S(2)}, u32[]{:S(2)}) collective-permute-start(f32[64,256]{1,0:T(8,128)S(1)} %convolution_bitcast_fusion), channel_id=1, source_target_pairs={{0,12},{4,0},{8,4},{12,8},{1,13},{5,1},{9,5},{13,9},{2,14},{6,2},{... | collective-permute-start | bytes 196616 | tf_op jit(solution)/shard_map/ppermute | solution.py:13

commit v7 on v4

--- a/solution.py
+++ b/solution.py
@@ -42,11 +42,14 @@
         tile = kernel_tile(own_scaled, right).astype(jnp.bfloat16)
         return jnp.einsum("nr,srm->snm", tile, values, preferred_element_type=jnp.float32)
 
+    task_input = vectors
     if n_dp <= 4:
         moved = [shift(vectors, "dp", k, n_dp) for k in range(1, n_dp)]
+        peer_coords = [shift(coords, "dp", k, n_dp) for k in range(1, n_dp)]
+        task_input = lax.optimization_barrier((vectors, peer_coords))[0]
         summed = block(coords, vectors)
         for k in range(1, n_dp):
-            summed = summed + block(shift(coords, "dp", k, n_dp), moved[k - 1])
+            summed = summed + block(peer_coords[k - 1], moved[k - 1])
     else:
 
         def ring(_, carry):
@@ -58,7 +61,7 @@
         summed = block(coords, vectors)
         summed = lax.fori_loop(0, n_dp - 1, ring, (summed, coords, vectors))[0]
 
-    whole_vectors = lax.all_gather(vectors, "task", axis=2, tiled=True)
+    whole_vectors = lax.all_gather(task_input, "task", axis=2, tiled=True)
     images = summed.astype(jnp.bfloat16)
     signs = jnp.array([1.0, -1.0], jnp.bfloat16)
     signed = images * signs[:, None, None]

time: 46.2 us -> 44.9 us (0.972)
  starting transfers between devices: 15.9 us -> 14.9 us
    ppermute x9, starting transfers between devices: 15.9 us -> 14.9 us  [shift(): return lax.ppermute(x, axis, [(i, (i + k) % n) for i in range(n)])]
  transfers between devices with their start and end apart: 9 -> 9, of which waited for: 1 -> 0; matrix products, arithmetic and copies ran while one was open for 22% -> 23% of each run, Pallas kernels for 0% -> 0%
where the time goes in v7:
time: 44.9 us; the launch traced here: 44.7 us
  blocking collectives  16.5 us (37%)
  starting transfers between devices  14.9 us (33%)
  other arithmetic  6.81 us (15%)
  matrix products  5.69 us (13%)
  between operations  0.71 us (2%)
    ppermute x9, starting transfers between devices, shift(): return lax.ppermute(x, axis, [(i, (i + k) % n) for i in range(n)])  14.9 us
    all_gather x1, blocking collectives, per_device(): whole_vectors = lax.all_gather(task_input, 'task', axis=2, tiled=True)  8.59 us
    all_gather x1, blocking collectives, per_device(): lax.all_gather(jnp.transpose(images, (2, 0, 1)), 'task', axis=0, tiled=True)  7.87 us
    reduce_sum x1, other arithmetic, kernel_tile(): return jnp.exp(0.1 - jnp.sqrt(jnp.sum(diff * diff, axis=0) + 0.01))  4.65 us
    unnamed x4, matrix products  4.38 us
    dot_general x1, matrix products, per_device(): jnp.einsum('asn,ca->snc', whole_images, own_rows, preferred_element_type=...  0.94 us
  transfers between devices with their start and end apart: 9, of which 0 were waited for; matrix products, arithmetic and copies ran while one was open for 23% of the time, Pallas kernels for 0%

profile of v7, /device:TPU:0, one launch (start us, length us, event | category | flops | bytes accessed | tf_op | source)
XLA Modules:
  0.0 44.7 jit_solution(13970564383328238922)
XLA Ops:
  0.6 0.0 copy-start
  0.6 3.1 %collective-permute-start = (bf16[3,768]{1,0:T(4,128)(2,1)}, bf16[3,768]{1,0:T(4,128)(2,1)S(1)}, u32[]{:S(2)}, u32[]{:S(2)}) collective-permute-start(bf16[3,768]{1,0:T(4,128)(2,1)} %param.6), channel_id=1, source_target_pairs={{0,4},{4,8},{8,12},{12,0},{1,5},{5,9},{9,13},{13,1},{2,6},{6,10},{... | collective-permute-start | bytes 13832 | tf_op jit(solution)/shard_map/ppermute | solution.py:13
  3.7 2.6 %collective-permute-start.2 = (bf16[3,768]{1,0:T(4,128)(2,1)}, bf16[3,768]{1,0:T(4,128)(2,1)S(1)}, u32[]{:S(2)}, u32[]{:S(2)}) collective-permute-start(bf16[3,768]{1,0:T(4,128)(2,1)} %param.6), channel_id=1, source_target_pairs={{0,8},{4,12},{8,0},{12,4},{1,9},{5,13},{9,1},{13,5},{2,10},{6,14},... | collective-permute-start | bytes 13832 | tf_op jit(solution)/shard_map/ppermute | solution.py:13
  6.3 1.3 %collective-permute-start.4 = (bf16[3,768]{1,0:T(4,128)(2,1)}, bf16[3,768]{1,0:T(4,128)(2,1)S(1)}, u32[]{:S(2)}, u32[]{:S(2)}) collective-permute-start(bf16[3,768]{1,0:T(4,128)(2,1)} %param.6), channel_id=1, source_target_pairs={{0,12},{4,0},{8,4},{12,8},{1,13},{5,1},{9,5},{13,9},{2,14},{6,2},{... | collective-permute-start | bytes 13832 | tf_op jit(solution)/shard_map/ppermute | solution.py:13
  7.7 0.7 %collective-permute-start.1 = (bf16[2,768,64]{1,2,0:T(8,128)(2,1)}, bf16[2,768,64]{1,2,0:T(8,128)(2,1)S(1)}, u32[]{:S(2)}, u32[]{:S(2)}) collective-permute-start(bf16[2,768,64]{1,2,0:T(8,128)(2,1)} %param.8), channel_id=1, source_target_pairs={{0,4},{4,8},{8,12},{12,0},{1,5},{5,9},{9,13},{13,1},{2,6},{6,10},{... | collective-permute-start | bytes 589832 | tf_op jit(solution)/shard_map/ppermute | solution.py:13
  8.3 0.3 collective-permute-start.3
  8.7 0.7 %broadcast_divide_fusion = f32[3]{0:T(128)S(1)} fusion(f32[3]{0:T(128)} %param.7), kind=kLoop, calls=%fused_computation.27 | loop fusion | flops 3 | bytes 24 | tf_op jit(solution)/shard_map/div | solution.py:37
  9.3 2.8 %collective-permute-start.5 = (bf16[2,768,64]{1,2,0:T(8,128)(2,1)}, bf16[2,768,64]{1,2,0:T(8,128)(2,1)S(1)}, u32[]{:S(2)}, u32[]{:S(2)}) collective-permute-start(bf16[2,768,64]{1,2,0:T(8,128)(2,1)} %param.8), channel_id=1, source_target_pairs={{0,12},{4,0},{8,4},{12,8},{1,13},{5,1},{9,5},{13,9},{2,14},{6,2},{... | collective-permute-start | bytes 589832 | tf_op jit(solution)/shard_map/ppermute | solution.py:13
  12.2 0.8 %convert_multiply_fusion = (f32[3,768]{1,0:T(4,128)S(1)}, f32[3,768]{1,0:T(4,128)S(1)}, f32[3,768]{1,0:T(4,128)S(1)}, f32[3,768]{1,0:T(4,128)S(1)}) fusion(bf16[3,768]{1,0:T(4,128)(2,1)S(1)} %collective-permute-done.4, f32[3]{0:T(128)S(1)} %broadcast_divide_fusion, bf16[3,768]{1,0:T(4,128)(2,1)S(1)} %collective-permute-done, ...), kind=kLoop, calls=%fused_computation.22 | loop fusion | flops 18432 | bytes 55308 | tf_op jit(solution)/shard_map/mul | solution.py:41
  12.9 4.7 %multiply_reduce_fusion.2 = (f32[768,768]{1,0:T(8,128)S(1)}, f32[768,768]{1,0:T(8,128)S(1)}, f32[768,768]{1,0:T(8,128)S(1)}, f32[768,768]{1,0:T(8,128)S(1)}) fusion(f32[3,768]{1,0:T(4,128)S(1)} %get-tuple-element.9, f32[3,768]{1,0:T(4,128)S(1)} %get-tuple-element.11, f32[3,768]{1,0:T(4,128)S(1)} %get-tuple-element.10, f32[3,768]{1,0:T(4,128)S(1)} %get-tuple-element.8), kind=kLoop, calls=%fused_computation.2 | loop fusion | flops 18874368 | bytes 9474048 | tf_op jit(solution)/shard_map/reduce_sum | solution.py:9
  17.6 1.1 %fusion = f32[768,128]{0,1:S(1)} fusion(bf16[768,128]{0,1:T(8,128)(2,1)S(1)} %bitcast.32, f32[768,768]{1,0:T(8,128)S(1)} %get-tuple-element.7), kind=kOutput, calls=%fused_computation.9 | convolution fusion | flops 152764416 | bytes 2949120
  18.7 8.6 %all_gather.7 = bf16[2,768,256]{1,2,0:T(8,128)(2,1)S(1)} all-gather(bf16[2,768,64]{1,2,0:T(8,128)(2,1)S(1)} %copy-done.1), channel_id=1, replica_groups=mesh['groups'=2,'dp'=4,'task'=4] {'task'}, dimensions={2}, use_global_device_ids=true | all-gather | bytes 983040 | tf_op jit(solution)/shard_map/all_gather | solution.py:64
  27.3 1.1 %fusion.1 = f32[768,128]{0,1:S(1)} fusion(bf16[768,128]{0,1:T(8,128)(2,1)S(1)} %bitcast.38, f32[768,768]{1,0:T(8,128)S(1)} %get-tuple-element.4), kind=kOutput, calls=%fused_computation.10 | convolution fusion | flops 152764416 | bytes 2949120
  28.4 1.1 %fusion.2 = f32[768,128]{0,1:S(1)} fusion(bf16[768,128]{0,1:T(8,128)(2,1)S(1)} %bitcast.37, f32[768,768]{1,0:T(8,128)S(1)} %get-tuple-element.5), kind=kOutput, calls=%fused_computation.11 | convolution fusion | flops 152764416 | bytes 2949120
  29.5 0.0 copy-start.3
  29.5 1.1 %fusion.3 = f32[768,128]{0,1:S(1)} fusion(bf16[768,128]{0,1:T(8,128)(2,1)S(1)} %bitcast.39, f32[768,768]{1,0:T(8,128)S(1)} %get-tuple-element.6), kind=kOutput, calls=%fused_computation.12 | convolution fusion | flops 152764416 | bytes 2949120
  30.6 0.1 add_convert_fusion
  30.7 0.4 convolution_bitcast_fusion
  31.1 1.3 %collective-permute-start.6 = (f32[64,256]{1,0:T(8,128)S(1)}, f32[64,256]{1,0:T(8,128)S(1)}, u32[]{:S(2)}, u32[]{:S(2)}) collective-permute-start(f32[64,256]{1,0:T(8,128)S(1)} %convolution_bitcast_fusion), channel_id=1, source_target_pairs={{0,12},{4,0},{8,4},{12,8},{1,13},{5,1},{9,5},{13,9},{2,14},{6,2},{... | collective-permute-start | bytes 196616 | tf_op jit(solution)/shard_map/ppermute | solution.py:13
  32.4 0.8 %collective-permute-start.7 = (f32[64,256]{1,0:T(8,128)S(1)}, f32[64,256]{1,0:T(8,128)S(1)}, u32[]{:S(2)}, u32[]{:S(2)}) collective-permute-start(f32[64,256]{1,0:T(8,128)S(1)} %convolution_bitcast_fusion), channel_id=1, source_target_pairs={{0,4},{4,8},{8,12},{12,0},{1,5},{5,9},{9,13},{13,1},{2,6},{6,10},{... | collective-permute-start | bytes 196616 | tf_op jit(solution)/shard_map/ppermute | solution.py:13
  33.2 2.0 %collective-permute-start.8 = (f32[64,256]{1,0:T(8,128)S(1)}, f32[64,256]{1,0:T(8,128)S(1)}, u32[]{:S(2)}, u32[]{:S(2)}) collective-permute-start(f32[64,256]{1,0:T(8,128)S(1)} %convolution_bitcast_fusion), channel_id=1, source_target_pairs={{0,8},{4,12},{8,0},{12,4},{1,9},{5,13},{9,1},{13,5},{2,10},{6,14},... | collective-permute-start | bytes 196616 | tf_op jit(solution)/shard_map/ppermute | solution.py:13
  35.2 7.9 %all_gather.6 = bf16[256,2,768]{2,0,1:T(8,128)(2,1)S(1)} all-gather(bf16[64,2,768]{2,0,1:T(8,128)(2,1)S(1)} %bitcast.31), channel_id=1, replica_groups=mesh['groups'=2,'dp'=4,'task'=4] {'task'}, dimensions={0}, use_global_device_ids=true | all-gather | bytes 983040 | tf_op jit(solution)/shard_map/all_gather | solution.py:72
  43.0 0.9 %fusion.4 = bf16[2,768,64]{1,2,0:T(8,128)(2,1)} fusion(bf16[256,2,768]{2,0,1:T(8,128)(2,1)S(1)} %all_gather.6, bf16[2,768,64]{1,2,0:T(8,128)(2,1)S(1)} %copy-done.1, f32[64]{0:T(128)S(1)} %copy-done.2, bf16[256,256]{1,0:T(8,128)(2,1)S(1)} %copy-done, s32[]{:T(128)S(6)} %select_n.22), kind=kOutput, calls=%fused_computation.13 | convolution fusion | flops 50724864 | bytes 1212932 | tf_op jit(solution)/shard_map/asn,ca->snc/dot_general | solution.py:74
  44.0 0.7 %add_multiply_fusion = f32[64,256]{1,0:T(8,128)} fusion(f32[64,256]{1,0:T(8,128)S(1)} %collective-permute-done.8, f32[64,256]{1,0:T(8,128)S(1)} %collective-permute-done.7, f32[64,256]{1,0:T(8,128)S(1)} %collective-permute-done.6, f32[64,256]{1,0:T(8,128)S(1)} %convolution_bitcast_fusion, pred[]{:T(512)S(6)} %eq.5), kind=kLoop, calls=%fused_computation.19 | loop fusion | flops 98304 | bytes 327681 | tf_op jit(solution)/shard_map/div | solution.py:76
  (15 shorter events, 0.0 us)
Async XLA Ops:
  0.6 42.4 %copy-start = (bf16[256,256]{1,0:T(8,128)(2,1)S(1)}, bf16[256,256]{1,0:T(8,128)(2,1)}, u32[]{:S(2)}) copy-start(bf16[256,256]{1,0:T(8,128)(2,1)} %param.9) | copy-start | bytes 393220
  0.6 8.7 %collective-permute-start = (bf16[3,768]{1,0:T(4,128)(2,1)}, bf16[3,768]{1,0:T(4,128)(2,1)S(1)}, u32[]{:S(2)}, u32[]{:S(2)}) collective-permute-start(bf16[3,768]{1,0:T(4,128)(2,1)} %param.6), channel_id=1, source_target_pairs={{0,4},{4,8},{8,12},{12,0},{1,5},{5,9},{9,13},{13,1},{2,6},{6,10},{... | collective-permute-start | bytes 13832 | tf_op jit(solution)/shard_map/ppermute | solution.py:13
  3.7 8.4 %collective-permute-start.2 = (bf16[3,768]{1,0:T(4,128)(2,1)}, bf16[3,768]{1,0:T(4,128)(2,1)S(1)}, u32[]{:S(2)}, u32[]{:S(2)}) collective-permute-start(bf16[3,768]{1,0:T(4,128)(2,1)} %param.6), channel_id=1, source_target_pairs={{0,8},{4,12},{8,0},{12,4},{1,9},{5,13},{9,1},{13,5},{2,10},{6,14},... | collective-permute-start | bytes 13832 | tf_op jit(solution)/shard_map/ppermute | solution.py:13
  6.3 5.8 %collective-permute-start.4 = (bf16[3,768]{1,0:T(4,128)(2,1)}, bf16[3,768]{1,0:T(4,128)(2,1)S(1)}, u32[]{:S(2)}, u32[]{:S(2)}) collective-permute-start(bf16[3,768]{1,0:T(4,128)(2,1)} %param.6), channel_id=1, source_target_pairs={{0,12},{4,0},{8,4},{12,8},{1,13},{5,1},{9,5},{13,9},{2,14},{6,2},{... | collective-permute-start | bytes 13832 | tf_op jit(solution)/shard_map/ppermute | solution.py:13
  7.7 19.6 %collective-permute-start.1 = (bf16[2,768,64]{1,2,0:T(8,128)(2,1)}, bf16[2,768,64]{1,2,0:T(8,128)(2,1)S(1)}, u32[]{:S(2)}, u32[]{:S(2)}) collective-permute-start(bf16[2,768,64]{1,2,0:T(8,128)(2,1)} %param.8), channel_id=1, source_target_pairs={{0,4},{4,8},{8,12},{12,0},{1,5},{5,9},{9,13},{13,1},{2,6},{6,10},{... | collective-permute-start | bytes 589832 | tf_op jit(solution)/shard_map/ppermute | solution.py:13
  8.3 20.1 %collective-permute-start.3 = (bf16[2,768,64]{1,2,0:T(8,128)(2,1)}, bf16[2,768,64]{1,2,0:T(8,128)(2,1)S(1)}, u32[]{:S(2)}, u32[]{:S(2)}) collective-permute-start(bf16[2,768,64]{1,2,0:T(8,128)(2,1)} %param.8), channel_id=1, source_target_pairs={{0,8},{4,12},{8,0},{12,4},{1,9},{5,13},{9,1},{13,5},{2,10},{6,14},... | collective-permute-start | bytes 589832 | tf_op jit(solution)/shard_map/ppermute | solution.py:13
  9.3 20.2 %collective-permute-start.5 = (bf16[2,768,64]{1,2,0:T(8,128)(2,1)}, bf16[2,768,64]{1,2,0:T(8,128)(2,1)S(1)}, u32[]{:S(2)}, u32[]{:S(2)}) collective-permute-start(bf16[2,768,64]{1,2,0:T(8,128)(2,1)} %param.8), channel_id=1, source_target_pairs={{0,12},{4,0},{8,4},{12,8},{1,13},{5,1},{9,5},{13,9},{2,14},{6,2},{... | collective-permute-start | bytes 589832 | tf_op jit(solution)/shard_map/ppermute | solution.py:13
  12.9 4.7 %copy-start.1 = (bf16[2,768,64]{1,2,0:T(8,128)(2,1)S(1)}, bf16[2,768,64]{1,2,0:T(8,128)(2,1)}, u32[]{:S(2)}) copy-start(bf16[2,768,64]{1,2,0:T(8,128)(2,1)} %param.8) | copy-start | bytes 589828
  29.5 1.2 %copy-start.3 = (bf16[2]{0:T(256)(128)(2,1)S(1)}, bf16[2]{0:T(256)(128)(2,1)}, u32[]{:S(2)}) copy-start(bf16[2]{0:T(256)(128)(2,1)} %constant.38.clone) | copy-start | bytes 16
  30.6 12.4 %copy-start.2 = (f32[64]{0:T(128)S(1)}, f32[64]{0:T(128)}, u32[]{:S(2)}) copy-start(f32[64]{0:T(128)} %param.10) | copy-start | bytes 772
  31.1 12.9 %collective-permute-start.6 = (f32[64,256]{1,0:T(8,128)S(1)}, f32[64,256]{1,0:T(8,128)S(1)}, u32[]{:S(2)}, u32[]{:S(2)}) collective-permute-start(f32[64,256]{1,0:T(8,128)S(1)} %convolution_bitcast_fusion), channel_id=1, source_target_pairs={{0,12},{4,0},{8,4},{12,8},{1,13},{5,1},{9,5},{13,9},{2,14},{6,2},{... | collective-permute-start | bytes 196616 | tf_op jit(solution)/shard_map/ppermute | solution.py:13
  32.4 11.6 %collective-permute-start.7 = (f32[64,256]{1,0:T(8,128)S(1)}, f32[64,256]{1,0:T(8,128)S(1)}, u32[]{:S(2)}, u32[]{:S(2)}) collective-permute-start(f32[64,256]{1,0:T(8,128)S(1)} %convolution_bitcast_fusion), channel_id=1, source_target_pairs={{0,4},{4,8},{8,12},{12,0},{1,5},{5,9},{9,13},{13,1},{2,6},{6,10},{... | collective-permute-start | bytes 196616 | tf_op jit(solution)/shard_map/ppermute | solution.py:13
  33.2 10.8 %collective-permute-start.8 = (f32[64,256]{1,0:T(8,128)S(1)}, f32[64,256]{1,0:T(8,128)S(1)}, u32[]{:S(2)}, u32[]{:S(2)}) collective-permute-start(f32[64,256]{1,0:T(8,128)S(1)} %convolution_bitcast_fusion), channel_id=1, source_target_pairs={{0,8},{4,12},{8,0},{12,4},{1,9},{5,13},{9,1},{13,5},{2,10},{6,14},... | collective-permute-start | bytes 196616 | tf_op jit(solution)/shard_map/ppermute | solution.py:13

commit v8 on v7

--- a/solution.py
+++ b/solution.py
@@ -5,8 +5,11 @@
 
 
 def kernel_tile(left, right):
-    diff = left[:, :, None] - right[:, None, :]
-    return jnp.exp(0.1 - jnp.sqrt(jnp.sum(diff * diff, axis=0) + 0.01))
+    total = None
+    for c in range(left.shape[0]):
+        diff = left[c][:, None] - right[c][None, :]
+        total = diff * diff if total is None else total + diff * diff
+    return jnp.exp(0.1 - jnp.sqrt(total + 0.01))
 
 
 def shift(x, axis, k, n):

time: 44.9 us -> 46.2 us (1.029)
  other arithmetic: 6.81 us -> 2.16 us
  matrix products: 5.69 us -> 9.78 us
  blocking collectives: 16.5 us -> 17.5 us
  waiting for transfers between devices: 0.02 us -> 0.99 us
  starting transfers between devices: 14.9 us -> 14.1 us
  local copies, waits for them, and re-layouts: 0.02 us -> 0.71 us
    reduce_sum x1 -> x0, other arithmetic: 4.65 us -> none  [kernel_tile(): return jnp.exp(0.1 - jnp.sqrt(jnp.sum(diff * diff, axis=0) + 0.01))]
    unnamed x4, matrix products: 4.38 us -> 8.48 us
    ppermute x9, waiting for transfers between devices: 0.02 us -> 0.99 us  [shift(): return lax.ppermute(x, axis, [(i, (i + k) % n) for i in range(n)])]
    ppermute x9, starting transfers between devices: 14.9 us -> 14.1 us  [shift(): return lax.ppermute(x, axis, [(i, (i + k) % n) for i in range(n)])]
    all_gather x1, blocking collectives: 7.87 us -> 8.58 us  [per_device(): lax.all_gather(jnp.transpose(images, (2, 0, 1)), 'task', axis=0, tiled=True)]
    unnamed x8, local copies, waits for them, and re-layouts: 0.02 us -> 0.58 us
  transfers between devices with their start and end apart: 9 -> 9, of which waited for: 0 -> 1; matrix products, arithmetic and copies ran while one was open for 23% -> 19% of each run, Pallas kernels for 0% -> 0%
where the time goes in v8:
time: 46.2 us; the launch traced here: 46 us
  blocking collectives  17.5 us (38%)
  starting transfers between devices  14.1 us (31%)
  matrix products  9.78 us (21%)
  other arithmetic  2.16 us (5%)
  waiting for transfers between devices  0.99 us (2%)
  between operations  0.74 us (2%)
  local copies, waits for them, and re-layouts  0.71 us (2%)
    ppermute x9, starting transfers between devices, shift(): return lax.ppermute(x, axis, [(i, (i + k) % n) for i in range(n)])  14.1 us
    all_gather x1, blocking collectives, per_device(): whole_vectors = lax.all_gather(task_input, 'task', axis=2, tiled=True)  8.96 us
    all_gather x1, blocking collectives, per_device(): lax.all_gather(jnp.transpose(images, (2, 0, 1)), 'task', axis=0, tiled=True)  8.58 us
    unnamed x4, matrix products  8.48 us
    ppermute x9, waiting for transfers between devices, shift(): return lax.ppermute(x, axis, [(i, (i + k) % n) for i in range(n)])  0.99 us
    dot_general x1, matrix products, per_device(): jnp.einsum('asn,ca->snc', whole_images, own_rows, preferred_element_type=...  0.94 us
  transfers between devices with their start and end apart: 9, of which 1 were waited for; matrix products, arithmetic and copies ran while one was open for 19% of the time, Pallas kernels for 0%

profile of v8, /device:TPU:0, one launch (start us, length us, event | category | flops | bytes accessed | tf_op | source)
XLA Modules:
  0.0 46.0 jit_solution(17921291521850325900)
XLA Ops:
  0.6 0.0 copy-start
  0.7 3.1 %collective-permute-start = (bf16[3,768]{1,0:T(4,128)(2,1)}, bf16[3,768]{1,0:T(4,128)(2,1)S(1)}, u32[]{:S(2)}, u32[]{:S(2)}) collective-permute-start(bf16[3,768]{1,0:T(4,128)(2,1)} %param.6), channel_id=1, source_target_pairs={{0,4},{4,8},{8,12},{12,0},{1,5},{5,9},{9,13},{13,1},{2,6},{6,10},{... | collective-permute-start | bytes 13832 | tf_op jit(solution)/shard_map/ppermute | solution.py:16
  3.7 2.1 %collective-permute-start.4 = (bf16[3,768]{1,0:T(4,128)(2,1)}, bf16[3,768]{1,0:T(4,128)(2,1)S(1)}, u32[]{:S(2)}, u32[]{:S(2)}) collective-permute-start(bf16[3,768]{1,0:T(4,128)(2,1)} %param.6), channel_id=1, source_target_pairs={{0,12},{4,0},{8,4},{12,8},{1,13},{5,1},{9,5},{13,9},{2,14},{6,2},{... | collective-permute-start | bytes 13832 | tf_op jit(solution)/shard_map/ppermute | solution.py:16
  5.8 0.9 %collective-permute-start.2 = (bf16[3,768]{1,0:T(4,128)(2,1)}, bf16[3,768]{1,0:T(4,128)(2,1)S(1)}, u32[]{:S(2)}, u32[]{:S(2)}) collective-permute-start(bf16[3,768]{1,0:T(4,128)(2,1)} %param.6), channel_id=1, source_target_pairs={{0,8},{4,12},{8,0},{12,4},{1,9},{5,13},{9,1},{13,5},{2,10},{6,14},... | collective-permute-start | bytes 13832 | tf_op jit(solution)/shard_map/ppermute | solution.py:16
  6.8 1.3 %collective-permute-start.5 = (bf16[2,768,64]{1,2,0:T(8,128)(2,1)}, bf16[2,768,64]{1,2,0:T(8,128)(2,1)S(1)}, u32[]{:S(2)}, u32[]{:S(2)}) collective-permute-start(bf16[2,768,64]{1,2,0:T(8,128)(2,1)} %param.8), channel_id=1, source_target_pairs={{0,12},{4,0},{8,4},{12,8},{1,13},{5,1},{9,5},{13,9},{2,14},{6,2},{... | collective-permute-start | bytes 589832 | tf_op jit(solution)/shard_map/ppermute | solution.py:16
  8.1 1.7 %collective-permute-start.3 = (bf16[2,768,64]{1,2,0:T(8,128)(2,1)}, bf16[2,768,64]{1,2,0:T(8,128)(2,1)S(1)}, u32[]{:S(2)}, u32[]{:S(2)}) collective-permute-start(bf16[2,768,64]{1,2,0:T(8,128)(2,1)} %param.8), channel_id=1, source_target_pairs={{0,8},{4,12},{8,0},{12,4},{1,9},{5,13},{9,1},{13,5},{2,10},{6,14},... | collective-permute-start | bytes 589832 | tf_op jit(solution)/shard_map/ppermute | solution.py:16
  9.8 0.7 %broadcast_divide_fusion = f32[3]{0:T(128)S(1)} fusion(f32[3]{0:T(128)} %param.7), kind=kLoop, calls=%fused_computation.35 | loop fusion | flops 3 | bytes 24 | tf_op jit(solution)/shard_map/div | solution.py:40
  10.5 1.0 %collective-permute-start.1 = (bf16[2,768,64]{1,2,0:T(8,128)(2,1)}, bf16[2,768,64]{1,2,0:T(8,128)(2,1)S(1)}, u32[]{:S(2)}, u32[]{:S(2)}) collective-permute-start(bf16[2,768,64]{1,2,0:T(8,128)(2,1)} %param.8), channel_id=1, source_target_pairs={{0,4},{4,8},{8,12},{12,0},{1,5},{5,9},{9,13},{13,1},{2,6},{6,10},{... | collective-permute-start | bytes 589832 | tf_op jit(solution)/shard_map/ppermute | solution.py:16
  11.5 0.8 %convert_multiply_fusion.2 = (f32[3,768]{1,0:T(4,128)S(1)}, f32[3,768]{1,0:T(4,128)S(1)}, f32[3,768]{1,0:T(4,128)S(1)}, f32[3,768]{1,0:T(4,128)S(1)}) fusion(bf16[3,768]{1,0:T(4,128)(2,1)S(1)} %collective-permute-done, f32[3]{0:T(128)S(1)} %broadcast_divide_fusion, bf16[3,768]{1,0:T(4,128)(2,1)S(1)} %collective-permute-done.2, ...), kind=kLoop, calls=%fused_computation.20 | loop fusion | flops 18432 | bytes 55308 | tf_op jit(solution)/shard_map/mul | solution.py:44
  12.3 9.0 %all_gather.7 = bf16[2,768,256]{1,2,0:T(8,128)(2,1)S(1)} all-gather(bf16[2,768,64]{1,2,0:T(8,128)(2,1)} %param.8), channel_id=1, replica_groups=mesh['groups'=2,'dp'=4,'task'=4] {'task'}, dimensions={2}, use_global_device_ids=true | all-gather | bytes 983040 | tf_op jit(solution)/shard_map/all_gather | solution.py:67
  21.3 2.1 %fusion = f32[768,128]{0,1:S(1)} fusion(bf16[768,128]{0,1:T(8,128)(2,1)S(1)} %bitcast.32, f32[768]{0:T(1024)S(1)} %get-tuple-element.11, f32[768]{0:T(1024)S(1)} %get-tuple-element.12, f32[768]{0:T(1024)S(1)} %get-tuple-element.10), kind=kOutput, calls=%fused_computation.5 | convolution fusion | flops 157483008 | bytes 599040
  23.5 2.1 %fusion.3 = f32[768,128]{0,1:S(1)} fusion(bf16[768,128]{0,1:T(8,128)(2,1)S(1)} %bitcast.38, f32[768]{0:T(1024)S(1)} %get-tuple-element.14, f32[768]{0:T(1024)S(1)} %get-tuple-element.15, f32[768]{0:T(1024)S(1)} %get-tuple-element.13, f32[768]{0:T(1024)S(1)} %get-tuple-element.11, f32[768]{0:T(1024)S(1)} %get-tuple-element.12, f32[768]{0:T(1024)S(1)} %get-tuple-element.10), kind=kOutput, calls=%fused_computation.8 | convolution fusion | flops 157483008 | bytes 608256
  25.6 1.0 %collective-permute-done.3 = bf16[2,768,64]{1,2,0:T(8,128)(2,1)S(1)} collective-permute-done((bf16[2,768,64]{1,2,0:T(8,128)(2,1)}, bf16[2,768,64]{1,2,0:T(8,128)(2,1)S(1)}, u32[]{:S(2)}, u32[]{:S(2)}) %collective-permute-start.3) | collective-permute-done | bytes 196640 | tf_op jit(solution)/shard_map/ppermute | solution.py:16
  26.6 2.1 %fusion.2 = f32[768,128]{0,1:S(1)} fusion(bf16[768,128]{0,1:T(8,128)(2,1)S(1)} %bitcast.37, f32[768]{0:T(1024)S(1)} %get-tuple-element.8, f32[768]{0:T(1024)S(1)} %get-tuple-element.9, f32[768]{0:T(1024)S(1)} %get-tuple-element.7, f32[768]{0:T(1024)S(1)} %get-tuple-element.11, f32[768]{0:T(1024)S(1)} %get-tuple-element.12, f32[768]{0:T(1024)S(1)} %get-tuple-element.10), kind=kOutput, calls=%fused_computation.7 | convolution fusion | flops 157483008 | bytes 608256
  28.7 2.1 %fusion.1 = f32[768,128]{0,1:S(1)} fusion(bf16[768,128]{0,1:T(8,128)(2,1)S(1)} %bitcast.39, f32[768]{0:T(1024)S(1)} %get-tuple-element.5, f32[768]{0:T(1024)S(1)} %get-tuple-element.6, f32[768]{0:T(1024)S(1)} %get-tuple-element.4, f32[768]{0:T(1024)S(1)} %get-tuple-element.11, f32[768]{0:T(1024)S(1)} %get-tuple-element.12, f32[768]{0:T(1024)S(1)} %get-tuple-element.10), kind=kOutput, calls=%fused_computation.6 | convolution fusion | flops 157483008 | bytes 608256
  30.8 0.1 add_convert_fusion
  30.9 0.6 %copy-done.3 = bf16[2]{0:T(256)(128)(2,1)S(1)} copy-done((bf16[2]{0:T(256)(128)(2,1)S(1)}, bf16[2]{0:T(256)(128)(2,1)}, u32[]{:S(2)}) %copy-start.3) | copy-done | bytes 28
  31.5 0.4 convolution_bitcast_fusion
  31.9 0.1 collective-permute-start.8
  31.9 2.3 %collective-permute-start.7 = (f32[64,256]{1,0:T(8,128)S(1)}, f32[64,256]{1,0:T(8,128)S(1)}, u32[]{:S(2)}, u32[]{:S(2)}) collective-permute-start(f32[64,256]{1,0:T(8,128)S(1)} %convolution_bitcast_fusion), channel_id=1, source_target_pairs={{0,4},{4,8},{8,12},{12,0},{1,5},{5,9},{9,13},{13,1},{2,6},{6,10},{... | collective-permute-start | bytes 196616 | tf_op jit(solution)/shard_map/ppermute | solution.py:16
  34.2 1.6 %collective-permute-start.6 = (f32[64,256]{1,0:T(8,128)S(1)}, f32[64,256]{1,0:T(8,128)S(1)}, u32[]{:S(2)}, u32[]{:S(2)}) collective-permute-start(f32[64,256]{1,0:T(8,128)S(1)} %convolution_bitcast_fusion), channel_id=1, source_target_pairs={{0,12},{4,0},{8,4},{12,8},{1,13},{5,1},{9,5},{13,9},{2,14},{6,2},{... | collective-permute-start | bytes 196616 | tf_op jit(solution)/shard_map/ppermute | solution.py:16
  35.8 8.6 %all_gather.6 = bf16[256,2,768]{2,0,1:T(8,128)(2,1)S(1)} all-gather(bf16[64,2,768]{2,0,1:T(8,128)(2,1)S(1)} %bitcast.31), channel_id=1, replica_groups=mesh['groups'=2,'dp'=4,'task'=4] {'task'}, dimensions={0}, use_global_device_ids=true | all-gather | bytes 983040 | tf_op jit(solution)/shard_map/all_gather | solution.py:75
  44.4 0.9 %fusion.4 = bf16[2,768,64]{1,2,0:T(8,128)(2,1)} fusion(bf16[256,2,768]{2,0,1:T(8,128)(2,1)S(1)} %all_gather.6, bf16[2,768,64]{1,2,0:T(8,128)(2,1)S(1)} %copy-done.1, f32[64]{0:T(128)S(1)} %copy-done.2, bf16[256,256]{1,0:T(8,128)(2,1)S(1)} %copy-done, s32[]{:T(128)S(6)} %select_n.22), kind=kOutput, calls=%fused_computation.9 | convolution fusion | flops 50724864 | bytes 1212932 | tf_op jit(solution)/shard_map/asn,ca->snc/dot_general | solution.py:77
  45.4 0.7 %add_multiply_fusion = f32[64,256]{1,0:T(8,128)} fusion(f32[64,256]{1,0:T(8,128)S(1)} %collective-permute-done.8, f32[64,256]{1,0:T(8,128)S(1)} %collective-permute-done.7, f32[64,256]{1,0:T(8,128)S(1)} %collective-permute-done.6, f32[64,256]{1,0:T(8,128)S(1)} %convolution_bitcast_fusion, pred[]{:T(512)S(6)} %eq.5), kind=kLoop, calls=%fused_computation.15 | loop fusion | flops 98304 | bytes 327681 | tf_op jit(solution)/shard_map/div | solution.py:79
  (18 shorter events, 0.2 us)
Async XLA Ops:
  0.6 43.8 %copy-start = (bf16[256,256]{1,0:T(8,128)(2,1)S(1)}, bf16[256,256]{1,0:T(8,128)(2,1)}, u32[]{:S(2)}) copy-start(bf16[256,256]{1,0:T(8,128)(2,1)} %param.9) | copy-start | bytes 393220
  0.6 20.6 %copy-start.1 = (bf16[2,768,64]{1,2,0:T(8,128)(2,1)S(1)}, bf16[2,768,64]{1,2,0:T(8,128)(2,1)}, u32[]{:S(2)}) copy-start(bf16[2,768,64]{1,2,0:T(8,128)(2,1)} %param.8) | copy-start | bytes 589828
  0.7 9.8 %collective-permute-start = (bf16[3,768]{1,0:T(4,128)(2,1)}, bf16[3,768]{1,0:T(4,128)(2,1)S(1)}, u32[]{:S(2)}, u32[]{:S(2)}) collective-permute-start(bf16[3,768]{1,0:T(4,128)(2,1)} %param.6), channel_id=1, source_target_pairs={{0,4},{4,8},{8,12},{12,0},{1,5},{5,9},{9,13},{13,1},{2,6},{6,10},{... | collective-permute-start | bytes 13832 | tf_op jit(solution)/shard_map/ppermute | solution.py:16
  3.7 7.7 %collective-permute-start.4 = (bf16[3,768]{1,0:T(4,128)(2,1)}, bf16[3,768]{1,0:T(4,128)(2,1)S(1)}, u32[]{:S(2)}, u32[]{:S(2)}) collective-permute-start(bf16[3,768]{1,0:T(4,128)(2,1)} %param.6), channel_id=1, source_target_pairs={{0,12},{4,0},{8,4},{12,8},{1,13},{5,1},{9,5},{13,9},{2,14},{6,2},{... | collective-permute-start | bytes 13832 | tf_op jit(solution)/shard_map/ppermute | solution.py:16
  5.8 5.6 %collective-permute-start.2 = (bf16[3,768]{1,0:T(4,128)(2,1)}, bf16[3,768]{1,0:T(4,128)(2,1)S(1)}, u32[]{:S(2)}, u32[]{:S(2)}) collective-permute-start(bf16[3,768]{1,0:T(4,128)(2,1)} %param.6), channel_id=1, source_target_pairs={{0,8},{4,12},{8,0},{12,4},{1,9},{5,13},{9,1},{13,5},{2,10},{6,14},... | collective-permute-start | bytes 13832 | tf_op jit(solution)/shard_map/ppermute | solution.py:16
  6.8 16.7 %collective-permute-start.5 = (bf16[2,768,64]{1,2,0:T(8,128)(2,1)}, bf16[2,768,64]{1,2,0:T(8,128)(2,1)S(1)}, u32[]{:S(2)}, u32[]{:S(2)}) collective-permute-start(bf16[2,768,64]{1,2,0:T(8,128)(2,1)} %param.8), channel_id=1, source_target_pairs={{0,12},{4,0},{8,4},{12,8},{1,13},{5,1},{9,5},{13,9},{2,14},{6,2},{... | collective-permute-start | bytes 589832 | tf_op jit(solution)/shard_map/ppermute | solution.py:16
  8.1 18.4 %collective-permute-start.3 = (bf16[2,768,64]{1,2,0:T(8,128)(2,1)}, bf16[2,768,64]{1,2,0:T(8,128)(2,1)S(1)}, u32[]{:S(2)}, u32[]{:S(2)}) collective-permute-start(bf16[2,768,64]{1,2,0:T(8,128)(2,1)} %param.8), channel_id=1, source_target_pairs={{0,8},{4,12},{8,0},{12,4},{1,9},{5,13},{9,1},{13,5},{2,10},{6,14},... | collective-permute-start | bytes 589832 | tf_op jit(solution)/shard_map/ppermute | solution.py:16
  10.5 18.2 %collective-permute-start.1 = (bf16[2,768,64]{1,2,0:T(8,128)(2,1)}, bf16[2,768,64]{1,2,0:T(8,128)(2,1)S(1)}, u32[]{:S(2)}, u32[]{:S(2)}) collective-permute-start(bf16[2,768,64]{1,2,0:T(8,128)(2,1)} %param.8), channel_id=1, source_target_pairs={{0,4},{4,8},{8,12},{12,0},{1,5},{5,9},{9,13},{13,1},{2,6},{6,10},{... | collective-permute-start | bytes 589832 | tf_op jit(solution)/shard_map/ppermute | solution.py:16
  30.8 0.7 %copy-start.3 = (bf16[2]{0:T(256)(128)(2,1)S(1)}, bf16[2]{0:T(256)(128)(2,1)}, u32[]{:S(2)}) copy-start(bf16[2]{0:T(256)(128)(2,1)} %constant.36.clone) | copy-start | bytes 16
  31.5 12.9 %copy-start.2 = (f32[64]{0:T(128)S(1)}, f32[64]{0:T(128)}, u32[]{:S(2)}) copy-start(f32[64]{0:T(128)} %param.10) | copy-start | bytes 772
  31.9 13.5 %collective-permute-start.8 = (f32[64,256]{1,0:T(8,128)S(1)}, f32[64,256]{1,0:T(8,128)S(1)}, u32[]{:S(2)}, u32[]{:S(2)}) collective-permute-start(f32[64,256]{1,0:T(8,128)S(1)} %convolution_bitcast_fusion), channel_id=1, source_target_pairs={{0,8},{4,12},{8,0},{12,4},{1,9},{5,13},{9,1},{13,5},{2,10},{6,14},... | collective-permute-start | bytes 196616 | tf_op jit(solution)/shard_map/ppermute | solution.py:16
  31.9 13.4 %collective-permute-start.7 = (f32[64,256]{1,0:T(8,128)S(1)}, f32[64,256]{1,0:T(8,128)S(1)}, u32[]{:S(2)}, u32[]{:S(2)}) collective-permute-start(f32[64,256]{1,0:T(8,128)S(1)} %convolution_bitcast_fusion), channel_id=1, source_target_pairs={{0,4},{4,8},{8,12},{12,0},{1,5},{5,9},{9,13},{13,1},{2,6},{6,10},{... | collective-permute-start | bytes 196616 | tf_op jit(solution)/shard_map/ppermute | solution.py:16
  34.2 11.1 %collective-permute-start.6 = (f32[64,256]{1,0:T(8,128)S(1)}, f32[64,256]{1,0:T(8,128)S(1)}, u32[]{:S(2)}, u32[]{:S(2)}) collective-permute-start(f32[64,256]{1,0:T(8,128)S(1)} %convolution_bitcast_fusion), channel_id=1, source_target_pairs={{0,12},{4,0},{8,4},{12,8},{1,13},{5,1},{9,5},{13,9},{2,14},{6,2},{... | collective-permute-start | bytes 196616 | tf_op jit(solution)/shard_map/ppermute | solution.py:16

commit v9 on v7

--- a/solution.py
+++ b/solution.py
@@ -44,10 +44,12 @@
 
     task_input = vectors
     if n_dp <= 4:
-        moved = [shift(vectors, "dp", k, n_dp) for k in range(1, n_dp)]
-        peer_coords = [shift(coords, "dp", k, n_dp) for k in range(1, n_dp)]
+        summed, sent_vectors, sent_coords = lax.optimization_barrier(
+            (block(coords, vectors), vectors, coords)
+        )
+        moved = [shift(sent_vectors, "dp", k, n_dp) for k in range(1, n_dp)]
+        peer_coords = [shift(sent_coords, "dp", k, n_dp) for k in range(1, n_dp)]
         task_input = lax.optimization_barrier((vectors, peer_coords))[0]
-        summed = block(coords, vectors)
         for k in range(1, n_dp):
             summed = summed + block(peer_coords[k - 1], moved[k - 1])
     else:

time: 44.9 us -> 45.5 us (1.013)
  other arithmetic: 6.81 us -> 5.89 us
  blocking collectives: 16.5 us -> 17.2 us
  waiting for transfers between devices: 0.02 us -> 0.64 us
    dot_general x0 -> x3, matrix products: none -> 3.34 us  [block(): jnp.einsum('nr,srm->snm', tile, values, preferred_element_type=jnp.float32)]
    unnamed x4 -> x1, matrix products: 4.38 us -> 1.1 us
    reduce_sum x1 -> x2, other arithmetic: 4.65 us -> 3.68 us  [kernel_tile(): return jnp.exp(0.1 - jnp.sqrt(jnp.sum(diff * diff, axis=0) + 0.01))]
    mul x0 -> x1, other arithmetic: none -> 0.77 us  [per_device(): own_scaled = coords.astype(jnp.float32) * inverse[:, None]]
    all_gather x1, blocking collectives: 7.87 us -> 8.58 us  [per_device(): lax.all_gather(jnp.transpose(images, (2, 0, 1)), 'task', axis=0, tiled=True)]
    mul x1, other arithmetic: 0.77 us -> 0.08 us  [block(): right = right_coords.astype(jnp.float32) * inverse[:, None]]
    ppermute x9, waiting for transfers between devices: 0.02 us -> 0.64 us  [shift(): return lax.ppermute(x, axis, [(i, (i + k) % n) for i in range(n)])]
  transfers between devices with their start and end apart: 9 -> 9, of which waited for: 0 -> 1; matrix products, arithmetic and copies ran while one was open for 23% -> 14% of each run, Pallas kernels for 0% -> 0%
where the time goes in v9:
time: 45.5 us; the launch traced here: 45.3 us
  blocking collectives  17.2 us (38%)
  starting transfers between devices  15 us (33%)
  other arithmetic  5.89 us (13%)
  matrix products  5.75 us (13%)
  between operations  0.74 us (2%)
  waiting for transfers between devices  0.64 us (1%)
    ppermute x9, starting transfers between devices, shift(): return lax.ppermute(x, axis, [(i, (i + k) % n) for i in range(n)])  15 us
    all_gather x1, blocking collectives, per_device(): whole_vectors = lax.all_gather(task_input, 'task', axis=2, tiled=True)  8.6 us
    all_gather x1, blocking collectives, per_device(): lax.all_gather(jnp.transpose(images, (2, 0, 1)), 'task', axis=0, tiled=True)  8.58 us
    reduce_sum x2, other arithmetic, kernel_tile(): return jnp.exp(0.1 - jnp.sqrt(jnp.sum(diff * diff, axis=0) + 0.01))  3.68 us
    dot_general x3, matrix products, block(): jnp.einsum('nr,srm->snm', tile, values, preferred_element_type=jnp.float32)  3.34 us
    unnamed x1, matrix products  1.1 us
    dot_general x1, matrix products, per_device(): jnp.einsum('asn,ca->snc', whole_images, own_rows, preferred_element_type=...  0.94 us
  transfers between devices with their start and end apart: 9, of which 1 were waited for; matrix products, arithmetic and copies ran while one was open for 14% of the time, Pallas kernels for 0%

profile of v9, /device:TPU:0, one launch (start us, length us, event | category | flops | bytes accessed | tf_op | source)
XLA Modules:
  0.0 45.3 jit_solution(7390977582965760708)
XLA Ops:
  0.6 0.0 copy-start
  0.7 0.7 %broadcast_divide_fusion = f32[3]{0:T(128)S(1)} fusion(f32[3]{0:T(128)} %param.7), kind=kLoop, calls=%fused_computation.38 | loop fusion | flops 3 | bytes 24 | tf_op jit(solution)/shard_map/div | solution.py:37
  1.4 0.8 %convert_multiply_fusion.3 = f32[3,768]{1,0:T(4,128)S(1)} fusion(bf16[3,768]{1,0:T(4,128)(2,1)} %param.6, f32[3]{0:T(128)S(1)} %broadcast_divide_fusion), kind=kLoop, calls=%fused_computation.36 | loop fusion | flops 4608 | bytes 13836 | tf_op jit(solution)/shard_map/mul | solution.py:38
  2.1 0.7 %multiply_reduce_fusion.3 = f32[768,768]{1,0:T(8,128)S(1)} fusion(f32[3,768]{1,0:T(4,128)S(1)} %convert_multiply_fusion.3), kind=kLoop, calls=%fused_computation.3 | loop fusion | flops 4718592 | bytes 2368512 | tf_op jit(solution)/shard_map/reduce_sum | solution.py:9
  2.9 1.1 %fusion.15 = f32[768,128]{0,1:S(1)} fusion(bf16[768,128]{0,1:T(8,128)(2,1)S(1)} %bitcast.44, f32[768,768]{1,0:T(8,128)S(1)} %multiply_reduce_fusion.3), kind=kOutput, calls=%fused_computation.24 | convolution fusion | flops 152764416 | bytes 2949120
  4.0 3.1 %collective-permute-start.1 = (bf16[3,768]{1,0:T(4,128)(2,1)S(1)}, bf16[3,768]{1,0:T(4,128)(2,1)S(1)}, u32[]{:S(2)}, u32[]{:S(2)}) collective-permute-start(bf16[3,768]{1,0:T(4,128)(2,1)S(1)} %copy-done.2), channel_id=1, source_target_pairs={{0,4},{4,8},{8,12},{12,0},{1,5},{5,9},{9,13},{13,1},{2,6},{6,10},{... | collective-permute-start | bytes 13832 | tf_op jit(solution)/shard_map/ppermute | solution.py:13
  7.0 2.6 %collective-permute-start.3 = (bf16[3,768]{1,0:T(4,128)(2,1)S(1)}, bf16[3,768]{1,0:T(4,128)(2,1)S(1)}, u32[]{:S(2)}, u32[]{:S(2)}) collective-permute-start(bf16[3,768]{1,0:T(4,128)(2,1)S(1)} %copy-done.2), channel_id=1, source_target_pairs={{0,8},{4,12},{8,0},{12,4},{1,9},{5,13},{9,1},{13,5},{2,10},{6,14},... | collective-permute-start | bytes 13832 | tf_op jit(solution)/shard_map/ppermute | solution.py:13
  9.6 1.3 %collective-permute-start.5 = (bf16[3,768]{1,0:T(4,128)(2,1)S(1)}, bf16[3,768]{1,0:T(4,128)(2,1)S(1)}, u32[]{:S(2)}, u32[]{:S(2)}) collective-permute-start(bf16[3,768]{1,0:T(4,128)(2,1)S(1)} %copy-done.2), channel_id=1, source_target_pairs={{0,12},{4,0},{8,4},{12,8},{1,13},{5,1},{9,5},{13,9},{2,14},{6,2},{... | collective-permute-start | bytes 13832 | tf_op jit(solution)/shard_map/ppermute | solution.py:13
  11.0 0.2 collective-permute-start.2
  11.2 2.8 %collective-permute-start.4 = (bf16[2,768,64]{1,2,0:T(8,128)(2,1)S(1)}, bf16[2,768,64]{1,2,0:T(8,128)(2,1)S(1)}, u32[]{:S(2)}, u32[]{:S(2)}) collective-permute-start(bf16[2,768,64]{1,2,0:T(8,128)(2,1)S(1)} %copy-done.1), channel_id=1, source_target_pairs={{0,12},{4,0},{8,4},{12,8},{1,13},{5,1},{9,5},{13,9},{2,14},{6,2},{... | collective-permute-start | bytes 589832 | tf_op jit(solution)/shard_map/ppermute | solution.py:13
  14.0 0.1 convert_multiply_fusion
  14.1 3.0 %multiply_reduce_fusion.2 = (f32[768,768]{1,0:T(8,128)S(1)}, f32[768,768]{1,0:T(8,128)S(1)}, f32[768,768]{1,0:T(8,128)S(1)}) fusion(f32[3,768]{1,0:T(4,128)S(1)} %get-tuple-element.14, f32[3,768]{1,0:T(4,128)S(1)} %convert_multiply_fusion.3, f32[3,768]{1,0:T(4,128)S(1)} %get-tuple-element.15, f32[3,768]{1,0:T(4,128)S(1)} %get-tuple-element.13), kind=kLoop, calls=%fused_computation.2 | loop fusion | flops 14155776 | bytes 7114752 | tf_op jit(solution)/shard_map/reduce_sum | solution.py:9
  17.1 8.6 %all_gather.7 = bf16[2,768,256]{1,2,0:T(8,128)(2,1)S(1)} all-gather(bf16[2,768,64]{1,2,0:T(8,128)(2,1)S(1)} %copy-done.1), channel_id=1, replica_groups=mesh['groups'=2,'dp'=4,'task'=4] {'task'}, dimensions={2}, use_global_device_ids=true | all-gather | bytes 983040 | tf_op jit(solution)/shard_map/all_gather | solution.py:66
  25.7 0.6 %collective-permute-done.2 = bf16[2,768,64]{1,2,0:T(8,128)(2,1)S(1)} collective-permute-done((bf16[2,768,64]{1,2,0:T(8,128)(2,1)S(1)}, bf16[2,768,64]{1,2,0:T(8,128)(2,1)S(1)}, u32[]{:S(2)}, u32[]{:S(2)}) %collective-permute-start.2) | collective-permute-done | bytes 196640 | tf_op jit(solution)/shard_map/ppermute | solution.py:13
  26.3 1.1 %convolution_bitcast_fusion.1 = f32[2,768,64]{1,2,0:T(8,128)S(1)} fusion(bf16[2,768,64]{1,2,0:T(8,128)(2,1)S(1)} %collective-permute-done.2, f32[768,768]{1,0:T(8,128)S(1)} %get-tuple-element.11), kind=kOutput, calls=%fused_computation.9 | convolution fusion | flops 152764416 | bytes 2949120 | tf_op jit(solution)/shard_map/nr,srm->snm/dot_general | solution.py:43
  27.4 1.1 %convolution_bitcast_fusion = f32[2,768,64]{1,2,0:T(8,128)S(1)} fusion(bf16[2,768,64]{1,2,0:T(8,128)(2,1)S(1)} %collective-permute-done.4, f32[768,768]{1,0:T(8,128)S(1)} %get-tuple-element.12), kind=kOutput, calls=%fused_computation.8 | convolution fusion | flops 152764416 | bytes 2949120 | tf_op jit(solution)/shard_map/nr,srm->snm/dot_general | solution.py:43
  28.5 1.1 %fusion.16 = bf16[2,768,64]{1,2,0:T(8,128)(2,1)S(1)} fusion(f32[2,768,64]{1,2,0:T(8,128)S(1)} %convolution_bitcast_fusion, f32[2,768,64]{1,2,0:T(8,128)S(1)} %convolution_bitcast_fusion.1, f32[2,768,64]{1,2,0:T(8,128)S(1)} %bitcast.45, bf16[2,768,64]{1,2,0:T(8,128)(2,1)S(1)} %collective-permute-done, f32[768,768]{1,0:T(8,128)S(1)} %get-tuple-element.10), kind=kOutput, calls=%fused_computation.25 | convolution fusion | flops 153157632 | bytes 3932160 | tf_op jit(solution)/shard_map/nr,srm->snm/dot_general | solution.py:43
  29.7 0.4 convolution_bitcast_fusion.3
  30.1 3.2 %collective-permute-start.6 = (f32[64,256]{1,0:T(8,128)S(1)}, f32[64,256]{1,0:T(8,128)S(1)}, u32[]{:S(2)}, u32[]{:S(2)}) collective-permute-start(f32[64,256]{1,0:T(8,128)S(1)} %convolution_bitcast_fusion.3), channel_id=1, source_target_pairs={{0,12},{4,0},{8,4},{12,8},{1,13},{5,1},{9,5},{13,9},{2,14},{6,2},{... | collective-permute-start | bytes 196616 | tf_op jit(solution)/shard_map/ppermute | solution.py:13
  33.3 0.3 collective-permute-start.7
  33.7 1.4 %collective-permute-start.8 = (f32[64,256]{1,0:T(8,128)S(1)}, f32[64,256]{1,0:T(8,128)S(1)}, u32[]{:S(2)}, u32[]{:S(2)}) collective-permute-start(f32[64,256]{1,0:T(8,128)S(1)} %convolution_bitcast_fusion.3), channel_id=1, source_target_pairs={{0,8},{4,12},{8,0},{12,4},{1,9},{5,13},{9,1},{13,5},{2,10},{6,14},... | collective-permute-start | bytes 196616 | tf_op jit(solution)/shard_map/ppermute | solution.py:13
  35.1 8.6 %all_gather.6 = bf16[256,2,768]{2,0,1:T(8,128)(2,1)S(1)} all-gather(bf16[64,2,768]{2,0,1:T(8,128)(2,1)S(1)} %bitcast.43), channel_id=1, replica_groups=mesh['groups'=2,'dp'=4,'task'=4] {'task'}, dimensions={0}, use_global_device_ids=true | all-gather | bytes 983040 | tf_op jit(solution)/shard_map/all_gather | solution.py:74
  43.6 0.9 %fusion.19 = bf16[2,768,64]{1,2,0:T(8,128)(2,1)} fusion(bf16[256,2,768]{2,0,1:T(8,128)(2,1)S(1)} %all_gather.6, bf16[2,768,64]{1,2,0:T(8,128)(2,1)S(1)} %copy-done.1, f32[64]{0:T(128)S(1)} %copy-done.3, bf16[256,256]{1,0:T(8,128)(2,1)S(1)} %copy-done, s32[]{:T(128)S(6)} %select_n.22), kind=kOutput, calls=%fused_computation.26 | convolution fusion | flops 50724864 | bytes 1212932 | tf_op jit(solution)/shard_map/asn,ca->snc/dot_general | solution.py:76
  44.6 0.7 %add_multiply_fusion = f32[64,256]{1,0:T(8,128)} fusion(f32[64,256]{1,0:T(8,128)S(1)} %collective-permute-done.8, f32[64,256]{1,0:T(8,128)S(1)} %collective-permute-done.7, f32[64,256]{1,0:T(8,128)S(1)} %collective-permute-done.6, f32[64,256]{1,0:T(8,128)S(1)} %convolution_bitcast_fusion.3, pred[]{:T(512)S(6)} %eq.5), kind=kLoop, calls=%fused_computation.30 | loop fusion | flops 98304 | bytes 327681 | tf_op jit(solution)/shard_map/div | solution.py:78
  (18 shorter events, 0.0 us)
Async XLA Ops:
  0.6 43.0 %copy-start = (bf16[256,256]{1,0:T(8,128)(2,1)S(1)}, bf16[256,256]{1,0:T(8,128)(2,1)}, u32[]{:S(2)}) copy-start(bf16[256,256]{1,0:T(8,128)(2,1)} %param.9) | copy-start | bytes 393220
  0.6 2.2 %copy-start.1 = (bf16[2,768,64]{1,2,0:T(8,128)(2,1)S(1)}, bf16[2,768,64]{1,2,0:T(8,128)(2,1)}, u32[]{:S(2)}) copy-start(bf16[2,768,64]{1,2,0:T(8,128)(2,1)} %param.8) | copy-start | bytes 589828
  2.1 1.8 %copy-start.2 = (bf16[3,768]{1,0:T(4,128)(2,1)S(1)}, bf16[3,768]{1,0:T(4,128)(2,1)}, u32[]{:S(2)}) copy-start(bf16[3,768]{1,0:T(4,128)(2,1)} %param.6) | copy-start | bytes 13828
  4.0 10.1 %collective-permute-start.1 = (bf16[3,768]{1,0:T(4,128)(2,1)S(1)}, bf16[3,768]{1,0:T(4,128)(2,1)S(1)}, u32[]{:S(2)}, u32[]{:S(2)}) collective-permute-start(bf16[3,768]{1,0:T(4,128)(2,1)S(1)} %copy-done.2), channel_id=1, source_target_pairs={{0,4},{4,8},{8,12},{12,0},{1,5},{5,9},{9,13},{13,1},{2,6},{6,10},{... | collective-permute-start | bytes 13832 | tf_op jit(solution)/shard_map/ppermute | solution.py:13
  7.0 7.0 %collective-permute-start.3 = (bf16[3,768]{1,0:T(4,128)(2,1)S(1)}, bf16[3,768]{1,0:T(4,128)(2,1)S(1)}, u32[]{:S(2)}, u32[]{:S(2)}) collective-permute-start(bf16[3,768]{1,0:T(4,128)(2,1)S(1)} %copy-done.2), channel_id=1, source_target_pairs={{0,8},{4,12},{8,0},{12,4},{1,9},{5,13},{9,1},{13,5},{2,10},{6,14},... | collective-permute-start | bytes 13832 | tf_op jit(solution)/shard_map/ppermute | solution.py:13
  9.6 4.4 %collective-permute-start.5 = (bf16[3,768]{1,0:T(4,128)(2,1)S(1)}, bf16[3,768]{1,0:T(4,128)(2,1)S(1)}, u32[]{:S(2)}, u32[]{:S(2)}) collective-permute-start(bf16[3,768]{1,0:T(4,128)(2,1)S(1)} %copy-done.2), channel_id=1, source_target_pairs={{0,12},{4,0},{8,4},{12,8},{1,13},{5,1},{9,5},{13,9},{2,14},{6,2},{... | collective-permute-start | bytes 13832 | tf_op jit(solution)/shard_map/ppermute | solution.py:13
  11.0 15.3 %collective-permute-start.2 = (bf16[2,768,64]{1,2,0:T(8,128)(2,1)S(1)}, bf16[2,768,64]{1,2,0:T(8,128)(2,1)S(1)}, u32[]{:S(2)}, u32[]{:S(2)}) collective-permute-start(bf16[2,768,64]{1,2,0:T(8,128)(2,1)S(1)} %copy-done.1), channel_id=1, source_target_pairs={{0,8},{4,12},{8,0},{12,4},{1,9},{5,13},{9,1},{13,5},{2,10},{6,14},... | collective-permute-start | bytes 589832 | tf_op jit(solution)/shard_map/ppermute | solution.py:13
  11.2 16.2 %collective-permute-start.4 = (bf16[2,768,64]{1,2,0:T(8,128)(2,1)S(1)}, bf16[2,768,64]{1,2,0:T(8,128)(2,1)S(1)}, u32[]{:S(2)}, u32[]{:S(2)}) collective-permute-start(bf16[2,768,64]{1,2,0:T(8,128)(2,1)S(1)} %copy-done.1), channel_id=1, source_target_pairs={{0,12},{4,0},{8,4},{12,8},{1,13},{5,1},{9,5},{13,9},{2,14},{6,2},{... | collective-permute-start | bytes 589832 | tf_op jit(solution)/shard_map/ppermute | solution.py:13
  14.0 14.5 %collective-permute-start = (bf16[2,768,64]{1,2,0:T(8,128)(2,1)S(1)}, bf16[2,768,64]{1,2,0:T(8,128)(2,1)S(1)}, u32[]{:S(2)}, u32[]{:S(2)}) collective-permute-start(bf16[2,768,64]{1,2,0:T(8,128)(2,1)S(1)} %copy-done.1), channel_id=1, source_target_pairs={{0,4},{4,8},{8,12},{12,0},{1,5},{5,9},{9,13},{13,1},{2,6},{6,10},{... | collective-permute-start | bytes 589832 | tf_op jit(solution)/shard_map/ppermute | solution.py:13
  28.5 1.2 %copy-start.4 = (bf16[2]{0:T(256)(128)(2,1)S(1)}, bf16[2]{0:T(256)(128)(2,1)}, u32[]{:S(2)}) copy-start(bf16[2]{0:T(256)(128)(2,1)} %constant.38.clone) | copy-start | bytes 16
  28.5 15.1 %copy-start.3 = (f32[64]{0:T(128)S(1)}, f32[64]{0:T(128)}, u32[]{:S(2)}) copy-start(f32[64]{0:T(128)} %param.10) | copy-start | bytes 772
  30.1 14.5 %collective-permute-start.6 = (f32[64,256]{1,0:T(8,128)S(1)}, f32[64,256]{1,0:T(8,128)S(1)}, u32[]{:S(2)}, u32[]{:S(2)}) collective-permute-start(f32[64,256]{1,0:T(8,128)S(1)} %convolution_bitcast_fusion.3), channel_id=1, source_target_pairs={{0,12},{4,0},{8,4},{12,8},{1,13},{5,1},{9,5},{13,9},{2,14},{6,2},{... | collective-permute-start | bytes 196616 | tf_op jit(solution)/shard_map/ppermute | solution.py:13
  33.3 11.3 %collective-permute-start.7 = (f32[64,256]{1,0:T(8,128)S(1)}, f32[64,256]{1,0:T(8,128)S(1)}, u32[]{:S(2)}, u32[]{:S(2)}) collective-permute-start(f32[64,256]{1,0:T(8,128)S(1)} %convolution_bitcast_fusion.3), channel_id=1, source_target_pairs={{0,4},{4,8},{8,12},{12,0},{1,5},{5,9},{9,13},{13,1},{2,6},{6,10},{... | collective-permute-start | bytes 196616 | tf_op jit(solution)/shard_map/ppermute | solution.py:13
  33.7 10.9 %collective-permute-start.8 = (f32[64,256]{1,0:T(8,128)S(1)}, f32[64,256]{1,0:T(8,128)S(1)}, u32[]{:S(2)}, u32[]{:S(2)}) collective-permute-start(f32[64,256]{1,0:T(8,128)S(1)} %convolution_bitcast_fusion.3), channel_id=1, source_target_pairs={{0,8},{4,12},{8,0},{12,4},{1,9},{5,13},{9,1},{13,5},{2,10},{6,14},... | collective-permute-start | bytes 196616 | tf_op jit(solution)/shard_map/ppermute | solution.py:13

commit v10 on v7

--- a/solution.py
+++ b/solution.py
@@ -61,7 +61,18 @@
         summed = block(coords, vectors)
         summed = lax.fori_loop(0, n_dp - 1, ring, (summed, coords, vectors))[0]
 
-    whole_vectors = lax.all_gather(task_input, "task", axis=2, tiled=True)
+    n_task = lax.axis_size("task")
+    task_index = lax.axis_index("task")
+    if n_task == 4:
+        partner = lax.ppermute(task_input, "task", [(i, i ^ 1) for i in range(4)])
+        even = task_index % 2 == 0
+        pair = jnp.concatenate(
+            [jnp.where(even, task_input, partner), jnp.where(even, partner, task_input)], axis=2
+        )
+        other = lax.ppermute(pair, "task", [(i, i ^ 2) for i in range(4)])
+        whole_vectors = jnp.concatenate([pair, other], axis=2)
+    else:
+        whole_vectors = lax.all_gather(task_input, "task", axis=2, tiled=True)
     images = summed.astype(jnp.bfloat16)
     signs = jnp.array([1.0, -1.0], jnp.bfloat16)
     signed = images * signs[:, None, None]
@@ -69,10 +80,15 @@
         "sna,snb->ab", signed, whole_vectors, preferred_element_type=jnp.float32
     )
     total = sum_over(partial_grad, "dp", n_dp)
-    whole_images = lax.all_gather(jnp.transpose(images, (2, 0, 1)), "task", axis=0, tiled=True)
+    gather_input = lax.optimization_barrier((images, whole_vectors))[0]
+    whole_images = lax.all_gather(jnp.transpose(gather_input, (2, 0, 1)), "task", axis=0, tiled=True)
     own_rows = lax.dynamic_slice_in_dim(mixing, task_start, local_tasks, 0)
     mixed = jnp.einsum("asn,ca->snc", whole_images, own_rows, preferred_element_type=jnp.float32)
     product = (mixed + noise[None, None, :] * vectors.astype(jnp.float32)).astype(jnp.bfloat16)
+    if n_task == 4:
+        half = 2 * local_tasks
+        swapped = jnp.concatenate([total[:, half:], total[:, :half]], axis=1)
+        total = jnp.where(task_index < 2, total, swapped)
     gradient = total / (2.0 * n_rows * n_dp)
     return (product, gradient)
 

time: 44.9 us -> 54.3 us (1.21)
  waiting for transfers between devices: 0.02 us -> 13.9 us
  blocking collectives: 16.5 us -> 8.58 us
  starting transfers between devices: 14.9 us -> 16.5 us
  local copies, waits for them, and re-layouts: 0.02 us -> 1.19 us
  other arithmetic: 6.81 us -> 7.47 us
    all_gather x2 -> x1, blocking collectives: 16.5 us -> 8.58 us  [per_device(): lax.all_gather(jnp.transpose(gather_input, (2, 0, 1)), 'task', axis=0, ti...]
    ppermute x9, waiting for transfers between devices: 0.02 us -> 7.18 us  [shift(): return lax.ppermute(x, axis, [(i, (i + k) % n) for i in range(n)])]
    ppermute x0 -> x2, waiting for transfers between devices: none -> 6.73 us  [the longest x1 6.73 us: per_device(): other = lax.ppermute(pair, 'task', [(i, i ^ 2) for i in range(4)])]
    ppermute x0 -> x2, starting transfers between devices: none -> 1.63 us  [the longest x1 1.55 us: per_device(): other = lax.ppermute(pair, 'task', [(i, i ^ 2) for i in range(4)])]
    optimization_barrier x0 -> x1, local copies, waits for them, and re-layouts: none -> 1.16 us  [per_device(): task_input = lax.optimization_barrier((vectors, peer_coords))[0]]
    concatenate x0 -> x2, other arithmetic: none -> 0.58 us  [the longest x1 0.36 us: per_device(): whole_vectors = jnp.concatenate([pair, other], axis=2)]
  transfers between devices with their start and end apart: 9 -> 11, of which waited for: 0 -> 2; matrix products, arithmetic and copies ran while one was open for 23% -> 24% of each run, Pallas kernels for 0% -> 0%
where the time goes in v10:
time: 54.3 us; the launch traced here: 54.1 us
  starting transfers between devices  16.5 us (30%)
  waiting for transfers between devices  13.9 us (26%)
  blocking collectives  8.58 us (16%)
  other arithmetic  7.47 us (14%)
  matrix products  5.61 us (10%)
  local copies, waits for them, and re-layouts  1.19 us (2%)
  between operations  0.78 us (1%)
    ppermute x9, starting transfers between devices, shift(): return lax.ppermute(x, axis, [(i, (i + k) % n) for i in range(n)])  14.9 us
    all_gather x1, blocking collectives, per_device(): lax.all_gather(jnp.transpose(gather_input, (2, 0, 1)), 'task', axis=0, ti...  8.58 us
    ppermute x9, waiting for transfers between devices, shift(): return lax.ppermute(x, axis, [(i, (i + k) % n) for i in range(n)])  7.18 us
    ppermute x1, waiting for transfers between devices, per_device(): other = lax.ppermute(pair, 'task', [(i, i ^ 2) for i in range(4)])  6.73 us
    reduce_sum x1, other arithmetic, kernel_tile(): return jnp.exp(0.1 - jnp.sqrt(jnp.sum(diff * diff, axis=0) + 0.01))  4.65 us
    unnamed x4, matrix products  4.38 us
    ppermute x1, starting transfers between devices, per_device(): other = lax.ppermute(pair, 'task', [(i, i ^ 2) for i in range(4)])  1.55 us
    optimization_barrier x1, local copies, waits for them, and re-layouts, per_device(): task_input = lax.optimization_barrier((vectors, peer_coords))[0]  1.16 us
  transfers between devices with their start and end apart: 11, of which 2 were waited for; matrix products, arithmetic and copies ran while one was open for 24% of the time, Pallas kernels for 0%

profile of v10, /device:TPU:0, one launch (start us, length us, event | category | flops | bytes accessed | tf_op | source)
XLA Modules:
  0.0 54.1 jit_solution(6915415327564298389)
XLA Ops:
  0.6 5.1 %collective-permute-start.4 = (bf16[3,768]{1,0:T(4,128)(2,1)}, bf16[3,768]{1,0:T(4,128)(2,1)S(1)}, u32[]{:S(2)}, u32[]{:S(2)}) collective-permute-start(bf16[3,768]{1,0:T(4,128)(2,1)} %param.6), channel_id=1, source_target_pairs={{0,12},{4,0},{8,4},{12,8},{1,13},{5,1},{9,5},{13,9},{2,14},{6,2},{... | collective-permute-start | bytes 13832 | tf_op jit(solution)/shard_map/ppermute | solution.py:13
  5.8 1.0 %collective-permute-start.2 = (bf16[3,768]{1,0:T(4,128)(2,1)}, bf16[3,768]{1,0:T(4,128)(2,1)S(1)}, u32[]{:S(2)}, u32[]{:S(2)}) collective-permute-start(bf16[3,768]{1,0:T(4,128)(2,1)} %param.6), channel_id=1, source_target_pairs={{0,8},{4,12},{8,0},{12,4},{1,9},{5,13},{9,1},{13,5},{2,10},{6,14},... | collective-permute-start | bytes 13832 | tf_op jit(solution)/shard_map/ppermute | solution.py:13
  6.8 2.8 %collective-permute-start.5 = (bf16[2,768,64]{1,2,0:T(8,128)(2,1)}, bf16[2,768,64]{1,2,0:T(8,128)(2,1)S(1)}, u32[]{:S(2)}, u32[]{:S(2)}) collective-permute-start(bf16[2,768,64]{1,2,0:T(8,128)(2,1)} %param.8), channel_id=1, source_target_pairs={{0,12},{4,0},{8,4},{12,8},{1,13},{5,1},{9,5},{13,9},{2,14},{6,2},{... | collective-permute-start | bytes 589832 | tf_op jit(solution)/shard_map/ppermute | solution.py:13
  9.6 2.0 %collective-permute-start.3 = (bf16[2,768,64]{1,2,0:T(8,128)(2,1)}, bf16[2,768,64]{1,2,0:T(8,128)(2,1)S(1)}, u32[]{:S(2)}, u32[]{:S(2)}) collective-permute-start(bf16[2,768,64]{1,2,0:T(8,128)(2,1)} %param.8), channel_id=1, source_target_pairs={{0,8},{4,12},{8,0},{12,4},{1,9},{5,13},{9,1},{13,5},{2,10},{6,14},... | collective-permute-start | bytes 589832 | tf_op jit(solution)/shard_map/ppermute | solution.py:13
  11.6 0.7 %broadcast_divide_fusion = f32[3]{0:T(128)S(1)} fusion(f32[3]{0:T(128)} %param.7), kind=kLoop, calls=%fused_computation.33 | loop fusion | flops 3 | bytes 24 | tf_op jit(solution)/shard_map/div | solution.py:37
  12.3 1.2 %copy.12 = bf16[2,768,64]{2,1,0:T(8,128)(2,1)S(1)} copy(bf16[2,768,64]{1,2,0:T(8,128)(2,1)} %param.8) | data formatting | bytes 393216 | tf_op jit(solution)/shard_map/optimization_barrier | solution.py:49
  13.5 0.1 collective-permute-start.6
  13.5 0.8 %convert_multiply_fusion = (f32[3,768]{1,0:T(4,128)S(1)}, f32[3,768]{1,0:T(4,128)S(1)}, f32[3,768]{1,0:T(4,128)S(1)}, f32[3,768]{1,0:T(4,128)S(1)}) fusion(bf16[3,768]{1,0:T(4,128)(2,1)S(1)} %collective-permute-done.4, f32[3]{0:T(128)S(1)} %broadcast_divide_fusion, bf16[3,768]{1,0:T(4,128)(2,1)S(1)} %collective-permute-done, ...), kind=kLoop, calls=%fused_computation.28 | loop fusion | flops 18432 | bytes 55308 | tf_op jit(solution)/shard_map/mul | solution.py:41
  14.3 4.7 %multiply_reduce_fusion.2 = (f32[768,768]{1,0:T(8,128)S(1)}, f32[768,768]{1,0:T(8,128)S(1)}, f32[768,768]{1,0:T(8,128)S(1)}, f32[768,768]{1,0:T(8,128)S(1)}) fusion(f32[3,768]{1,0:T(4,128)S(1)} %get-tuple-element.15, f32[3,768]{1,0:T(4,128)S(1)} %get-tuple-element.17, f32[3,768]{1,0:T(4,128)S(1)} %get-tuple-element.16, f32[3,768]{1,0:T(4,128)S(1)} %get-tuple-element.14), kind=kLoop, calls=%fused_computation.2 | loop fusion | flops 18874368 | bytes 9474048 | tf_op jit(solution)/shard_map/reduce_sum | solution.py:9
  19.0 1.1 %fusion = f32[768,128]{0,1:S(1)} fusion(bf16[768,128]{0,1:T(8,128)(2,1)S(1)} %bitcast.31, f32[768,768]{1,0:T(8,128)S(1)} %get-tuple-element.9), kind=kOutput, calls=%fused_computation.9 | convolution fusion | flops 152764416 | bytes 2949120
  20.1 1.1 %fusion.3 = f32[768,128]{0,1:S(1)} fusion(bf16[768,128]{0,1:T(8,128)(2,1)S(1)} %bitcast.37, f32[768,768]{1,0:T(8,128)S(1)} %get-tuple-element.8), kind=kOutput, calls=%fused_computation.12 | convolution fusion | flops 152764416 | bytes 2949120
  21.2 7.2 %collective-permute-done.3 = bf16[2,768,64]{1,2,0:T(8,128)(2,1)S(1)} collective-permute-done((bf16[2,768,64]{1,2,0:T(8,128)(2,1)}, bf16[2,768,64]{1,2,0:T(8,128)(2,1)S(1)}, u32[]{:S(2)}, u32[]{:S(2)}) %collective-permute-start.3) | collective-permute-done | bytes 196640 | tf_op jit(solution)/shard_map/ppermute | solution.py:13
  28.3 1.1 %fusion.2 = f32[768,128]{0,1:S(1)} fusion(bf16[768,128]{0,1:T(8,128)(2,1)S(1)} %bitcast.36, f32[768,768]{1,0:T(8,128)S(1)} %get-tuple-element.7), kind=kOutput, calls=%fused_computation.11 | convolution fusion | flops 152764416 | bytes 2949120
  29.5 0.2 pad_maximum_fusion.1
  29.7 1.6 %collective-permute-start.7 = (bf16[2,768,128]{2,1,0:T(8,128)(2,1)S(1)}, bf16[2,768,128]{2,1,0:T(8,128)(2,1)S(1)}, u32[]{:S(2)}, u32[]{:S(2)}) collective-permute-start(bf16[2,768,128]{2,1,0:T(8,128)(2,1)S(1)} %pad_maximum_fusion.1), channel_id=1, source_target_pairs={{0,2},{1,3},{2,0},{3,1},{4,6},{5,7},{6,4},{7,5},{8,10},{9,11},{10,... | collective-permute-start | bytes 1179656 | tf_op jit(solution)/shard_map/ppermute | solution.py:72
  31.3 1.1 %fusion.1 = f32[768,128]{0,1:S(1)} fusion(bf16[768,128]{0,1:T(8,128)(2,1)S(1)} %bitcast.38, f32[768,768]{1,0:T(8,128)S(1)} %get-tuple-element.6), kind=kOutput, calls=%fused_computation.10 | convolution fusion | flops 152764416 | bytes 2949120
  32.4 0.1 fusion.5
  32.5 6.7 %collective-permute-done.7 = bf16[2,768,128]{2,1,0:T(8,128)(2,1)S(1)} collective-permute-done((bf16[2,768,128]{2,1,0:T(8,128)(2,1)S(1)}, bf16[2,768,128]{2,1,0:T(8,128)(2,1)S(1)}, u32[]{:S(2)}, u32[]{:S(2)}) %collective-permute-start.7) | collective-permute-done | bytes 393248 | tf_op jit(solution)/shard_map/ppermute | solution.py:72
  39.2 0.4 pad_maximum_fusion
  39.6 0.3 convolution_bitcast_fusion
  40.0 3.9 %collective-permute-start.9 = (f32[64,256]{1,0:T(8,128)S(1)}, f32[64,256]{1,0:T(8,128)S(1)}, u32[]{:S(2)}, u32[]{:S(2)}) collective-permute-start(f32[64,256]{1,0:T(8,128)S(1)} %convolution_bitcast_fusion), channel_id=1, source_target_pairs={{0,4},{4,8},{8,12},{12,0},{1,5},{5,9},{9,13},{13,1},{2,6},{6,10},{... | collective-permute-start | bytes 196616 | tf_op jit(solution)/shard_map/ppermute | solution.py:13
  43.9 8.6 %all_gather.3 = bf16[256,2,768]{2,0,1:T(8,128)(2,1)S(1)} all-gather(bf16[64,2,768]{2,0,1:T(8,128)(2,1)S(1)} %bitcast.30), channel_id=1, replica_groups=mesh['groups'=2,'dp'=4,'task'=4] {'task'}, dimensions={0}, use_global_device_ids=true | all-gather | bytes 983040 | tf_op jit(solution)/shard_map/all_gather | solution.py:84
  52.4 0.9 %fusion.4 = bf16[2,768,64]{1,2,0:T(8,128)(2,1)} fusion(bf16[256,2,768]{2,0,1:T(8,128)(2,1)S(1)} %all_gather.3, bf16[2,768,64]{1,2,0:T(8,128)(2,1)S(1)} %copy-done.1, f32[64]{0:T(128)S(1)} %copy-done.2, bf16[256,256]{1,0:T(8,128)(2,1)S(1)} %copy-done, s32[]{:T(128)S(6)} %select_n.48), kind=kOutput, calls=%fused_computation.13 | convolution fusion | flops 50724864 | bytes 1212932 | tf_op jit(solution)/shard_map/asn,ca->snc/dot_general | solution.py:86
  53.4 0.6 %fusion.8 = f32[64,256]{1,0:T(8,128)} fusion(f32[64,256]{1,0:T(8,128)S(1)} %add_add_fusion, f32[64,128]{1,0:T(8,128)S(1)} %get-tuple-element.13, f32[64,128]{1,0:T(8,128)S(1)} %get-tuple-element.12, pred[]{:T(512)S(6)} %lt.18), kind=kLoop, calls=%fused_computation.24 | loop fusion | flops 49152 | bytes 196609 | tf_op jit(solution)/shard_map/div | solution.py:92
  (24 shorter events, 0.2 us)
Async XLA Ops:
  0.6 51.8 %copy-start = (bf16[256,256]{1,0:T(8,128)(2,1)S(1)}, bf16[256,256]{1,0:T(8,128)(2,1)}, u32[]{:S(2)}) copy-start(bf16[256,256]{1,0:T(8,128)(2,1)} %param.9) | copy-start | bytes 393220
  0.6 11.6 %collective-permute-start.4 = (bf16[3,768]{1,0:T(4,128)(2,1)}, bf16[3,768]{1,0:T(4,128)(2,1)S(1)}, u32[]{:S(2)}, u32[]{:S(2)}) collective-permute-start(bf16[3,768]{1,0:T(4,128)(2,1)} %param.6), channel_id=1, source_target_pairs={{0,12},{4,0},{8,4},{12,8},{1,13},{5,1},{9,5},{13,9},{2,14},{6,2},{... | collective-permute-start | bytes 13832 | tf_op jit(solution)/shard_map/ppermute | solution.py:13
  5.7 6.5 %collective-permute-start = (bf16[3,768]{1,0:T(4,128)(2,1)}, bf16[3,768]{1,0:T(4,128)(2,1)S(1)}, u32[]{:S(2)}, u32[]{:S(2)}) collective-permute-start(bf16[3,768]{1,0:T(4,128)(2,1)} %param.6), channel_id=1, source_target_pairs={{0,4},{4,8},{8,12},{12,0},{1,5},{5,9},{9,13},{13,1},{2,6},{6,10},{... | collective-permute-start | bytes 13832 | tf_op jit(solution)/shard_map/ppermute | solution.py:13
  5.8 6.5 %collective-permute-start.2 = (bf16[3,768]{1,0:T(4,128)(2,1)}, bf16[3,768]{1,0:T(4,128)(2,1)S(1)}, u32[]{:S(2)}, u32[]{:S(2)}) collective-permute-start(bf16[3,768]{1,0:T(4,128)(2,1)} %param.6), channel_id=1, source_target_pairs={{0,8},{4,12},{8,0},{12,4},{1,9},{5,13},{9,1},{13,5},{2,10},{6,14},... | collective-permute-start | bytes 13832 | tf_op jit(solution)/shard_map/ppermute | solution.py:13
  6.8 13.3 %collective-permute-start.5 = (bf16[2,768,64]{1,2,0:T(8,128)(2,1)}, bf16[2,768,64]{1,2,0:T(8,128)(2,1)S(1)}, u32[]{:S(2)}, u32[]{:S(2)}) collective-permute-start(bf16[2,768,64]{1,2,0:T(8,128)(2,1)} %param.8), channel_id=1, source_target_pairs={{0,12},{4,0},{8,4},{12,8},{1,13},{5,1},{9,5},{13,9},{2,14},{6,2},{... | collective-permute-start | bytes 589832 | tf_op jit(solution)/shard_map/ppermute | solution.py:13
  9.6 18.8 %collective-permute-start.3 = (bf16[2,768,64]{1,2,0:T(8,128)(2,1)}, bf16[2,768,64]{1,2,0:T(8,128)(2,1)S(1)}, u32[]{:S(2)}, u32[]{:S(2)}) collective-permute-start(bf16[2,768,64]{1,2,0:T(8,128)(2,1)} %param.8), channel_id=1, source_target_pairs={{0,8},{4,12},{8,0},{12,4},{1,9},{5,13},{9,1},{13,5},{2,10},{6,14},... | collective-permute-start | bytes 589832 | tf_op jit(solution)/shard_map/ppermute | solution.py:13
  12.3 19.0 %collective-permute-start.1 = (bf16[2,768,64]{1,2,0:T(8,128)(2,1)}, bf16[2,768,64]{1,2,0:T(8,128)(2,1)S(1)}, u32[]{:S(2)}, u32[]{:S(2)}) collective-permute-start(bf16[2,768,64]{1,2,0:T(8,128)(2,1)} %param.8), channel_id=1, source_target_pairs={{0,4},{4,8},{8,12},{12,0},{1,5},{5,9},{9,13},{13,1},{2,6},{6,10},{... | collective-permute-start | bytes 589832 | tf_op jit(solution)/shard_map/ppermute | solution.py:13
  13.5 16.0 %collective-permute-start.6 = (bf16[2,768,64]{2,1,0:T(8,128)(2,1)S(1)}, bf16[2,768,64]{2,1,0:T(8,128)(2,1)S(1)}, u32[]{:S(2)}, u32[]{:S(2)}) collective-permute-start(bf16[2,768,64]{2,1,0:T(8,128)(2,1)S(1)} %copy.12), channel_id=1, source_target_pairs={{0,1},{1,0},{2,3},{3,2},{4,5},{5,4},{6,7},{7,6},{8,9},{9,8},{10,11... | collective-permute-start | bytes 589832 | tf_op jit(solution)/shard_map/ppermute | solution.py:67
  14.3 4.7 %copy-start.1 = (bf16[2,768,64]{1,2,0:T(8,128)(2,1)S(1)}, bf16[2,768,64]{1,2,0:T(8,128)(2,1)}, u32[]{:S(2)}) copy-start(bf16[2,768,64]{1,2,0:T(8,128)(2,1)} %param.8) | copy-start | bytes 589828
  29.7 9.5 %collective-permute-start.7 = (bf16[2,768,128]{2,1,0:T(8,128)(2,1)S(1)}, bf16[2,768,128]{2,1,0:T(8,128)(2,1)S(1)}, u32[]{:S(2)}, u32[]{:S(2)}) collective-permute-start(bf16[2,768,128]{2,1,0:T(8,128)(2,1)S(1)} %pad_maximum_fusion.1), channel_id=1, source_target_pairs={{0,2},{1,3},{2,0},{3,1},{4,6},{5,7},{6,4},{7,5},{8,10},{9,11},{10,... | collective-permute-start | bytes 1179656 | tf_op jit(solution)/shard_map/ppermute | solution.py:72
  32.4 7.2 %copy-start.3 = (bf16[2]{0:T(256)(128)(2,1)S(1)}, bf16[2]{0:T(256)(128)(2,1)}, u32[]{:S(2)}) copy-start(bf16[2]{0:T(256)(128)(2,1)} %constant.42.clone) | copy-start | bytes 16
  32.5 20.0 %copy-start.2 = (f32[64]{0:T(128)S(1)}, f32[64]{0:T(128)}, u32[]{:S(2)}) copy-start(f32[64]{0:T(128)} %param.10) | copy-start | bytes 772
  39.9 13.5 %collective-permute-start.10 = (f32[64,256]{1,0:T(8,128)S(1)}, f32[64,256]{1,0:T(8,128)S(1)}, u32[]{:S(2)}, u32[]{:S(2)}) collective-permute-start(f32[64,256]{1,0:T(8,128)S(1)} %convolution_bitcast_fusion), channel_id=1, source_target_pairs={{0,8},{4,12},{8,0},{12,4},{1,9},{5,13},{9,1},{13,5},{2,10},{6,14},... | collective-permute-start | bytes 196616 | tf_op jit(solution)/shard_map/ppermute | solution.py:13
  40.0 13.4 %collective-permute-start.9 = (f32[64,256]{1,0:T(8,128)S(1)}, f32[64,256]{1,0:T(8,128)S(1)}, u32[]{:S(2)}, u32[]{:S(2)}) collective-permute-start(f32[64,256]{1,0:T(8,128)S(1)} %convolution_bitcast_fusion), channel_id=1, source_target_pairs={{0,4},{4,8},{8,12},{12,0},{1,5},{5,9},{9,13},{13,1},{2,6},{6,10},{... | collective-permute-start | bytes 196616 | tf_op jit(solution)/shard_map/ppermute | solution.py:13
  43.8 9.6 %collective-permute-start.8 = (f32[64,256]{1,0:T(8,128)S(1)}, f32[64,256]{1,0:T(8,128)S(1)}, u32[]{:S(2)}, u32[]{:S(2)}) collective-permute-start(f32[64,256]{1,0:T(8,128)S(1)} %convolution_bitcast_fusion), channel_id=1, source_target_pairs={{0,12},{4,0},{8,4},{12,8},{1,13},{5,1},{9,5},{13,9},{2,14},{6,2},{... | collective-permute-start | bytes 196616 | tf_op jit(solution)/shard_map/ppermute | solution.py:13

commit v11 on v7

--- a/solution.py
+++ b/solution.py
@@ -61,7 +61,9 @@
         summed = block(coords, vectors)
         summed = lax.fori_loop(0, n_dp - 1, ring, (summed, coords, vectors))[0]
 
-    whole_vectors = lax.all_gather(task_input, "task", axis=2, tiled=True)
+    n_task = lax.axis_size("task")
+    copies = jnp.concatenate([task_input] * n_task, axis=2)
+    whole_vectors = lax.all_to_all(copies, "task", 2, 2, tiled=True)
     images = summed.astype(jnp.bfloat16)
     signs = jnp.array([1.0, -1.0], jnp.bfloat16)
     signed = images * signs[:, None, None]
@@ -69,7 +71,8 @@
         "sna,snb->ab", signed, whole_vectors, preferred_element_type=jnp.float32
     )
     total = sum_over(partial_grad, "dp", n_dp)
-    whole_images = lax.all_gather(jnp.transpose(images, (2, 0, 1)), "task", axis=0, tiled=True)
+    gather_input = lax.optimization_barrier((images, whole_vectors))[0]
+    whole_images = lax.all_gather(jnp.transpose(gather_input, (2, 0, 1)), "task", axis=0, tiled=True)
     own_rows = lax.dynamic_slice_in_dim(mixing, task_start, local_tasks, 0)
     mixed = jnp.einsum("asn,ca->snc", whole_images, own_rows, preferred_element_type=jnp.float32)
     product = (mixed + noise[None, None, :] * vectors.astype(jnp.float32)).astype(jnp.bfloat16)

time: 44.9 us -> 44.2 us (0.984)
  blocking collectives: 16.5 us -> 7.45 us
  starting transfers between devices: 14.9 us -> 18.4 us
  waiting for transfers between devices: 0.02 us -> 2.37 us
  other arithmetic: 6.81 us -> 8.07 us
  local copies, waits for them, and re-layouts: 0.02 us -> 1.18 us
    all_gather x2 -> x1, blocking collectives: 16.5 us -> 7.45 us  [per_device(): lax.all_gather(jnp.transpose(gather_input, (2, 0, 1)), 'task', axis=0, ti...]
    all_to_all x0 -> x1, starting transfers between devices: none -> 3.49 us  [per_device(): whole_vectors = lax.all_to_all(copies, 'task', 2, 2, tiled=True)]
    all_to_all x0 -> x1, waiting for transfers between devices: none -> 2.35 us  [per_device(): whole_vectors = lax.all_to_all(copies, 'task', 2, 2, tiled=True)]
    concatenate x0 -> x1, other arithmetic: none -> 1.95 us  [per_device(): copies = jnp.concatenate([task_input] * n_task, axis=2)]
    optimization_barrier x0 -> x1, local copies, waits for them, and re-layouts: none -> 1.16 us  [per_device(): task_input = lax.optimization_barrier((vectors, peer_coords))[0]]
    mul x1, other arithmetic: 0.77 us -> 0.08 us  [block(): right = right_coords.astype(jnp.float32) * inverse[:, None]]
  transfers between devices with their start and end apart: 9 -> 10, of which waited for: 0 -> 1; matrix products, arithmetic and copies ran while one was open for 23% -> 32% of each run, Pallas kernels for 0% -> 0%
where the time goes in v11:
time: 44.2 us; the launch traced here: 43.9 us
  starting transfers between devices  18.4 us (42%)
  other arithmetic  8.07 us (18%)
  blocking collectives  7.45 us (17%)
  matrix products  5.69 us (13%)
  waiting for transfers between devices  2.37 us (5%)
  local copies, waits for them, and re-layouts  1.18 us (3%)
  between operations  0.73 us (2%)
    ppermute x9, starting transfers between devices, shift(): return lax.ppermute(x, axis, [(i, (i + k) % n) for i in range(n)])  14.9 us
    all_gather x1, blocking collectives, per_device(): lax.all_gather(jnp.transpose(gather_input, (2, 0, 1)), 'task', axis=0, ti...  7.45 us
    reduce_sum x1, other arithmetic, kernel_tile(): return jnp.exp(0.1 - jnp.sqrt(jnp.sum(diff * diff, axis=0) + 0.01))  4.65 us
    unnamed x4, matrix products  4.38 us
    all_to_all x1, starting transfers between devices, per_device(): whole_vectors = lax.all_to_all(copies, 'task', 2, 2, tiled=True)  3.49 us
    all_to_all x1, waiting for transfers between devices, per_device(): whole_vectors = lax.all_to_all(copies, 'task', 2, 2, tiled=True)  2.35 us
    concatenate x1, other arithmetic, per_device(): copies = jnp.concatenate([task_input] * n_task, axis=2)  1.95 us
    optimization_barrier x1, local copies, waits for them, and re-layouts, per_device(): task_input = lax.optimization_barrier((vectors, peer_coords))[0]  1.16 us
  transfers between devices with their start and end apart: 10, of which 1 were waited for; matrix products, arithmetic and copies ran while one was open for 32% of the time, Pallas kernels for 0%

profile of v11, /device:TPU:0, one launch (start us, length us, event | category | flops | bytes accessed | tf_op | source)
XLA Modules:
  0.0 43.9 jit_solution(2874764318818082760)
XLA Ops:
  0.7 3.1 %collective-permute-start = (bf16[3,768]{1,0:T(4,128)(2,1)}, bf16[3,768]{1,0:T(4,128)(2,1)S(1)}, u32[]{:S(2)}, u32[]{:S(2)}) collective-permute-start(bf16[3,768]{1,0:T(4,128)(2,1)} %param.6), channel_id=1, source_target_pairs={{0,4},{4,8},{8,12},{12,0},{1,5},{5,9},{9,13},{13,1},{2,6},{6,10},{... | collective-permute-start | bytes 13832 | tf_op jit(solution)/shard_map/ppermute | solution.py:13
  3.7 2.6 %collective-permute-start.2 = (bf16[3,768]{1,0:T(4,128)(2,1)}, bf16[3,768]{1,0:T(4,128)(2,1)S(1)}, u32[]{:S(2)}, u32[]{:S(2)}) collective-permute-start(bf16[3,768]{1,0:T(4,128)(2,1)} %param.6), channel_id=1, source_target_pairs={{0,8},{4,12},{8,0},{12,4},{1,9},{5,13},{9,1},{13,5},{2,10},{6,14},... | collective-permute-start | bytes 13832 | tf_op jit(solution)/shard_map/ppermute | solution.py:13
  6.3 1.3 %collective-permute-start.4 = (bf16[3,768]{1,0:T(4,128)(2,1)}, bf16[3,768]{1,0:T(4,128)(2,1)S(1)}, u32[]{:S(2)}, u32[]{:S(2)}) collective-permute-start(bf16[3,768]{1,0:T(4,128)(2,1)} %param.6), channel_id=1, source_target_pairs={{0,12},{4,0},{8,4},{12,8},{1,13},{5,1},{9,5},{13,9},{2,14},{6,2},{... | collective-permute-start | bytes 13832 | tf_op jit(solution)/shard_map/ppermute | solution.py:13
  7.7 0.7 %collective-permute-start.1 = (bf16[2,768,64]{1,2,0:T(8,128)(2,1)}, bf16[2,768,64]{1,2,0:T(8,128)(2,1)S(1)}, u32[]{:S(2)}, u32[]{:S(2)}) collective-permute-start(bf16[2,768,64]{1,2,0:T(8,128)(2,1)} %param.8), channel_id=1, source_target_pairs={{0,4},{4,8},{8,12},{12,0},{1,5},{5,9},{9,13},{13,1},{2,6},{6,10},{... | collective-permute-start | bytes 589832 | tf_op jit(solution)/shard_map/ppermute | solution.py:13
  8.3 0.3 collective-permute-start.3
  8.7 0.7 %broadcast_divide_fusion = f32[3]{0:T(128)S(1)} fusion(f32[3]{0:T(128)} %param.7), kind=kLoop, calls=%fused_computation.29 | loop fusion | flops 3 | bytes 24 | tf_op jit(solution)/shard_map/div | solution.py:37
  9.3 2.8 %collective-permute-start.5 = (bf16[2,768,64]{1,2,0:T(8,128)(2,1)}, bf16[2,768,64]{1,2,0:T(8,128)(2,1)S(1)}, u32[]{:S(2)}, u32[]{:S(2)}) collective-permute-start(bf16[2,768,64]{1,2,0:T(8,128)(2,1)} %param.8), channel_id=1, source_target_pairs={{0,12},{4,0},{8,4},{12,8},{1,13},{5,1},{9,5},{13,9},{2,14},{6,2},{... | collective-permute-start | bytes 589832 | tf_op jit(solution)/shard_map/ppermute | solution.py:13
  12.2 1.2 %copy.17 = bf16[2,768,64]{1,0,2:T(2,128)(2,1)S(1)} copy(bf16[2,768,64]{1,2,0:T(8,128)(2,1)} %param.8) | data formatting | bytes 393216 | tf_op jit(solution)/shard_map/optimization_barrier | solution.py:49
  13.3 1.9 %pad_maximum_fusion = bf16[2,768,256]{1,0,2:T(2,128)(2,1)} fusion(bf16[2,768,64]{1,0,2:T(2,128)(2,1)S(1)} %copy.17), kind=kLoop, calls=%fused_computation.15 | loop fusion | flops 1179648 | bytes 983040 | tf_op jit(solution)/shard_map/concatenate | solution.py:65
  15.3 3.5 %all-to-all-start = ((bf16[2,768,256]{1,0,2:T(2,128)(2,1)}), bf16[2,768,256]{1,0,2:T(2,128)(2,1)S(1)}, u32[]{:S(2)}, u32[]{:S(2)}) async-start(bf16[2,768,256]{1,0,2:T(2,128)(2,1)} %pad_maximum_fusion), calls=%async_computation | async-start | bytes 1572864 | tf_op jit(solution)/shard_map/all_to_all | solution.py:66
  18.9 4.7 %multiply_reduce_fusion.2 = (f32[768,768]{1,0:T(8,128)S(1)}, f32[768,768]{1,0:T(8,128)S(1)}, f32[768,768]{1,0:T(8,128)S(1)}, f32[768,768]{1,0:T(8,128)S(1)}) fusion(f32[3,768]{1,0:T(4,128)S(1)} %get-tuple-element.11, f32[3,768]{1,0:T(4,128)S(1)} %get-tuple-element.13, f32[3,768]{1,0:T(4,128)S(1)} %get-tuple-element.12, f32[3,768]{1,0:T(4,128)S(1)} %get-tuple-element.10), kind=kLoop, calls=%fused_computation.2 | loop fusion | flops 18874368 | bytes 9474048 | tf_op jit(solution)/shard_map/reduce_sum | solution.py:9
  23.5 1.1 %fusion = f32[768,128]{0,1:S(1)} fusion(bf16[768,128]{0,1:T(8,128)(2,1)S(1)} %bitcast.30, f32[768,768]{1,0:T(8,128)S(1)} %get-tuple-element.9), kind=kOutput, calls=%fused_computation.9 | convolution fusion | flops 152764416 | bytes 2949120
  24.6 1.1 %fusion.1 = f32[768,128]{0,1:S(1)} fusion(bf16[768,128]{0,1:T(8,128)(2,1)S(1)} %bitcast.36, f32[768,768]{1,0:T(8,128)S(1)} %get-tuple-element.6), kind=kOutput, calls=%fused_computation.10 | convolution fusion | flops 152764416 | bytes 2949120
  25.7 1.1 %fusion.2 = f32[768,128]{0,1:S(1)} fusion(bf16[768,128]{0,1:T(8,128)(2,1)S(1)} %bitcast.35, f32[768,768]{1,0:T(8,128)S(1)} %get-tuple-element.7), kind=kOutput, calls=%fused_computation.11 | convolution fusion | flops 152764416 | bytes 2949120
  26.9 1.1 %fusion.3 = f32[768,128]{0,1:S(1)} fusion(bf16[768,128]{0,1:T(8,128)(2,1)S(1)} %bitcast.37, f32[768,768]{1,0:T(8,128)S(1)} %get-tuple-element.8), kind=kOutput, calls=%fused_computation.12 | convolution fusion | flops 152764416 | bytes 2949120
  28.0 0.1 fusion.6
  28.1 2.3 %all-to-all-done = bf16[2,768,256]{1,0,2:T(2,128)(2,1)S(1)} async-done(((bf16[2,768,256]{1,0,2:T(2,128)(2,1)}), bf16[2,768,256]{1,0,2:T(2,128)(2,1)S(1)}, u32[]{:S(2)}, u32[]{:S(2)}) %all-to-all-start) | async-done | bytes 786464 | tf_op jit(solution)/shard_map/all_to_all | solution.py:66
  30.4 0.4 convolution_bitcast_fusion
  30.8 1.3 %collective-permute-start.6 = (f32[64,256]{1,0:T(8,128)S(1)}, f32[64,256]{1,0:T(8,128)S(1)}, u32[]{:S(2)}, u32[]{:S(2)}) collective-permute-start(f32[64,256]{1,0:T(8,128)S(1)} %convolution_bitcast_fusion), channel_id=1, source_target_pairs={{0,12},{4,0},{8,4},{12,8},{1,13},{5,1},{9,5},{13,9},{2,14},{6,2},{... | collective-permute-start | bytes 196616 | tf_op jit(solution)/shard_map/ppermute | solution.py:13
  32.1 0.8 %collective-permute-start.7 = (f32[64,256]{1,0:T(8,128)S(1)}, f32[64,256]{1,0:T(8,128)S(1)}, u32[]{:S(2)}, u32[]{:S(2)}) collective-permute-start(f32[64,256]{1,0:T(8,128)S(1)} %convolution_bitcast_fusion), channel_id=1, source_target_pairs={{0,4},{4,8},{8,12},{12,0},{1,5},{5,9},{9,13},{13,1},{2,6},{6,10},{... | collective-permute-start | bytes 196616 | tf_op jit(solution)/shard_map/ppermute | solution.py:13
  32.8 2.0 %collective-permute-start.8 = (f32[64,256]{1,0:T(8,128)S(1)}, f32[64,256]{1,0:T(8,128)S(1)}, u32[]{:S(2)}, u32[]{:S(2)}) collective-permute-start(f32[64,256]{1,0:T(8,128)S(1)} %convolution_bitcast_fusion), channel_id=1, source_target_pairs={{0,8},{4,12},{8,0},{12,4},{1,9},{5,13},{9,1},{13,5},{2,10},{6,14},... | collective-permute-start | bytes 196616 | tf_op jit(solution)/shard_map/ppermute | solution.py:13
  34.9 7.5 %all_gather.3 = bf16[256,2,768]{2,0,1:T(8,128)(2,1)S(1)} all-gather(bf16[64,2,768]{2,0,1:T(8,128)(2,1)S(1)} %bitcast.29), channel_id=1, replica_groups=mesh['groups'=2,'dp'=4,'task'=4] {'task'}, dimensions={0}, use_global_device_ids=true | all-gather | bytes 983040 | tf_op jit(solution)/shard_map/all_gather | solution.py:75
  42.3 0.9 %fusion.4 = bf16[2,768,64]{1,2,0:T(8,128)(2,1)} fusion(bf16[256,2,768]{2,0,1:T(8,128)(2,1)S(1)} %all_gather.3, bf16[2,768,64]{1,2,0:T(8,128)(2,1)S(1)} %copy-done.1, f32[64]{0:T(128)S(1)} %copy-done.3, bf16[256,256]{1,0:T(8,128)(2,1)S(1)} %copy-done, s32[]{:T(128)S(6)} %select_n.22), kind=kOutput, calls=%fused_computation.13 | convolution fusion | flops 50724864 | bytes 1212932 | tf_op jit(solution)/shard_map/asn,ca->snc/dot_general | solution.py:77
  43.3 0.7 %add_multiply_fusion = f32[64,256]{1,0:T(8,128)} fusion(f32[64,256]{1,0:T(8,128)S(1)} %collective-permute-done.8, f32[64,256]{1,0:T(8,128)S(1)} %collective-permute-done.7, f32[64,256]{1,0:T(8,128)S(1)} %collective-permute-done.6, f32[64,256]{1,0:T(8,128)S(1)} %convolution_bitcast_fusion, pred[]{:T(512)S(6)} %eq.5), kind=kLoop, calls=%fused_computation.21 | loop fusion | flops 98304 | bytes 327681 | tf_op jit(solution)/shard_map/div | solution.py:79
  (20 shorter events, 0.1 us)
Async XLA Ops:
  0.6 41.7 %copy-start = (bf16[256,256]{1,0:T(8,128)(2,1)S(1)}, bf16[256,256]{1,0:T(8,128)(2,1)}, u32[]{:S(2)}) copy-start(bf16[256,256]{1,0:T(8,128)(2,1)} %param.9) | copy-start | bytes 393220
  0.6 18.1 %copy-start.2 = (bf16[3,768]{1,0:T(4,128)(2,1)S(1)}, bf16[3,768]{1,0:T(4,128)(2,1)}, u32[]{:S(2)}) copy-start(bf16[3,768]{1,0:T(4,128)(2,1)} %param.6) | copy-start | bytes 13828
  0.7 8.7 %collective-permute-start = (bf16[3,768]{1,0:T(4,128)(2,1)}, bf16[3,768]{1,0:T(4,128)(2,1)S(1)}, u32[]{:S(2)}, u32[]{:S(2)}) collective-permute-start(bf16[3,768]{1,0:T(4,128)(2,1)} %param.6), channel_id=1, source_target_pairs={{0,4},{4,8},{8,12},{12,0},{1,5},{5,9},{9,13},{13,1},{2,6},{6,10},{... | collective-permute-start | bytes 13832 | tf_op jit(solution)/shard_map/ppermute | solution.py:13
  3.7 8.4 %collective-permute-start.2 = (bf16[3,768]{1,0:T(4,128)(2,1)}, bf16[3,768]{1,0:T(4,128)(2,1)S(1)}, u32[]{:S(2)}, u32[]{:S(2)}) collective-permute-start(bf16[3,768]{1,0:T(4,128)(2,1)} %param.6), channel_id=1, source_target_pairs={{0,8},{4,12},{8,0},{12,4},{1,9},{5,13},{9,1},{13,5},{2,10},{6,14},... | collective-permute-start | bytes 13832 | tf_op jit(solution)/shard_map/ppermute | solution.py:13
  6.3 5.8 %collective-permute-start.4 = (bf16[3,768]{1,0:T(4,128)(2,1)}, bf16[3,768]{1,0:T(4,128)(2,1)S(1)}, u32[]{:S(2)}, u32[]{:S(2)}) collective-permute-start(bf16[3,768]{1,0:T(4,128)(2,1)} %param.6), channel_id=1, source_target_pairs={{0,12},{4,0},{8,4},{12,8},{1,13},{5,1},{9,5},{13,9},{2,14},{6,2},{... | collective-permute-start | bytes 13832 | tf_op jit(solution)/shard_map/ppermute | solution.py:13
  7.7 17.0 %collective-permute-start.1 = (bf16[2,768,64]{1,2,0:T(8,128)(2,1)}, bf16[2,768,64]{1,2,0:T(8,128)(2,1)S(1)}, u32[]{:S(2)}, u32[]{:S(2)}) collective-permute-start(bf16[2,768,64]{1,2,0:T(8,128)(2,1)} %param.8), channel_id=1, source_target_pairs={{0,4},{4,8},{8,12},{12,0},{1,5},{5,9},{9,13},{13,1},{2,6},{6,10},{... | collective-permute-start | bytes 589832 | tf_op jit(solution)/shard_map/ppermute | solution.py:13
  8.3 17.4 %collective-permute-start.3 = (bf16[2,768,64]{1,2,0:T(8,128)(2,1)}, bf16[2,768,64]{1,2,0:T(8,128)(2,1)S(1)}, u32[]{:S(2)}, u32[]{:S(2)}) collective-permute-start(bf16[2,768,64]{1,2,0:T(8,128)(2,1)} %param.8), channel_id=1, source_target_pairs={{0,8},{4,12},{8,0},{12,4},{1,9},{5,13},{9,1},{13,5},{2,10},{6,14},... | collective-permute-start | bytes 589832 | tf_op jit(solution)/shard_map/ppermute | solution.py:13
  9.3 17.5 %collective-permute-start.5 = (bf16[2,768,64]{1,2,0:T(8,128)(2,1)}, bf16[2,768,64]{1,2,0:T(8,128)(2,1)S(1)}, u32[]{:S(2)}, u32[]{:S(2)}) collective-permute-start(bf16[2,768,64]{1,2,0:T(8,128)(2,1)} %param.8), channel_id=1, source_target_pairs={{0,12},{4,0},{8,4},{12,8},{1,13},{5,1},{9,5},{13,9},{2,14},{6,2},{... | collective-permute-start | bytes 589832 | tf_op jit(solution)/shard_map/ppermute | solution.py:13
  15.3 15.1 %all-to-all-start = ((bf16[2,768,256]{1,0,2:T(2,128)(2,1)}), bf16[2,768,256]{1,0,2:T(2,128)(2,1)S(1)}, u32[]{:S(2)}, u32[]{:S(2)}) async-start(bf16[2,768,256]{1,0,2:T(2,128)(2,1)} %pad_maximum_fusion), calls=%async_computation | async-start | bytes 1572864 | tf_op jit(solution)/shard_map/all_to_all | solution.py:66
  18.9 4.7 %copy-start.1 = (bf16[2,768,64]{1,2,0:T(8,128)(2,1)S(1)}, bf16[2,768,64]{1,2,0:T(8,128)(2,1)}, u32[]{:S(2)}) copy-start(bf16[2,768,64]{1,2,0:T(8,128)(2,1)} %param.8) | copy-start | bytes 589828
  26.8 3.6 %copy-start.4 = (bf16[2]{0:T(256)(128)(2,1)S(1)}, bf16[2]{0:T(256)(128)(2,1)}, u32[]{:S(2)}) copy-start(bf16[2]{0:T(256)(128)(2,1)} %constant.38.clone) | copy-start | bytes 16
  28.0 14.4 %copy-start.3 = (f32[64]{0:T(128)S(1)}, f32[64]{0:T(128)}, u32[]{:S(2)}) copy-start(f32[64]{0:T(128)} %param.10) | copy-start | bytes 772
  30.8 12.5 %collective-permute-start.6 = (f32[64,256]{1,0:T(8,128)S(1)}, f32[64,256]{1,0:T(8,128)S(1)}, u32[]{:S(2)}, u32[]{:S(2)}) collective-permute-start(f32[64,256]{1,0:T(8,128)S(1)} %convolution_bitcast_fusion), channel_id=1, source_target_pairs={{0,12},{4,0},{8,4},{12,8},{1,13},{5,1},{9,5},{13,9},{2,14},{6,2},{... | collective-permute-start | bytes 196616 | tf_op jit(solution)/shard_map/ppermute | solution.py:13
  32.1 11.2 %collective-permute-start.7 = (f32[64,256]{1,0:T(8,128)S(1)}, f32[64,256]{1,0:T(8,128)S(1)}, u32[]{:S(2)}, u32[]{:S(2)}) collective-permute-start(f32[64,256]{1,0:T(8,128)S(1)} %convolution_bitcast_fusion), channel_id=1, source_target_pairs={{0,4},{4,8},{8,12},{12,0},{1,5},{5,9},{9,13},{13,1},{2,6},{6,10},{... | collective-permute-start | bytes 196616 | tf_op jit(solution)/shard_map/ppermute | solution.py:13
  32.8 10.4 %collective-permute-start.8 = (f32[64,256]{1,0:T(8,128)S(1)}, f32[64,256]{1,0:T(8,128)S(1)}, u32[]{:S(2)}, u32[]{:S(2)}) collective-permute-start(f32[64,256]{1,0:T(8,128)S(1)} %convolution_bitcast_fusion), channel_id=1, source_target_pairs={{0,8},{4,12},{8,0},{12,4},{1,9},{5,13},{9,1},{13,5},{2,10},{6,14},... | collective-permute-start | bytes 196616 | tf_op jit(solution)/shard_map/ppermute | solution.py:13

commit v12 on v11

--- a/solution.py
+++ b/solution.py
@@ -62,16 +62,16 @@
         summed = lax.fori_loop(0, n_dp - 1, ring, (summed, coords, vectors))[0]
 
     n_task = lax.axis_size("task")
-    copies = jnp.concatenate([task_input] * n_task, axis=2)
-    whole_vectors = lax.all_to_all(copies, "task", 2, 2, tiled=True)
+    copies = jnp.broadcast_to(task_input[None], (n_task,) + vectors.shape)
+    task_blocks = lax.all_to_all(copies, "task", 0, 0, tiled=True)
     images = summed.astype(jnp.bfloat16)
     signs = jnp.array([1.0, -1.0], jnp.bfloat16)
     signed = images * signs[:, None, None]
     partial_grad = jnp.einsum(
-        "sna,snb->ab", signed, whole_vectors, preferred_element_type=jnp.float32
-    )
+        "sna,ksnb->akb", signed, task_blocks, preferred_element_type=jnp.float32
+    ).reshape(local_tasks, n_task * local_tasks)
     total = sum_over(partial_grad, "dp", n_dp)
-    gather_input = lax.optimization_barrier((images, whole_vectors))[0]
+    gather_input = lax.optimization_barrier((images, task_blocks))[0]
     whole_images = lax.all_gather(jnp.transpose(gather_input, (2, 0, 1)), "task", axis=0, tiled=True)
     own_rows = lax.dynamic_slice_in_dim(mixing, task_start, local_tasks, 0)
     mixed = jnp.einsum("asn,ca->snc", whole_images, own_rows, preferred_element_type=jnp.float32)

time: 44.2 us -> 43.3 us (0.980)
  other arithmetic: 8.07 us -> 6.12 us
  local copies, waits for them, and re-layouts: 1.18 us -> 2.16 us
    concatenate x1 -> x0, other arithmetic: 1.95 us -> none  [per_device(): copies = jnp.concatenate([task_input] * n_task, axis=2)]
    broadcast_in_dim x0 -> x1, local copies, waits for them, and re-layouts: none -> 1.9 us  [per_device(): copies = jnp.broadcast_to(task_input[None], (n_task,) + vectors.shape)]
    optimization_barrier x1 -> x0, local copies, waits for them, and re-layouts: 1.16 us -> none  [per_device(): task_input = lax.optimization_barrier((vectors, peer_coords))[0]]
  transfers between devices with their start and end apart: 10 -> 10, of which waited for: 1 -> 1; matrix products, arithmetic and copies ran while one was open for 32% -> 29% of each run, Pallas kernels for 0% -> 0%
where the time goes in v12:
time: 43.3 us; the launch traced here: 43.1 us
  starting transfers between devices  18.4 us (42%)
  blocking collectives  7.45 us (17%)
  other arithmetic  6.12 us (14%)
  matrix products  5.84 us (13%)
  waiting for transfers between devices  2.37 us (5%)
  local copies, waits for them, and re-layouts  2.16 us (5%)
  between operations  0.73 us (2%)
    ppermute x9, starting transfers between devices, shift(): return lax.ppermute(x, axis, [(i, (i + k) % n) for i in range(n)])  14.9 us
    all_gather x1, blocking collectives, per_device(): lax.all_gather(jnp.transpose(gather_input, (2, 0, 1)), 'task', axis=0, ti...  7.45 us
    reduce_sum x1, other arithmetic, kernel_tile(): return jnp.exp(0.1 - jnp.sqrt(jnp.sum(diff * diff, axis=0) + 0.01))  4.65 us
    unnamed x4, matrix products  4.38 us
    all_to_all x1, starting transfers between devices, per_device(): task_blocks = lax.all_to_all(copies, 'task', 0, 0, tiled=True)  3.49 us
    all_to_all x1, waiting for transfers between devices, per_device(): task_blocks = lax.all_to_all(copies, 'task', 0, 0, tiled=True)  2.35 us
    broadcast_in_dim x1, local copies, waits for them, and re-layouts, per_device(): copies = jnp.broadcast_to(task_input[None], (n_task,) + vectors.shape)  1.9 us
    dot_general x1, matrix products, per_device(): jnp.einsum('asn,ca->snc', whole_images, own_rows, preferred_element_type=...  0.94 us
  transfers between devices with their start and end apart: 10, of which 1 were waited for; matrix products, arithmetic and copies ran while one was open for 29% of the time, Pallas kernels for 0%

profile of v12, /device:TPU:0, one launch (start us, length us, event | category | flops | bytes accessed | tf_op | source)
XLA Modules:
  0.0 43.1 jit_solution(3753910342009639272)
XLA Ops:
  0.7 3.1 %collective-permute-start = (bf16[3,768]{1,0:T(4,128)(2,1)}, bf16[3,768]{1,0:T(4,128)(2,1)S(1)}, u32[]{:S(2)}, u32[]{:S(2)}) collective-permute-start(bf16[3,768]{1,0:T(4,128)(2,1)} %param.6), channel_id=1, source_target_pairs={{0,4},{4,8},{8,12},{12,0},{1,5},{5,9},{9,13},{13,1},{2,6},{6,10},{... | collective-permute-start | bytes 13832 | tf_op jit(solution)/shard_map/ppermute | solution.py:13
  3.7 2.6 %collective-permute-start.2 = (bf16[3,768]{1,0:T(4,128)(2,1)}, bf16[3,768]{1,0:T(4,128)(2,1)S(1)}, u32[]{:S(2)}, u32[]{:S(2)}) collective-permute-start(bf16[3,768]{1,0:T(4,128)(2,1)} %param.6), channel_id=1, source_target_pairs={{0,8},{4,12},{8,0},{12,4},{1,9},{5,13},{9,1},{13,5},{2,10},{6,14},... | collective-permute-start | bytes 13832 | tf_op jit(solution)/shard_map/ppermute | solution.py:13
  6.3 1.3 %collective-permute-start.4 = (bf16[3,768]{1,0:T(4,128)(2,1)}, bf16[3,768]{1,0:T(4,128)(2,1)S(1)}, u32[]{:S(2)}, u32[]{:S(2)}) collective-permute-start(bf16[3,768]{1,0:T(4,128)(2,1)} %param.6), channel_id=1, source_target_pairs={{0,12},{4,0},{8,4},{12,8},{1,13},{5,1},{9,5},{13,9},{2,14},{6,2},{... | collective-permute-start | bytes 13832 | tf_op jit(solution)/shard_map/ppermute | solution.py:13
  7.7 0.7 %collective-permute-start.1 = (bf16[2,768,64]{1,2,0:T(8,128)(2,1)}, bf16[2,768,64]{1,2,0:T(8,128)(2,1)S(1)}, u32[]{:S(2)}, u32[]{:S(2)}) collective-permute-start(bf16[2,768,64]{1,2,0:T(8,128)(2,1)} %param.8), channel_id=1, source_target_pairs={{0,4},{4,8},{8,12},{12,0},{1,5},{5,9},{9,13},{13,1},{2,6},{6,10},{... | collective-permute-start | bytes 589832 | tf_op jit(solution)/shard_map/ppermute | solution.py:13
  8.3 0.3 collective-permute-start.3
  8.7 0.7 %broadcast_divide_fusion = f32[3]{0:T(128)S(1)} fusion(f32[3]{0:T(128)} %param.7), kind=kLoop, calls=%fused_computation.28 | loop fusion | flops 3 | bytes 24 | tf_op jit(solution)/shard_map/div | solution.py:37
  9.3 2.8 %collective-permute-start.5 = (bf16[2,768,64]{1,2,0:T(8,128)(2,1)}, bf16[2,768,64]{1,2,0:T(8,128)(2,1)S(1)}, u32[]{:S(2)}, u32[]{:S(2)}) collective-permute-start(bf16[2,768,64]{1,2,0:T(8,128)(2,1)} %param.8), channel_id=1, source_target_pairs={{0,12},{4,0},{8,4},{12,8},{1,13},{5,1},{9,5},{13,9},{2,14},{6,2},{... | collective-permute-start | bytes 589832 | tf_op jit(solution)/shard_map/ppermute | solution.py:13
  12.2 1.9 %broadcast_in_dim.2 = bf16[4,2,768,64]{2,3,1,0:T(8,128)(2,1)} broadcast(bf16[2,768,64]{1,2,0:T(8,128)(2,1)} %param.8), dimensions={1,2,3} | broadcast | bytes 983040 | tf_op jit(solution)/shard_map/broadcast_in_dim | solution.py:65
  14.1 3.5 %all-to-all-start = ((bf16[4,2,768,64]{2,3,1,0:T(8,128)(2,1)}), bf16[4,2,768,64]{2,3,1,0:T(8,128)(2,1)S(1)}, u32[]{:S(2)}, u32[]{:S(2)}) async-start(bf16[4,2,768,64]{2,3,1,0:T(8,128)(2,1)} %broadcast_in_dim.2), calls=%async_computation | async-start | bytes 1572864 | tf_op jit(solution)/shard_map/all_to_all | solution.py:66
  17.7 4.7 %multiply_reduce_fusion.2 = (f32[768,768]{1,0:T(8,128)S(1)}, f32[768,768]{1,0:T(8,128)S(1)}, f32[768,768]{1,0:T(8,128)S(1)}, f32[768,768]{1,0:T(8,128)S(1)}) fusion(f32[3,768]{1,0:T(4,128)S(1)} %get-tuple-element.11, f32[3,768]{1,0:T(4,128)S(1)} %get-tuple-element.13, f32[3,768]{1,0:T(4,128)S(1)} %get-tuple-element.12, f32[3,768]{1,0:T(4,128)S(1)} %get-tuple-element.10), kind=kLoop, calls=%fused_computation.2 | loop fusion | flops 18874368 | bytes 9474048 | tf_op jit(solution)/shard_map/reduce_sum | solution.py:9
  22.3 1.1 %fusion = f32[768,128]{0,1:S(1)} fusion(bf16[768,128]{0,1:T(8,128)(2,1)S(1)} %bitcast.35, f32[768,768]{1,0:T(8,128)S(1)} %get-tuple-element.9), kind=kOutput, calls=%fused_computation.9 | convolution fusion | flops 152764416 | bytes 2949120
  23.4 1.1 %fusion.1 = f32[768,128]{0,1:S(1)} fusion(bf16[768,128]{0,1:T(8,128)(2,1)S(1)} %bitcast.41, f32[768,768]{1,0:T(8,128)S(1)} %get-tuple-element.6), kind=kOutput, calls=%fused_computation.10 | convolution fusion | flops 152764416 | bytes 2949120
  24.5 1.1 %fusion.2 = f32[768,128]{0,1:S(1)} fusion(bf16[768,128]{0,1:T(8,128)(2,1)S(1)} %bitcast.40, f32[768,768]{1,0:T(8,128)S(1)} %get-tuple-element.7), kind=kOutput, calls=%fused_computation.11 | convolution fusion | flops 152764416 | bytes 2949120
  25.7 1.1 %fusion.3 = f32[768,128]{0,1:S(1)} fusion(bf16[768,128]{0,1:T(8,128)(2,1)S(1)} %bitcast.42, f32[768,768]{1,0:T(8,128)S(1)} %get-tuple-element.8), kind=kOutput, calls=%fused_computation.12 | convolution fusion | flops 152764416 | bytes 2949120
  26.8 2.3 %all-to-all-done = bf16[4,2,768,64]{2,3,1,0:T(8,128)(2,1)S(1)} async-done(((bf16[4,2,768,64]{2,3,1,0:T(8,128)(2,1)}), bf16[4,2,768,64]{2,3,1,0:T(8,128)(2,1)S(1)}, u32[]{:S(2)}, u32[]{:S(2)}) %all-to-all-start) | async-done | bytes 786464 | tf_op jit(solution)/shard_map/all_to_all | solution.py:66
  29.2 0.5 %convolution_bitcast_fusion = f32[64,4,64]{2,0,1:T(8,128)S(1)} fusion(bf16[4,2,768,64]{2,3,1,0:T(8,128)(2,1)S(1)} %all-to-all-done, bf16[2,768,64]{1,2,0:T(8,128)(2,1)S(1)} %fusion.5, bf16[2]{0:T(256)(128)(2,1)S(1)} %copy-done.4), kind=kOutput, calls=%fused_computation.14 | convolution fusion | flops 50724864 | bytes 1048580 | tf_op jit(solution)/shard_map/sna,ksnb->akb/dot_general | solution.py:70
  29.7 0.1 copy.9
  29.8 0.1 reshape.16
  29.9 1.3 %collective-permute-start.6 = (f32[64,256]{1,0:T(8,128)S(1)}, f32[64,256]{1,0:T(8,128)S(1)}, u32[]{:S(2)}, u32[]{:S(2)}) collective-permute-start(f32[64,256]{1,0:T(8,128)S(1)} %reshape.16), channel_id=1, source_target_pairs={{0,12},{4,0},{8,4},{12,8},{1,13},{5,1},{9,5},{13,9},{2,14},{6,2},{... | collective-permute-start | bytes 196616 | tf_op jit(solution)/shard_map/ppermute | solution.py:13
  31.2 0.8 %collective-permute-start.7 = (f32[64,256]{1,0:T(8,128)S(1)}, f32[64,256]{1,0:T(8,128)S(1)}, u32[]{:S(2)}, u32[]{:S(2)}) collective-permute-start(f32[64,256]{1,0:T(8,128)S(1)} %reshape.16), channel_id=1, source_target_pairs={{0,4},{4,8},{8,12},{12,0},{1,5},{5,9},{9,13},{13,1},{2,6},{6,10},{... | collective-permute-start | bytes 196616 | tf_op jit(solution)/shard_map/ppermute | solution.py:13
  32.0 2.0 %collective-permute-start.8 = (f32[64,256]{1,0:T(8,128)S(1)}, f32[64,256]{1,0:T(8,128)S(1)}, u32[]{:S(2)}, u32[]{:S(2)}) collective-permute-start(f32[64,256]{1,0:T(8,128)S(1)} %reshape.16), channel_id=1, source_target_pairs={{0,8},{4,12},{8,0},{12,4},{1,9},{5,13},{9,1},{13,5},{2,10},{6,14},... | collective-permute-start | bytes 196616 | tf_op jit(solution)/shard_map/ppermute | solution.py:13
  34.0 7.4 %all_gather.3 = bf16[256,2,768]{2,0,1:T(8,128)(2,1)S(1)} all-gather(bf16[64,2,768]{2,0,1:T(8,128)(2,1)S(1)} %bitcast.34), channel_id=1, replica_groups=mesh['groups'=2,'dp'=4,'task'=4] {'task'}, dimensions={0}, use_global_device_ids=true | all-gather | bytes 983040 | tf_op jit(solution)/shard_map/all_gather | solution.py:75
  41.5 0.9 %fusion.4 = bf16[2,768,64]{1,2,0:T(8,128)(2,1)} fusion(bf16[256,2,768]{2,0,1:T(8,128)(2,1)S(1)} %all_gather.3, bf16[2,768,64]{1,2,0:T(8,128)(2,1)S(1)} %copy-done.1, f32[64]{0:T(128)S(1)} %copy-done.3, bf16[256,256]{1,0:T(8,128)(2,1)S(1)} %copy-done, s32[]{:T(128)S(6)} %select_n.22), kind=kOutput, calls=%fused_computation.13 | convolution fusion | flops 50724864 | bytes 1212932 | tf_op jit(solution)/shard_map/asn,ca->snc/dot_general | solution.py:77
  42.4 0.7 %add_multiply_fusion = f32[64,256]{1,0:T(8,128)} fusion(f32[64,256]{1,0:T(8,128)S(1)} %collective-permute-done.8, f32[64,256]{1,0:T(8,128)S(1)} %collective-permute-done.7, f32[64,256]{1,0:T(8,128)S(1)} %collective-permute-done.6, f32[64,256]{1,0:T(8,128)S(1)} %reshape.16, pred[]{:T(512)S(6)} %eq.5), kind=kLoop, calls=%fused_computation.20 | loop fusion | flops 98304 | bytes 327681 | tf_op jit(solution)/shard_map/div | solution.py:79
  (21 shorter events, 0.2 us)
Async XLA Ops:
  0.6 40.9 %copy-start = (bf16[256,256]{1,0:T(8,128)(2,1)S(1)}, bf16[256,256]{1,0:T(8,128)(2,1)}, u32[]{:S(2)}) copy-start(bf16[256,256]{1,0:T(8,128)(2,1)} %param.9) | copy-start | bytes 393220
  0.6 16.9 %copy-start.2 = (bf16[3,768]{1,0:T(4,128)(2,1)S(1)}, bf16[3,768]{1,0:T(4,128)(2,1)}, u32[]{:S(2)}) copy-start(bf16[3,768]{1,0:T(4,128)(2,1)} %param.6) | copy-start | bytes 13828
  0.7 8.7 %collective-permute-start = (bf16[3,768]{1,0:T(4,128)(2,1)}, bf16[3,768]{1,0:T(4,128)(2,1)S(1)}, u32[]{:S(2)}, u32[]{:S(2)}) collective-permute-start(bf16[3,768]{1,0:T(4,128)(2,1)} %param.6), channel_id=1, source_target_pairs={{0,4},{4,8},{8,12},{12,0},{1,5},{5,9},{9,13},{13,1},{2,6},{6,10},{... | collective-permute-start | bytes 13832 | tf_op jit(solution)/shard_map/ppermute | solution.py:13
  3.7 8.4 %collective-permute-start.2 = (bf16[3,768]{1,0:T(4,128)(2,1)}, bf16[3,768]{1,0:T(4,128)(2,1)S(1)}, u32[]{:S(2)}, u32[]{:S(2)}) collective-permute-start(bf16[3,768]{1,0:T(4,128)(2,1)} %param.6), channel_id=1, source_target_pairs={{0,8},{4,12},{8,0},{12,4},{1,9},{5,13},{9,1},{13,5},{2,10},{6,14},... | collective-permute-start | bytes 13832 | tf_op jit(solution)/shard_map/ppermute | solution.py:13
  6.3 5.8 %collective-permute-start.4 = (bf16[3,768]{1,0:T(4,128)(2,1)}, bf16[3,768]{1,0:T(4,128)(2,1)S(1)}, u32[]{:S(2)}, u32[]{:S(2)}) collective-permute-start(bf16[3,768]{1,0:T(4,128)(2,1)} %param.6), channel_id=1, source_target_pairs={{0,12},{4,0},{8,4},{12,8},{1,13},{5,1},{9,5},{13,9},{2,14},{6,2},{... | collective-permute-start | bytes 13832 | tf_op jit(solution)/shard_map/ppermute | solution.py:13
  7.7 15.8 %collective-permute-start.1 = (bf16[2,768,64]{1,2,0:T(8,128)(2,1)}, bf16[2,768,64]{1,2,0:T(8,128)(2,1)S(1)}, u32[]{:S(2)}, u32[]{:S(2)}) collective-permute-start(bf16[2,768,64]{1,2,0:T(8,128)(2,1)} %param.8), channel_id=1, source_target_pairs={{0,4},{4,8},{8,12},{12,0},{1,5},{5,9},{9,13},{13,1},{2,6},{6,10},{... | collective-permute-start | bytes 589832 | tf_op jit(solution)/shard_map/ppermute | solution.py:13
  8.3 16.2 %collective-permute-start.3 = (bf16[2,768,64]{1,2,0:T(8,128)(2,1)}, bf16[2,768,64]{1,2,0:T(8,128)(2,1)S(1)}, u32[]{:S(2)}, u32[]{:S(2)}) collective-permute-start(bf16[2,768,64]{1,2,0:T(8,128)(2,1)} %param.8), channel_id=1, source_target_pairs={{0,8},{4,12},{8,0},{12,4},{1,9},{5,13},{9,1},{13,5},{2,10},{6,14},... | collective-permute-start | bytes 589832 | tf_op jit(solution)/shard_map/ppermute | solution.py:13
  9.3 16.3 %collective-permute-start.5 = (bf16[2,768,64]{1,2,0:T(8,128)(2,1)}, bf16[2,768,64]{1,2,0:T(8,128)(2,1)S(1)}, u32[]{:S(2)}, u32[]{:S(2)}) collective-permute-start(bf16[2,768,64]{1,2,0:T(8,128)(2,1)} %param.8), channel_id=1, source_target_pairs={{0,12},{4,0},{8,4},{12,8},{1,13},{5,1},{9,5},{13,9},{2,14},{6,2},{... | collective-permute-start | bytes 589832 | tf_op jit(solution)/shard_map/ppermute | solution.py:13
  14.1 15.1 %all-to-all-start = ((bf16[4,2,768,64]{2,3,1,0:T(8,128)(2,1)}), bf16[4,2,768,64]{2,3,1,0:T(8,128)(2,1)S(1)}, u32[]{:S(2)}, u32[]{:S(2)}) async-start(bf16[4,2,768,64]{2,3,1,0:T(8,128)(2,1)} %broadcast_in_dim.2), calls=%async_computation | async-start | bytes 1572864 | tf_op jit(solution)/shard_map/all_to_all | solution.py:66
  17.7 4.7 %copy-start.1 = (bf16[2,768,64]{1,2,0:T(8,128)(2,1)S(1)}, bf16[2,768,64]{1,2,0:T(8,128)(2,1)}, u32[]{:S(2)}) copy-start(bf16[2,768,64]{1,2,0:T(8,128)(2,1)} %param.8) | copy-start | bytes 589828
  25.6 3.6 %copy-start.4 = (bf16[2]{0:T(256)(128)(2,1)S(1)}, bf16[2]{0:T(256)(128)(2,1)}, u32[]{:S(2)}) copy-start(bf16[2]{0:T(256)(128)(2,1)} %constant.38.clone) | copy-start | bytes 16
  26.7 14.7 %copy-start.3 = (f32[64]{0:T(128)S(1)}, f32[64]{0:T(128)}, u32[]{:S(2)}) copy-start(f32[64]{0:T(128)} %param.10) | copy-start | bytes 772
  29.9 12.5 %collective-permute-start.6 = (f32[64,256]{1,0:T(8,128)S(1)}, f32[64,256]{1,0:T(8,128)S(1)}, u32[]{:S(2)}, u32[]{:S(2)}) collective-permute-start(f32[64,256]{1,0:T(8,128)S(1)} %reshape.16), channel_id=1, source_target_pairs={{0,12},{4,0},{8,4},{12,8},{1,13},{5,1},{9,5},{13,9},{2,14},{6,2},{... | collective-permute-start | bytes 196616 | tf_op jit(solution)/shard_map/ppermute | solution.py:13
  31.2 11.2 %collective-permute-start.7 = (f32[64,256]{1,0:T(8,128)S(1)}, f32[64,256]{1,0:T(8,128)S(1)}, u32[]{:S(2)}, u32[]{:S(2)}) collective-permute-start(f32[64,256]{1,0:T(8,128)S(1)} %reshape.16), channel_id=1, source_target_pairs={{0,4},{4,8},{8,12},{12,0},{1,5},{5,9},{9,13},{13,1},{2,6},{6,10},{... | collective-permute-start | bytes 196616 | tf_op jit(solution)/shard_map/ppermute | solution.py:13
  32.0 10.4 %collective-permute-start.8 = (f32[64,256]{1,0:T(8,128)S(1)}, f32[64,256]{1,0:T(8,128)S(1)}, u32[]{:S(2)}, u32[]{:S(2)}) collective-permute-start(f32[64,256]{1,0:T(8,128)S(1)} %reshape.16), channel_id=1, source_target_pairs={{0,8},{4,12},{8,0},{12,4},{1,9},{5,13},{9,1},{13,5},{2,10},{6,14},... | collective-permute-start | bytes 196616 | tf_op jit(solution)/shard_map/ppermute | solution.py:13

commit v13 on v12

--- a/solution.py
+++ b/solution.py
@@ -15,11 +15,8 @@
 
 def sum_over(x, axis, n):
     if n == 4:
-        got = [shift(x, axis, k, n) for k in range(1, n)]
-        even = lax.axis_index(axis) % 2 == 0
-        first = x + jnp.where(even, got[2], got[0])
-        second = got[1] + jnp.where(even, got[0], got[2])
-        return first + second
+        got = lax.all_to_all(jnp.broadcast_to(x[None], (n,) + x.shape), axis, 0, 0, tiled=True)
+        return (got[0] + got[1]) + (got[2] + got[3])
     if n & (n - 1):
         return lax.psum(x, axis)
     step = 1

time: 43.3 us -> 44 us (1.016)
  local copies, waits for them, and re-layouts: 2.16 us -> 2.88 us
  starting transfers between devices: 18.4 us -> 17.7 us
  blocking collectives: 7.45 us -> 8.01 us
    ppermute x9 -> x6, starting transfers between devices: 14.9 us -> 10.8 us  [shift(): return lax.ppermute(x, axis, [(i, (i + k) % n) for i in range(n)])]
    all_to_all x0 -> x1, starting transfers between devices: none -> 3.4 us  [sum_over(): lax.all_to_all(jnp.broadcast_to(x[None], (n,) + x.shape), axis, 0, 0, til...]
    broadcast_in_dim x0 -> x2, local copies, waits for them, and re-layouts: none -> 0.86 us  [sum_over(): jnp.broadcast_to(x[None], (n,) + x.shape)]
    all_gather x1, blocking collectives: 7.45 us -> 8.01 us  [per_device(): lax.all_gather(jnp.transpose(gather_input, (2, 0, 1)), 'task', axis=0, ti...]
  transfers between devices with their start and end apart: 10 -> 8, of which waited for: 1 -> 1; matrix products, arithmetic and copies ran while one was open for 29% -> 29% of each run, Pallas kernels for 0% -> 0%
where the time goes in v13:
time: 44 us; the launch traced here: 43.7 us
  starting transfers between devices  17.7 us (40%)
  blocking collectives  8.01 us (18%)
  other arithmetic  6.12 us (14%)
  matrix products  5.83 us (13%)
  local copies, waits for them, and re-layouts  2.88 us (7%)
  waiting for transfers between devices  2.37 us (5%)
  between operations  0.74 us (2%)
    ppermute x6, starting transfers between devices, shift(): return lax.ppermute(x, axis, [(i, (i + k) % n) for i in range(n)])  10.8 us
    all_gather x1, blocking collectives, per_device(): lax.all_gather(jnp.transpose(gather_input, (2, 0, 1)), 'task', axis=0, ti...  8.01 us
    reduce_sum x1, other arithmetic, kernel_tile(): return jnp.exp(0.1 - jnp.sqrt(jnp.sum(diff * diff, axis=0) + 0.01))  4.65 us
    unnamed x4, matrix products  4.38 us
    all_to_all x1, starting transfers between devices, per_device(): task_blocks = lax.all_to_all(copies, 'task', 0, 0, tiled=True)  3.49 us
    all_to_all x1, starting transfers between devices, sum_over(): lax.all_to_all(jnp.broadcast_to(x[None], (n,) + x.shape), axis, 0, 0, til...  3.4 us
    all_to_all x1, waiting for transfers between devices, per_device(): task_blocks = lax.all_to_all(copies, 'task', 0, 0, tiled=True)  2.35 us
    broadcast_in_dim x1, local copies, waits for them, and re-layouts, per_device(): copies = jnp.broadcast_to(task_input[None], (n_task,) + vectors.shape)  1.9 us
  transfers between devices with their start and end apart: 8, of which 1 were waited for; matrix products, arithmetic and copies ran while one was open for 29% of the time, Pallas kernels for 0%

profile of v13, /device:TPU:0, one launch (start us, length us, event | category | flops | bytes accessed | tf_op | source)
XLA Modules:
  0.0 43.7 jit_solution(11036838446238876066)
XLA Ops:
  0.7 3.1 %collective-permute-start = (bf16[3,768]{1,0:T(4,128)(2,1)}, bf16[3,768]{1,0:T(4,128)(2,1)S(1)}, u32[]{:S(2)}, u32[]{:S(2)}) collective-permute-start(bf16[3,768]{1,0:T(4,128)(2,1)} %param.6), channel_id=1, source_target_pairs={{0,4},{4,8},{8,12},{12,0},{1,5},{5,9},{9,13},{13,1},{2,6},{6,10},{... | collective-permute-start | bytes 13832 | tf_op jit(solution)/shard_map/ppermute | solution.py:13
  3.7 2.6 %collective-permute-start.2 = (bf16[3,768]{1,0:T(4,128)(2,1)}, bf16[3,768]{1,0:T(4,128)(2,1)S(1)}, u32[]{:S(2)}, u32[]{:S(2)}) collective-permute-start(bf16[3,768]{1,0:T(4,128)(2,1)} %param.6), channel_id=1, source_target_pairs={{0,8},{4,12},{8,0},{12,4},{1,9},{5,13},{9,1},{13,5},{2,10},{6,14},... | collective-permute-start | bytes 13832 | tf_op jit(solution)/shard_map/ppermute | solution.py:13
  6.3 1.3 %collective-permute-start.4 = (bf16[3,768]{1,0:T(4,128)(2,1)}, bf16[3,768]{1,0:T(4,128)(2,1)S(1)}, u32[]{:S(2)}, u32[]{:S(2)}) collective-permute-start(bf16[3,768]{1,0:T(4,128)(2,1)} %param.6), channel_id=1, source_target_pairs={{0,12},{4,0},{8,4},{12,8},{1,13},{5,1},{9,5},{13,9},{2,14},{6,2},{... | collective-permute-start | bytes 13832 | tf_op jit(solution)/shard_map/ppermute | solution.py:13
  7.7 0.7 %collective-permute-start.1 = (bf16[2,768,64]{1,2,0:T(8,128)(2,1)}, bf16[2,768,64]{1,2,0:T(8,128)(2,1)S(1)}, u32[]{:S(2)}, u32[]{:S(2)}) collective-permute-start(bf16[2,768,64]{1,2,0:T(8,128)(2,1)} %param.8), channel_id=1, source_target_pairs={{0,4},{4,8},{8,12},{12,0},{1,5},{5,9},{9,13},{13,1},{2,6},{6,10},{... | collective-permute-start | bytes 589832 | tf_op jit(solution)/shard_map/ppermute | solution.py:13
  8.3 0.3 collective-permute-start.3
  8.7 0.7 %broadcast_divide_fusion = f32[3]{0:T(128)S(1)} fusion(f32[3]{0:T(128)} %param.7), kind=kLoop, calls=%fused_computation.32 | loop fusion | flops 3 | bytes 24 | tf_op jit(solution)/shard_map/div | solution.py:34
  9.3 2.8 %collective-permute-start.5 = (bf16[2,768,64]{1,2,0:T(8,128)(2,1)}, bf16[2,768,64]{1,2,0:T(8,128)(2,1)S(1)}, u32[]{:S(2)}, u32[]{:S(2)}) collective-permute-start(bf16[2,768,64]{1,2,0:T(8,128)(2,1)} %param.8), channel_id=1, source_target_pairs={{0,12},{4,0},{8,4},{12,8},{1,13},{5,1},{9,5},{13,9},{2,14},{6,2},{... | collective-permute-start | bytes 589832 | tf_op jit(solution)/shard_map/ppermute | solution.py:13
  12.2 1.9 %broadcast_in_dim.6 = bf16[4,2,768,64]{2,3,1,0:T(8,128)(2,1)} broadcast(bf16[2,768,64]{1,2,0:T(8,128)(2,1)} %param.8), dimensions={1,2,3} | broadcast | bytes 983040 | tf_op jit(solution)/shard_map/broadcast_in_dim | solution.py:62
  14.1 3.5 %all-to-all-start = ((bf16[4,2,768,64]{2,3,1,0:T(8,128)(2,1)}), bf16[4,2,768,64]{2,3,1,0:T(8,128)(2,1)S(1)}, u32[]{:S(2)}, u32[]{:S(2)}) async-start(bf16[4,2,768,64]{2,3,1,0:T(8,128)(2,1)} %broadcast_in_dim.6), calls=%async_computation | async-start | bytes 1572864 | tf_op jit(solution)/shard_map/all_to_all | solution.py:63
  17.7 4.7 %multiply_reduce_fusion.2 = (f32[768,768]{1,0:T(8,128)S(1)}, f32[768,768]{1,0:T(8,128)S(1)}, f32[768,768]{1,0:T(8,128)S(1)}, f32[768,768]{1,0:T(8,128)S(1)}) fusion(f32[3,768]{1,0:T(4,128)S(1)} %get-tuple-element.11, f32[3,768]{1,0:T(4,128)S(1)} %get-tuple-element.13, f32[3,768]{1,0:T(4,128)S(1)} %get-tuple-element.12, f32[3,768]{1,0:T(4,128)S(1)} %get-tuple-element.10), kind=kLoop, calls=%fused_computation.2 | loop fusion | flops 18874368 | bytes 9474048 | tf_op jit(solution)/shard_map/reduce_sum | solution.py:9
  22.3 1.1 %fusion = f32[768,128]{0,1:S(1)} fusion(bf16[768,128]{0,1:T(8,128)(2,1)S(1)} %bitcast.37, f32[768,768]{1,0:T(8,128)S(1)} %get-tuple-element.9), kind=kOutput, calls=%fused_computation.9 | convolution fusion | flops 152764416 | bytes 2949120
  23.4 1.1 %fusion.1 = f32[768,128]{0,1:S(1)} fusion(bf16[768,128]{0,1:T(8,128)(2,1)S(1)} %bitcast.43, f32[768,768]{1,0:T(8,128)S(1)} %get-tuple-element.6), kind=kOutput, calls=%fused_computation.10 | convolution fusion | flops 152764416 | bytes 2949120
  24.5 1.1 %fusion.2 = f32[768,128]{0,1:S(1)} fusion(bf16[768,128]{0,1:T(8,128)(2,1)S(1)} %bitcast.42, f32[768,768]{1,0:T(8,128)S(1)} %get-tuple-element.7), kind=kOutput, calls=%fused_computation.11 | convolution fusion | flops 152764416 | bytes 2949120
  25.7 1.1 %fusion.3 = f32[768,128]{0,1:S(1)} fusion(bf16[768,128]{0,1:T(8,128)(2,1)S(1)} %bitcast.44, f32[768,768]{1,0:T(8,128)S(1)} %get-tuple-element.8), kind=kOutput, calls=%fused_computation.12 | convolution fusion | flops 152764416 | bytes 2949120
  26.8 0.1 fusion.5
  26.8 2.3 %all-to-all-done = bf16[4,2,768,64]{2,3,1,0:T(8,128)(2,1)S(1)} async-done(((bf16[4,2,768,64]{2,3,1,0:T(8,128)(2,1)}), bf16[4,2,768,64]{2,3,1,0:T(8,128)(2,1)S(1)}, u32[]{:S(2)}, u32[]{:S(2)}) %all-to-all-start) | async-done | bytes 786464 | tf_op jit(solution)/shard_map/all_to_all | solution.py:63
  29.2 0.5 %convolution_bitcast_fusion = f32[64,4,64]{2,0,1:T(8,128)S(1)} fusion(bf16[4,2,768,64]{2,3,1,0:T(8,128)(2,1)S(1)} %all-to-all-done, bf16[2,768,64]{1,2,0:T(8,128)(2,1)S(1)} %fusion.5, bf16[2]{0:T(256)(128)(2,1)S(1)} %copy-done.4), kind=kOutput, calls=%fused_computation.14 | convolution fusion | flops 50724864 | bytes 1048580 | tf_op jit(solution)/shard_map/sna,ksnb->akb/dot_general | solution.py:67
  29.7 0.1 copy.9
  29.8 0.1 broadcast_in_dim.7
  30.0 0.7 %broadcast_in_dim.8 = f32[4,64,256]{2,1,0:T(8,128)} broadcast(f32[64,256]{1,0:T(8,128)S(1)} %broadcast_in_dim.7), dimensions={1,2} | broadcast | bytes 327680 | tf_op jit(solution)/shard_map/broadcast_in_dim | solution.py:18
  30.7 3.4 %all-to-all-start.1 = ((f32[4,64,256]{2,1,0:T(8,128)}), f32[4,64,256]{2,1,0:T(8,128)S(1)}, u32[]{:S(2)}, u32[]{:S(2)}) async-start(f32[4,64,256]{2,1,0:T(8,128)} %broadcast_in_dim.8), calls=%async_computation.1 | async-start | bytes 524288 | tf_op jit(solution)/shard_map/all_to_all | solution.py:18
  34.1 8.0 %all_gather.3 = bf16[256,2,768]{2,0,1:T(8,128)(2,1)S(1)} all-gather(bf16[64,2,768]{2,0,1:T(8,128)(2,1)S(1)} %bitcast.36), channel_id=1, replica_groups=mesh['groups'=2,'dp'=4,'task'=4] {'task'}, dimensions={0}, use_global_device_ids=true | all-gather | bytes 983040 | tf_op jit(solution)/shard_map/all_gather | solution.py:72
  42.1 0.9 %fusion.4 = bf16[2,768,64]{1,2,0:T(8,128)(2,1)} fusion(bf16[256,2,768]{2,0,1:T(8,128)(2,1)S(1)} %all_gather.3, bf16[2,768,64]{1,2,0:T(8,128)(2,1)S(1)} %copy-done.1, f32[64]{0:T(128)S(1)} %copy-done.3, bf16[256,256]{1,0:T(8,128)(2,1)S(1)} %copy-done, s32[]{:T(128)S(6)} %select_n.3), kind=kOutput, calls=%fused_computation.13 | convolution fusion | flops 50724864 | bytes 1212932 | tf_op jit(solution)/shard_map/asn,ca->snc/dot_general | solution.py:74
  43.0 0.6 %fusion.11 = f32[64,256]{1,0:T(8,128)} fusion(f32[4,64,256]{2,1,0:T(8,128)S(1)} %all-to-all-done.1), kind=kLoop, calls=%fused_computation.23 | loop fusion | flops 65536 | bytes 327680 | tf_op jit(solution)/shard_map/div | solution.py:76
  (18 shorter events, 0.1 us)
Async XLA Ops:
  0.6 41.5 %copy-start = (bf16[256,256]{1,0:T(8,128)(2,1)S(1)}, bf16[256,256]{1,0:T(8,128)(2,1)}, u32[]{:S(2)}) copy-start(bf16[256,256]{1,0:T(8,128)(2,1)} %param.9) | copy-start | bytes 393220
  0.6 16.9 %copy-start.2 = (bf16[3,768]{1,0:T(4,128)(2,1)S(1)}, bf16[3,768]{1,0:T(4,128)(2,1)}, u32[]{:S(2)}) copy-start(bf16[3,768]{1,0:T(4,128)(2,1)} %param.6) | copy-start | bytes 13828
  0.7 8.7 %collective-permute-start = (bf16[3,768]{1,0:T(4,128)(2,1)}, bf16[3,768]{1,0:T(4,128)(2,1)S(1)}, u32[]{:S(2)}, u32[]{:S(2)}) collective-permute-start(bf16[3,768]{1,0:T(4,128)(2,1)} %param.6), channel_id=1, source_target_pairs={{0,4},{4,8},{8,12},{12,0},{1,5},{5,9},{9,13},{13,1},{2,6},{6,10},{... | collective-permute-start | bytes 13832 | tf_op jit(solution)/shard_map/ppermute | solution.py:13
  3.7 8.4 %collective-permute-start.2 = (bf16[3,768]{1,0:T(4,128)(2,1)}, bf16[3,768]{1,0:T(4,128)(2,1)S(1)}, u32[]{:S(2)}, u32[]{:S(2)}) collective-permute-start(bf16[3,768]{1,0:T(4,128)(2,1)} %param.6), channel_id=1, source_target_pairs={{0,8},{4,12},{8,0},{12,4},{1,9},{5,13},{9,1},{13,5},{2,10},{6,14},... | collective-permute-start | bytes 13832 | tf_op jit(solution)/shard_map/ppermute | solution.py:13
  6.3 5.8 %collective-permute-start.4 = (bf16[3,768]{1,0:T(4,128)(2,1)}, bf16[3,768]{1,0:T(4,128)(2,1)S(1)}, u32[]{:S(2)}, u32[]{:S(2)}) collective-permute-start(bf16[3,768]{1,0:T(4,128)(2,1)} %param.6), channel_id=1, source_target_pairs={{0,12},{4,0},{8,4},{12,8},{1,13},{5,1},{9,5},{13,9},{2,14},{6,2},{... | collective-permute-start | bytes 13832 | tf_op jit(solution)/shard_map/ppermute | solution.py:13
  7.7 15.8 %collective-permute-start.1 = (bf16[2,768,64]{1,2,0:T(8,128)(2,1)}, bf16[2,768,64]{1,2,0:T(8,128)(2,1)S(1)}, u32[]{:S(2)}, u32[]{:S(2)}) collective-permute-start(bf16[2,768,64]{1,2,0:T(8,128)(2,1)} %param.8), channel_id=1, source_target_pairs={{0,4},{4,8},{8,12},{12,0},{1,5},{5,9},{9,13},{13,1},{2,6},{6,10},{... | collective-permute-start | bytes 589832 | tf_op jit(solution)/shard_map/ppermute | solution.py:13
  8.3 16.2 %collective-permute-start.3 = (bf16[2,768,64]{1,2,0:T(8,128)(2,1)}, bf16[2,768,64]{1,2,0:T(8,128)(2,1)S(1)}, u32[]{:S(2)}, u32[]{:S(2)}) collective-permute-start(bf16[2,768,64]{1,2,0:T(8,128)(2,1)} %param.8), channel_id=1, source_target_pairs={{0,8},{4,12},{8,0},{12,4},{1,9},{5,13},{9,1},{13,5},{2,10},{6,14},... | collective-permute-start | bytes 589832 | tf_op jit(solution)/shard_map/ppermute | solution.py:13
  9.3 16.3 %collective-permute-start.5 = (bf16[2,768,64]{1,2,0:T(8,128)(2,1)}, bf16[2,768,64]{1,2,0:T(8,128)(2,1)S(1)}, u32[]{:S(2)}, u32[]{:S(2)}) collective-permute-start(bf16[2,768,64]{1,2,0:T(8,128)(2,1)} %param.8), channel_id=1, source_target_pairs={{0,12},{4,0},{8,4},{12,8},{1,13},{5,1},{9,5},{13,9},{2,14},{6,2},{... | collective-permute-start | bytes 589832 | tf_op jit(solution)/shard_map/ppermute | solution.py:13
  14.1 15.1 %all-to-all-start = ((bf16[4,2,768,64]{2,3,1,0:T(8,128)(2,1)}), bf16[4,2,768,64]{2,3,1,0:T(8,128)(2,1)S(1)}, u32[]{:S(2)}, u32[]{:S(2)}) async-start(bf16[4,2,768,64]{2,3,1,0:T(8,128)(2,1)} %broadcast_in_dim.6), calls=%async_computation | async-start | bytes 1572864 | tf_op jit(solution)/shard_map/all_to_all | solution.py:63
  17.7 4.7 %copy-start.1 = (bf16[2,768,64]{1,2,0:T(8,128)(2,1)S(1)}, bf16[2,768,64]{1,2,0:T(8,128)(2,1)}, u32[]{:S(2)}) copy-start(bf16[2,768,64]{1,2,0:T(8,128)(2,1)} %param.8) | copy-start | bytes 589828
  25.6 3.6 %copy-start.4 = (bf16[2]{0:T(256)(128)(2,1)S(1)}, bf16[2]{0:T(256)(128)(2,1)}, u32[]{:S(2)}) copy-start(bf16[2]{0:T(256)(128)(2,1)} %constant.23.clone) | copy-start | bytes 16
  26.7 15.3 %copy-start.3 = (f32[64]{0:T(128)S(1)}, f32[64]{0:T(128)}, u32[]{:S(2)}) copy-start(f32[64]{0:T(128)} %param.10) | copy-start | bytes 772
  30.7 12.4 %all-to-all-start.1 = ((f32[4,64,256]{2,1,0:T(8,128)}), f32[4,64,256]{2,1,0:T(8,128)S(1)}, u32[]{:S(2)}, u32[]{:S(2)}) async-start(f32[4,64,256]{2,1,0:T(8,128)} %broadcast_in_dim.8), calls=%async_computation.1 | async-start | bytes 524288 | tf_op jit(solution)/shard_map/all_to_all | solution.py:18

commit v14 on v13

--- a/solution.py
+++ b/solution.py
@@ -15,8 +15,8 @@
 
 def sum_over(x, axis, n):
     if n == 4:
-        got = lax.all_to_all(jnp.broadcast_to(x[None], (n,) + x.shape), axis, 0, 0, tiled=True)
-        return (got[0] + got[1]) + (got[2] + got[3])
+        got = [lax.ppermute(x, axis, [(i, i ^ k) for i in range(n)]) for k in range(1, n)]
+        return (x + got[0]) + (got[1] + got[2])
     if n & (n - 1):
         return lax.psum(x, axis)
     step = 1

time: 44 us -> 43.7 us (level)
  starting transfers between devices: 17.7 us -> 18.8 us
  local copies, waits for them, and re-layouts: 2.88 us -> 2.16 us
  blocking collectives: 8.01 us -> 7.45 us
    ppermute x0 -> x3, starting transfers between devices: none -> 4.44 us  [sum_over(): lax.ppermute(x, axis, [(i, i ^ k) for i in range(n)])]
    all_to_all x1 -> x0, starting transfers between devices: 3.4 us -> none  [sum_over(): lax.all_to_all(jnp.broadcast_to(x[None], (n,) + x.shape), axis, 0, 0, til...]
    broadcast_in_dim x2 -> x0, local copies, waits for them, and re-layouts: 0.86 us -> none  [sum_over(): jnp.broadcast_to(x[None], (n,) + x.shape)]
    all_gather x1, blocking collectives: 8.01 us -> 7.45 us  [per_device(): lax.all_gather(jnp.transpose(gather_input, (2, 0, 1)), 'task', axis=0, ti...]
  transfers between devices with their start and end apart: 8 -> 10, of which waited for: 1 -> 1; matrix products, arithmetic and copies ran while one was open for 29% -> 29% of each run, Pallas kernels for 0% -> 0%
where the time goes in v14:
time: 43.7 us; the launch traced here: 43.4 us
  starting transfers between devices  18.8 us (43%)
  blocking collectives  7.45 us (17%)
  other arithmetic  6.12 us (14%)
  matrix products  5.84 us (13%)
  waiting for transfers between devices  2.37 us (5%)
  local copies, waits for them, and re-layouts  2.16 us (5%)
  between operations  0.73 us (2%)
    ppermute x6, starting transfers between devices, shift(): return lax.ppermute(x, axis, [(i, (i + k) % n) for i in range(n)])  10.8 us
    all_gather x1, blocking collectives, per_device(): lax.all_gather(jnp.transpose(gather_input, (2, 0, 1)), 'task', axis=0, ti...  7.45 us
    reduce_sum x1, other arithmetic, kernel_tile(): return jnp.exp(0.1 - jnp.sqrt(jnp.sum(diff * diff, axis=0) + 0.01))  4.65 us
    ppermute x3, starting transfers between devices, sum_over(): lax.ppermute(x, axis, [(i, i ^ k) for i in range(n)])  4.44 us
    unnamed x4, matrix products  4.38 us
    all_to_all x1, starting transfers between devices, per_device(): task_blocks = lax.all_to_all(copies, 'task', 0, 0, tiled=True)  3.49 us
    all_to_all x1, waiting for transfers between devices, per_device(): task_blocks = lax.all_to_all(copies, 'task', 0, 0, tiled=True)  2.35 us
    broadcast_in_dim x1, local copies, waits for them, and re-layouts, per_device(): copies = jnp.broadcast_to(task_input[None], (n_task,) + vectors.shape)  1.9 us
  transfers between devices with their start and end apart: 10, of which 1 were waited for; matrix products, arithmetic and copies ran while one was open for 29% of the time, Pallas kernels for 0%

profile of v14, /device:TPU:0, one launch (start us, length us, event | category | flops | bytes accessed | tf_op | source)
XLA Modules:
  0.0 43.4 jit_solution(444910275048025326)
XLA Ops:
  0.7 3.1 %collective-permute-start = (bf16[3,768]{1,0:T(4,128)(2,1)}, bf16[3,768]{1,0:T(4,128)(2,1)S(1)}, u32[]{:S(2)}, u32[]{:S(2)}) collective-permute-start(bf16[3,768]{1,0:T(4,128)(2,1)} %param.6), channel_id=1, source_target_pairs={{0,4},{4,8},{8,12},{12,0},{1,5},{5,9},{9,13},{13,1},{2,6},{6,10},{... | collective-permute-start | bytes 13832 | tf_op jit(solution)/shard_map/ppermute | solution.py:13
  3.7 2.6 %collective-permute-start.2 = (bf16[3,768]{1,0:T(4,128)(2,1)}, bf16[3,768]{1,0:T(4,128)(2,1)S(1)}, u32[]{:S(2)}, u32[]{:S(2)}) collective-permute-start(bf16[3,768]{1,0:T(4,128)(2,1)} %param.6), channel_id=1, source_target_pairs={{0,8},{4,12},{8,0},{12,4},{1,9},{5,13},{9,1},{13,5},{2,10},{6,14},... | collective-permute-start | bytes 13832 | tf_op jit(solution)/shard_map/ppermute | solution.py:13
  6.3 1.3 %collective-permute-start.4 = (bf16[3,768]{1,0:T(4,128)(2,1)}, bf16[3,768]{1,0:T(4,128)(2,1)S(1)}, u32[]{:S(2)}, u32[]{:S(2)}) collective-permute-start(bf16[3,768]{1,0:T(4,128)(2,1)} %param.6), channel_id=1, source_target_pairs={{0,12},{4,0},{8,4},{12,8},{1,13},{5,1},{9,5},{13,9},{2,14},{6,2},{... | collective-permute-start | bytes 13832 | tf_op jit(solution)/shard_map/ppermute | solution.py:13
  7.7 0.7 %collective-permute-start.1 = (bf16[2,768,64]{1,2,0:T(8,128)(2,1)}, bf16[2,768,64]{1,2,0:T(8,128)(2,1)S(1)}, u32[]{:S(2)}, u32[]{:S(2)}) collective-permute-start(bf16[2,768,64]{1,2,0:T(8,128)(2,1)} %param.8), channel_id=1, source_target_pairs={{0,4},{4,8},{8,12},{12,0},{1,5},{5,9},{9,13},{13,1},{2,6},{6,10},{... | collective-permute-start | bytes 589832 | tf_op jit(solution)/shard_map/ppermute | solution.py:13
  8.3 0.3 collective-permute-start.3
  8.7 0.7 %broadcast_divide_fusion = f32[3]{0:T(128)S(1)} fusion(f32[3]{0:T(128)} %param.7), kind=kLoop, calls=%fused_computation.28 | loop fusion | flops 3 | bytes 24 | tf_op jit(solution)/shard_map/div | solution.py:34
  9.3 2.8 %collective-permute-start.5 = (bf16[2,768,64]{1,2,0:T(8,128)(2,1)}, bf16[2,768,64]{1,2,0:T(8,128)(2,1)S(1)}, u32[]{:S(2)}, u32[]{:S(2)}) collective-permute-start(bf16[2,768,64]{1,2,0:T(8,128)(2,1)} %param.8), channel_id=1, source_target_pairs={{0,12},{4,0},{8,4},{12,8},{1,13},{5,1},{9,5},{13,9},{2,14},{6,2},{... | collective-permute-start | bytes 589832 | tf_op jit(solution)/shard_map/ppermute | solution.py:13
  12.2 1.9 %broadcast_in_dim.2 = bf16[4,2,768,64]{2,3,1,0:T(8,128)(2,1)} broadcast(bf16[2,768,64]{1,2,0:T(8,128)(2,1)} %param.8), dimensions={1,2,3} | broadcast | bytes 983040 | tf_op jit(solution)/shard_map/broadcast_in_dim | solution.py:62
  14.1 3.5 %all-to-all-start = ((bf16[4,2,768,64]{2,3,1,0:T(8,128)(2,1)}), bf16[4,2,768,64]{2,3,1,0:T(8,128)(2,1)S(1)}, u32[]{:S(2)}, u32[]{:S(2)}) async-start(bf16[4,2,768,64]{2,3,1,0:T(8,128)(2,1)} %broadcast_in_dim.2), calls=%async_computation | async-start | bytes 1572864 | tf_op jit(solution)/shard_map/all_to_all | solution.py:63
  17.7 4.7 %multiply_reduce_fusion.2 = (f32[768,768]{1,0:T(8,128)S(1)}, f32[768,768]{1,0:T(8,128)S(1)}, f32[768,768]{1,0:T(8,128)S(1)}, f32[768,768]{1,0:T(8,128)S(1)}) fusion(f32[3,768]{1,0:T(4,128)S(1)} %get-tuple-element.11, f32[3,768]{1,0:T(4,128)S(1)} %get-tuple-element.13, f32[3,768]{1,0:T(4,128)S(1)} %get-tuple-element.12, f32[3,768]{1,0:T(4,128)S(1)} %get-tuple-element.10), kind=kLoop, calls=%fused_computation.2 | loop fusion | flops 18874368 | bytes 9474048 | tf_op jit(solution)/shard_map/reduce_sum | solution.py:9
  22.3 1.1 %fusion = f32[768,128]{0,1:S(1)} fusion(bf16[768,128]{0,1:T(8,128)(2,1)S(1)} %bitcast.35, f32[768,768]{1,0:T(8,128)S(1)} %get-tuple-element.9), kind=kOutput, calls=%fused_computation.9 | convolution fusion | flops 152764416 | bytes 2949120
  23.4 1.1 %fusion.1 = f32[768,128]{0,1:S(1)} fusion(bf16[768,128]{0,1:T(8,128)(2,1)S(1)} %bitcast.41, f32[768,768]{1,0:T(8,128)S(1)} %get-tuple-element.6), kind=kOutput, calls=%fused_computation.10 | convolution fusion | flops 152764416 | bytes 2949120
  24.5 1.1 %fusion.2 = f32[768,128]{0,1:S(1)} fusion(bf16[768,128]{0,1:T(8,128)(2,1)S(1)} %bitcast.40, f32[768,768]{1,0:T(8,128)S(1)} %get-tuple-element.7), kind=kOutput, calls=%fused_computation.11 | convolution fusion | flops 152764416 | bytes 2949120
  25.7 1.1 %fusion.3 = f32[768,128]{0,1:S(1)} fusion(bf16[768,128]{0,1:T(8,128)(2,1)S(1)} %bitcast.42, f32[768,768]{1,0:T(8,128)S(1)} %get-tuple-element.8), kind=kOutput, calls=%fused_computation.12 | convolution fusion | flops 152764416 | bytes 2949120
  26.8 2.3 %all-to-all-done = bf16[4,2,768,64]{2,3,1,0:T(8,128)(2,1)S(1)} async-done(((bf16[4,2,768,64]{2,3,1,0:T(8,128)(2,1)}), bf16[4,2,768,64]{2,3,1,0:T(8,128)(2,1)S(1)}, u32[]{:S(2)}, u32[]{:S(2)}) %all-to-all-start) | async-done | bytes 786464 | tf_op jit(solution)/shard_map/all_to_all | solution.py:63
  29.2 0.5 %convolution_bitcast_fusion = f32[64,4,64]{2,0,1:T(8,128)S(1)} fusion(bf16[4,2,768,64]{2,3,1,0:T(8,128)(2,1)S(1)} %all-to-all-done, bf16[2,768,64]{1,2,0:T(8,128)(2,1)S(1)} %fusion.5, bf16[2]{0:T(256)(128)(2,1)S(1)} %copy-done.4), kind=kOutput, calls=%fused_computation.14 | convolution fusion | flops 50724864 | bytes 1048580 | tf_op jit(solution)/shard_map/sna,ksnb->akb/dot_general | solution.py:67
  29.7 0.1 copy.9
  29.8 0.1 reshape.16
  29.9 0.6 %collective-permute-start.6 = (f32[64,256]{1,0:T(8,128)S(1)}, f32[64,256]{1,0:T(8,128)S(1)}, u32[]{:S(2)}, u32[]{:S(2)}) collective-permute-start(f32[64,256]{1,0:T(8,128)S(1)} %reshape.16), channel_id=1, source_target_pairs={{0,4},{4,0},{8,12},{12,8},{1,5},{5,1},{9,13},{13,9},{2,6},{6,2},{1... | collective-permute-start | bytes 196616 | tf_op jit(solution)/shard_map/ppermute | solution.py:18
  30.6 1.5 %collective-permute-start.7 = (f32[64,256]{1,0:T(8,128)S(1)}, f32[64,256]{1,0:T(8,128)S(1)}, u32[]{:S(2)}, u32[]{:S(2)}) collective-permute-start(f32[64,256]{1,0:T(8,128)S(1)} %reshape.16), channel_id=1, source_target_pairs={{0,8},{4,12},{8,0},{12,4},{1,9},{5,13},{9,1},{13,5},{2,10},{6,14},... | collective-permute-start | bytes 196616 | tf_op jit(solution)/shard_map/ppermute | solution.py:18
  32.1 2.3 %collective-permute-start.8 = (f32[64,256]{1,0:T(8,128)S(1)}, f32[64,256]{1,0:T(8,128)S(1)}, u32[]{:S(2)}, u32[]{:S(2)}) collective-permute-start(f32[64,256]{1,0:T(8,128)S(1)} %reshape.16), channel_id=1, source_target_pairs={{0,12},{4,8},{8,4},{12,0},{1,13},{5,9},{9,5},{13,1},{2,14},{6,10},... | collective-permute-start | bytes 196616 | tf_op jit(solution)/shard_map/ppermute | solution.py:18
  34.4 7.5 %all_gather.3 = bf16[256,2,768]{2,0,1:T(8,128)(2,1)S(1)} all-gather(bf16[64,2,768]{2,0,1:T(8,128)(2,1)S(1)} %bitcast.34), channel_id=1, replica_groups=mesh['groups'=2,'dp'=4,'task'=4] {'task'}, dimensions={0}, use_global_device_ids=true | all-gather | bytes 983040 | tf_op jit(solution)/shard_map/all_gather | solution.py:72
  41.8 0.9 %fusion.4 = bf16[2,768,64]{1,2,0:T(8,128)(2,1)} fusion(bf16[256,2,768]{2,0,1:T(8,128)(2,1)S(1)} %all_gather.3, bf16[2,768,64]{1,2,0:T(8,128)(2,1)S(1)} %copy-done.1, f32[64]{0:T(128)S(1)} %copy-done.3, bf16[256,256]{1,0:T(8,128)(2,1)S(1)} %copy-done, s32[]{:T(128)S(6)} %select_n.3), kind=kOutput, calls=%fused_computation.13 | convolution fusion | flops 50724864 | bytes 1212932 | tf_op jit(solution)/shard_map/asn,ca->snc/dot_general | solution.py:74
  42.8 0.6 %add_multiply_fusion = f32[64,256]{1,0:T(8,128)} fusion(f32[64,256]{1,0:T(8,128)S(1)} %collective-permute-done.7, f32[64,256]{1,0:T(8,128)S(1)} %collective-permute-done.8, f32[64,256]{1,0:T(8,128)S(1)} %reshape.16, f32[64,256]{1,0:T(8,128)S(1)} %collective-permute-done.6), kind=kLoop, calls=%fused_computation.20 | loop fusion | flops 65536 | bytes 327680 | tf_op jit(solution)/shard_map/div | solution.py:76
  (21 shorter events, 0.2 us)
Async XLA Ops:
  0.6 41.2 %copy-start = (bf16[256,256]{1,0:T(8,128)(2,1)S(1)}, bf16[256,256]{1,0:T(8,128)(2,1)}, u32[]{:S(2)}) copy-start(bf16[256,256]{1,0:T(8,128)(2,1)} %param.9) | copy-start | bytes 393220
  0.6 16.9 %copy-start.2 = (bf16[3,768]{1,0:T(4,128)(2,1)S(1)}, bf16[3,768]{1,0:T(4,128)(2,1)}, u32[]{:S(2)}) copy-start(bf16[3,768]{1,0:T(4,128)(2,1)} %param.6) | copy-start | bytes 13828
  0.7 8.7 %collective-permute-start = (bf16[3,768]{1,0:T(4,128)(2,1)}, bf16[3,768]{1,0:T(4,128)(2,1)S(1)}, u32[]{:S(2)}, u32[]{:S(2)}) collective-permute-start(bf16[3,768]{1,0:T(4,128)(2,1)} %param.6), channel_id=1, source_target_pairs={{0,4},{4,8},{8,12},{12,0},{1,5},{5,9},{9,13},{13,1},{2,6},{6,10},{... | collective-permute-start | bytes 13832 | tf_op jit(solution)/shard_map/ppermute | solution.py:13
  3.7 8.4 %collective-permute-start.2 = (bf16[3,768]{1,0:T(4,128)(2,1)}, bf16[3,768]{1,0:T(4,128)(2,1)S(1)}, u32[]{:S(2)}, u32[]{:S(2)}) collective-permute-start(bf16[3,768]{1,0:T(4,128)(2,1)} %param.6), channel_id=1, source_target_pairs={{0,8},{4,12},{8,0},{12,4},{1,9},{5,13},{9,1},{13,5},{2,10},{6,14},... | collective-permute-start | bytes 13832 | tf_op jit(solution)/shard_map/ppermute | solution.py:13
  6.3 5.8 %collective-permute-start.4 = (bf16[3,768]{1,0:T(4,128)(2,1)}, bf16[3,768]{1,0:T(4,128)(2,1)S(1)}, u32[]{:S(2)}, u32[]{:S(2)}) collective-permute-start(bf16[3,768]{1,0:T(4,128)(2,1)} %param.6), channel_id=1, source_target_pairs={{0,12},{4,0},{8,4},{12,8},{1,13},{5,1},{9,5},{13,9},{2,14},{6,2},{... | collective-permute-start | bytes 13832 | tf_op jit(solution)/shard_map/ppermute | solution.py:13
  7.7 15.8 %collective-permute-start.1 = (bf16[2,768,64]{1,2,0:T(8,128)(2,1)}, bf16[2,768,64]{1,2,0:T(8,128)(2,1)S(1)}, u32[]{:S(2)}, u32[]{:S(2)}) collective-permute-start(bf16[2,768,64]{1,2,0:T(8,128)(2,1)} %param.8), channel_id=1, source_target_pairs={{0,4},{4,8},{8,12},{12,0},{1,5},{5,9},{9,13},{13,1},{2,6},{6,10},{... | collective-permute-start | bytes 589832 | tf_op jit(solution)/shard_map/ppermute | solution.py:13
  8.3 16.2 %collective-permute-start.3 = (bf16[2,768,64]{1,2,0:T(8,128)(2,1)}, bf16[2,768,64]{1,2,0:T(8,128)(2,1)S(1)}, u32[]{:S(2)}, u32[]{:S(2)}) collective-permute-start(bf16[2,768,64]{1,2,0:T(8,128)(2,1)} %param.8), channel_id=1, source_target_pairs={{0,8},{4,12},{8,0},{12,4},{1,9},{5,13},{9,1},{13,5},{2,10},{6,14},... | collective-permute-start | bytes 589832 | tf_op jit(solution)/shard_map/ppermute | solution.py:13
  9.3 16.3 %collective-permute-start.5 = (bf16[2,768,64]{1,2,0:T(8,128)(2,1)}, bf16[2,768,64]{1,2,0:T(8,128)(2,1)S(1)}, u32[]{:S(2)}, u32[]{:S(2)}) collective-permute-start(bf16[2,768,64]{1,2,0:T(8,128)(2,1)} %param.8), channel_id=1, source_target_pairs={{0,12},{4,0},{8,4},{12,8},{1,13},{5,1},{9,5},{13,9},{2,14},{6,2},{... | collective-permute-start | bytes 589832 | tf_op jit(solution)/shard_map/ppermute | solution.py:13
  14.1 15.1 %all-to-all-start = ((bf16[4,2,768,64]{2,3,1,0:T(8,128)(2,1)}), bf16[4,2,768,64]{2,3,1,0:T(8,128)(2,1)S(1)}, u32[]{:S(2)}, u32[]{:S(2)}) async-start(bf16[4,2,768,64]{2,3,1,0:T(8,128)(2,1)} %broadcast_in_dim.2), calls=%async_computation | async-start | bytes 1572864 | tf_op jit(solution)/shard_map/all_to_all | solution.py:63
  17.7 4.7 %copy-start.1 = (bf16[2,768,64]{1,2,0:T(8,128)(2,1)S(1)}, bf16[2,768,64]{1,2,0:T(8,128)(2,1)}, u32[]{:S(2)}) copy-start(bf16[2,768,64]{1,2,0:T(8,128)(2,1)} %param.8) | copy-start | bytes 589828
  25.6 3.6 %copy-start.4 = (bf16[2]{0:T(256)(128)(2,1)S(1)}, bf16[2]{0:T(256)(128)(2,1)}, u32[]{:S(2)}) copy-start(bf16[2]{0:T(256)(128)(2,1)} %constant.23.clone) | copy-start | bytes 16
  26.7 15.1 %copy-start.3 = (f32[64]{0:T(128)S(1)}, f32[64]{0:T(128)}, u32[]{:S(2)}) copy-start(f32[64]{0:T(128)} %param.10) | copy-start | bytes 772
  29.9 12.8 %collective-permute-start.6 = (f32[64,256]{1,0:T(8,128)S(1)}, f32[64,256]{1,0:T(8,128)S(1)}, u32[]{:S(2)}, u32[]{:S(2)}) collective-permute-start(f32[64,256]{1,0:T(8,128)S(1)} %reshape.16), channel_id=1, source_target_pairs={{0,4},{4,0},{8,12},{12,8},{1,5},{5,1},{9,13},{13,9},{2,6},{6,2},{1... | collective-permute-start | bytes 196616 | tf_op jit(solution)/shard_map/ppermute | solution.py:18
  30.6 12.2 %collective-permute-start.7 = (f32[64,256]{1,0:T(8,128)S(1)}, f32[64,256]{1,0:T(8,128)S(1)}, u32[]{:S(2)}, u32[]{:S(2)}) collective-permute-start(f32[64,256]{1,0:T(8,128)S(1)} %reshape.16), channel_id=1, source_target_pairs={{0,8},{4,12},{8,0},{12,4},{1,9},{5,13},{9,1},{13,5},{2,10},{6,14},... | collective-permute-start | bytes 196616 | tf_op jit(solution)/shard_map/ppermute | solution.py:18
  32.1 10.7 %collective-permute-start.8 = (f32[64,256]{1,0:T(8,128)S(1)}, f32[64,256]{1,0:T(8,128)S(1)}, u32[]{:S(2)}, u32[]{:S(2)}) collective-permute-start(f32[64,256]{1,0:T(8,128)S(1)} %reshape.16), channel_id=1, source_target_pairs={{0,12},{4,8},{8,4},{12,0},{1,13},{5,9},{9,5},{13,1},{2,14},{6,10},... | collective-permute-start | bytes 196616 | tf_op jit(solution)/shard_map/ppermute | solution.py:18

commit v15 on v12

--- a/solution.py
+++ b/solution.py
@@ -46,7 +46,6 @@
     if n_dp <= 4:
         moved = [shift(vectors, "dp", k, n_dp) for k in range(1, n_dp)]
         peer_coords = [shift(coords, "dp", k, n_dp) for k in range(1, n_dp)]
-        task_input = lax.optimization_barrier((vectors, peer_coords))[0]
         summed = block(coords, vectors)
         for k in range(1, n_dp):
             summed = summed + block(peer_coords[k - 1], moved[k - 1])

time: 43.3 us -> 45.8 us (1.058)
  waiting for transfers between devices: 2.37 us -> 4.29 us
  blocking collectives: 7.45 us -> 8.58 us
  other arithmetic: 6.12 us -> 5.47 us
    ppermute x9, waiting for transfers between devices: 0.02 us -> 4.28 us  [shift(): return lax.ppermute(x, axis, [(i, (i + k) % n) for i in range(n)])]
    all_to_all x1, waiting for transfers between devices: 2.35 us -> 0.01 us  [per_device(): task_blocks = lax.all_to_all(copies, 'task', 0, 0, tiled=True)]
    all_gather x1, blocking collectives: 7.45 us -> 8.58 us  [per_device(): lax.all_gather(jnp.transpose(gather_input, (2, 0, 1)), 'task', axis=0, ti...]
    div x1, other arithmetic: 0.66 us -> 0.01 us  [per_device(): inverse = 1.0 / lengthscales]
  transfers between devices with their start and end apart: 10 -> 10, of which waited for: 1 -> 1; matrix products, arithmetic and copies ran while one was open for 29% -> 26% of each run, Pallas kernels for 0% -> 0%
where the time goes in v15:
time: 45.8 us; the launch traced here: 45.6 us
  starting transfers between devices  18.4 us (40%)
  blocking collectives  8.58 us (19%)
  matrix products  5.83 us (13%)
  other arithmetic  5.47 us (12%)
  waiting for transfers between devices  4.29 us (9%)
  local copies, waits for them, and re-layouts  2.16 us (5%)
  between operations  0.82 us (2%)
    ppermute x9, starting transfers between devices, shift(): return lax.ppermute(x, axis, [(i, (i + k) % n) for i in range(n)])  14.9 us
    all_gather x1, blocking collectives, per_device(): lax.all_gather(jnp.transpose(gather_input, (2, 0, 1)), 'task', axis=0, ti...  8.58 us
    reduce_sum x1, other arithmetic, kernel_tile(): return jnp.exp(0.1 - jnp.sqrt(jnp.sum(diff * diff, axis=0) + 0.01))  4.65 us
    unnamed x4, matrix products  4.37 us
    ppermute x9, waiting for transfers between devices, shift(): return lax.ppermute(x, axis, [(i, (i + k) % n) for i in range(n)])  4.28 us
    all_to_all x1, starting transfers between devices, per_device(): task_blocks = lax.all_to_all(copies, 'task', 0, 0, tiled=True)  3.49 us
    broadcast_in_dim x1, local copies, waits for them, and re-layouts, per_device(): copies = jnp.broadcast_to(task_input[None], (n_task,) + vectors.shape)  1.89 us
    dot_general x1, matrix products, per_device(): jnp.einsum('asn,ca->snc', whole_images, own_rows, preferred_element_type=...  0.94 us
  transfers between devices with their start and end apart: 10, of which 1 were waited for; matrix products, arithmetic and copies ran while one was open for 26% of the time, Pallas kernels for 0%

profile of v15, /device:TPU:0, one launch (start us, length us, event | category | flops | bytes accessed | tf_op | source)
XLA Modules:
  0.0 45.6 jit_solution(10776250200305464711)
XLA Ops:
  0.7 5.1 %collective-permute-start.4 = (bf16[3,768]{1,0:T(4,128)(2,1)}, bf16[3,768]{1,0:T(4,128)(2,1)S(1)}, u32[]{:S(2)}, u32[]{:S(2)}) collective-permute-start(bf16[3,768]{1,0:T(4,128)(2,1)} %param.6), channel_id=1, source_target_pairs={{0,12},{4,0},{8,4},{12,8},{1,13},{5,1},{9,5},{13,9},{2,14},{6,2},{... | collective-permute-start | bytes 13832 | tf_op jit(solution)/shard_map/ppermute | solution.py:13
  5.8 1.0 %collective-permute-start.2 = (bf16[3,768]{1,0:T(4,128)(2,1)}, bf16[3,768]{1,0:T(4,128)(2,1)S(1)}, u32[]{:S(2)}, u32[]{:S(2)}) collective-permute-start(bf16[3,768]{1,0:T(4,128)(2,1)} %param.6), channel_id=1, source_target_pairs={{0,8},{4,12},{8,0},{12,4},{1,9},{5,13},{9,1},{13,5},{2,10},{6,14},... | collective-permute-start | bytes 13832 | tf_op jit(solution)/shard_map/ppermute | solution.py:13
  6.8 2.8 %collective-permute-start.5 = (bf16[2,768,64]{1,2,0:T(8,128)(2,1)}, bf16[2,768,64]{1,2,0:T(8,128)(2,1)S(1)}, u32[]{:S(2)}, u32[]{:S(2)}) collective-permute-start(bf16[2,768,64]{1,2,0:T(8,128)(2,1)} %param.8), channel_id=1, source_target_pairs={{0,12},{4,0},{8,4},{12,8},{1,13},{5,1},{9,5},{13,9},{2,14},{6,2},{... | collective-permute-start | bytes 589832 | tf_op jit(solution)/shard_map/ppermute | solution.py:13
  9.6 2.0 %collective-permute-start.3 = (bf16[2,768,64]{1,2,0:T(8,128)(2,1)}, bf16[2,768,64]{1,2,0:T(8,128)(2,1)S(1)}, u32[]{:S(2)}, u32[]{:S(2)}) collective-permute-start(bf16[2,768,64]{1,2,0:T(8,128)(2,1)} %param.8), channel_id=1, source_target_pairs={{0,8},{4,12},{8,0},{12,4},{1,9},{5,13},{9,1},{13,5},{2,10},{6,14},... | collective-permute-start | bytes 589832 | tf_op jit(solution)/shard_map/ppermute | solution.py:13
  11.6 1.9 %broadcast_in_dim.2 = bf16[4,2,768,64]{2,3,1,0:T(8,128)(2,1)} broadcast(bf16[2,768,64]{1,2,0:T(8,128)(2,1)} %param.8), dimensions={1,2,3} | broadcast | bytes 983040 | tf_op jit(solution)/shard_map/broadcast_in_dim | solution.py:64
  13.5 3.5 %all-to-all-start = ((bf16[4,2,768,64]{2,3,1,0:T(8,128)(2,1)}), bf16[4,2,768,64]{2,3,1,0:T(8,128)(2,1)S(1)}, u32[]{:S(2)}, u32[]{:S(2)}) async-start(bf16[4,2,768,64]{2,3,1,0:T(8,128)(2,1)} %broadcast_in_dim.2), calls=%async_computation | async-start | bytes 1572864 | tf_op jit(solution)/shard_map/all_to_all | solution.py:65
  17.1 0.1 collective-permute-start.1
  17.2 0.1 convert_multiply_fusion
  17.3 4.6 %multiply_reduce_fusion.2 = (f32[768,768]{1,0:T(8,128)S(1)}, f32[768,768]{1,0:T(8,128)S(1)}, f32[768,768]{1,0:T(8,128)S(1)}, f32[768,768]{1,0:T(8,128)S(1)}) fusion(f32[3,768]{1,0:T(4,128)S(1)} %get-tuple-element.9, f32[3,768]{1,0:T(4,128)S(1)} %get-tuple-element.11, f32[3,768]{1,0:T(4,128)S(1)} %get-tuple-element.10, f32[3,768]{1,0:T(4,128)S(1)} %get-tuple-element.8), kind=kLoop, calls=%fused_computation.2 | loop fusion | flops 18874368 | bytes 9474048 | tf_op jit(solution)/shard_map/reduce_sum | solution.py:9
  21.9 1.1 %fusion = f32[768,128]{0,1:S(1)} fusion(bf16[768,128]{0,1:T(8,128)(2,1)S(1)} %bitcast.35, f32[768,768]{1,0:T(8,128)S(1)} %get-tuple-element.7), kind=kOutput, calls=%fused_computation.9 | convolution fusion | flops 152764416 | bytes 2949120
  23.0 1.1 %fusion.3 = f32[768,128]{0,1:S(1)} fusion(bf16[768,128]{0,1:T(8,128)(2,1)S(1)} %bitcast.41, f32[768,768]{1,0:T(8,128)S(1)} %get-tuple-element.6), kind=kOutput, calls=%fused_computation.12 | convolution fusion | flops 152764416 | bytes 2949120
  24.1 4.3 %collective-permute-done.3 = bf16[2,768,64]{1,2,0:T(8,128)(2,1)S(1)} collective-permute-done((bf16[2,768,64]{1,2,0:T(8,128)(2,1)}, bf16[2,768,64]{1,2,0:T(8,128)(2,1)S(1)}, u32[]{:S(2)}, u32[]{:S(2)}) %collective-permute-start.3) | collective-permute-done | bytes 196640 | tf_op jit(solution)/shard_map/ppermute | solution.py:13
  28.4 1.1 %fusion.2 = f32[768,128]{0,1:S(1)} fusion(bf16[768,128]{0,1:T(8,128)(2,1)S(1)} %bitcast.40, f32[768,768]{1,0:T(8,128)S(1)} %get-tuple-element.5), kind=kOutput, calls=%fused_computation.11 | convolution fusion | flops 152764416 | bytes 2949120
  29.5 1.1 %fusion.1 = f32[768,128]{0,1:S(1)} fusion(bf16[768,128]{0,1:T(8,128)(2,1)S(1)} %bitcast.42, f32[768,768]{1,0:T(8,128)S(1)} %get-tuple-element.4), kind=kOutput, calls=%fused_computation.10 | convolution fusion | flops 152764416 | bytes 2949120
  30.6 0.1 fusion.5
  30.7 0.5 %convolution_bitcast_fusion = f32[64,4,64]{2,0,1:T(8,128)S(1)} fusion(bf16[4,2,768,64]{2,3,1,0:T(8,128)(2,1)S(1)} %all-to-all-done, bf16[2,768,64]{1,2,0:T(8,128)(2,1)S(1)} %fusion.5, bf16[2]{0:T(256)(128)(2,1)S(1)} %copy-done.4), kind=kOutput, calls=%fused_computation.14 | convolution fusion | flops 50724864 | bytes 1048580 | tf_op jit(solution)/shard_map/sna,ksnb->akb/dot_general | solution.py:69
  31.2 0.1 copy.9
  31.3 0.1 reshape.16
  31.4 0.1 collective-permute-start.8
  31.5 1.4 %collective-permute-start.7 = (f32[64,256]{1,0:T(8,128)S(1)}, f32[64,256]{1,0:T(8,128)S(1)}, u32[]{:S(2)}, u32[]{:S(2)}) collective-permute-start(f32[64,256]{1,0:T(8,128)S(1)} %reshape.16), channel_id=1, source_target_pairs={{0,4},{4,8},{8,12},{12,0},{1,5},{5,9},{9,13},{13,1},{2,6},{6,10},{... | collective-permute-start | bytes 196616 | tf_op jit(solution)/shard_map/ppermute | solution.py:13
  32.9 2.5 %collective-permute-start.6 = (f32[64,256]{1,0:T(8,128)S(1)}, f32[64,256]{1,0:T(8,128)S(1)}, u32[]{:S(2)}, u32[]{:S(2)}) collective-permute-start(f32[64,256]{1,0:T(8,128)S(1)} %reshape.16), channel_id=1, source_target_pairs={{0,12},{4,0},{8,4},{12,8},{1,13},{5,1},{9,5},{13,9},{2,14},{6,2},{... | collective-permute-start | bytes 196616 | tf_op jit(solution)/shard_map/ppermute | solution.py:13
  35.4 8.6 %all_gather.3 = bf16[256,2,768]{2,0,1:T(8,128)(2,1)S(1)} all-gather(bf16[64,2,768]{2,0,1:T(8,128)(2,1)S(1)} %bitcast.34), channel_id=1, replica_groups=mesh['groups'=2,'dp'=4,'task'=4] {'task'}, dimensions={0}, use_global_device_ids=true | all-gather | bytes 983040 | tf_op jit(solution)/shard_map/all_gather | solution.py:74
  44.0 0.9 %fusion.4 = bf16[2,768,64]{1,2,0:T(8,128)(2,1)} fusion(bf16[256,2,768]{2,0,1:T(8,128)(2,1)S(1)} %all_gather.3, bf16[2,768,64]{1,2,0:T(8,128)(2,1)S(1)} %copy-done.1, f32[64]{0:T(128)S(1)} %copy-done.3, bf16[256,256]{1,0:T(8,128)(2,1)S(1)} %copy-done, s32[]{:T(128)S(6)} %select_n.22), kind=kOutput, calls=%fused_computation.13 | convolution fusion | flops 50724864 | bytes 1212932 | tf_op jit(solution)/shard_map/asn,ca->snc/dot_general | solution.py:76
  44.9 0.7 %add_multiply_fusion = f32[64,256]{1,0:T(8,128)} fusion(f32[64,256]{1,0:T(8,128)S(1)} %collective-permute-done.8, f32[64,256]{1,0:T(8,128)S(1)} %collective-permute-done.7, f32[64,256]{1,0:T(8,128)S(1)} %collective-permute-done.6, f32[64,256]{1,0:T(8,128)S(1)} %reshape.16, pred[]{:T(512)S(6)} %eq.5), kind=kLoop, calls=%fused_computation.20 | loop fusion | flops 98304 | bytes 327681 | tf_op jit(solution)/shard_map/div | solution.py:78
  (23 shorter events, 0.1 us)
Async XLA Ops:
  0.6 43.3 %copy-start = (bf16[256,256]{1,0:T(8,128)(2,1)S(1)}, bf16[256,256]{1,0:T(8,128)(2,1)}, u32[]{:S(2)}) copy-start(bf16[256,256]{1,0:T(8,128)(2,1)} %param.9) | copy-start | bytes 393220
  0.6 16.5 %copy-start.2 = (bf16[3,768]{1,0:T(4,128)(2,1)S(1)}, bf16[3,768]{1,0:T(4,128)(2,1)}, u32[]{:S(2)}) copy-start(bf16[3,768]{1,0:T(4,128)(2,1)} %param.6) | copy-start | bytes 13828
  0.7 16.4 %copy-start.1 = (bf16[2,768,64]{1,2,0:T(8,128)(2,1)S(1)}, bf16[2,768,64]{1,2,0:T(8,128)(2,1)}, u32[]{:S(2)}) copy-start(bf16[2,768,64]{1,2,0:T(8,128)(2,1)} %param.8) | copy-start | bytes 589828
  0.7 16.4 %copy-start.5 = (f32[3]{0:T(128)S(1)}, f32[3]{0:T(128)}, u32[]{:S(2)}) copy-start(f32[3]{0:T(128)} %param.7) | copy-start | bytes 40
  0.7 16.4 %collective-permute-start.4 = (bf16[3,768]{1,0:T(4,128)(2,1)}, bf16[3,768]{1,0:T(4,128)(2,1)S(1)}, u32[]{:S(2)}, u32[]{:S(2)}) collective-permute-start(bf16[3,768]{1,0:T(4,128)(2,1)} %param.6), channel_id=1, source_target_pairs={{0,12},{4,0},{8,4},{12,8},{1,13},{5,1},{9,5},{13,9},{2,14},{6,2},{... | collective-permute-start | bytes 13832 | tf_op jit(solution)/shard_map/ppermute | solution.py:13
  5.8 11.4 %collective-permute-start = (bf16[3,768]{1,0:T(4,128)(2,1)}, bf16[3,768]{1,0:T(4,128)(2,1)S(1)}, u32[]{:S(2)}, u32[]{:S(2)}) collective-permute-start(bf16[3,768]{1,0:T(4,128)(2,1)} %param.6), channel_id=1, source_target_pairs={{0,4},{4,8},{8,12},{12,0},{1,5},{5,9},{9,13},{13,1},{2,6},{6,10},{... | collective-permute-start | bytes 13832 | tf_op jit(solution)/shard_map/ppermute | solution.py:13
  5.8 11.4 %collective-permute-start.2 = (bf16[3,768]{1,0:T(4,128)(2,1)}, bf16[3,768]{1,0:T(4,128)(2,1)S(1)}, u32[]{:S(2)}, u32[]{:S(2)}) collective-permute-start(bf16[3,768]{1,0:T(4,128)(2,1)} %param.6), channel_id=1, source_target_pairs={{0,8},{4,12},{8,0},{12,4},{1,9},{5,13},{9,1},{13,5},{2,10},{6,14},... | collective-permute-start | bytes 13832 | tf_op jit(solution)/shard_map/ppermute | solution.py:13
  6.8 16.2 %collective-permute-start.5 = (bf16[2,768,64]{1,2,0:T(8,128)(2,1)}, bf16[2,768,64]{1,2,0:T(8,128)(2,1)S(1)}, u32[]{:S(2)}, u32[]{:S(2)}) collective-permute-start(bf16[2,768,64]{1,2,0:T(8,128)(2,1)} %param.8), channel_id=1, source_target_pairs={{0,12},{4,0},{8,4},{12,8},{1,13},{5,1},{9,5},{13,9},{2,14},{6,2},{... | collective-permute-start | bytes 589832 | tf_op jit(solution)/shard_map/ppermute | solution.py:13
  9.6 18.8 %collective-permute-start.3 = (bf16[2,768,64]{1,2,0:T(8,128)(2,1)}, bf16[2,768,64]{1,2,0:T(8,128)(2,1)S(1)}, u32[]{:S(2)}, u32[]{:S(2)}) collective-permute-start(bf16[2,768,64]{1,2,0:T(8,128)(2,1)} %param.8), channel_id=1, source_target_pairs={{0,8},{4,12},{8,0},{12,4},{1,9},{5,13},{9,1},{13,5},{2,10},{6,14},... | collective-permute-start | bytes 589832 | tf_op jit(solution)/shard_map/ppermute | solution.py:13
  13.5 17.1 %all-to-all-start = ((bf16[4,2,768,64]{2,3,1,0:T(8,128)(2,1)}), bf16[4,2,768,64]{2,3,1,0:T(8,128)(2,1)S(1)}, u32[]{:S(2)}, u32[]{:S(2)}) async-start(bf16[4,2,768,64]{2,3,1,0:T(8,128)(2,1)} %broadcast_in_dim.2), calls=%async_computation | async-start | bytes 1572864 | tf_op jit(solution)/shard_map/all_to_all | solution.py:65
  17.1 12.4 %collective-permute-start.1 = (bf16[2,768,64]{1,2,0:T(8,128)(2,1)S(1)}, bf16[2,768,64]{1,2,0:T(8,128)(2,1)S(1)}, u32[]{:S(2)}, u32[]{:S(2)}) collective-permute-start(bf16[2,768,64]{1,2,0:T(8,128)(2,1)S(1)} %copy-done.1), channel_id=1, source_target_pairs={{0,4},{4,8},{8,12},{12,0},{1,5},{5,9},{9,13},{13,1},{2,6},{6,10},{... | collective-permute-start | bytes 589832 | tf_op jit(solution)/shard_map/ppermute | solution.py:13
  29.5 1.2 %copy-start.4 = (bf16[2]{0:T(256)(128)(2,1)S(1)}, bf16[2]{0:T(256)(128)(2,1)}, u32[]{:S(2)}) copy-start(bf16[2]{0:T(256)(128)(2,1)} %constant.38.clone) | copy-start | bytes 16
  30.6 13.4 %copy-start.3 = (f32[64]{0:T(128)S(1)}, f32[64]{0:T(128)}, u32[]{:S(2)}) copy-start(f32[64]{0:T(128)} %param.10) | copy-start | bytes 772
  31.4 13.5 %collective-permute-start.8 = (f32[64,256]{1,0:T(8,128)S(1)}, f32[64,256]{1,0:T(8,128)S(1)}, u32[]{:S(2)}, u32[]{:S(2)}) collective-permute-start(f32[64,256]{1,0:T(8,128)S(1)} %reshape.16), channel_id=1, source_target_pairs={{0,8},{4,12},{8,0},{12,4},{1,9},{5,13},{9,1},{13,5},{2,10},{6,14},... | collective-permute-start | bytes 196616 | tf_op jit(solution)/shard_map/ppermute | solution.py:13
  31.5 13.4 %collective-permute-start.7 = (f32[64,256]{1,0:T(8,128)S(1)}, f32[64,256]{1,0:T(8,128)S(1)}, u32[]{:S(2)}, u32[]{:S(2)}) collective-permute-start(f32[64,256]{1,0:T(8,128)S(1)} %reshape.16), channel_id=1, source_target_pairs={{0,4},{4,8},{8,12},{12,0},{1,5},{5,9},{9,13},{13,1},{2,6},{6,10},{... | collective-permute-start | bytes 196616 | tf_op jit(solution)/shard_map/ppermute | solution.py:13
  32.9 12.0 %collective-permute-start.6 = (f32[64,256]{1,0:T(8,128)S(1)}, f32[64,256]{1,0:T(8,128)S(1)}, u32[]{:S(2)}, u32[]{:S(2)}) collective-permute-start(f32[64,256]{1,0:T(8,128)S(1)} %reshape.16), channel_id=1, source_target_pairs={{0,12},{4,0},{8,4},{12,8},{1,13},{5,1},{9,5},{13,9},{2,14},{6,2},{... | collective-permute-start | bytes 196616 | tf_op jit(solution)/shard_map/ppermute | solution.py:13

commit v16 on v12

--- a/solution.py
+++ b/solution.py
@@ -72,9 +72,11 @@
     ).reshape(local_tasks, n_task * local_tasks)
     total = sum_over(partial_grad, "dp", n_dp)
     gather_input = lax.optimization_barrier((images, task_blocks))[0]
-    whole_images = lax.all_gather(jnp.transpose(gather_input, (2, 0, 1)), "task", axis=0, tiled=True)
+    image_copies = jnp.broadcast_to(gather_input[None], (n_task,) + images.shape)
+    image_blocks = lax.all_to_all(image_copies, "task", 0, 0, tiled=True)
     own_rows = lax.dynamic_slice_in_dim(mixing, task_start, local_tasks, 0)
-    mixed = jnp.einsum("asn,ca->snc", whole_images, own_rows, preferred_element_type=jnp.float32)
+    own_rows = own_rows.reshape(local_tasks, n_task, local_tasks)
+    mixed = jnp.einsum("ksna,cka->snc", image_blocks, own_rows, preferred_element_type=jnp.float32)
     product = (mixed + noise[None, None, :] * vectors.astype(jnp.float32)).astype(jnp.bfloat16)
     gradient = total / (2.0 * n_rows * n_dp)
     return (product, gradient)

time: 43.3 us -> 46.5 us (1.074)
  blocking collectives: 7.45 us -> 0 us
  waiting for transfers between devices: 2.37 us -> 8.36 us
  starting transfers between devices: 18.4 us -> 21.9 us
  local copies, waits for them, and re-layouts: 2.16 us -> 3.2 us
    all_gather x1 -> x0, blocking collectives: 7.45 us -> none  [per_device(): lax.all_gather(jnp.transpose(gather_input, (2, 0, 1)), 'task', axis=0, ti...]
    ppermute x9, waiting for transfers between devices: 0.02 us -> 5.47 us  [shift(): return lax.ppermute(x, axis, [(i, (i + k) % n) for i in range(n)])]
    all_to_all x0 -> x1, starting transfers between devices: none -> 3.49 us  [per_device(): image_blocks = lax.all_to_all(image_copies, 'task', 0, 0, tiled=True)]
    broadcast_in_dim x0 -> x1, local copies, waits for them, and re-layouts: none -> 0.94 us  [per_device(): jnp.broadcast_to(gather_input[None], (n_task,) + images.shape)]
    all_to_all x0 -> x1, waiting for transfers between devices: none -> 0.54 us  [per_device(): image_blocks = lax.all_to_all(image_copies, 'task', 0, 0, tiled=True)]
  transfers between devices with their start and end apart: 10 -> 11, of which waited for: 1 -> 5; matrix products, arithmetic and copies ran while one was open for 29% -> 29% of each run, Pallas kernels for 0% -> 0%
where the time goes in v16:
time: 46.5 us; the launch traced here: 46.2 us
  starting transfers between devices  21.9 us (47%)
  waiting for transfers between devices  8.36 us (18%)
  other arithmetic  6.12 us (13%)
  matrix products  5.87 us (13%)
  local copies, waits for them, and re-layouts  3.2 us (7%)
  between operations  0.77 us (2%)
    ppermute x9, starting transfers between devices, shift(): return lax.ppermute(x, axis, [(i, (i + k) % n) for i in range(n)])  14.9 us
    ppermute x9, waiting for transfers between devices, shift(): return lax.ppermute(x, axis, [(i, (i + k) % n) for i in range(n)])  5.47 us
    reduce_sum x1, other arithmetic, kernel_tile(): return jnp.exp(0.1 - jnp.sqrt(jnp.sum(diff * diff, axis=0) + 0.01))  4.65 us
    unnamed x4, matrix products  4.38 us
    all_to_all x1, starting transfers between devices, per_device(): task_blocks = lax.all_to_all(copies, 'task', 0, 0, tiled=True)  3.49 us
    all_to_all x1, starting transfers between devices, per_device(): image_blocks = lax.all_to_all(image_copies, 'task', 0, 0, tiled=True)  3.49 us
    all_to_all x1, waiting for transfers between devices, per_device(): task_blocks = lax.all_to_all(copies, 'task', 0, 0, tiled=True)  2.34 us
    broadcast_in_dim x1, local copies, waits for them, and re-layouts, per_device(): copies = jnp.broadcast_to(task_input[None], (n_task,) + vectors.shape)  1.89 us
  transfers between devices with their start and end apart: 11, of which 5 were waited for; matrix products, arithmetic and copies ran while one was open for 29% of the time, Pallas kernels for 0%

profile of v16, /device:TPU:0, one launch (start us, length us, event | category | flops | bytes accessed | tf_op | source)
XLA Modules:
  0.0 46.2 jit_solution(13351767963564277813)
XLA Ops:
  0.7 3.1 %collective-permute-start = (bf16[3,768]{1,0:T(4,128)(2,1)}, bf16[3,768]{1,0:T(4,128)(2,1)S(1)}, u32[]{:S(2)}, u32[]{:S(2)}) collective-permute-start(bf16[3,768]{1,0:T(4,128)(2,1)} %param.6), channel_id=1, source_target_pairs={{0,4},{4,8},{8,12},{12,0},{1,5},{5,9},{9,13},{13,1},{2,6},{6,10},{... | collective-permute-start | bytes 13832 | tf_op jit(solution)/shard_map/ppermute | solution.py:13
  3.7 2.6 %collective-permute-start.2 = (bf16[3,768]{1,0:T(4,128)(2,1)}, bf16[3,768]{1,0:T(4,128)(2,1)S(1)}, u32[]{:S(2)}, u32[]{:S(2)}) collective-permute-start(bf16[3,768]{1,0:T(4,128)(2,1)} %param.6), channel_id=1, source_target_pairs={{0,8},{4,12},{8,0},{12,4},{1,9},{5,13},{9,1},{13,5},{2,10},{6,14},... | collective-permute-start | bytes 13832 | tf_op jit(solution)/shard_map/ppermute | solution.py:13
  6.3 1.3 %collective-permute-start.4 = (bf16[3,768]{1,0:T(4,128)(2,1)}, bf16[3,768]{1,0:T(4,128)(2,1)S(1)}, u32[]{:S(2)}, u32[]{:S(2)}) collective-permute-start(bf16[3,768]{1,0:T(4,128)(2,1)} %param.6), channel_id=1, source_target_pairs={{0,12},{4,0},{8,4},{12,8},{1,13},{5,1},{9,5},{13,9},{2,14},{6,2},{... | collective-permute-start | bytes 13832 | tf_op jit(solution)/shard_map/ppermute | solution.py:13
  7.7 0.7 %collective-permute-start.1 = (bf16[2,768,64]{1,2,0:T(8,128)(2,1)}, bf16[2,768,64]{1,2,0:T(8,128)(2,1)S(1)}, u32[]{:S(2)}, u32[]{:S(2)}) collective-permute-start(bf16[2,768,64]{1,2,0:T(8,128)(2,1)} %param.8), channel_id=1, source_target_pairs={{0,4},{4,8},{8,12},{12,0},{1,5},{5,9},{9,13},{13,1},{2,6},{6,10},{... | collective-permute-start | bytes 589832 | tf_op jit(solution)/shard_map/ppermute | solution.py:13
  8.7 0.7 %broadcast_divide_fusion = f32[3]{0:T(128)S(1)} fusion(f32[3]{0:T(128)} %param.7), kind=kLoop, calls=%fused_computation.28 | loop fusion | flops 3 | bytes 24 | tf_op jit(solution)/shard_map/div | solution.py:37
  9.3 2.8 %collective-permute-start.5 = (bf16[2,768,64]{1,2,0:T(8,128)(2,1)}, bf16[2,768,64]{1,2,0:T(8,128)(2,1)S(1)}, u32[]{:S(2)}, u32[]{:S(2)}) collective-permute-start(bf16[2,768,64]{1,2,0:T(8,128)(2,1)} %param.8), channel_id=1, source_target_pairs={{0,12},{4,0},{8,4},{12,8},{1,13},{5,1},{9,5},{13,9},{2,14},{6,2},{... | collective-permute-start | bytes 589832 | tf_op jit(solution)/shard_map/ppermute | solution.py:13
  12.2 1.9 %broadcast_in_dim.4 = bf16[4,2,768,64]{2,3,1,0:T(8,128)(2,1)} broadcast(bf16[2,768,64]{1,2,0:T(8,128)(2,1)} %param.8), dimensions={1,2,3} | broadcast | bytes 983040 | tf_op jit(solution)/shard_map/broadcast_in_dim | solution.py:65
  14.1 3.5 %all-to-all-start = ((bf16[4,2,768,64]{2,3,1,0:T(8,128)(2,1)}), bf16[4,2,768,64]{2,3,1,0:T(8,128)(2,1)S(1)}, u32[]{:S(2)}, u32[]{:S(2)}) async-start(bf16[4,2,768,64]{2,3,1,0:T(8,128)(2,1)} %broadcast_in_dim.4), calls=%async_computation | async-start | bytes 1572864 | tf_op jit(solution)/shard_map/all_to_all | solution.py:66
  17.7 4.7 %multiply_reduce_fusion.2 = (f32[768,768]{1,0:T(8,128)S(1)}, f32[768,768]{1,0:T(8,128)S(1)}, f32[768,768]{1,0:T(8,128)S(1)}, f32[768,768]{1,0:T(8,128)S(1)}) fusion(f32[3,768]{1,0:T(4,128)S(1)} %get-tuple-element.11, f32[3,768]{1,0:T(4,128)S(1)} %get-tuple-element.13, f32[3,768]{1,0:T(4,128)S(1)} %get-tuple-element.12, f32[3,768]{1,0:T(4,128)S(1)} %get-tuple-element.10), kind=kLoop, calls=%fused_computation.2 | loop fusion | flops 18874368 | bytes 9474048 | tf_op jit(solution)/shard_map/reduce_sum | solution.py:9
  22.3 1.1 %fusion.1 = f32[768,128]{0,1:S(1)} fusion(bf16[768,128]{0,1:T(8,128)(2,1)S(1)} %bitcast.37, f32[768,768]{1,0:T(8,128)S(1)} %get-tuple-element.9), kind=kOutput, calls=%fused_computation.10 | convolution fusion | flops 152764416 | bytes 2949120
  23.4 1.1 %fusion.2 = f32[768,128]{0,1:S(1)} fusion(bf16[768,128]{0,1:T(8,128)(2,1)S(1)} %bitcast.45, f32[768,768]{1,0:T(8,128)S(1)} %get-tuple-element.6), kind=kOutput, calls=%fused_computation.11 | convolution fusion | flops 152764416 | bytes 2949120
  24.5 1.1 %fusion.3 = f32[768,128]{0,1:S(1)} fusion(bf16[768,128]{0,1:T(8,128)(2,1)S(1)} %bitcast.43, f32[768,768]{1,0:T(8,128)S(1)} %get-tuple-element.7), kind=kOutput, calls=%fused_computation.12 | convolution fusion | flops 152764416 | bytes 2949120
  25.6 1.1 %fusion.4 = f32[768,128]{0,1:S(1)} fusion(bf16[768,128]{0,1:T(8,128)(2,1)S(1)} %bitcast.44, f32[768,768]{1,0:T(8,128)S(1)} %get-tuple-element.8), kind=kOutput, calls=%fused_computation.13 | convolution fusion | flops 152764416 | bytes 2949120
  26.8 2.3 %all-to-all-done = bf16[4,2,768,64]{2,3,1,0:T(8,128)(2,1)S(1)} async-done(((bf16[4,2,768,64]{2,3,1,0:T(8,128)(2,1)}), bf16[4,2,768,64]{2,3,1,0:T(8,128)(2,1)S(1)}, u32[]{:S(2)}, u32[]{:S(2)}) %all-to-all-start) | async-done | bytes 786464 | tf_op jit(solution)/shard_map/all_to_all | solution.py:66
  29.2 0.9 %broadcast_in_dim.5 = bf16[4,2,768,64]{2,3,1,0:T(8,128)(2,1)} broadcast(bf16[2,768,64]{1,2,0:T(8,128)(2,1)S(1)} %fusion.6), dimensions={1,2,3} | broadcast | bytes 983040 | tf_op jit(solution)/shard_map/broadcast_in_dim | solution.py:75
  30.1 3.5 %all-to-all-start.1 = ((bf16[4,2,768,64]{2,3,1,0:T(8,128)(2,1)}), bf16[4,2,768,64]{2,3,1,0:T(8,128)(2,1)S(1)}, u32[]{:S(2)}, u32[]{:S(2)}) async-start(bf16[4,2,768,64]{2,3,1,0:T(8,128)(2,1)} %broadcast_in_dim.5), calls=%async_computation.1 | async-start | bytes 1572864 | tf_op jit(solution)/shard_map/all_to_all | solution.py:76
  34.4 1.3 %collective-permute-start.6 = (f32[64,256]{1,0:T(8,128)S(1)}, f32[64,256]{1,0:T(8,128)S(1)}, u32[]{:S(2)}, u32[]{:S(2)}) collective-permute-start(f32[64,256]{1,0:T(8,128)S(1)} %reshape.21), channel_id=1, source_target_pairs={{0,12},{4,0},{8,4},{12,8},{1,13},{5,1},{9,5},{13,9},{2,14},{6,2},{... | collective-permute-start | bytes 196616 | tf_op jit(solution)/shard_map/ppermute | solution.py:13
  35.7 0.8 %collective-permute-start.7 = (f32[64,256]{1,0:T(8,128)S(1)}, f32[64,256]{1,0:T(8,128)S(1)}, u32[]{:S(2)}, u32[]{:S(2)}) collective-permute-start(f32[64,256]{1,0:T(8,128)S(1)} %reshape.21), channel_id=1, source_target_pairs={{0,4},{4,8},{8,12},{12,0},{1,5},{5,9},{9,13},{13,1},{2,6},{6,10},{... | collective-permute-start | bytes 196616 | tf_op jit(solution)/shard_map/ppermute | solution.py:13
  36.5 2.0 %collective-permute-start.8 = (f32[64,256]{1,0:T(8,128)S(1)}, f32[64,256]{1,0:T(8,128)S(1)}, u32[]{:S(2)}, u32[]{:S(2)}) collective-permute-start(f32[64,256]{1,0:T(8,128)S(1)} %reshape.21), channel_id=1, source_target_pairs={{0,8},{4,12},{8,0},{12,4},{1,9},{5,13},{9,1},{13,5},{2,10},{6,14},... | collective-permute-start | bytes 196616 | tf_op jit(solution)/shard_map/ppermute | solution.py:13
  38.9 3.5 %collective-permute-done.7 = f32[64,256]{1,0:T(8,128)S(1)} collective-permute-done((f32[64,256]{1,0:T(8,128)S(1)}, f32[64,256]{1,0:T(8,128)S(1)}, u32[]{:S(2)}, u32[]{:S(2)}) %collective-permute-start.7) | collective-permute-done | bytes 65568 | tf_op jit(solution)/shard_map/ppermute | solution.py:13
  42.4 1.7 %collective-permute-done.8 = f32[64,256]{1,0:T(8,128)S(1)} collective-permute-done((f32[64,256]{1,0:T(8,128)S(1)}, f32[64,256]{1,0:T(8,128)S(1)}, u32[]{:S(2)}, u32[]{:S(2)}) %collective-permute-start.8) | collective-permute-done | bytes 65568 | tf_op jit(solution)/shard_map/ppermute | solution.py:13
  44.1 0.6 %add_multiply_fusion = f32[64,256]{1,0:T(8,128)} fusion(f32[64,256]{1,0:T(8,128)S(1)} %collective-permute-done.8, f32[64,256]{1,0:T(8,128)S(1)} %collective-permute-done.7, f32[64,256]{1,0:T(8,128)S(1)} %collective-permute-done.6, f32[64,256]{1,0:T(8,128)S(1)} %reshape.21, pred[]{:T(512)S(6)} %eq.5), kind=kLoop, calls=%fused_computation.22 | loop fusion | flops 98304 | bytes 327681 | tf_op jit(solution)/shard_map/div | solution.py:81
  44.7 0.5 %all-to-all-done.1 = bf16[4,2,768,64]{2,3,1,0:T(8,128)(2,1)S(1)} async-done(((bf16[4,2,768,64]{2,3,1,0:T(8,128)(2,1)}), bf16[4,2,768,64]{2,3,1,0:T(8,128)(2,1)S(1)}, u32[]{:S(2)}, u32[]{:S(2)}) %all-to-all-start.1) | async-done | bytes 786464 | tf_op jit(solution)/shard_map/all_to_all | solution.py:76
  45.3 1.0 %fusion.5 = bf16[2,768,64]{1,2,0:T(8,128)(2,1)} fusion(bf16[4,2,768,64]{2,3,1,0:T(8,128)(2,1)S(1)} %all-to-all-done.1, bf16[2,768,64]{1,2,0:T(8,128)(2,1)S(1)} %copy-done.1, f32[64]{0:T(128)S(1)} %copy-done.3, bf16[64,4,64,1]{2,1,0,3:T(4,128)(2,1)S(1)} %bitcast.42), kind=kOutput, calls=%fused_computation.14 | convolution fusion | flops 50724864 | bytes 1212672 | tf_op jit(solution)/shard_map/ksna,cka->snc/dot_general | solution.py:79
  (25 shorter events, 1.7 us)
Async XLA Ops:
  0.6 37.9 %copy-start = (bf16[256,256]{1,0:T(8,128)(2,1)S(1)}, bf16[256,256]{1,0:T(8,128)(2,1)}, u32[]{:S(2)}) copy-start(bf16[256,256]{1,0:T(8,128)(2,1)} %param.9) | copy-start | bytes 393220
  0.6 16.9 %copy-start.2 = (bf16[3,768]{1,0:T(4,128)(2,1)S(1)}, bf16[3,768]{1,0:T(4,128)(2,1)}, u32[]{:S(2)}) copy-start(bf16[3,768]{1,0:T(4,128)(2,1)} %param.6) | copy-start | bytes 13828
  0.7 8.7 %collective-permute-start = (bf16[3,768]{1,0:T(4,128)(2,1)}, bf16[3,768]{1,0:T(4,128)(2,1)S(1)}, u32[]{:S(2)}, u32[]{:S(2)}) collective-permute-start(bf16[3,768]{1,0:T(4,128)(2,1)} %param.6), channel_id=1, source_target_pairs={{0,4},{4,8},{8,12},{12,0},{1,5},{5,9},{9,13},{13,1},{2,6},{6,10},{... | collective-permute-start | bytes 13832 | tf_op jit(solution)/shard_map/ppermute | solution.py:13
  3.7 8.4 %collective-permute-start.2 = (bf16[3,768]{1,0:T(4,128)(2,1)}, bf16[3,768]{1,0:T(4,128)(2,1)S(1)}, u32[]{:S(2)}, u32[]{:S(2)}) collective-permute-start(bf16[3,768]{1,0:T(4,128)(2,1)} %param.6), channel_id=1, source_target_pairs={{0,8},{4,12},{8,0},{12,4},{1,9},{5,13},{9,1},{13,5},{2,10},{6,14},... | collective-permute-start | bytes 13832 | tf_op jit(solution)/shard_map/ppermute | solution.py:13
  6.3 5.8 %collective-permute-start.4 = (bf16[3,768]{1,0:T(4,128)(2,1)}, bf16[3,768]{1,0:T(4,128)(2,1)S(1)}, u32[]{:S(2)}, u32[]{:S(2)}) collective-permute-start(bf16[3,768]{1,0:T(4,128)(2,1)} %param.6), channel_id=1, source_target_pairs={{0,12},{4,0},{8,4},{12,8},{1,13},{5,1},{9,5},{13,9},{2,14},{6,2},{... | collective-permute-start | bytes 13832 | tf_op jit(solution)/shard_map/ppermute | solution.py:13
  7.7 15.8 %collective-permute-start.1 = (bf16[2,768,64]{1,2,0:T(8,128)(2,1)}, bf16[2,768,64]{1,2,0:T(8,128)(2,1)S(1)}, u32[]{:S(2)}, u32[]{:S(2)}) collective-permute-start(bf16[2,768,64]{1,2,0:T(8,128)(2,1)} %param.8), channel_id=1, source_target_pairs={{0,4},{4,8},{8,12},{12,0},{1,5},{5,9},{9,13},{13,1},{2,6},{6,10},{... | collective-permute-start | bytes 589832 | tf_op jit(solution)/shard_map/ppermute | solution.py:13
  8.3 16.2 %collective-permute-start.3 = (bf16[2,768,64]{1,2,0:T(8,128)(2,1)}, bf16[2,768,64]{1,2,0:T(8,128)(2,1)S(1)}, u32[]{:S(2)}, u32[]{:S(2)}) collective-permute-start(bf16[2,768,64]{1,2,0:T(8,128)(2,1)} %param.8), channel_id=1, source_target_pairs={{0,8},{4,12},{8,0},{12,4},{1,9},{5,13},{9,1},{13,5},{2,10},{6,14},... | collective-permute-start | bytes 589832 | tf_op jit(solution)/shard_map/ppermute | solution.py:13
  9.3 16.3 %collective-permute-start.5 = (bf16[2,768,64]{1,2,0:T(8,128)(2,1)}, bf16[2,768,64]{1,2,0:T(8,128)(2,1)S(1)}, u32[]{:S(2)}, u32[]{:S(2)}) collective-permute-start(bf16[2,768,64]{1,2,0:T(8,128)(2,1)} %param.8), channel_id=1, source_target_pairs={{0,12},{4,0},{8,4},{12,8},{1,13},{5,1},{9,5},{13,9},{2,14},{6,2},{... | collective-permute-start | bytes 589832 | tf_op jit(solution)/shard_map/ppermute | solution.py:13
  14.1 15.1 %all-to-all-start = ((bf16[4,2,768,64]{2,3,1,0:T(8,128)(2,1)}), bf16[4,2,768,64]{2,3,1,0:T(8,128)(2,1)S(1)}, u32[]{:S(2)}, u32[]{:S(2)}) async-start(bf16[4,2,768,64]{2,3,1,0:T(8,128)(2,1)} %broadcast_in_dim.4), calls=%async_computation | async-start | bytes 1572864 | tf_op jit(solution)/shard_map/all_to_all | solution.py:66
  17.7 4.7 %copy-start.1 = (bf16[2,768,64]{1,2,0:T(8,128)(2,1)S(1)}, bf16[2,768,64]{1,2,0:T(8,128)(2,1)}, u32[]{:S(2)}) copy-start(bf16[2,768,64]{1,2,0:T(8,128)(2,1)} %param.8) | copy-start | bytes 589828
  26.7 6.9 %copy-start.4 = (bf16[2]{0:T(256)(128)(2,1)S(1)}, bf16[2]{0:T(256)(128)(2,1)}, u32[]{:S(2)}) copy-start(bf16[2]{0:T(256)(128)(2,1)} %constant.38.clone) | copy-start | bytes 16
  26.8 18.4 %copy-start.3 = (f32[64]{0:T(128)S(1)}, f32[64]{0:T(128)}, u32[]{:S(2)}) copy-start(f32[64]{0:T(128)} %param.10) | copy-start | bytes 772
  30.1 15.1 %all-to-all-start.1 = ((bf16[4,2,768,64]{2,3,1,0:T(8,128)(2,1)}), bf16[4,2,768,64]{2,3,1,0:T(8,128)(2,1)S(1)}, u32[]{:S(2)}, u32[]{:S(2)}) async-start(bf16[4,2,768,64]{2,3,1,0:T(8,128)(2,1)} %broadcast_in_dim.5), calls=%async_computation.1 | async-start | bytes 1572864 | tf_op jit(solution)/shard_map/all_to_all | solution.py:76
  34.4 4.5 %collective-permute-start.6 = (f32[64,256]{1,0:T(8,128)S(1)}, f32[64,256]{1,0:T(8,128)S(1)}, u32[]{:S(2)}, u32[]{:S(2)}) collective-permute-start(f32[64,256]{1,0:T(8,128)S(1)} %reshape.21), channel_id=1, source_target_pairs={{0,12},{4,0},{8,4},{12,8},{1,13},{5,1},{9,5},{13,9},{2,14},{6,2},{... | collective-permute-start | bytes 196616 | tf_op jit(solution)/shard_map/ppermute | solution.py:13
  35.7 6.7 %collective-permute-start.7 = (f32[64,256]{1,0:T(8,128)S(1)}, f32[64,256]{1,0:T(8,128)S(1)}, u32[]{:S(2)}, u32[]{:S(2)}) collective-permute-start(f32[64,256]{1,0:T(8,128)S(1)} %reshape.21), channel_id=1, source_target_pairs={{0,4},{4,8},{8,12},{12,0},{1,5},{5,9},{9,13},{13,1},{2,6},{6,10},{... | collective-permute-start | bytes 196616 | tf_op jit(solution)/shard_map/ppermute | solution.py:13
  36.5 7.6 %collective-permute-start.8 = (f32[64,256]{1,0:T(8,128)S(1)}, f32[64,256]{1,0:T(8,128)S(1)}, u32[]{:S(2)}, u32[]{:S(2)}) collective-permute-start(f32[64,256]{1,0:T(8,128)S(1)} %reshape.21), channel_id=1, source_target_pairs={{0,8},{4,12},{8,0},{12,4},{1,9},{5,13},{9,1},{13,5},{2,10},{6,14},... | collective-permute-start | bytes 196616 | tf_op jit(solution)/shard_map/ppermute | solution.py:13

commit v17 on v15

--- a/solution.py
+++ b/solution.py
@@ -46,6 +46,7 @@
     if n_dp <= 4:
         moved = [shift(vectors, "dp", k, n_dp) for k in range(1, n_dp)]
         peer_coords = [shift(coords, "dp", k, n_dp) for k in range(1, n_dp)]
+        task_input = lax.optimization_barrier((vectors, peer_coords[0]))[0]
         summed = block(coords, vectors)
         for k in range(1, n_dp):
             summed = summed + block(peer_coords[k - 1], moved[k - 1])

time: 45.8 us -> 45.8 us (level)
  other arithmetic: 5.47 us -> 6.12 us
  waiting for transfers between devices: 4.29 us -> 3.7 us
    div x1, other arithmetic: 0.01 us -> 0.66 us  [per_device(): inverse = 1.0 / lengthscales]
    ppermute x9, waiting for transfers between devices: 4.28 us -> 3.7 us  [shift(): return lax.ppermute(x, axis, [(i, (i + k) % n) for i in range(n)])]
  transfers between devices with their start and end apart: 10 -> 10, of which waited for: 1 -> 1; matrix products, arithmetic and copies ran while one was open for 26% -> 28% of each run, Pallas kernels for 0% -> 0%
where the time goes in v17:
time: 45.8 us; the launch traced here: 45.6 us
  starting transfers between devices  18.4 us (40%)
  blocking collectives  8.55 us (19%)
  other arithmetic  6.12 us (13%)
  matrix products  5.84 us (13%)
  waiting for transfers between devices  3.7 us (8%)
  local copies, waits for them, and re-layouts  2.17 us (5%)
  between operations  0.76 us (2%)
    ppermute x9, starting transfers between devices, shift(): return lax.ppermute(x, axis, [(i, (i + k) % n) for i in range(n)])  14.9 us
    all_gather x1, blocking collectives, per_device(): lax.all_gather(jnp.transpose(gather_input, (2, 0, 1)), 'task', axis=0, ti...  8.55 us
    reduce_sum x1, other arithmetic, kernel_tile(): return jnp.exp(0.1 - jnp.sqrt(jnp.sum(diff * diff, axis=0) + 0.01))  4.65 us
    unnamed x4, matrix products  4.38 us
    ppermute x9, waiting for transfers between devices, shift(): return lax.ppermute(x, axis, [(i, (i + k) % n) for i in range(n)])  3.7 us
    all_to_all x1, starting transfers between devices, per_device(): task_blocks = lax.all_to_all(copies, 'task', 0, 0, tiled=True)  3.49 us
    broadcast_in_dim x1, local copies, waits for them, and re-layouts, per_device(): copies = jnp.broadcast_to(task_input[None], (n_task,) + vectors.shape)  1.91 us
    dot_general x1, matrix products, per_device(): jnp.einsum('asn,ca->snc', whole_images, own_rows, preferred_element_type=...  0.94 us
  transfers between devices with their start and end apart: 10, of which 1 were waited for; matrix products, arithmetic and copies ran while one was open for 28% of the time, Pallas kernels for 0%

profile of v17, /device:TPU:0, one launch (start us, length us, event | category | flops | bytes accessed | tf_op | source)
XLA Modules:
  0.0 45.6 jit_solution(17653612675666074570)
XLA Ops:
  0.7 5.1 %collective-permute-start.4 = (bf16[3,768]{1,0:T(4,128)(2,1)}, bf16[3,768]{1,0:T(4,128)(2,1)S(1)}, u32[]{:S(2)}, u32[]{:S(2)}) collective-permute-start(bf16[3,768]{1,0:T(4,128)(2,1)} %param.6), channel_id=1, source_target_pairs={{0,12},{4,0},{8,4},{12,8},{1,13},{5,1},{9,5},{13,9},{2,14},{6,2},{... | collective-permute-start | bytes 13832 | tf_op jit(solution)/shard_map/ppermute | solution.py:13
  5.8 1.0 %collective-permute-start.2 = (bf16[3,768]{1,0:T(4,128)(2,1)}, bf16[3,768]{1,0:T(4,128)(2,1)S(1)}, u32[]{:S(2)}, u32[]{:S(2)}) collective-permute-start(bf16[3,768]{1,0:T(4,128)(2,1)} %param.6), channel_id=1, source_target_pairs={{0,8},{4,12},{8,0},{12,4},{1,9},{5,13},{9,1},{13,5},{2,10},{6,14},... | collective-permute-start | bytes 13832 | tf_op jit(solution)/shard_map/ppermute | solution.py:13
  6.8 2.8 %collective-permute-start.5 = (bf16[2,768,64]{1,2,0:T(8,128)(2,1)}, bf16[2,768,64]{1,2,0:T(8,128)(2,1)S(1)}, u32[]{:S(2)}, u32[]{:S(2)}) collective-permute-start(bf16[2,768,64]{1,2,0:T(8,128)(2,1)} %param.8), channel_id=1, source_target_pairs={{0,12},{4,0},{8,4},{12,8},{1,13},{5,1},{9,5},{13,9},{2,14},{6,2},{... | collective-permute-start | bytes 589832 | tf_op jit(solution)/shard_map/ppermute | solution.py:13
  9.6 2.0 %collective-permute-start.3 = (bf16[2,768,64]{1,2,0:T(8,128)(2,1)}, bf16[2,768,64]{1,2,0:T(8,128)(2,1)S(1)}, u32[]{:S(2)}, u32[]{:S(2)}) collective-permute-start(bf16[2,768,64]{1,2,0:T(8,128)(2,1)} %param.8), channel_id=1, source_target_pairs={{0,8},{4,12},{8,0},{12,4},{1,9},{5,13},{9,1},{13,5},{2,10},{6,14},... | collective-permute-start | bytes 589832 | tf_op jit(solution)/shard_map/ppermute | solution.py:13
  11.6 0.7 %broadcast_divide_fusion = f32[3]{0:T(128)S(1)} fusion(f32[3]{0:T(128)} %param.7), kind=kLoop, calls=%fused_computation.28 | loop fusion | flops 3 | bytes 24 | tf_op jit(solution)/shard_map/div | solution.py:37
  12.3 1.9 %broadcast_in_dim.2 = bf16[4,2,768,64]{2,3,1,0:T(8,128)(2,1)} broadcast(bf16[2,768,64]{1,2,0:T(8,128)(2,1)} %param.8), dimensions={1,2,3} | broadcast | bytes 983040 | tf_op jit(solution)/shard_map/broadcast_in_dim | solution.py:65
  14.2 3.5 %all-to-all-start = ((bf16[4,2,768,64]{2,3,1,0:T(8,128)(2,1)}), bf16[4,2,768,64]{2,3,1,0:T(8,128)(2,1)S(1)}, u32[]{:S(2)}, u32[]{:S(2)}) async-start(bf16[4,2,768,64]{2,3,1,0:T(8,128)(2,1)} %broadcast_in_dim.2), calls=%async_computation | async-start | bytes 1572864 | tf_op jit(solution)/shard_map/all_to_all | solution.py:66
  17.7 0.1 convert_multiply_fusion
  17.8 4.7 %multiply_reduce_fusion.2 = (f32[768,768]{1,0:T(8,128)S(1)}, f32[768,768]{1,0:T(8,128)S(1)}, f32[768,768]{1,0:T(8,128)S(1)}, f32[768,768]{1,0:T(8,128)S(1)}) fusion(f32[3,768]{1,0:T(4,128)S(1)} %get-tuple-element.11, f32[3,768]{1,0:T(4,128)S(1)} %get-tuple-element.13, f32[3,768]{1,0:T(4,128)S(1)} %get-tuple-element.12, f32[3,768]{1,0:T(4,128)S(1)} %get-tuple-element.10), kind=kLoop, calls=%fused_computation.2 | loop fusion | flops 18874368 | bytes 9474048 | tf_op jit(solution)/shard_map/reduce_sum | solution.py:9
  22.5 1.1 %fusion = f32[768,128]{0,1:S(1)} fusion(bf16[768,128]{0,1:T(8,128)(2,1)S(1)} %bitcast.35, f32[768,768]{1,0:T(8,128)S(1)} %get-tuple-element.9), kind=kOutput, calls=%fused_computation.9 | convolution fusion | flops 152764416 | bytes 2949120
  23.6 1.1 %fusion.3 = f32[768,128]{0,1:S(1)} fusion(bf16[768,128]{0,1:T(8,128)(2,1)S(1)} %bitcast.41, f32[768,768]{1,0:T(8,128)S(1)} %get-tuple-element.8), kind=kOutput, calls=%fused_computation.12 | convolution fusion | flops 152764416 | bytes 2949120
  24.7 3.7 %collective-permute-done.3 = bf16[2,768,64]{1,2,0:T(8,128)(2,1)S(1)} collective-permute-done((bf16[2,768,64]{1,2,0:T(8,128)(2,1)}, bf16[2,768,64]{1,2,0:T(8,128)(2,1)S(1)}, u32[]{:S(2)}, u32[]{:S(2)}) %collective-permute-start.3) | collective-permute-done | bytes 196640 | tf_op jit(solution)/shard_map/ppermute | solution.py:13
  28.3 1.1 %fusion.2 = f32[768,128]{0,1:S(1)} fusion(bf16[768,128]{0,1:T(8,128)(2,1)S(1)} %bitcast.40, f32[768,768]{1,0:T(8,128)S(1)} %get-tuple-element.7), kind=kOutput, calls=%fused_computation.11 | convolution fusion | flops 152764416 | bytes 2949120
  29.5 1.1 %fusion.1 = f32[768,128]{0,1:S(1)} fusion(bf16[768,128]{0,1:T(8,128)(2,1)S(1)} %bitcast.42, f32[768,768]{1,0:T(8,128)S(1)} %get-tuple-element.6), kind=kOutput, calls=%fused_computation.10 | convolution fusion | flops 152764416 | bytes 2949120
  30.6 0.1 fusion.5
  30.7 0.5 %convolution_bitcast_fusion = f32[64,4,64]{2,0,1:T(8,128)S(1)} fusion(bf16[4,2,768,64]{2,3,1,0:T(8,128)(2,1)S(1)} %all-to-all-done, bf16[2,768,64]{1,2,0:T(8,128)(2,1)S(1)} %fusion.5, bf16[2]{0:T(256)(128)(2,1)S(1)} %copy-done.4), kind=kOutput, calls=%fused_computation.14 | convolution fusion | flops 50724864 | bytes 1048580 | tf_op jit(solution)/shard_map/sna,ksnb->akb/dot_general | solution.py:70
  31.2 0.1 copy.9
  31.3 0.1 reshape.16
  31.4 0.1 collective-permute-start.8
  31.6 2.9 %collective-permute-start.7 = (f32[64,256]{1,0:T(8,128)S(1)}, f32[64,256]{1,0:T(8,128)S(1)}, u32[]{:S(2)}, u32[]{:S(2)}) collective-permute-start(f32[64,256]{1,0:T(8,128)S(1)} %reshape.16), channel_id=1, source_target_pairs={{0,4},{4,8},{8,12},{12,0},{1,5},{5,9},{9,13},{13,1},{2,6},{6,10},{... | collective-permute-start | bytes 196616 | tf_op jit(solution)/shard_map/ppermute | solution.py:13
  34.5 0.9 %collective-permute-start.6 = (f32[64,256]{1,0:T(8,128)S(1)}, f32[64,256]{1,0:T(8,128)S(1)}, u32[]{:S(2)}, u32[]{:S(2)}) collective-permute-start(f32[64,256]{1,0:T(8,128)S(1)} %reshape.16), channel_id=1, source_target_pairs={{0,12},{4,0},{8,4},{12,8},{1,13},{5,1},{9,5},{13,9},{2,14},{6,2},{... | collective-permute-start | bytes 196616 | tf_op jit(solution)/shard_map/ppermute | solution.py:13
  35.4 8.6 %all_gather.3 = bf16[256,2,768]{2,0,1:T(8,128)(2,1)S(1)} all-gather(bf16[64,2,768]{2,0,1:T(8,128)(2,1)S(1)} %bitcast.34), channel_id=1, replica_groups=mesh['groups'=2,'dp'=4,'task'=4] {'task'}, dimensions={0}, use_global_device_ids=true | all-gather | bytes 983040 | tf_op jit(solution)/shard_map/all_gather | solution.py:75
  44.0 0.9 %fusion.4 = bf16[2,768,64]{1,2,0:T(8,128)(2,1)} fusion(bf16[256,2,768]{2,0,1:T(8,128)(2,1)S(1)} %all_gather.3, bf16[2,768,64]{1,2,0:T(8,128)(2,1)S(1)} %copy-done.1, f32[64]{0:T(128)S(1)} %copy-done.3, bf16[256,256]{1,0:T(8,128)(2,1)S(1)} %copy-done, s32[]{:T(128)S(6)} %select_n.22), kind=kOutput, calls=%fused_computation.13 | convolution fusion | flops 50724864 | bytes 1212932 | tf_op jit(solution)/shard_map/asn,ca->snc/dot_general | solution.py:77
  44.9 0.7 %add_multiply_fusion = f32[64,256]{1,0:T(8,128)} fusion(f32[64,256]{1,0:T(8,128)S(1)} %collective-permute-done.8, f32[64,256]{1,0:T(8,128)S(1)} %collective-permute-done.7, f32[64,256]{1,0:T(8,128)S(1)} %collective-permute-done.6, f32[64,256]{1,0:T(8,128)S(1)} %reshape.16, pred[]{:T(512)S(6)} %eq.5), kind=kLoop, calls=%fused_computation.20 | loop fusion | flops 98304 | bytes 327681 | tf_op jit(solution)/shard_map/div | solution.py:79
  (21 shorter events, 0.1 us)
Async XLA Ops:
  0.6 43.3 %copy-start = (bf16[256,256]{1,0:T(8,128)(2,1)S(1)}, bf16[256,256]{1,0:T(8,128)(2,1)}, u32[]{:S(2)}) copy-start(bf16[256,256]{1,0:T(8,128)(2,1)} %param.9) | copy-start | bytes 393220
  0.6 17.1 %copy-start.2 = (bf16[3,768]{1,0:T(4,128)(2,1)S(1)}, bf16[3,768]{1,0:T(4,128)(2,1)}, u32[]{:S(2)}) copy-start(bf16[3,768]{1,0:T(4,128)(2,1)} %param.6) | copy-start | bytes 13828
  0.7 17.0 %collective-permute-start.4 = (bf16[3,768]{1,0:T(4,128)(2,1)}, bf16[3,768]{1,0:T(4,128)(2,1)S(1)}, u32[]{:S(2)}, u32[]{:S(2)}) collective-permute-start(bf16[3,768]{1,0:T(4,128)(2,1)} %param.6), channel_id=1, source_target_pairs={{0,12},{4,0},{8,4},{12,8},{1,13},{5,1},{9,5},{13,9},{2,14},{6,2},{... | collective-permute-start | bytes 13832 | tf_op jit(solution)/shard_map/ppermute | solution.py:13
  5.8 6.5 %collective-permute-start = (bf16[3,768]{1,0:T(4,128)(2,1)}, bf16[3,768]{1,0:T(4,128)(2,1)S(1)}, u32[]{:S(2)}, u32[]{:S(2)}) collective-permute-start(bf16[3,768]{1,0:T(4,128)(2,1)} %param.6), channel_id=1, source_target_pairs={{0,4},{4,8},{8,12},{12,0},{1,5},{5,9},{9,13},{13,1},{2,6},{6,10},{... | collective-permute-start | bytes 13832 | tf_op jit(solution)/shard_map/ppermute | solution.py:13
  5.8 11.9 %collective-permute-start.2 = (bf16[3,768]{1,0:T(4,128)(2,1)}, bf16[3,768]{1,0:T(4,128)(2,1)S(1)}, u32[]{:S(2)}, u32[]{:S(2)}) collective-permute-start(bf16[3,768]{1,0:T(4,128)(2,1)} %param.6), channel_id=1, source_target_pairs={{0,8},{4,12},{8,0},{12,4},{1,9},{5,13},{9,1},{13,5},{2,10},{6,14},... | collective-permute-start | bytes 13832 | tf_op jit(solution)/shard_map/ppermute | solution.py:13
  6.8 16.8 %collective-permute-start.5 = (bf16[2,768,64]{1,2,0:T(8,128)(2,1)}, bf16[2,768,64]{1,2,0:T(8,128)(2,1)S(1)}, u32[]{:S(2)}, u32[]{:S(2)}) collective-permute-start(bf16[2,768,64]{1,2,0:T(8,128)(2,1)} %param.8), channel_id=1, source_target_pairs={{0,12},{4,0},{8,4},{12,8},{1,13},{5,1},{9,5},{13,9},{2,14},{6,2},{... | collective-permute-start | bytes 589832 | tf_op jit(solution)/shard_map/ppermute | solution.py:13
  9.6 18.8 %collective-permute-start.3 = (bf16[2,768,64]{1,2,0:T(8,128)(2,1)}, bf16[2,768,64]{1,2,0:T(8,128)(2,1)S(1)}, u32[]{:S(2)}, u32[]{:S(2)}) collective-permute-start(bf16[2,768,64]{1,2,0:T(8,128)(2,1)} %param.8), channel_id=1, source_target_pairs={{0,8},{4,12},{8,0},{12,4},{1,9},{5,13},{9,1},{13,5},{2,10},{6,14},... | collective-permute-start | bytes 589832 | tf_op jit(solution)/shard_map/ppermute | solution.py:13
  12.3 17.2 %collective-permute-start.1 = (bf16[2,768,64]{1,2,0:T(8,128)(2,1)}, bf16[2,768,64]{1,2,0:T(8,128)(2,1)S(1)}, u32[]{:S(2)}, u32[]{:S(2)}) collective-permute-start(bf16[2,768,64]{1,2,0:T(8,128)(2,1)} %param.8), channel_id=1, source_target_pairs={{0,4},{4,8},{8,12},{12,0},{1,5},{5,9},{9,13},{13,1},{2,6},{6,10},{... | collective-permute-start | bytes 589832 | tf_op jit(solution)/shard_map/ppermute | solution.py:13
  14.2 16.5 %all-to-all-start = ((bf16[4,2,768,64]{2,3,1,0:T(8,128)(2,1)}), bf16[4,2,768,64]{2,3,1,0:T(8,128)(2,1)S(1)}, u32[]{:S(2)}, u32[]{:S(2)}) async-start(bf16[4,2,768,64]{2,3,1,0:T(8,128)(2,1)} %broadcast_in_dim.2), calls=%async_computation | async-start | bytes 1572864 | tf_op jit(solution)/shard_map/all_to_all | solution.py:66
  17.8 4.7 %copy-start.1 = (bf16[2,768,64]{1,2,0:T(8,128)(2,1)S(1)}, bf16[2,768,64]{1,2,0:T(8,128)(2,1)}, u32[]{:S(2)}) copy-start(bf16[2,768,64]{1,2,0:T(8,128)(2,1)} %param.8) | copy-start | bytes 589828
  29.4 1.2 %copy-start.4 = (bf16[2]{0:T(256)(128)(2,1)S(1)}, bf16[2]{0:T(256)(128)(2,1)}, u32[]{:S(2)}) copy-start(bf16[2]{0:T(256)(128)(2,1)} %constant.38.clone) | copy-start | bytes 16
  30.6 13.4 %copy-start.3 = (f32[64]{0:T(128)S(1)}, f32[64]{0:T(128)}, u32[]{:S(2)}) copy-start(f32[64]{0:T(128)} %param.10) | copy-start | bytes 772
  31.4 13.5 %collective-permute-start.8 = (f32[64,256]{1,0:T(8,128)S(1)}, f32[64,256]{1,0:T(8,128)S(1)}, u32[]{:S(2)}, u32[]{:S(2)}) collective-permute-start(f32[64,256]{1,0:T(8,128)S(1)} %reshape.16), channel_id=1, source_target_pairs={{0,8},{4,12},{8,0},{12,4},{1,9},{5,13},{9,1},{13,5},{2,10},{6,14},... | collective-permute-start | bytes 196616 | tf_op jit(solution)/shard_map/ppermute | solution.py:13
  31.6 13.3 %collective-permute-start.7 = (f32[64,256]{1,0:T(8,128)S(1)}, f32[64,256]{1,0:T(8,128)S(1)}, u32[]{:S(2)}, u32[]{:S(2)}) collective-permute-start(f32[64,256]{1,0:T(8,128)S(1)} %reshape.16), channel_id=1, source_target_pairs={{0,4},{4,8},{8,12},{12,0},{1,5},{5,9},{9,13},{13,1},{2,6},{6,10},{... | collective-permute-start | bytes 196616 | tf_op jit(solution)/shard_map/ppermute | solution.py:13
  34.5 10.4 %collective-permute-start.6 = (f32[64,256]{1,0:T(8,128)S(1)}, f32[64,256]{1,0:T(8,128)S(1)}, u32[]{:S(2)}, u32[]{:S(2)}) collective-permute-start(f32[64,256]{1,0:T(8,128)S(1)} %reshape.16), channel_id=1, source_target_pairs={{0,12},{4,0},{8,4},{12,8},{1,13},{5,1},{9,5},{13,9},{2,14},{6,2},{... | collective-permute-start | bytes 196616 | tf_op jit(solution)/shard_map/ppermute | solution.py:13

commit v18 on v12

--- a/solution.py
+++ b/solution.py
@@ -44,8 +44,16 @@
 
     task_input = vectors
     if n_dp <= 4:
-        moved = [shift(vectors, "dp", k, n_dp) for k in range(1, n_dp)]
-        peer_coords = [shift(coords, "dp", k, n_dp) for k in range(1, n_dp)]
+        if n_dp & (n_dp - 1) == 0:
+            def peer(x, k):
+                return lax.ppermute(x, "dp", [(i, i ^ k) for i in range(n_dp)])
+        else:
+
+            def peer(x, k):
+                return shift(x, "dp", k, n_dp)
+
+        moved = [peer(vectors, k) for k in range(1, n_dp)]
+        peer_coords = [peer(coords, k) for k in range(1, n_dp)]
         task_input = lax.optimization_barrier((vectors, peer_coords))[0]
         summed = block(coords, vectors)
         for k in range(1, n_dp):

time: 43.3 us -> 44.4 us (1.025)
  the two profiles are of different devices: /device:TPU:0 before, /device:TPU:11 now
where the time goes in v18:
time: 44.4 us; the launch traced here: 44.1 us
  starting transfers between devices  18.8 us (42%)
  blocking collectives  10 us (23%)
  other arithmetic  6.12 us (14%)
  matrix products  5.83 us (13%)
  local copies, waits for them, and re-layouts  2.16 us (5%)
  between operations  0.71 us (2%)
  waiting for transfers between devices  0.52 us (1%)
    all_gather x1, blocking collectives, per_device(): lax.all_gather(jnp.transpose(gather_input, (2, 0, 1)), 'task', axis=0, ti...  10 us
    ppermute x3, starting transfers between devices, shift(): return lax.ppermute(x, axis, [(i, (i + k) % n) for i in range(n)])  6.84 us
    ppermute x6, starting transfers between devices, peer(): return lax.ppermute(x, 'dp', [(i, i ^ k) for i in range(n_dp)])  6.21 us
    all_to_all x1, starting transfers between devices, per_device(): task_blocks = lax.all_to_all(copies, 'task', 0, 0, tiled=True)  5.71 us
    reduce_sum x1, other arithmetic, kernel_tile(): return jnp.exp(0.1 - jnp.sqrt(jnp.sum(diff * diff, axis=0) + 0.01))  4.65 us
    unnamed x4, matrix products  4.38 us
    broadcast_in_dim x1, local copies, waits for them, and re-layouts, per_device(): copies = jnp.broadcast_to(task_input[None], (n_task,) + vectors.shape)  1.9 us
    dot_general x1, matrix products, per_device(): jnp.einsum('asn,ca->snc', whole_images, own_rows, preferred_element_type=...  0.94 us
  transfers between devices with their start and end apart: 10, of which 2 were waited for; matrix products, arithmetic and copies ran while one was open for 29% of the time, Pallas kernels for 0%

profile of v18, /device:TPU:11, one launch (start us, length us, event | category | flops | bytes accessed | tf_op | source)
XLA Modules:
  0.0 44.1 jit_solution(4147056894089760654)
XLA Ops:
  0.7 0.2 collective-permute-start
  0.9 2.3 %collective-permute-start.2 = (bf16[3,768]{1,0:T(4,128)(2,1)}, bf16[3,768]{1,0:T(4,128)(2,1)S(1)}, u32[]{:S(2)}, u32[]{:S(2)}) collective-permute-start(bf16[3,768]{1,0:T(4,128)(2,1)} %param.6), channel_id=1, source_target_pairs={{0,8},{4,12},{8,0},{12,4},{1,9},{5,13},{9,1},{13,5},{2,10},{6,14},... | collective-permute-start | bytes 13832 | tf_op jit(solution)/shard_map/ppermute | solution.py:49
  3.2 0.2 collective-permute-start.4
  3.4 1.1 %collective-permute-start.1 = (bf16[2,768,64]{1,2,0:T(8,128)(2,1)}, bf16[2,768,64]{1,2,0:T(8,128)(2,1)S(1)}, u32[]{:S(2)}, u32[]{:S(2)}) collective-permute-start(bf16[2,768,64]{1,2,0:T(8,128)(2,1)} %param.8), channel_id=1, source_target_pairs={{0,4},{4,0},{8,12},{12,8},{1,5},{5,1},{9,13},{13,9},{2,6},{6,2},{1... | collective-permute-start | bytes 589832 | tf_op jit(solution)/shard_map/ppermute | solution.py:49
  4.5 2.1 %collective-permute-start.3 = (bf16[2,768,64]{1,2,0:T(8,128)(2,1)}, bf16[2,768,64]{1,2,0:T(8,128)(2,1)S(1)}, u32[]{:S(2)}, u32[]{:S(2)}) collective-permute-start(bf16[2,768,64]{1,2,0:T(8,128)(2,1)} %param.8), channel_id=1, source_target_pairs={{0,8},{4,12},{8,0},{12,4},{1,9},{5,13},{9,1},{13,5},{2,10},{6,14},... | collective-permute-start | bytes 589832 | tf_op jit(solution)/shard_map/ppermute | solution.py:49
  6.6 0.7 %broadcast_divide_fusion = f32[3]{0:T(128)S(1)} fusion(f32[3]{0:T(128)} %param.7), kind=kLoop, calls=%fused_computation.28 | loop fusion | flops 3 | bytes 24 | tf_op jit(solution)/shard_map/div | solution.py:37
  7.2 0.3 collective-permute-start.5
  7.5 1.9 %broadcast_in_dim.2 = bf16[4,2,768,64]{2,3,1,0:T(8,128)(2,1)} broadcast(bf16[2,768,64]{1,2,0:T(8,128)(2,1)} %param.8), dimensions={1,2,3} | broadcast | bytes 983040 | tf_op jit(solution)/shard_map/broadcast_in_dim | solution.py:73
  9.4 5.7 %all-to-all-start = ((bf16[4,2,768,64]{2,3,1,0:T(8,128)(2,1)}), bf16[4,2,768,64]{2,3,1,0:T(8,128)(2,1)S(1)}, u32[]{:S(2)}, u32[]{:S(2)}) async-start(bf16[4,2,768,64]{2,3,1,0:T(8,128)(2,1)} %broadcast_in_dim.2), calls=%async_computation | async-start | bytes 1572864 | tf_op jit(solution)/shard_map/all_to_all | solution.py:74
  15.2 4.7 %multiply_reduce_fusion.2 = (f32[768,768]{1,0:T(8,128)S(1)}, f32[768,768]{1,0:T(8,128)S(1)}, f32[768,768]{1,0:T(8,128)S(1)}, f32[768,768]{1,0:T(8,128)S(1)}) fusion(f32[3,768]{1,0:T(4,128)S(1)} %get-tuple-element.11, f32[3,768]{1,0:T(4,128)S(1)} %get-tuple-element.13, f32[3,768]{1,0:T(4,128)S(1)} %get-tuple-element.12, f32[3,768]{1,0:T(4,128)S(1)} %get-tuple-element.10), kind=kLoop, calls=%fused_computation.2 | loop fusion | flops 18874368 | bytes 9474048 | tf_op jit(solution)/shard_map/reduce_sum | solution.py:9
  19.9 1.1 %fusion = f32[768,128]{0,1:S(1)} fusion(bf16[768,128]{0,1:T(8,128)(2,1)S(1)} %bitcast.35, f32[768,768]{1,0:T(8,128)S(1)} %get-tuple-element.9), kind=kOutput, calls=%fused_computation.9 | convolution fusion | flops 152764416 | bytes 2949120
  21.0 1.1 %fusion.1 = f32[768,128]{0,1:S(1)} fusion(bf16[768,128]{0,1:T(8,128)(2,1)S(1)} %bitcast.41, f32[768,768]{1,0:T(8,128)S(1)} %get-tuple-element.6), kind=kOutput, calls=%fused_computation.10 | convolution fusion | flops 152764416 | bytes 2949120
  22.1 1.1 %fusion.2 = f32[768,128]{0,1:S(1)} fusion(bf16[768,128]{0,1:T(8,128)(2,1)S(1)} %bitcast.40, f32[768,768]{1,0:T(8,128)S(1)} %get-tuple-element.7), kind=kOutput, calls=%fused_computation.11 | convolution fusion | flops 152764416 | bytes 2949120
  23.3 1.1 %fusion.3 = f32[768,128]{0,1:S(1)} fusion(bf16[768,128]{0,1:T(8,128)(2,1)S(1)} %bitcast.42, f32[768,768]{1,0:T(8,128)S(1)} %get-tuple-element.8), kind=kOutput, calls=%fused_computation.12 | convolution fusion | flops 152764416 | bytes 2949120
  24.4 0.1 fusion.5
  24.5 0.4 all-to-all-done
  24.9 0.5 %convolution_bitcast_fusion = f32[64,4,64]{2,0,1:T(8,128)S(1)} fusion(bf16[4,2,768,64]{2,3,1,0:T(8,128)(2,1)S(1)} %all-to-all-done, bf16[2,768,64]{1,2,0:T(8,128)(2,1)S(1)} %fusion.5, bf16[2]{0:T(256)(128)(2,1)S(1)} %copy-done.4), kind=kOutput, calls=%fused_computation.14 | convolution fusion | flops 50724864 | bytes 1048580 | tf_op jit(solution)/shard_map/sna,ksnb->akb/dot_general | solution.py:78
  25.4 0.1 copy.9
  25.5 0.1 reshape.16
  25.7 2.0 %collective-permute-start.6 = (f32[64,256]{1,0:T(8,128)S(1)}, f32[64,256]{1,0:T(8,128)S(1)}, u32[]{:S(2)}, u32[]{:S(2)}) collective-permute-start(f32[64,256]{1,0:T(8,128)S(1)} %reshape.16), channel_id=1, source_target_pairs={{0,12},{4,0},{8,4},{12,8},{1,13},{5,1},{9,5},{13,9},{2,14},{6,2},{... | collective-permute-start | bytes 196616 | tf_op jit(solution)/shard_map/ppermute | solution.py:13
  27.6 4.9 %collective-permute-start.8 = (f32[64,256]{1,0:T(8,128)S(1)}, f32[64,256]{1,0:T(8,128)S(1)}, u32[]{:S(2)}, u32[]{:S(2)}) collective-permute-start(f32[64,256]{1,0:T(8,128)S(1)} %reshape.16), channel_id=1, source_target_pairs={{0,8},{4,12},{8,0},{12,4},{1,9},{5,13},{9,1},{13,5},{2,10},{6,14},... | collective-permute-start | bytes 196616 | tf_op jit(solution)/shard_map/ppermute | solution.py:13
  32.5 10.0 %all_gather.3 = bf16[256,2,768]{2,0,1:T(8,128)(2,1)S(1)} all-gather(bf16[64,2,768]{2,0,1:T(8,128)(2,1)S(1)} %bitcast.34), channel_id=1, replica_groups=mesh['groups'=2,'dp'=4,'task'=4] {'task'}, dimensions={0}, use_global_device_ids=true | all-gather | bytes 983040 | tf_op jit(solution)/shard_map/all_gather | solution.py:83
  42.5 0.9 %fusion.4 = bf16[2,768,64]{1,2,0:T(8,128)(2,1)} fusion(bf16[256,2,768]{2,0,1:T(8,128)(2,1)S(1)} %all_gather.3, bf16[2,768,64]{1,2,0:T(8,128)(2,1)S(1)} %copy-done.1, f32[64]{0:T(128)S(1)} %copy-done.3, bf16[256,256]{1,0:T(8,128)(2,1)S(1)} %copy-done, s32[]{:T(128)S(6)} %select_n.22), kind=kOutput, calls=%fused_computation.13 | convolution fusion | flops 50724864 | bytes 1212932 | tf_op jit(solution)/shard_map/asn,ca->snc/dot_general | solution.py:85
  43.5 0.7 %add_multiply_fusion = f32[64,256]{1,0:T(8,128)} fusion(f32[64,256]{1,0:T(8,128)S(1)} %collective-permute-done.8, f32[64,256]{1,0:T(8,128)S(1)} %collective-permute-done.7, f32[64,256]{1,0:T(8,128)S(1)} %collective-permute-done.6, f32[64,256]{1,0:T(8,128)S(1)} %reshape.16, pred[]{:T(512)S(6)} %eq.5), kind=kLoop, calls=%fused_computation.20 | loop fusion | flops 98304 | bytes 327681 | tf_op jit(solution)/shard_map/div | solution.py:87
  (21 shorter events, 0.2 us)
Async XLA Ops:
  0.6 41.9 %copy-start = (bf16[256,256]{1,0:T(8,128)(2,1)S(1)}, bf16[256,256]{1,0:T(8,128)(2,1)}, u32[]{:S(2)}) copy-start(bf16[256,256]{1,0:T(8,128)(2,1)} %param.9) | copy-start | bytes 393220
  0.6 14.5 %copy-start.2 = (bf16[3,768]{1,0:T(4,128)(2,1)S(1)}, bf16[3,768]{1,0:T(4,128)(2,1)}, u32[]{:S(2)}) copy-start(bf16[3,768]{1,0:T(4,128)(2,1)} %param.6) | copy-start | bytes 13828
  0.7 6.6 %collective-permute-start = (bf16[3,768]{1,0:T(4,128)(2,1)}, bf16[3,768]{1,0:T(4,128)(2,1)S(1)}, u32[]{:S(2)}, u32[]{:S(2)}) collective-permute-start(bf16[3,768]{1,0:T(4,128)(2,1)} %param.6), channel_id=1, source_target_pairs={{0,4},{4,0},{8,12},{12,8},{1,5},{5,1},{9,13},{13,9},{2,6},{6,2},{1... | collective-permute-start | bytes 13832 | tf_op jit(solution)/shard_map/ppermute | solution.py:49
  0.9 6.6 %collective-permute-start.2 = (bf16[3,768]{1,0:T(4,128)(2,1)}, bf16[3,768]{1,0:T(4,128)(2,1)S(1)}, u32[]{:S(2)}, u32[]{:S(2)}) collective-permute-start(bf16[3,768]{1,0:T(4,128)(2,1)} %param.6), channel_id=1, source_target_pairs={{0,8},{4,12},{8,0},{12,4},{1,9},{5,13},{9,1},{13,5},{2,10},{6,14},... | collective-permute-start | bytes 13832 | tf_op jit(solution)/shard_map/ppermute | solution.py:49
  3.2 4.3 %collective-permute-start.4 = (bf16[3,768]{1,0:T(4,128)(2,1)}, bf16[3,768]{1,0:T(4,128)(2,1)S(1)}, u32[]{:S(2)}, u32[]{:S(2)}) collective-permute-start(bf16[3,768]{1,0:T(4,128)(2,1)} %param.6), channel_id=1, source_target_pairs={{0,12},{4,8},{8,4},{12,0},{1,13},{5,9},{9,5},{13,1},{2,14},{6,10},... | collective-permute-start | bytes 13832 | tf_op jit(solution)/shard_map/ppermute | solution.py:49
  3.4 17.6 %collective-permute-start.1 = (bf16[2,768,64]{1,2,0:T(8,128)(2,1)}, bf16[2,768,64]{1,2,0:T(8,128)(2,1)S(1)}, u32[]{:S(2)}, u32[]{:S(2)}) collective-permute-start(bf16[2,768,64]{1,2,0:T(8,128)(2,1)} %param.8), channel_id=1, source_target_pairs={{0,4},{4,0},{8,12},{12,8},{1,5},{5,1},{9,13},{13,9},{2,6},{6,2},{1... | collective-permute-start | bytes 589832 | tf_op jit(solution)/shard_map/ppermute | solution.py:49
  4.5 17.6 %collective-permute-start.3 = (bf16[2,768,64]{1,2,0:T(8,128)(2,1)}, bf16[2,768,64]{1,2,0:T(8,128)(2,1)S(1)}, u32[]{:S(2)}, u32[]{:S(2)}) collective-permute-start(bf16[2,768,64]{1,2,0:T(8,128)(2,1)} %param.8), channel_id=1, source_target_pairs={{0,8},{4,12},{8,0},{12,4},{1,9},{5,13},{9,1},{13,5},{2,10},{6,14},... | collective-permute-start | bytes 589832 | tf_op jit(solution)/shard_map/ppermute | solution.py:49
  7.2 16.0 %collective-permute-start.5 = (bf16[2,768,64]{1,2,0:T(8,128)(2,1)}, bf16[2,768,64]{1,2,0:T(8,128)(2,1)S(1)}, u32[]{:S(2)}, u32[]{:S(2)}) collective-permute-start(bf16[2,768,64]{1,2,0:T(8,128)(2,1)} %param.8), channel_id=1, source_target_pairs={{0,12},{4,8},{8,4},{12,0},{1,13},{5,9},{9,5},{13,1},{2,14},{6,10},... | collective-permute-start | bytes 589832 | tf_op jit(solution)/shard_map/ppermute | solution.py:49
  9.4 15.5 %all-to-all-start = ((bf16[4,2,768,64]{2,3,1,0:T(8,128)(2,1)}), bf16[4,2,768,64]{2,3,1,0:T(8,128)(2,1)S(1)}, u32[]{:S(2)}, u32[]{:S(2)}) async-start(bf16[4,2,768,64]{2,3,1,0:T(8,128)(2,1)} %broadcast_in_dim.2), calls=%async_computation | async-start | bytes 1572864 | tf_op jit(solution)/shard_map/all_to_all | solution.py:74
  15.2 4.7 %copy-start.1 = (bf16[2,768,64]{1,2,0:T(8,128)(2,1)S(1)}, bf16[2,768,64]{1,2,0:T(8,128)(2,1)}, u32[]{:S(2)}) copy-start(bf16[2,768,64]{1,2,0:T(8,128)(2,1)} %param.8) | copy-start | bytes 589828
  23.3 1.6 %copy-start.4 = (bf16[2]{0:T(256)(128)(2,1)S(1)}, bf16[2]{0:T(256)(128)(2,1)}, u32[]{:S(2)}) copy-start(bf16[2]{0:T(256)(128)(2,1)} %constant.38.clone) | copy-start | bytes 16
  24.4 18.2 %copy-start.3 = (f32[64]{0:T(128)S(1)}, f32[64]{0:T(128)}, u32[]{:S(2)}) copy-start(f32[64]{0:T(128)} %param.10) | copy-start | bytes 772
  25.7 17.8 %collective-permute-start.6 = (f32[64,256]{1,0:T(8,128)S(1)}, f32[64,256]{1,0:T(8,128)S(1)}, u32[]{:S(2)}, u32[]{:S(2)}) collective-permute-start(f32[64,256]{1,0:T(8,128)S(1)} %reshape.16), channel_id=1, source_target_pairs={{0,12},{4,0},{8,4},{12,8},{1,13},{5,1},{9,5},{13,9},{2,14},{6,2},{... | collective-permute-start | bytes 196616 | tf_op jit(solution)/shard_map/ppermute | solution.py:13
  27.6 15.9 %collective-permute-start.7 = (f32[64,256]{1,0:T(8,128)S(1)}, f32[64,256]{1,0:T(8,128)S(1)}, u32[]{:S(2)}, u32[]{:S(2)}) collective-permute-start(f32[64,256]{1,0:T(8,128)S(1)} %reshape.16), channel_id=1, source_target_pairs={{0,4},{4,8},{8,12},{12,0},{1,5},{5,9},{9,13},{13,1},{2,6},{6,10},{... | collective-permute-start | bytes 196616 | tf_op jit(solution)/shard_map/ppermute | solution.py:13
  27.6 15.9 %collective-permute-start.8 = (f32[64,256]{1,0:T(8,128)S(1)}, f32[64,256]{1,0:T(8,128)S(1)}, u32[]{:S(2)}, u32[]{:S(2)}) collective-permute-start(f32[64,256]{1,0:T(8,128)S(1)} %reshape.16), channel_id=1, source_target_pairs={{0,8},{4,12},{8,0},{12,4},{1,9},{5,13},{9,1},{13,5},{2,10},{6,14},... | collective-permute-start | bytes 196616 | tf_op jit(solution)/shard_map/ppermute | solution.py:13

commit v19 on v12

--- a/solution.py
+++ b/solution.py
@@ -48,8 +48,10 @@
         peer_coords = [shift(coords, "dp", k, n_dp) for k in range(1, n_dp)]
         task_input = lax.optimization_barrier((vectors, peer_coords))[0]
         summed = block(coords, vectors)
-        for k in range(1, n_dp):
-            summed = summed + block(peer_coords[k - 1], moved[k - 1])
+        if n_dp > 1:
+            summed = summed + block(
+                jnp.concatenate(peer_coords, axis=1), jnp.concatenate(moved, axis=1)
+            )
     else:
 
         def ring(_, carry):

time: 43.3 us -> 47 us (1.085)
  waiting for transfers between devices: 2.37 us -> 6.47 us
  other arithmetic: 6.12 us -> 4.95 us
  local copies, waits for them, and re-layouts: 2.16 us -> 1.19 us
  starting transfers between devices: 18.4 us -> 19.3 us
  matrix products: 5.84 us -> 6.46 us
    ppermute x9, waiting for transfers between devices: 0.02 us -> 5.83 us  [shift(): return lax.ppermute(x, axis, [(i, (i + k) % n) for i in range(n)])]
    dot_general x0 -> x1, matrix products: none -> 2.98 us  [block(): jnp.einsum('nr,srm->snm', tile, values, preferred_element_type=jnp.float32)]
    unnamed x4 -> x1, matrix products: 4.38 us -> 2.02 us
    reduce_sum x1 -> x2, other arithmetic: 4.65 us -> 2.8 us  [kernel_tile(): return jnp.exp(0.1 - jnp.sqrt(jnp.sum(diff * diff, axis=0) + 0.01))]
    all_to_all x1, waiting for transfers between devices: 2.35 us -> 0.64 us  [per_device(): task_blocks = lax.all_to_all(copies, 'task', 0, 0, tiled=True)]
    broadcast_in_dim x1, local copies, waits for them, and re-layouts: 1.9 us -> 0.94 us  [per_device(): copies = jnp.broadcast_to(task_input[None], (n_task,) + vectors.shape)]
    ppermute x9, starting transfers between devices: 14.9 us -> 15.8 us  [shift(): return lax.ppermute(x, axis, [(i, (i + k) % n) for i in range(n)])]
    mul x0 -> x1, other arithmetic: none -> 0.77 us  [per_device(): own_scaled = coords.astype(jnp.float32) * inverse[:, None]]
  transfers between devices with their start and end apart: 10 -> 10, of which waited for: 1 -> 2; matrix products, arithmetic and copies ran while one was open for 29% -> 24% of each run, Pallas kernels for 0% -> 0%
where the time goes in v19:
time: 47 us; the launch traced here: 46.7 us
  starting transfers between devices  19.3 us (41%)
  blocking collectives  7.66 us (16%)
  waiting for transfers between devices  6.47 us (14%)
  matrix products  6.46 us (14%)
  other arithmetic  4.95 us (11%)
  local copies, waits for them, and re-layouts  1.19 us (3%)
  between operations  0.76 us (2%)
    ppermute x9, starting transfers between devices, shift(): return lax.ppermute(x, axis, [(i, (i + k) % n) for i in range(n)])  15.8 us
    all_gather x1, blocking collectives, per_device(): lax.all_gather(jnp.transpose(gather_input, (2, 0, 1)), 'task', axis=0, ti...  7.66 us
    ppermute x9, waiting for transfers between devices, shift(): return lax.ppermute(x, axis, [(i, (i + k) % n) for i in range(n)])  5.83 us
    all_to_all x1, starting transfers between devices, per_device(): task_blocks = lax.all_to_all(copies, 'task', 0, 0, tiled=True)  3.49 us
    dot_general x1, matrix products, block(): jnp.einsum('nr,srm->snm', tile, values, preferred_element_type=jnp.float32)  2.98 us
    reduce_sum x2, other arithmetic, kernel_tile(): return jnp.exp(0.1 - jnp.sqrt(jnp.sum(diff * diff, axis=0) + 0.01))  2.8 us
    unnamed x1, matrix products  2.02 us
    dot_general x1, matrix products, per_device(): jnp.einsum('asn,ca->snc', whole_images, own_rows, preferred_element_type=...  0.94 us
  transfers between devices with their start and end apart: 10, of which 2 were waited for; matrix products, arithmetic and copies ran while one was open for 24% of the time, Pallas kernels for 0%

profile of v19, /device:TPU:0, one launch (start us, length us, event | category | flops | bytes accessed | tf_op | source)
XLA Modules:
  0.0 46.7 jit_solution(14520439608131996904)
XLA Ops:
  0.7 5.1 %collective-permute-start.5 = (bf16[3,768]{1,0:T(4,128)(2,1)}, bf16[3,768]{1,0:T(4,128)(2,1)S(1)}, u32[]{:S(2)}, u32[]{:S(2)}) collective-permute-start(bf16[3,768]{1,0:T(4,128)(2,1)} %param.6), channel_id=1, source_target_pairs={{0,12},{4,0},{8,4},{12,8},{1,13},{5,1},{9,5},{13,9},{2,14},{6,2},{... | collective-permute-start | bytes 13832 | tf_op jit(solution)/shard_map/ppermute | solution.py:13
  5.8 1.0 %collective-permute-start.3 = (bf16[3,768]{1,0:T(4,128)(2,1)}, bf16[3,768]{1,0:T(4,128)(2,1)S(1)}, u32[]{:S(2)}, u32[]{:S(2)}) collective-permute-start(bf16[3,768]{1,0:T(4,128)(2,1)} %param.6), channel_id=1, source_target_pairs={{0,4},{4,8},{8,12},{12,0},{1,5},{5,9},{9,13},{13,1},{2,6},{6,10},{... | collective-permute-start | bytes 13832 | tf_op jit(solution)/shard_map/ppermute | solution.py:13
  6.8 2.8 %collective-permute-start.2 = (bf16[2,768,64]{1,2,0:T(8,128)(2,1)}, bf16[2,768,64]{1,2,0:T(8,128)(2,1)S(1)}, u32[]{:S(2)}, u32[]{:S(2)}) collective-permute-start(bf16[2,768,64]{1,2,0:T(8,128)(2,1)} %param.8), channel_id=1, source_target_pairs={{0,12},{4,0},{8,4},{12,8},{1,13},{5,1},{9,5},{13,9},{2,14},{6,2},{... | collective-permute-start | bytes 589832 | tf_op jit(solution)/shard_map/ppermute | solution.py:13
  9.6 1.1 %collective-permute-start.1 = (bf16[2,768,64]{1,2,0:T(8,128)(2,1)}, bf16[2,768,64]{1,2,0:T(8,128)(2,1)S(1)}, u32[]{:S(2)}, u32[]{:S(2)}) collective-permute-start(bf16[2,768,64]{1,2,0:T(8,128)(2,1)} %param.8), channel_id=1, source_target_pairs={{0,8},{4,12},{8,0},{12,4},{1,9},{5,13},{9,1},{13,5},{2,10},{6,14},... | collective-permute-start | bytes 589832 | tf_op jit(solution)/shard_map/ppermute | solution.py:13
  10.7 0.7 %broadcast_divide_fusion = f32[3]{0:T(128)S(1)} fusion(f32[3]{0:T(128)} %param.7), kind=kLoop, calls=%fused_computation.27 | loop fusion | flops 3 | bytes 24 | tf_op jit(solution)/shard_map/div | solution.py:37
  11.4 0.8 %convert_multiply_fusion.1 = f32[3,768]{1,0:T(4,128)S(1)} fusion(bf16[3,768]{1,0:T(4,128)(2,1)} %param.6, f32[3]{0:T(128)S(1)} %broadcast_divide_fusion), kind=kLoop, calls=%fused_computation.25 | loop fusion | flops 4608 | bytes 13836 | tf_op jit(solution)/shard_map/mul | solution.py:38
  12.1 0.7 %multiply_reduce_fusion.1 = f32[768,768]{1,0:T(8,128)S(1)} fusion(f32[3,768]{1,0:T(4,128)S(1)} %convert_multiply_fusion.1), kind=kLoop, calls=%fused_computation.2 | loop fusion | flops 4718592 | bytes 2368512 | tf_op jit(solution)/shard_map/reduce_sum | solution.py:9
  12.9 2.0 %fusion.9 = f32[768,128]{0,1:S(1)} fusion(bf16[768,128]{0,1:T(8,128)(2,1)} %bitcast.34, f32[768,768]{1,0:T(8,128)S(1)} %multiply_reduce_fusion.1), kind=kOutput, calls=%fused_computation.9 | convolution fusion | flops 152764416 | bytes 2949120
  15.0 0.9 %broadcast_in_dim.2 = bf16[4,2,768,64]{2,3,1,0:T(8,128)(2,1)} broadcast(bf16[2,768,64]{1,2,0:T(8,128)(2,1)S(1)} %copy-done.1), dimensions={1,2,3} | broadcast | bytes 983040 | tf_op jit(solution)/shard_map/broadcast_in_dim | solution.py:67
  15.9 3.5 %all-to-all-start = ((bf16[4,2,768,64]{2,3,1,0:T(8,128)(2,1)}), bf16[4,2,768,64]{2,3,1,0:T(8,128)(2,1)S(1)}, u32[]{:S(2)}, u32[]{:S(2)}) async-start(bf16[4,2,768,64]{2,3,1,0:T(8,128)(2,1)} %broadcast_in_dim.2), calls=%async_computation | async-start | bytes 1572864 | tf_op jit(solution)/shard_map/all_to_all | solution.py:68
  19.4 0.1 convert_multiply_fusion
  19.5 2.1 %multiply_reduce_fusion = f32[768,2304]{1,0:T(8,128)S(1)} fusion(f32[3,2304]{1,0:T(4,128)S(1)} %convert_multiply_fusion, f32[3,768]{1,0:T(4,128)S(1)} %convert_multiply_fusion.1), kind=kLoop, calls=%fused_computation | loop fusion | flops 14155776 | bytes 7114752 | tf_op jit(solution)/shard_map/reduce_sum | solution.py:9
  21.6 5.8 %collective-permute-done.1 = bf16[2,768,64]{1,2,0:T(8,128)(2,1)S(1)} collective-permute-done((bf16[2,768,64]{1,2,0:T(8,128)(2,1)}, bf16[2,768,64]{1,2,0:T(8,128)(2,1)S(1)}, u32[]{:S(2)}, u32[]{:S(2)}) %collective-permute-start.1) | collective-permute-done | bytes 196640 | tf_op jit(solution)/shard_map/ppermute | solution.py:13
  27.4 3.0 %fusion.11 = bf16[2,768,64]{1,2,0:T(8,128)(2,1)S(1)} fusion(f32[2,768,64]{1,2,0:T(8,128)S(1)} %bitcast.36, f32[768,2304]{1,0:T(8,128)S(1)} %multiply_reduce_fusion, bf16[2,768,64]{1,2,0:T(8,128)(2,1)S(1)} %collective-permute-done.2, bf16[2,768,64]{1,2,0:T(8,128)(2,1)S(1)} %collective-permute-done.1, bf16[2,768,64]{1,2,0:T(8,128)(2,1)S(1)} %collective-permute-done), kind=kOutput, calls=%fused_computation.11 | convolution fusion | flops 460259328 | bytes 8257536 | tf_op jit(solution)/shard_map/nr,srm->snm/dot_general | solution.py:43
  30.4 0.6 %all-to-all-done = bf16[4,2,768,64]{2,3,1,0:T(8,128)(2,1)S(1)} async-done(((bf16[4,2,768,64]{2,3,1,0:T(8,128)(2,1)}), bf16[4,2,768,64]{2,3,1,0:T(8,128)(2,1)S(1)}, u32[]{:S(2)}, u32[]{:S(2)}) %all-to-all-start) | async-done | bytes 786464 | tf_op jit(solution)/shard_map/all_to_all | solution.py:68
  31.1 0.5 %convolution_bitcast_fusion = f32[64,4,64]{2,0,1:T(8,128)S(1)} fusion(bf16[4,2,768,64]{2,3,1,0:T(8,128)(2,1)S(1)} %all-to-all-done, bf16[2,768,64]{1,2,0:T(8,128)(2,1)S(1)} %fusion.11, bf16[2]{0:T(256)(128)(2,1)S(1)} %copy-done.3), kind=kOutput, calls=%fused_computation.12 | convolution fusion | flops 50724864 | bytes 1048580 | tf_op jit(solution)/shard_map/sna,ksnb->akb/dot_general | solution.py:72
  31.6 0.1 copy.9
  31.7 0.1 reshape.45
  31.8 1.8 %collective-permute-start.8 = (f32[64,256]{1,0:T(8,128)S(1)}, f32[64,256]{1,0:T(8,128)S(1)}, u32[]{:S(2)}, u32[]{:S(2)}) collective-permute-start(f32[64,256]{1,0:T(8,128)S(1)} %reshape.45), channel_id=1, source_target_pairs={{0,8},{4,12},{8,0},{12,4},{1,9},{5,13},{9,1},{13,5},{2,10},{6,14},... | collective-permute-start | bytes 196616 | tf_op jit(solution)/shard_map/ppermute | solution.py:13
  33.7 2.6 %collective-permute-start.7 = (f32[64,256]{1,0:T(8,128)S(1)}, f32[64,256]{1,0:T(8,128)S(1)}, u32[]{:S(2)}, u32[]{:S(2)}) collective-permute-start(f32[64,256]{1,0:T(8,128)S(1)} %reshape.45), channel_id=1, source_target_pairs={{0,4},{4,8},{8,12},{12,0},{1,5},{5,9},{9,13},{13,1},{2,6},{6,10},{... | collective-permute-start | bytes 196616 | tf_op jit(solution)/shard_map/ppermute | solution.py:13
  36.2 1.3 %collective-permute-start.6 = (f32[64,256]{1,0:T(8,128)S(1)}, f32[64,256]{1,0:T(8,128)S(1)}, u32[]{:S(2)}, u32[]{:S(2)}) collective-permute-start(f32[64,256]{1,0:T(8,128)S(1)} %reshape.45), channel_id=1, source_target_pairs={{0,12},{4,0},{8,4},{12,8},{1,13},{5,1},{9,5},{13,9},{2,14},{6,2},{... | collective-permute-start | bytes 196616 | tf_op jit(solution)/shard_map/ppermute | solution.py:13
  37.5 7.7 %all_gather.3 = bf16[256,2,768]{2,0,1:T(8,128)(2,1)S(1)} all-gather(bf16[64,2,768]{2,0,1:T(8,128)(2,1)S(1)} %bitcast.35), channel_id=1, replica_groups=mesh['groups'=2,'dp'=4,'task'=4] {'task'}, dimensions={0}, use_global_device_ids=true | all-gather | bytes 983040 | tf_op jit(solution)/shard_map/all_gather | solution.py:77
  45.1 0.9 %fusion.10 = bf16[2,768,64]{1,2,0:T(8,128)(2,1)} fusion(bf16[256,2,768]{2,0,1:T(8,128)(2,1)S(1)} %all_gather.3, bf16[2,768,64]{1,2,0:T(8,128)(2,1)S(1)} %copy-done.1, f32[64]{0:T(128)S(1)} %copy-done.2, bf16[256,256]{1,0:T(8,128)(2,1)S(1)} %copy-done, s32[]{:T(128)S(6)} %select_n.22), kind=kOutput, calls=%fused_computation.10 | convolution fusion | flops 50724864 | bytes 1212932 | tf_op jit(solution)/shard_map/asn,ca->snc/dot_general | solution.py:79
  46.1 0.7 %add_multiply_fusion = f32[64,256]{1,0:T(8,128)} fusion(f32[64,256]{1,0:T(8,128)S(1)} %collective-permute-done.8, f32[64,256]{1,0:T(8,128)S(1)} %collective-permute-done.7, f32[64,256]{1,0:T(8,128)S(1)} %collective-permute-done.6, f32[64,256]{1,0:T(8,128)S(1)} %reshape.45, pred[]{:T(512)S(6)} %eq.5), kind=kLoop, calls=%fused_computation.21 | loop fusion | flops 98304 | bytes 327681 | tf_op jit(solution)/shard_map/div | solution.py:81
  (18 shorter events, 0.1 us)
Async XLA Ops:
  0.6 44.5 %copy-start = (bf16[256,256]{1,0:T(8,128)(2,1)S(1)}, bf16[256,256]{1,0:T(8,128)(2,1)}, u32[]{:S(2)}) copy-start(bf16[256,256]{1,0:T(8,128)(2,1)} %param.9) | copy-start | bytes 393220
  0.6 14.3 %copy-start.1 = (bf16[2,768,64]{1,2,0:T(8,128)(2,1)S(1)}, bf16[2,768,64]{1,2,0:T(8,128)(2,1)}, u32[]{:S(2)}) copy-start(bf16[2,768,64]{1,2,0:T(8,128)(2,1)} %param.8) | copy-start | bytes 589828
  0.7 14.2 %collective-permute-start.5 = (bf16[3,768]{1,0:T(4,128)(2,1)}, bf16[3,768]{1,0:T(4,128)(2,1)S(1)}, u32[]{:S(2)}, u32[]{:S(2)}) collective-permute-start(bf16[3,768]{1,0:T(4,128)(2,1)} %param.6), channel_id=1, source_target_pairs={{0,12},{4,0},{8,4},{12,8},{1,13},{5,1},{9,5},{13,9},{2,14},{6,2},{... | collective-permute-start | bytes 13832 | tf_op jit(solution)/shard_map/ppermute | solution.py:13
  5.8 9.2 %collective-permute-start.4 = (bf16[3,768]{1,0:T(4,128)(2,1)}, bf16[3,768]{1,0:T(4,128)(2,1)S(1)}, u32[]{:S(2)}, u32[]{:S(2)}) collective-permute-start(bf16[3,768]{1,0:T(4,128)(2,1)} %param.6), channel_id=1, source_target_pairs={{0,8},{4,12},{8,0},{12,4},{1,9},{5,13},{9,1},{13,5},{2,10},{6,14},... | collective-permute-start | bytes 13832 | tf_op jit(solution)/shard_map/ppermute | solution.py:13
  5.8 9.2 %collective-permute-start.3 = (bf16[3,768]{1,0:T(4,128)(2,1)}, bf16[3,768]{1,0:T(4,128)(2,1)S(1)}, u32[]{:S(2)}, u32[]{:S(2)}) collective-permute-start(bf16[3,768]{1,0:T(4,128)(2,1)} %param.6), channel_id=1, source_target_pairs={{0,4},{4,8},{8,12},{12,0},{1,5},{5,9},{9,13},{13,1},{2,6},{6,10},{... | collective-permute-start | bytes 13832 | tf_op jit(solution)/shard_map/ppermute | solution.py:13
  6.8 14.8 %collective-permute-start.2 = (bf16[2,768,64]{1,2,0:T(8,128)(2,1)}, bf16[2,768,64]{1,2,0:T(8,128)(2,1)S(1)}, u32[]{:S(2)}, u32[]{:S(2)}) collective-permute-start(bf16[2,768,64]{1,2,0:T(8,128)(2,1)} %param.8), channel_id=1, source_target_pairs={{0,12},{4,0},{8,4},{12,8},{1,13},{5,1},{9,5},{13,9},{2,14},{6,2},{... | collective-permute-start | bytes 589832 | tf_op jit(solution)/shard_map/ppermute | solution.py:13
  9.6 17.8 %collective-permute-start.1 = (bf16[2,768,64]{1,2,0:T(8,128)(2,1)}, bf16[2,768,64]{1,2,0:T(8,128)(2,1)S(1)}, u32[]{:S(2)}, u32[]{:S(2)}) collective-permute-start(bf16[2,768,64]{1,2,0:T(8,128)(2,1)} %param.8), channel_id=1, source_target_pairs={{0,8},{4,12},{8,0},{12,4},{1,9},{5,13},{9,1},{13,5},{2,10},{6,14},... | collective-permute-start | bytes 589832 | tf_op jit(solution)/shard_map/ppermute | solution.py:13
  14.9 12.5 %collective-permute-start = (bf16[2,768,64]{1,2,0:T(8,128)(2,1)S(1)}, bf16[2,768,64]{1,2,0:T(8,128)(2,1)S(1)}, u32[]{:S(2)}, u32[]{:S(2)}) collective-permute-start(bf16[2,768,64]{1,2,0:T(8,128)(2,1)S(1)} %copy-done.1), channel_id=1, source_target_pairs={{0,4},{4,8},{8,12},{12,0},{1,5},{5,9},{9,13},{13,1},{2,6},{6,10},{... | collective-permute-start | bytes 589832 | tf_op jit(solution)/shard_map/ppermute | solution.py:13
  15.9 15.1 %all-to-all-start = ((bf16[4,2,768,64]{2,3,1,0:T(8,128)(2,1)}), bf16[4,2,768,64]{2,3,1,0:T(8,128)(2,1)S(1)}, u32[]{:S(2)}, u32[]{:S(2)}) async-start(bf16[4,2,768,64]{2,3,1,0:T(8,128)(2,1)} %broadcast_in_dim.2), calls=%async_computation | async-start | bytes 1572864 | tf_op jit(solution)/shard_map/all_to_all | solution.py:68
  27.4 3.6 %copy-start.3 = (bf16[2]{0:T(256)(128)(2,1)S(1)}, bf16[2]{0:T(256)(128)(2,1)}, u32[]{:S(2)}) copy-start(bf16[2]{0:T(256)(128)(2,1)} %constant.40.clone) | copy-start | bytes 16
  27.4 17.7 %copy-start.2 = (f32[64]{0:T(128)S(1)}, f32[64]{0:T(128)}, u32[]{:S(2)}) copy-start(f32[64]{0:T(128)} %param.10) | copy-start | bytes 772
  31.8 14.3 %collective-permute-start.8 = (f32[64,256]{1,0:T(8,128)S(1)}, f32[64,256]{1,0:T(8,128)S(1)}, u32[]{:S(2)}, u32[]{:S(2)}) collective-permute-start(f32[64,256]{1,0:T(8,128)S(1)} %reshape.45), channel_id=1, source_target_pairs={{0,8},{4,12},{8,0},{12,4},{1,9},{5,13},{9,1},{13,5},{2,10},{6,14},... | collective-permute-start | bytes 196616 | tf_op jit(solution)/shard_map/ppermute | solution.py:13
  33.7 12.4 %collective-permute-start.7 = (f32[64,256]{1,0:T(8,128)S(1)}, f32[64,256]{1,0:T(8,128)S(1)}, u32[]{:S(2)}, u32[]{:S(2)}) collective-permute-start(f32[64,256]{1,0:T(8,128)S(1)} %reshape.45), channel_id=1, source_target_pairs={{0,4},{4,8},{8,12},{12,0},{1,5},{5,9},{9,13},{13,1},{2,6},{6,10},{... | collective-permute-start | bytes 196616 | tf_op jit(solution)/shard_map/ppermute | solution.py:13
  36.2 9.9 %collective-permute-start.6 = (f32[64,256]{1,0:T(8,128)S(1)}, f32[64,256]{1,0:T(8,128)S(1)}, u32[]{:S(2)}, u32[]{:S(2)}) collective-permute-start(f32[64,256]{1,0:T(8,128)S(1)} %reshape.45), channel_id=1, source_target_pairs={{0,12},{4,0},{8,4},{12,8},{1,13},{5,1},{9,5},{13,9},{2,14},{6,2},{... | collective-permute-start | bytes 196616 | tf_op jit(solution)/shard_map/ppermute | solution.py:13

commit v20 on v12

--- a/solution.py
+++ b/solution.py
@@ -37,9 +37,16 @@
     inverse = 1.0 / lengthscales
     own_scaled = coords.astype(jnp.float32) * inverse[:, None]
 
-    def block(right_coords, values):
+    def block(right_coords, values, fused=False):
         right = right_coords.astype(jnp.float32) * inverse[:, None]
-        tile = kernel_tile(own_scaled, right).astype(jnp.bfloat16)
+        if fused:
+            total = None
+            for c in range(right.shape[0]):
+                diff = own_scaled[c][:, None] - right[c][None, :]
+                total = diff * diff if total is None else total + diff * diff
+            tile = jnp.exp(0.1 - jnp.sqrt(total + 0.01)).astype(jnp.bfloat16)
+        else:
+            tile = kernel_tile(own_scaled, right).astype(jnp.bfloat16)
         return jnp.einsum("nr,srm->snm", tile, values, preferred_element_type=jnp.float32)
 
     task_input = vectors
@@ -47,7 +54,7 @@
         moved = [shift(vectors, "dp", k, n_dp) for k in range(1, n_dp)]
         peer_coords = [shift(coords, "dp", k, n_dp) for k in range(1, n_dp)]
         task_input = lax.optimization_barrier((vectors, peer_coords))[0]
-        summed = block(coords, vectors)
+        summed = block(coords, vectors, fused=True)
         for k in range(1, n_dp):
             summed = summed + block(peer_coords[k - 1], moved[k - 1])
     else:

time: 43.3 us -> 44.1 us (1.018)
  matrix products: 5.84 us -> 6.86 us
  other arithmetic: 6.12 us -> 5.15 us
  waiting for transfers between devices: 2.37 us -> 3.08 us
    reduce_sum x1, other arithmetic: 4.65 us -> 2.99 us  [kernel_tile(): return jnp.exp(0.1 - jnp.sqrt(jnp.sum(diff * diff, axis=0) + 0.01))]
    unnamed x4, matrix products: 4.38 us -> 5.41 us
    all_to_all x1, waiting for transfers between devices: 2.35 us -> 3.05 us  [per_device(): task_blocks = lax.all_to_all(copies, 'task', 0, 0, tiled=True)]
    mul x1, other arithmetic: 0.08 us -> 0.77 us  [block(): right = right_coords.astype(jnp.float32) * inverse[:, None]]
where the time goes in v20:
time: 44.1 us; the launch traced here: 43.9 us
  starting transfers between devices  18.4 us (42%)
  blocking collectives  7.45 us (17%)
  matrix products  6.86 us (16%)
  other arithmetic  5.15 us (12%)
  waiting for transfers between devices  3.08 us (7%)
  local copies, waits for them, and re-layouts  2.16 us (5%)
  between operations  0.73 us (2%)
    ppermute x9, starting transfers between devices, shift(): return lax.ppermute(x, axis, [(i, (i + k) % n) for i in range(n)])  14.9 us
    all_gather x1, blocking collectives, per_device(): lax.all_gather(jnp.transpose(gather_input, (2, 0, 1)), 'task', axis=0, ti...  7.45 us
    unnamed x4, matrix products  5.41 us
    all_to_all x1, starting transfers between devices, per_device(): task_blocks = lax.all_to_all(copies, 'task', 0, 0, tiled=True)  3.49 us
    all_to_all x1, waiting for transfers between devices, per_device(): task_blocks = lax.all_to_all(copies, 'task', 0, 0, tiled=True)  3.05 us
    reduce_sum x1, other arithmetic, kernel_tile(): return jnp.exp(0.1 - jnp.sqrt(jnp.sum(diff * diff, axis=0) + 0.01))  2.99 us
    broadcast_in_dim x1, local copies, waits for them, and re-layouts, per_device(): copies = jnp.broadcast_to(task_input[None], (n_task,) + vectors.shape)  1.87 us
    dot_general x1, matrix products, per_device(): jnp.einsum('asn,ca->snc', whole_images, own_rows, preferred_element_type=...  0.94 us
  transfers between devices with their start and end apart: 10, of which 1 were waited for; matrix products, arithmetic and copies ran while one was open for 29% of the time, Pallas kernels for 0%

profile of v20, /device:TPU:0, one launch (start us, length us, event | category | flops | bytes accessed | tf_op | source)
XLA Modules:
  0.0 43.9 jit_solution(6778217785260006137)
XLA Ops:
  0.6 3.1 %collective-permute-start = (bf16[3,768]{1,0:T(4,128)(2,1)}, bf16[3,768]{1,0:T(4,128)(2,1)S(1)}, u32[]{:S(2)}, u32[]{:S(2)}) collective-permute-start(bf16[3,768]{1,0:T(4,128)(2,1)} %param.6), channel_id=1, source_target_pairs={{0,4},{4,8},{8,12},{12,0},{1,5},{5,9},{9,13},{13,1},{2,6},{6,10},{... | collective-permute-start | bytes 13832 | tf_op jit(solution)/shard_map/ppermute | solution.py:13
  3.7 2.6 %collective-permute-start.2 = (bf16[3,768]{1,0:T(4,128)(2,1)}, bf16[3,768]{1,0:T(4,128)(2,1)S(1)}, u32[]{:S(2)}, u32[]{:S(2)}) collective-permute-start(bf16[3,768]{1,0:T(4,128)(2,1)} %param.6), channel_id=1, source_target_pairs={{0,8},{4,12},{8,0},{12,4},{1,9},{5,13},{9,1},{13,5},{2,10},{6,14},... | collective-permute-start | bytes 13832 | tf_op jit(solution)/shard_map/ppermute | solution.py:13
  6.3 1.3 %collective-permute-start.4 = (bf16[3,768]{1,0:T(4,128)(2,1)}, bf16[3,768]{1,0:T(4,128)(2,1)S(1)}, u32[]{:S(2)}, u32[]{:S(2)}) collective-permute-start(bf16[3,768]{1,0:T(4,128)(2,1)} %param.6), channel_id=1, source_target_pairs={{0,12},{4,0},{8,4},{12,8},{1,13},{5,1},{9,5},{13,9},{2,14},{6,2},{... | collective-permute-start | bytes 13832 | tf_op jit(solution)/shard_map/ppermute | solution.py:13
  7.7 0.7 %collective-permute-start.1 = (bf16[2,768,64]{1,2,0:T(8,128)(2,1)}, bf16[2,768,64]{1,2,0:T(8,128)(2,1)S(1)}, u32[]{:S(2)}, u32[]{:S(2)}) collective-permute-start(bf16[2,768,64]{1,2,0:T(8,128)(2,1)} %param.8), channel_id=1, source_target_pairs={{0,4},{4,8},{8,12},{12,0},{1,5},{5,9},{9,13},{13,1},{2,6},{6,10},{... | collective-permute-start | bytes 589832 | tf_op jit(solution)/shard_map/ppermute | solution.py:13
  8.3 0.3 collective-permute-start.3
  8.7 0.7 %broadcast_divide_fusion = f32[3]{0:T(128)S(1)} fusion(f32[3]{0:T(128)} %param.7), kind=kLoop, calls=%fused_computation.30 | loop fusion | flops 3 | bytes 24 | tf_op jit(solution)/shard_map/div | solution.py:37
  9.3 2.8 %collective-permute-start.5 = (bf16[2,768,64]{1,2,0:T(8,128)(2,1)}, bf16[2,768,64]{1,2,0:T(8,128)(2,1)S(1)}, u32[]{:S(2)}, u32[]{:S(2)}) collective-permute-start(bf16[2,768,64]{1,2,0:T(8,128)(2,1)} %param.8), channel_id=1, source_target_pairs={{0,12},{4,0},{8,4},{12,8},{1,13},{5,1},{9,5},{13,9},{2,14},{6,2},{... | collective-permute-start | bytes 589832 | tf_op jit(solution)/shard_map/ppermute | solution.py:13
  12.2 0.8 %convert_multiply_fusion = (f32[3,768]{1,0:T(4,128)S(1)}, f32[3,768]{1,0:T(4,128)S(1)}, f32[3,768]{1,0:T(4,128)S(1)}, f32[3,768]{1,0:T(4,128)S(1)}) fusion(bf16[3,768]{1,0:T(4,128)(2,1)S(1)} %collective-permute-done.4, f32[3]{0:T(128)S(1)} %broadcast_divide_fusion, bf16[3,768]{1,0:T(4,128)(2,1)S(1)} %collective-permute-done, ...), kind=kLoop, calls=%fused_computation.22 | loop fusion | flops 18432 | bytes 55308 | tf_op jit(solution)/shard_map/mul | solution.py:41
  13.0 1.9 %broadcast_in_dim.2 = bf16[4,2,768,64]{2,3,1,0:T(8,128)(2,1)} broadcast(bf16[2,768,64]{1,2,0:T(8,128)(2,1)} %param.8), dimensions={1,2,3} | broadcast | bytes 983040 | tf_op jit(solution)/shard_map/broadcast_in_dim | solution.py:72
  14.8 3.5 %all-to-all-start = ((bf16[4,2,768,64]{2,3,1,0:T(8,128)(2,1)}), bf16[4,2,768,64]{2,3,1,0:T(8,128)(2,1)S(1)}, u32[]{:S(2)}, u32[]{:S(2)}) async-start(bf16[4,2,768,64]{2,3,1,0:T(8,128)(2,1)} %broadcast_in_dim.2), calls=%async_computation | async-start | bytes 1572864 | tf_op jit(solution)/shard_map/all_to_all | solution.py:73
  18.3 3.0 %multiply_reduce_fusion.2 = (f32[768,768]{1,0:T(8,128)S(1)}, f32[768,768]{1,0:T(8,128)S(1)}, f32[768,768]{1,0:T(8,128)S(1)}) fusion(f32[3,768]{1,0:T(4,128)S(1)} %get-tuple-element.13, f32[3,768]{1,0:T(4,128)S(1)} %get-tuple-element.15, f32[3,768]{1,0:T(4,128)S(1)} %get-tuple-element.14, f32[3,768]{1,0:T(4,128)S(1)} %get-tuple-element.12), kind=kLoop, calls=%fused_computation.2 | loop fusion | flops 14155776 | bytes 7114752 | tf_op jit(solution)/shard_map/reduce_sum | solution.py:9
  21.4 2.1 %fusion = f32[768,128]{0,1:S(1)} fusion(bf16[768,128]{0,1:T(8,128)(2,1)S(1)} %bitcast.35, f32[768]{0:T(1024)S(1)} %get-tuple-element.10, f32[768]{0:T(1024)S(1)} %get-tuple-element.11, f32[768]{0:T(1024)S(1)} %get-tuple-element.9), kind=kOutput, calls=%fused_computation.8 | convolution fusion | flops 157483008 | bytes 599040
  23.5 1.1 %fusion.1 = f32[768,128]{0,1:S(1)} fusion(bf16[768,128]{0,1:T(8,128)(2,1)S(1)} %bitcast.41, f32[768,768]{1,0:T(8,128)S(1)} %get-tuple-element.6), kind=kOutput, calls=%fused_computation.9 | convolution fusion | flops 152764416 | bytes 2949120
  24.6 1.1 %fusion.2 = f32[768,128]{0,1:S(1)} fusion(bf16[768,128]{0,1:T(8,128)(2,1)S(1)} %bitcast.40, f32[768,768]{1,0:T(8,128)S(1)} %get-tuple-element.7), kind=kOutput, calls=%fused_computation.10 | convolution fusion | flops 152764416 | bytes 2949120
  25.7 1.1 %fusion.3 = f32[768,128]{0,1:S(1)} fusion(bf16[768,128]{0,1:T(8,128)(2,1)S(1)} %bitcast.42, f32[768,768]{1,0:T(8,128)S(1)} %get-tuple-element.8), kind=kOutput, calls=%fused_computation.11 | convolution fusion | flops 152764416 | bytes 2949120
  26.9 3.1 %all-to-all-done = bf16[4,2,768,64]{2,3,1,0:T(8,128)(2,1)S(1)} async-done(((bf16[4,2,768,64]{2,3,1,0:T(8,128)(2,1)}), bf16[4,2,768,64]{2,3,1,0:T(8,128)(2,1)S(1)}, u32[]{:S(2)}, u32[]{:S(2)}) %all-to-all-start) | async-done | bytes 786464 | tf_op jit(solution)/shard_map/all_to_all | solution.py:73
  30.0 0.5 %convolution_bitcast_fusion = f32[64,4,64]{2,0,1:T(8,128)S(1)} fusion(bf16[4,2,768,64]{2,3,1,0:T(8,128)(2,1)S(1)} %all-to-all-done, bf16[2,768,64]{1,2,0:T(8,128)(2,1)S(1)} %fusion.5, bf16[2]{0:T(256)(128)(2,1)S(1)} %copy-done.3), kind=kOutput, calls=%fused_computation.13 | convolution fusion | flops 50724864 | bytes 1048580 | tf_op jit(solution)/shard_map/sna,ksnb->akb/dot_general | solution.py:77
  30.6 0.1 reshape.18
  30.7 1.3 %collective-permute-start.6 = (f32[64,256]{1,0:T(8,128)S(1)}, f32[64,256]{1,0:T(8,128)S(1)}, u32[]{:S(2)}, u32[]{:S(2)}) collective-permute-start(f32[64,256]{1,0:T(8,128)S(1)} %reshape.18), channel_id=1, source_target_pairs={{0,12},{4,0},{8,4},{12,8},{1,13},{5,1},{9,5},{13,9},{2,14},{6,2},{... | collective-permute-start | bytes 196616 | tf_op jit(solution)/shard_map/ppermute | solution.py:13
  32.0 0.8 %collective-permute-start.7 = (f32[64,256]{1,0:T(8,128)S(1)}, f32[64,256]{1,0:T(8,128)S(1)}, u32[]{:S(2)}, u32[]{:S(2)}) collective-permute-start(f32[64,256]{1,0:T(8,128)S(1)} %reshape.18), channel_id=1, source_target_pairs={{0,4},{4,8},{8,12},{12,0},{1,5},{5,9},{9,13},{13,1},{2,6},{6,10},{... | collective-permute-start | bytes 196616 | tf_op jit(solution)/shard_map/ppermute | solution.py:13
  32.8 2.0 %collective-permute-start.8 = (f32[64,256]{1,0:T(8,128)S(1)}, f32[64,256]{1,0:T(8,128)S(1)}, u32[]{:S(2)}, u32[]{:S(2)}) collective-permute-start(f32[64,256]{1,0:T(8,128)S(1)} %reshape.18), channel_id=1, source_target_pairs={{0,8},{4,12},{8,0},{12,4},{1,9},{5,13},{9,1},{13,5},{2,10},{6,14},... | collective-permute-start | bytes 196616 | tf_op jit(solution)/shard_map/ppermute | solution.py:13
  34.8 7.4 %all_gather.3 = bf16[256,2,768]{2,0,1:T(8,128)(2,1)S(1)} all-gather(bf16[64,2,768]{2,0,1:T(8,128)(2,1)S(1)} %bitcast.34), channel_id=1, replica_groups=mesh['groups'=2,'dp'=4,'task'=4] {'task'}, dimensions={0}, use_global_device_ids=true | all-gather | bytes 983040 | tf_op jit(solution)/shard_map/all_gather | solution.py:82
  42.2 0.9 %fusion.4 = bf16[2,768,64]{1,2,0:T(8,128)(2,1)} fusion(bf16[256,2,768]{2,0,1:T(8,128)(2,1)S(1)} %all_gather.3, bf16[2,768,64]{1,2,0:T(8,128)(2,1)S(1)} %copy-done.1, f32[64]{0:T(128)S(1)} %copy-done.2, bf16[256,256]{1,0:T(8,128)(2,1)S(1)} %copy-done, s32[]{:T(128)S(6)} %select_n.22), kind=kOutput, calls=%fused_computation.12 | convolution fusion | flops 50724864 | bytes 1212932 | tf_op jit(solution)/shard_map/asn,ca->snc/dot_general | solution.py:84
  43.2 0.7 %add_multiply_fusion = f32[64,256]{1,0:T(8,128)} fusion(f32[64,256]{1,0:T(8,128)S(1)} %collective-permute-done.8, f32[64,256]{1,0:T(8,128)S(1)} %collective-permute-done.7, f32[64,256]{1,0:T(8,128)S(1)} %collective-permute-done.6, f32[64,256]{1,0:T(8,128)S(1)} %reshape.18, pred[]{:T(512)S(6)} %eq.5), kind=kLoop, calls=%fused_computation.19 | loop fusion | flops 98304 | bytes 327681 | tf_op jit(solution)/shard_map/div | solution.py:86
  (20 shorter events, 0.3 us)
Async XLA Ops:
  0.6 41.6 %copy-start = (bf16[256,256]{1,0:T(8,128)(2,1)S(1)}, bf16[256,256]{1,0:T(8,128)(2,1)}, u32[]{:S(2)}) copy-start(bf16[256,256]{1,0:T(8,128)(2,1)} %param.9) | copy-start | bytes 393220
  0.6 8.7 %collective-permute-start = (bf16[3,768]{1,0:T(4,128)(2,1)}, bf16[3,768]{1,0:T(4,128)(2,1)S(1)}, u32[]{:S(2)}, u32[]{:S(2)}) collective-permute-start(bf16[3,768]{1,0:T(4,128)(2,1)} %param.6), channel_id=1, source_target_pairs={{0,4},{4,8},{8,12},{12,0},{1,5},{5,9},{9,13},{13,1},{2,6},{6,10},{... | collective-permute-start | bytes 13832 | tf_op jit(solution)/shard_map/ppermute | solution.py:13
  3.7 8.4 %collective-permute-start.2 = (bf16[3,768]{1,0:T(4,128)(2,1)}, bf16[3,768]{1,0:T(4,128)(2,1)S(1)}, u32[]{:S(2)}, u32[]{:S(2)}) collective-permute-start(bf16[3,768]{1,0:T(4,128)(2,1)} %param.6), channel_id=1, source_target_pairs={{0,8},{4,12},{8,0},{12,4},{1,9},{5,13},{9,1},{13,5},{2,10},{6,14},... | collective-permute-start | bytes 13832 | tf_op jit(solution)/shard_map/ppermute | solution.py:13
  6.3 5.8 %collective-permute-start.4 = (bf16[3,768]{1,0:T(4,128)(2,1)}, bf16[3,768]{1,0:T(4,128)(2,1)S(1)}, u32[]{:S(2)}, u32[]{:S(2)}) collective-permute-start(bf16[3,768]{1,0:T(4,128)(2,1)} %param.6), channel_id=1, source_target_pairs={{0,12},{4,0},{8,4},{12,8},{1,13},{5,1},{9,5},{13,9},{2,14},{6,2},{... | collective-permute-start | bytes 13832 | tf_op jit(solution)/shard_map/ppermute | solution.py:13
  7.7 15.8 %collective-permute-start.1 = (bf16[2,768,64]{1,2,0:T(8,128)(2,1)}, bf16[2,768,64]{1,2,0:T(8,128)(2,1)S(1)}, u32[]{:S(2)}, u32[]{:S(2)}) collective-permute-start(bf16[2,768,64]{1,2,0:T(8,128)(2,1)} %param.8), channel_id=1, source_target_pairs={{0,4},{4,8},{8,12},{12,0},{1,5},{5,9},{9,13},{13,1},{2,6},{6,10},{... | collective-permute-start | bytes 589832 | tf_op jit(solution)/shard_map/ppermute | solution.py:13
  8.3 16.2 %collective-permute-start.3 = (bf16[2,768,64]{1,2,0:T(8,128)(2,1)}, bf16[2,768,64]{1,2,0:T(8,128)(2,1)S(1)}, u32[]{:S(2)}, u32[]{:S(2)}) collective-permute-start(bf16[2,768,64]{1,2,0:T(8,128)(2,1)} %param.8), channel_id=1, source_target_pairs={{0,8},{4,12},{8,0},{12,4},{1,9},{5,13},{9,1},{13,5},{2,10},{6,14},... | collective-permute-start | bytes 589832 | tf_op jit(solution)/shard_map/ppermute | solution.py:13
  9.3 16.4 %collective-permute-start.5 = (bf16[2,768,64]{1,2,0:T(8,128)(2,1)}, bf16[2,768,64]{1,2,0:T(8,128)(2,1)S(1)}, u32[]{:S(2)}, u32[]{:S(2)}) collective-permute-start(bf16[2,768,64]{1,2,0:T(8,128)(2,1)} %param.8), channel_id=1, source_target_pairs={{0,12},{4,0},{8,4},{12,8},{1,13},{5,1},{9,5},{13,9},{2,14},{6,2},{... | collective-permute-start | bytes 589832 | tf_op jit(solution)/shard_map/ppermute | solution.py:13
  14.8 15.1 %all-to-all-start = ((bf16[4,2,768,64]{2,3,1,0:T(8,128)(2,1)}), bf16[4,2,768,64]{2,3,1,0:T(8,128)(2,1)S(1)}, u32[]{:S(2)}, u32[]{:S(2)}) async-start(bf16[4,2,768,64]{2,3,1,0:T(8,128)(2,1)} %broadcast_in_dim.2), calls=%async_computation | async-start | bytes 1572864 | tf_op jit(solution)/shard_map/all_to_all | solution.py:73
  18.3 3.0 %copy-start.1 = (bf16[2,768,64]{1,2,0:T(8,128)(2,1)S(1)}, bf16[2,768,64]{1,2,0:T(8,128)(2,1)}, u32[]{:S(2)}) copy-start(bf16[2,768,64]{1,2,0:T(8,128)(2,1)} %param.8) | copy-start | bytes 589828
  25.7 4.3 %copy-start.3 = (bf16[2]{0:T(256)(128)(2,1)S(1)}, bf16[2]{0:T(256)(128)(2,1)}, u32[]{:S(2)}) copy-start(bf16[2]{0:T(256)(128)(2,1)} %constant.38.clone) | copy-start | bytes 16
  26.8 15.4 %copy-start.2 = (f32[64]{0:T(128)S(1)}, f32[64]{0:T(128)}, u32[]{:S(2)}) copy-start(f32[64]{0:T(128)} %param.10) | copy-start | bytes 772
  30.7 12.5 %collective-permute-start.6 = (f32[64,256]{1,0:T(8,128)S(1)}, f32[64,256]{1,0:T(8,128)S(1)}, u32[]{:S(2)}, u32[]{:S(2)}) collective-permute-start(f32[64,256]{1,0:T(8,128)S(1)} %reshape.18), channel_id=1, source_target_pairs={{0,12},{4,0},{8,4},{12,8},{1,13},{5,1},{9,5},{13,9},{2,14},{6,2},{... | collective-permute-start | bytes 196616 | tf_op jit(solution)/shard_map/ppermute | solution.py:13
  32.0 11.2 %collective-permute-start.7 = (f32[64,256]{1,0:T(8,128)S(1)}, f32[64,256]{1,0:T(8,128)S(1)}, u32[]{:S(2)}, u32[]{:S(2)}) collective-permute-start(f32[64,256]{1,0:T(8,128)S(1)} %reshape.18), channel_id=1, source_target_pairs={{0,4},{4,8},{8,12},{12,0},{1,5},{5,9},{9,13},{13,1},{2,6},{6,10},{... | collective-permute-start | bytes 196616 | tf_op jit(solution)/shard_map/ppermute | solution.py:13
  32.8 10.4 %collective-permute-start.8 = (f32[64,256]{1,0:T(8,128)S(1)}, f32[64,256]{1,0:T(8,128)S(1)}, u32[]{:S(2)}, u32[]{:S(2)}) collective-permute-start(f32[64,256]{1,0:T(8,128)S(1)} %reshape.18), channel_id=1, source_target_pairs={{0,8},{4,12},{8,0},{12,4},{1,9},{5,13},{9,1},{13,5},{2,10},{6,14},... | collective-permute-start | bytes 196616 | tf_op jit(solution)/shard_map/ppermute | solution.py:13

commit v21 on v12

--- a/solution.py
+++ b/solution.py
@@ -48,7 +48,8 @@
         peer_coords = [shift(coords, "dp", k, n_dp) for k in range(1, n_dp)]
         task_input = lax.optimization_barrier((vectors, peer_coords))[0]
         summed = block(coords, vectors)
-        for k in range(1, n_dp):
+        order = [1, 3, 2] if n_dp == 4 else list(range(1, n_dp))
+        for k in order:
             summed = summed + block(peer_coords[k - 1], moved[k - 1])
     else:
 

time: 43.3 us -> 43.3 us (level)
  waiting for transfers between devices: 2.37 us -> 3.77 us
  starting transfers between devices: 18.4 us -> 17.1 us
    ppermute x9, waiting for transfers between devices: 0.02 us -> 2.42 us  [shift(): return lax.ppermute(x, axis, [(i, (i + k) % n) for i in range(n)])]
    ppermute x9, starting transfers between devices: 14.9 us -> 13.6 us  [shift(): return lax.ppermute(x, axis, [(i, (i + k) % n) for i in range(n)])]
    all_to_all x1, waiting for transfers between devices: 2.35 us -> 1.35 us  [per_device(): task_blocks = lax.all_to_all(copies, 'task', 0, 0, tiled=True)]
  transfers between devices with their start and end apart: 10 -> 10, of which waited for: 1 -> 3; matrix products, arithmetic and copies ran while one was open for 29% -> 29% of each run, Pallas kernels for 0% -> 0%
where the time goes in v21:
time: 43.3 us; the launch traced here: 43.1 us
  starting transfers between devices  17.1 us (39%)
  blocking collectives  7.45 us (17%)
  other arithmetic  6.12 us (14%)
  matrix products  5.83 us (13%)
  waiting for transfers between devices  3.77 us (9%)
  local copies, waits for them, and re-layouts  2.13 us (5%)
  between operations  0.73 us (2%)
    ppermute x9, starting transfers between devices, shift(): return lax.ppermute(x, axis, [(i, (i + k) % n) for i in range(n)])  13.6 us
    all_gather x1, blocking collectives, per_device(): lax.all_gather(jnp.transpose(gather_input, (2, 0, 1)), 'task', axis=0, ti...  7.45 us
    reduce_sum x1, other arithmetic, kernel_tile(): return jnp.exp(0.1 - jnp.sqrt(jnp.sum(diff * diff, axis=0) + 0.01))  4.65 us
    unnamed x4, matrix products  4.38 us
    all_to_all x1, starting transfers between devices, per_device(): task_blocks = lax.all_to_all(copies, 'task', 0, 0, tiled=True)  3.49 us
    ppermute x9, waiting for transfers between devices, shift(): return lax.ppermute(x, axis, [(i, (i + k) % n) for i in range(n)])  2.42 us
    broadcast_in_dim x1, local copies, waits for them, and re-layouts, per_device(): copies = jnp.broadcast_to(task_input[None], (n_task,) + vectors.shape)  1.87 us
    all_to_all x1, waiting for transfers between devices, per_device(): task_blocks = lax.all_to_all(copies, 'task', 0, 0, tiled=True)  1.35 us
  transfers between devices with their start and end apart: 10, of which 3 were waited for; matrix products, arithmetic and copies ran while one was open for 29% of the time, Pallas kernels for 0%

profile of v21, /device:TPU:0, one launch (start us, length us, event | category | flops | bytes accessed | tf_op | source)
XLA Modules:
  0.0 43.1 jit_solution(5332070643345993905)
XLA Ops:
  0.7 3.1 %collective-permute-start = (bf16[3,768]{1,0:T(4,128)(2,1)}, bf16[3,768]{1,0:T(4,128)(2,1)S(1)}, u32[]{:S(2)}, u32[]{:S(2)}) collective-permute-start(bf16[3,768]{1,0:T(4,128)(2,1)} %param.6), channel_id=1, source_target_pairs={{0,4},{4,8},{8,12},{12,0},{1,5},{5,9},{9,13},{13,1},{2,6},{6,10},{... | collective-permute-start | bytes 13832 | tf_op jit(solution)/shard_map/ppermute | solution.py:13
  3.7 2.1 %collective-permute-start.2 = (bf16[3,768]{1,0:T(4,128)(2,1)}, bf16[3,768]{1,0:T(4,128)(2,1)S(1)}, u32[]{:S(2)}, u32[]{:S(2)}) collective-permute-start(bf16[3,768]{1,0:T(4,128)(2,1)} %param.6), channel_id=1, source_target_pairs={{0,12},{4,0},{8,4},{12,8},{1,13},{5,1},{9,5},{13,9},{2,14},{6,2},{... | collective-permute-start | bytes 13832 | tf_op jit(solution)/shard_map/ppermute | solution.py:13
  5.8 0.9 %collective-permute-start.4 = (bf16[3,768]{1,0:T(4,128)(2,1)}, bf16[3,768]{1,0:T(4,128)(2,1)S(1)}, u32[]{:S(2)}, u32[]{:S(2)}) collective-permute-start(bf16[3,768]{1,0:T(4,128)(2,1)} %param.6), channel_id=1, source_target_pairs={{0,8},{4,12},{8,0},{12,4},{1,9},{5,13},{9,1},{13,5},{2,10},{6,14},... | collective-permute-start | bytes 13832 | tf_op jit(solution)/shard_map/ppermute | solution.py:13
  6.8 1.6 %collective-permute-start.1 = (bf16[2,768,64]{1,2,0:T(8,128)(2,1)}, bf16[2,768,64]{1,2,0:T(8,128)(2,1)S(1)}, u32[]{:S(2)}, u32[]{:S(2)}) collective-permute-start(bf16[2,768,64]{1,2,0:T(8,128)(2,1)} %param.8), channel_id=1, source_target_pairs={{0,4},{4,8},{8,12},{12,0},{1,5},{5,9},{9,13},{13,1},{2,6},{6,10},{... | collective-permute-start | bytes 589832 | tf_op jit(solution)/shard_map/ppermute | solution.py:13
  8.3 2.2 %collective-permute-start.3 = (bf16[2,768,64]{1,2,0:T(8,128)(2,1)}, bf16[2,768,64]{1,2,0:T(8,128)(2,1)S(1)}, u32[]{:S(2)}, u32[]{:S(2)}) collective-permute-start(bf16[2,768,64]{1,2,0:T(8,128)(2,1)} %param.8), channel_id=1, source_target_pairs={{0,12},{4,0},{8,4},{12,8},{1,13},{5,1},{9,5},{13,9},{2,14},{6,2},{... | collective-permute-start | bytes 589832 | tf_op jit(solution)/shard_map/ppermute | solution.py:13
  10.6 0.7 %broadcast_divide_fusion = f32[3]{0:T(128)S(1)} fusion(f32[3]{0:T(128)} %param.7), kind=kLoop, calls=%fused_computation.28 | loop fusion | flops 3 | bytes 24 | tf_op jit(solution)/shard_map/div | solution.py:37
  11.3 0.2 collective-permute-start.5
  11.4 1.4 %collective-permute-done.4 = bf16[3,768]{1,0:T(4,128)(2,1)S(1)} collective-permute-done((bf16[3,768]{1,0:T(4,128)(2,1)}, bf16[3,768]{1,0:T(4,128)(2,1)S(1)}, u32[]{:S(2)}, u32[]{:S(2)}) %collective-permute-start.4) | collective-permute-done | bytes 4640 | tf_op jit(solution)/shard_map/ppermute | solution.py:13
  12.8 1.9 %broadcast_in_dim.2 = bf16[4,2,768,64]{2,3,1,0:T(8,128)(2,1)} broadcast(bf16[2,768,64]{1,2,0:T(8,128)(2,1)} %param.8), dimensions={1,2,3} | broadcast | bytes 983040 | tf_op jit(solution)/shard_map/broadcast_in_dim | solution.py:66
  14.7 3.5 %all-to-all-start = ((bf16[4,2,768,64]{2,3,1,0:T(8,128)(2,1)}), bf16[4,2,768,64]{2,3,1,0:T(8,128)(2,1)S(1)}, u32[]{:S(2)}, u32[]{:S(2)}) async-start(bf16[4,2,768,64]{2,3,1,0:T(8,128)(2,1)} %broadcast_in_dim.2), calls=%async_computation | async-start | bytes 1572864 | tf_op jit(solution)/shard_map/all_to_all | solution.py:67
  18.3 4.7 %multiply_reduce_fusion.2 = (f32[768,768]{1,0:T(8,128)S(1)}, f32[768,768]{1,0:T(8,128)S(1)}, f32[768,768]{1,0:T(8,128)S(1)}, f32[768,768]{1,0:T(8,128)S(1)}) fusion(f32[3,768]{1,0:T(4,128)S(1)} %get-tuple-element.11, f32[3,768]{1,0:T(4,128)S(1)} %get-tuple-element.13, f32[3,768]{1,0:T(4,128)S(1)} %get-tuple-element.12, f32[3,768]{1,0:T(4,128)S(1)} %get-tuple-element.10), kind=kLoop, calls=%fused_computation.2 | loop fusion | flops 18874368 | bytes 9474048 | tf_op jit(solution)/shard_map/reduce_sum | solution.py:9
  23.0 1.1 %fusion = f32[768,128]{0,1:S(1)} fusion(bf16[768,128]{0,1:T(8,128)(2,1)S(1)} %bitcast.35, f32[768,768]{1,0:T(8,128)S(1)} %get-tuple-element.9), kind=kOutput, calls=%fused_computation.9 | convolution fusion | flops 152764416 | bytes 2949120
  24.1 1.1 %fusion.1 = f32[768,128]{0,1:S(1)} fusion(bf16[768,128]{0,1:T(8,128)(2,1)S(1)} %bitcast.41, f32[768,768]{1,0:T(8,128)S(1)} %get-tuple-element.6), kind=kOutput, calls=%fused_computation.10 | convolution fusion | flops 152764416 | bytes 2949120
  25.2 1.1 %fusion.2 = f32[768,128]{0,1:S(1)} fusion(bf16[768,128]{0,1:T(8,128)(2,1)S(1)} %bitcast.40, f32[768,768]{1,0:T(8,128)S(1)} %get-tuple-element.7), kind=kOutput, calls=%fused_computation.11 | convolution fusion | flops 152764416 | bytes 2949120
  26.3 1.0 %collective-permute-done.5 = bf16[2,768,64]{1,2,0:T(8,128)(2,1)S(1)} collective-permute-done((bf16[2,768,64]{1,2,0:T(8,128)(2,1)}, bf16[2,768,64]{1,2,0:T(8,128)(2,1)S(1)}, u32[]{:S(2)}, u32[]{:S(2)}) %collective-permute-start.5) | collective-permute-done | bytes 196640 | tf_op jit(solution)/shard_map/ppermute | solution.py:13
  27.3 1.1 %fusion.3 = f32[768,128]{0,1:S(1)} fusion(bf16[768,128]{0,1:T(8,128)(2,1)S(1)} %bitcast.42, f32[768,768]{1,0:T(8,128)S(1)} %get-tuple-element.8), kind=kOutput, calls=%fused_computation.12 | convolution fusion | flops 152764416 | bytes 2949120
  28.5 1.3 %all-to-all-done = bf16[4,2,768,64]{2,3,1,0:T(8,128)(2,1)S(1)} async-done(((bf16[4,2,768,64]{2,3,1,0:T(8,128)(2,1)}), bf16[4,2,768,64]{2,3,1,0:T(8,128)(2,1)S(1)}, u32[]{:S(2)}, u32[]{:S(2)}) %all-to-all-start) | async-done | bytes 786464 | tf_op jit(solution)/shard_map/all_to_all | solution.py:67
  29.8 0.5 %convolution_bitcast_fusion = f32[64,4,64]{2,0,1:T(8,128)S(1)} fusion(bf16[4,2,768,64]{2,3,1,0:T(8,128)(2,1)S(1)} %all-to-all-done, bf16[2,768,64]{1,2,0:T(8,128)(2,1)S(1)} %fusion.5, bf16[2]{0:T(256)(128)(2,1)S(1)} %copy-done.4), kind=kOutput, calls=%fused_computation.14 | convolution fusion | flops 50724864 | bytes 1048580 | tf_op jit(solution)/shard_map/sna,ksnb->akb/dot_general | solution.py:71
  30.6 0.6 %collective-permute-start.6 = (f32[64,256]{1,0:T(8,128)S(1)}, f32[64,256]{1,0:T(8,128)S(1)}, u32[]{:S(2)}, u32[]{:S(2)}) collective-permute-start(f32[64,256]{1,0:T(8,128)S(1)} %reshape.16), channel_id=1, source_target_pairs={{0,12},{4,0},{8,4},{12,8},{1,13},{5,1},{9,5},{13,9},{2,14},{6,2},{... | collective-permute-start | bytes 196616 | tf_op jit(solution)/shard_map/ppermute | solution.py:13
  31.2 1.4 %collective-permute-start.7 = (f32[64,256]{1,0:T(8,128)S(1)}, f32[64,256]{1,0:T(8,128)S(1)}, u32[]{:S(2)}, u32[]{:S(2)}) collective-permute-start(f32[64,256]{1,0:T(8,128)S(1)} %reshape.16), channel_id=1, source_target_pairs={{0,4},{4,8},{8,12},{12,0},{1,5},{5,9},{9,13},{13,1},{2,6},{6,10},{... | collective-permute-start | bytes 196616 | tf_op jit(solution)/shard_map/ppermute | solution.py:13
  32.6 1.4 %collective-permute-start.8 = (f32[64,256]{1,0:T(8,128)S(1)}, f32[64,256]{1,0:T(8,128)S(1)}, u32[]{:S(2)}, u32[]{:S(2)}) collective-permute-start(f32[64,256]{1,0:T(8,128)S(1)} %reshape.16), channel_id=1, source_target_pairs={{0,8},{4,12},{8,0},{12,4},{1,9},{5,13},{9,1},{13,5},{2,10},{6,14},... | collective-permute-start | bytes 196616 | tf_op jit(solution)/shard_map/ppermute | solution.py:13
  34.0 7.4 %all_gather.3 = bf16[256,2,768]{2,0,1:T(8,128)(2,1)S(1)} all-gather(bf16[64,2,768]{2,0,1:T(8,128)(2,1)S(1)} %bitcast.34), channel_id=1, replica_groups=mesh['groups'=2,'dp'=4,'task'=4] {'task'}, dimensions={0}, use_global_device_ids=true | all-gather | bytes 983040 | tf_op jit(solution)/shard_map/all_gather | solution.py:76
  41.5 0.9 %fusion.4 = bf16[2,768,64]{1,2,0:T(8,128)(2,1)} fusion(bf16[256,2,768]{2,0,1:T(8,128)(2,1)S(1)} %all_gather.3, bf16[2,768,64]{1,2,0:T(8,128)(2,1)S(1)} %copy-done.1, f32[64]{0:T(128)S(1)} %copy-done.3, bf16[256,256]{1,0:T(8,128)(2,1)S(1)} %copy-done, s32[]{:T(128)S(6)} %select_n.22), kind=kOutput, calls=%fused_computation.13 | convolution fusion | flops 50724864 | bytes 1212932 | tf_op jit(solution)/shard_map/asn,ca->snc/dot_general | solution.py:78
  42.4 0.7 %add_multiply_fusion = f32[64,256]{1,0:T(8,128)} fusion(f32[64,256]{1,0:T(8,128)S(1)} %collective-permute-done.8, f32[64,256]{1,0:T(8,128)S(1)} %collective-permute-done.7, f32[64,256]{1,0:T(8,128)S(1)} %collective-permute-done.6, f32[64,256]{1,0:T(8,128)S(1)} %reshape.16, pred[]{:T(512)S(6)} %eq.5), kind=kLoop, calls=%fused_computation.20 | loop fusion | flops 98304 | bytes 327681 | tf_op jit(solution)/shard_map/div | solution.py:80
  (21 shorter events, 0.4 us)
Async XLA Ops:
  0.6 40.9 %copy-start = (bf16[256,256]{1,0:T(8,128)(2,1)S(1)}, bf16[256,256]{1,0:T(8,128)(2,1)}, u32[]{:S(2)}) copy-start(bf16[256,256]{1,0:T(8,128)(2,1)} %param.9) | copy-start | bytes 393220
  0.6 17.6 %copy-start.2 = (bf16[3,768]{1,0:T(4,128)(2,1)S(1)}, bf16[3,768]{1,0:T(4,128)(2,1)}, u32[]{:S(2)}) copy-start(bf16[3,768]{1,0:T(4,128)(2,1)} %param.6) | copy-start | bytes 13828
  0.7 10.6 %collective-permute-start = (bf16[3,768]{1,0:T(4,128)(2,1)}, bf16[3,768]{1,0:T(4,128)(2,1)S(1)}, u32[]{:S(2)}, u32[]{:S(2)}) collective-permute-start(bf16[3,768]{1,0:T(4,128)(2,1)} %param.6), channel_id=1, source_target_pairs={{0,4},{4,8},{8,12},{12,0},{1,5},{5,9},{9,13},{13,1},{2,6},{6,10},{... | collective-permute-start | bytes 13832 | tf_op jit(solution)/shard_map/ppermute | solution.py:13
  3.7 7.7 %collective-permute-start.2 = (bf16[3,768]{1,0:T(4,128)(2,1)}, bf16[3,768]{1,0:T(4,128)(2,1)S(1)}, u32[]{:S(2)}, u32[]{:S(2)}) collective-permute-start(bf16[3,768]{1,0:T(4,128)(2,1)} %param.6), channel_id=1, source_target_pairs={{0,12},{4,0},{8,4},{12,8},{1,13},{5,1},{9,5},{13,9},{2,14},{6,2},{... | collective-permute-start | bytes 13832 | tf_op jit(solution)/shard_map/ppermute | solution.py:13
  5.8 7.0 %collective-permute-start.4 = (bf16[3,768]{1,0:T(4,128)(2,1)}, bf16[3,768]{1,0:T(4,128)(2,1)S(1)}, u32[]{:S(2)}, u32[]{:S(2)}) collective-permute-start(bf16[3,768]{1,0:T(4,128)(2,1)} %param.6), channel_id=1, source_target_pairs={{0,8},{4,12},{8,0},{12,4},{1,9},{5,13},{9,1},{13,5},{2,10},{6,14},... | collective-permute-start | bytes 13832 | tf_op jit(solution)/shard_map/ppermute | solution.py:13
  6.8 17.3 %collective-permute-start.1 = (bf16[2,768,64]{1,2,0:T(8,128)(2,1)}, bf16[2,768,64]{1,2,0:T(8,128)(2,1)S(1)}, u32[]{:S(2)}, u32[]{:S(2)}) collective-permute-start(bf16[2,768,64]{1,2,0:T(8,128)(2,1)} %param.8), channel_id=1, source_target_pairs={{0,4},{4,8},{8,12},{12,0},{1,5},{5,9},{9,13},{13,1},{2,6},{6,10},{... | collective-permute-start | bytes 589832 | tf_op jit(solution)/shard_map/ppermute | solution.py:13
  8.3 16.8 %collective-permute-start.3 = (bf16[2,768,64]{1,2,0:T(8,128)(2,1)}, bf16[2,768,64]{1,2,0:T(8,128)(2,1)S(1)}, u32[]{:S(2)}, u32[]{:S(2)}) collective-permute-start(bf16[2,768,64]{1,2,0:T(8,128)(2,1)} %param.8), channel_id=1, source_target_pairs={{0,12},{4,0},{8,4},{12,8},{1,13},{5,1},{9,5},{13,9},{2,14},{6,2},{... | collective-permute-start | bytes 589832 | tf_op jit(solution)/shard_map/ppermute | solution.py:13
  11.3 16.0 %collective-permute-start.5 = (bf16[2,768,64]{1,2,0:T(8,128)(2,1)}, bf16[2,768,64]{1,2,0:T(8,128)(2,1)S(1)}, u32[]{:S(2)}, u32[]{:S(2)}) collective-permute-start(bf16[2,768,64]{1,2,0:T(8,128)(2,1)} %param.8), channel_id=1, source_target_pairs={{0,8},{4,12},{8,0},{12,4},{1,9},{5,13},{9,1},{13,5},{2,10},{6,14},... | collective-permute-start | bytes 589832 | tf_op jit(solution)/shard_map/ppermute | solution.py:13
  14.7 15.1 %all-to-all-start = ((bf16[4,2,768,64]{2,3,1,0:T(8,128)(2,1)}), bf16[4,2,768,64]{2,3,1,0:T(8,128)(2,1)S(1)}, u32[]{:S(2)}, u32[]{:S(2)}) async-start(bf16[4,2,768,64]{2,3,1,0:T(8,128)(2,1)} %broadcast_in_dim.2), calls=%async_computation | async-start | bytes 1572864 | tf_op jit(solution)/shard_map/all_to_all | solution.py:67
  18.3 4.7 %copy-start.1 = (bf16[2,768,64]{1,2,0:T(8,128)(2,1)S(1)}, bf16[2,768,64]{1,2,0:T(8,128)(2,1)}, u32[]{:S(2)}) copy-start(bf16[2,768,64]{1,2,0:T(8,128)(2,1)} %param.8) | copy-start | bytes 589828
  27.3 2.5 %copy-start.4 = (bf16[2]{0:T(256)(128)(2,1)S(1)}, bf16[2]{0:T(256)(128)(2,1)}, u32[]{:S(2)}) copy-start(bf16[2]{0:T(256)(128)(2,1)} %constant.38.clone) | copy-start | bytes 16
  28.4 13.1 %copy-start.3 = (f32[64]{0:T(128)S(1)}, f32[64]{0:T(128)}, u32[]{:S(2)}) copy-start(f32[64]{0:T(128)} %param.10) | copy-start | bytes 772
  30.6 11.8 %collective-permute-start.6 = (f32[64,256]{1,0:T(8,128)S(1)}, f32[64,256]{1,0:T(8,128)S(1)}, u32[]{:S(2)}, u32[]{:S(2)}) collective-permute-start(f32[64,256]{1,0:T(8,128)S(1)} %reshape.16), channel_id=1, source_target_pairs={{0,12},{4,0},{8,4},{12,8},{1,13},{5,1},{9,5},{13,9},{2,14},{6,2},{... | collective-permute-start | bytes 196616 | tf_op jit(solution)/shard_map/ppermute | solution.py:13
  31.2 11.2 %collective-permute-start.7 = (f32[64,256]{1,0:T(8,128)S(1)}, f32[64,256]{1,0:T(8,128)S(1)}, u32[]{:S(2)}, u32[]{:S(2)}) collective-permute-start(f32[64,256]{1,0:T(8,128)S(1)} %reshape.16), channel_id=1, source_target_pairs={{0,4},{4,8},{8,12},{12,0},{1,5},{5,9},{9,13},{13,1},{2,6},{6,10},{... | collective-permute-start | bytes 196616 | tf_op jit(solution)/shard_map/ppermute | solution.py:13
  32.6 9.8 %collective-permute-start.8 = (f32[64,256]{1,0:T(8,128)S(1)}, f32[64,256]{1,0:T(8,128)S(1)}, u32[]{:S(2)}, u32[]{:S(2)}) collective-permute-start(f32[64,256]{1,0:T(8,128)S(1)} %reshape.16), channel_id=1, source_target_pairs={{0,8},{4,12},{8,0},{12,4},{1,9},{5,13},{9,1},{13,5},{2,10},{6,14},... | collective-permute-start | bytes 196616 | tf_op jit(solution)/shard_map/ppermute | solution.py:13

commit v22 on v21

--- a/solution.py
+++ b/solution.py
@@ -45,7 +45,11 @@
     task_input = vectors
     if n_dp <= 4:
         moved = [shift(vectors, "dp", k, n_dp) for k in range(1, n_dp)]
-        peer_coords = [shift(coords, "dp", k, n_dp) for k in range(1, n_dp)]
+        if n_dp == 4:
+            first = shift(coords, "dp", 1, n_dp)
+            peer_coords = [first, shift(first, "dp", 1, n_dp), shift(coords, "dp", 3, n_dp)]
+        else:
+            peer_coords = [shift(coords, "dp", k, n_dp) for k in range(1, n_dp)]
         task_input = lax.optimization_barrier((vectors, peer_coords))[0]
         summed = block(coords, vectors)
         order = [1, 3, 2] if n_dp == 4 else list(range(1, n_dp))

time: 43.3 us -> 55.1 us (1.27)
  waiting for transfers between devices: 3.77 us -> 14.2 us
  starting transfers between devices: 17.1 us -> 18.3 us
    ppermute x9, waiting for transfers between devices: 2.42 us -> 11.9 us  [shift(): return lax.ppermute(x, axis, [(i, (i + k) % n) for i in range(n)])]
    ppermute x9, starting transfers between devices: 13.6 us -> 14.8 us  [shift(): return lax.ppermute(x, axis, [(i, (i + k) % n) for i in range(n)])]
    all_to_all x1, waiting for transfers between devices: 1.35 us -> 2.32 us  [per_device(): task_blocks = lax.all_to_all(copies, 'task', 0, 0, tiled=True)]
  transfers between devices with their start and end apart: 10 -> 10, of which waited for: 3 -> 2; matrix products, arithmetic and copies ran while one was open for 29% -> 23% of each run, Pallas kernels for 0% -> 0%
where the time goes in v22:
time: 55.1 us; the launch traced here: 54.8 us
  starting transfers between devices  18.3 us (33%)
  waiting for transfers between devices  14.2 us (26%)
  blocking collectives  7.45 us (14%)
  other arithmetic  6.12 us (11%)
  matrix products  5.86 us (11%)
  local copies, waits for them, and re-layouts  2.13 us (4%)
  between operations  0.74 us (1%)
    ppermute x9, starting transfers between devices, shift(): return lax.ppermute(x, axis, [(i, (i + k) % n) for i in range(n)])  14.8 us
    ppermute x9, waiting for transfers between devices, shift(): return lax.ppermute(x, axis, [(i, (i + k) % n) for i in range(n)])  11.9 us
    all_gather x1, blocking collectives, per_device(): lax.all_gather(jnp.transpose(gather_input, (2, 0, 1)), 'task', axis=0, ti...  7.45 us
    reduce_sum x1, other arithmetic, kernel_tile(): return jnp.exp(0.1 - jnp.sqrt(jnp.sum(diff * diff, axis=0) + 0.01))  4.65 us
    unnamed x4, matrix products  4.41 us
    all_to_all x1, starting transfers between devices, per_device(): task_blocks = lax.all_to_all(copies, 'task', 0, 0, tiled=True)  3.49 us
    all_to_all x1, waiting for transfers between devices, per_device(): task_blocks = lax.all_to_all(copies, 'task', 0, 0, tiled=True)  2.32 us
    broadcast_in_dim x1, local copies, waits for them, and re-layouts, per_device(): copies = jnp.broadcast_to(task_input[None], (n_task,) + vectors.shape)  1.87 us
  transfers between devices with their start and end apart: 10, of which 2 were waited for; matrix products, arithmetic and copies ran while one was open for 23% of the time, Pallas kernels for 0%

profile of v22, /device:TPU:0, one launch (start us, length us, event | category | flops | bytes accessed | tf_op | source)
XLA Modules:
  0.0 54.8 jit_solution(17863950669732573691)
XLA Ops:
  0.7 3.1 %collective-permute-start = (bf16[3,768]{1,0:T(4,128)(2,1)}, bf16[3,768]{1,0:T(4,128)(2,1)S(1)}, u32[]{:S(2)}, u32[]{:S(2)}) collective-permute-start(bf16[3,768]{1,0:T(4,128)(2,1)} %param.6), channel_id=1, source_target_pairs={{0,4},{4,8},{8,12},{12,0},{1,5},{5,9},{9,13},{13,1},{2,6},{6,10},{... | collective-permute-start | bytes 13832 | tf_op jit(solution)/shard_map/ppermute | solution.py:13
  3.7 2.1 %collective-permute-start.2 = (bf16[3,768]{1,0:T(4,128)(2,1)}, bf16[3,768]{1,0:T(4,128)(2,1)S(1)}, u32[]{:S(2)}, u32[]{:S(2)}) collective-permute-start(bf16[3,768]{1,0:T(4,128)(2,1)} %param.6), channel_id=1, source_target_pairs={{0,12},{4,0},{8,4},{12,8},{1,13},{5,1},{9,5},{13,9},{2,14},{6,2},{... | collective-permute-start | bytes 13832 | tf_op jit(solution)/shard_map/ppermute | solution.py:13
  5.8 3.8 %collective-permute-start.3 = (bf16[2,768,64]{1,2,0:T(8,128)(2,1)}, bf16[2,768,64]{1,2,0:T(8,128)(2,1)S(1)}, u32[]{:S(2)}, u32[]{:S(2)}) collective-permute-start(bf16[2,768,64]{1,2,0:T(8,128)(2,1)} %param.8), channel_id=1, source_target_pairs={{0,12},{4,0},{8,4},{12,8},{1,13},{5,1},{9,5},{13,9},{2,14},{6,2},{... | collective-permute-start | bytes 589832 | tf_op jit(solution)/shard_map/ppermute | solution.py:13
  9.7 0.7 %collective-permute-start.4 = (bf16[3,768]{1,0:T(4,128)(2,1)S(1)}, bf16[3,768]{1,0:T(4,128)(2,1)S(1)}, u32[]{:S(2)}, u32[]{:S(2)}) collective-permute-start(bf16[3,768]{1,0:T(4,128)(2,1)S(1)} %collective-permute-done), channel_id=1, source_target_pairs={{0,4},{4,8},{8,12},{12,0},{1,5},{5,9},{9,13},{13,1},{2,6},{6,10},{... | collective-permute-start | bytes 13832 | tf_op jit(solution)/shard_map/ppermute | solution.py:13
  10.4 0.7 %broadcast_divide_fusion = f32[3]{0:T(128)S(1)} fusion(f32[3]{0:T(128)} %param.7), kind=kLoop, calls=%fused_computation.28 | loop fusion | flops 3 | bytes 24 | tf_op jit(solution)/shard_map/div | solution.py:37
  11.0 11.9 %collective-permute-done.4 = bf16[3,768]{1,0:T(4,128)(2,1)S(1)} collective-permute-done((bf16[3,768]{1,0:T(4,128)(2,1)S(1)}, bf16[3,768]{1,0:T(4,128)(2,1)S(1)}, u32[]{:S(2)}, u32[]{:S(2)}) %collective-permute-start.4) | collective-permute-done | bytes 4640 | tf_op jit(solution)/shard_map/ppermute | solution.py:13
  22.9 1.9 %broadcast_in_dim.2 = bf16[4,2,768,64]{2,3,1,0:T(8,128)(2,1)} broadcast(bf16[2,768,64]{1,2,0:T(8,128)(2,1)} %param.8), dimensions={1,2,3} | broadcast | bytes 983040 | tf_op jit(solution)/shard_map/broadcast_in_dim | solution.py:70
  24.8 3.5 %all-to-all-start = ((bf16[4,2,768,64]{2,3,1,0:T(8,128)(2,1)}), bf16[4,2,768,64]{2,3,1,0:T(8,128)(2,1)S(1)}, u32[]{:S(2)}, u32[]{:S(2)}) async-start(bf16[4,2,768,64]{2,3,1,0:T(8,128)(2,1)} %broadcast_in_dim.2), calls=%async_computation | async-start | bytes 1572864 | tf_op jit(solution)/shard_map/all_to_all | solution.py:71
  28.3 0.1 convert_multiply_fusion
  28.4 4.7 %multiply_reduce_fusion.2 = (f32[768,768]{1,0:T(8,128)S(1)}, f32[768,768]{1,0:T(8,128)S(1)}, f32[768,768]{1,0:T(8,128)S(1)}, f32[768,768]{1,0:T(8,128)S(1)}) fusion(f32[3,768]{1,0:T(4,128)S(1)} %get-tuple-element.11, f32[3,768]{1,0:T(4,128)S(1)} %get-tuple-element.13, f32[3,768]{1,0:T(4,128)S(1)} %get-tuple-element.12, f32[3,768]{1,0:T(4,128)S(1)} %get-tuple-element.10), kind=kLoop, calls=%fused_computation.2 | loop fusion | flops 18874368 | bytes 9474048 | tf_op jit(solution)/shard_map/reduce_sum | solution.py:9
  33.0 1.1 %fusion = f32[768,128]{0,1:S(1)} fusion(bf16[768,128]{0,1:T(8,128)(2,1)S(1)} %bitcast.35, f32[768,768]{1,0:T(8,128)S(1)} %get-tuple-element.9), kind=kOutput, calls=%fused_computation.9 | convolution fusion | flops 152764416 | bytes 2949120
  34.1 1.1 %fusion.1 = f32[768,128]{0,1:S(1)} fusion(bf16[768,128]{0,1:T(8,128)(2,1)S(1)} %bitcast.42, f32[768,768]{1,0:T(8,128)S(1)} %get-tuple-element.6), kind=kOutput, calls=%fused_computation.10 | convolution fusion | flops 152764416 | bytes 2949120
  35.2 1.1 %fusion.2 = f32[768,128]{0,1:S(1)} fusion(bf16[768,128]{0,1:T(8,128)(2,1)S(1)} %bitcast.41, f32[768,768]{1,0:T(8,128)S(1)} %get-tuple-element.7), kind=kOutput, calls=%fused_computation.11 | convolution fusion | flops 152764416 | bytes 2949120
  36.4 1.1 %fusion.3 = f32[768,128]{0,1:S(1)} fusion(bf16[768,128]{0,1:T(8,128)(2,1)S(1)} %bitcast.40, f32[768,768]{1,0:T(8,128)S(1)} %get-tuple-element.8), kind=kOutput, calls=%fused_computation.12 | convolution fusion | flops 152764416 | bytes 2949120
  37.5 0.1 fusion.5
  37.6 2.3 %all-to-all-done = bf16[4,2,768,64]{2,3,1,0:T(8,128)(2,1)S(1)} async-done(((bf16[4,2,768,64]{2,3,1,0:T(8,128)(2,1)}), bf16[4,2,768,64]{2,3,1,0:T(8,128)(2,1)S(1)}, u32[]{:S(2)}, u32[]{:S(2)}) %all-to-all-start) | async-done | bytes 786464 | tf_op jit(solution)/shard_map/all_to_all | solution.py:71
  39.9 0.5 convolution_bitcast_fusion
  40.4 0.1 copy.9
  40.5 0.1 reshape.16
  40.7 2.0 %collective-permute-start.7 = (f32[64,256]{1,0:T(8,128)S(1)}, f32[64,256]{1,0:T(8,128)S(1)}, u32[]{:S(2)}, u32[]{:S(2)}) collective-permute-start(f32[64,256]{1,0:T(8,128)S(1)} %reshape.16), channel_id=1, source_target_pairs={{0,4},{4,8},{8,12},{12,0},{1,5},{5,9},{9,13},{13,1},{2,6},{6,10},{... | collective-permute-start | bytes 196616 | tf_op jit(solution)/shard_map/ppermute | solution.py:13
  42.7 3.1 %collective-permute-start.8 = (f32[64,256]{1,0:T(8,128)S(1)}, f32[64,256]{1,0:T(8,128)S(1)}, u32[]{:S(2)}, u32[]{:S(2)}) collective-permute-start(f32[64,256]{1,0:T(8,128)S(1)} %reshape.16), channel_id=1, source_target_pairs={{0,8},{4,12},{8,0},{12,4},{1,9},{5,13},{9,1},{13,5},{2,10},{6,14},... | collective-permute-start | bytes 196616 | tf_op jit(solution)/shard_map/ppermute | solution.py:13
  45.8 7.4 %all_gather.3 = bf16[256,2,768]{2,0,1:T(8,128)(2,1)S(1)} all-gather(bf16[64,2,768]{2,0,1:T(8,128)(2,1)S(1)} %bitcast.34), channel_id=1, replica_groups=mesh['groups'=2,'dp'=4,'task'=4] {'task'}, dimensions={0}, use_global_device_ids=true | all-gather | bytes 983040 | tf_op jit(solution)/shard_map/all_gather | solution.py:80
  53.2 0.9 %fusion.4 = bf16[2,768,64]{1,2,0:T(8,128)(2,1)} fusion(bf16[256,2,768]{2,0,1:T(8,128)(2,1)S(1)} %all_gather.3, bf16[2,768,64]{1,2,0:T(8,128)(2,1)S(1)} %copy-done.1, f32[64]{0:T(128)S(1)} %copy-done.3, bf16[256,256]{1,0:T(8,128)(2,1)S(1)} %copy-done, s32[]{:T(128)S(6)} %select_n.22), kind=kOutput, calls=%fused_computation.13 | convolution fusion | flops 50724864 | bytes 1212932 | tf_op jit(solution)/shard_map/asn,ca->snc/dot_general | solution.py:82
  54.2 0.7 %add_multiply_fusion = f32[64,256]{1,0:T(8,128)} fusion(f32[64,256]{1,0:T(8,128)S(1)} %collective-permute-done.8, f32[64,256]{1,0:T(8,128)S(1)} %collective-permute-done.7, f32[64,256]{1,0:T(8,128)S(1)} %collective-permute-done.6, f32[64,256]{1,0:T(8,128)S(1)} %reshape.16, pred[]{:T(512)S(6)} %eq.5), kind=kLoop, calls=%fused_computation.20 | loop fusion | flops 98304 | bytes 327681 | tf_op jit(solution)/shard_map/div | solution.py:84
  (21 shorter events, 0.1 us)
Async XLA Ops:
  0.6 52.6 %copy-start = (bf16[256,256]{1,0:T(8,128)(2,1)S(1)}, bf16[256,256]{1,0:T(8,128)(2,1)}, u32[]{:S(2)}) copy-start(bf16[256,256]{1,0:T(8,128)(2,1)} %param.9) | copy-start | bytes 393220
  0.6 27.6 %copy-start.2 = (bf16[3,768]{1,0:T(4,128)(2,1)S(1)}, bf16[3,768]{1,0:T(4,128)(2,1)}, u32[]{:S(2)}) copy-start(bf16[3,768]{1,0:T(4,128)(2,1)} %param.6) | copy-start | bytes 13828
  0.7 9.0 %collective-permute-start = (bf16[3,768]{1,0:T(4,128)(2,1)}, bf16[3,768]{1,0:T(4,128)(2,1)S(1)}, u32[]{:S(2)}, u32[]{:S(2)}) collective-permute-start(bf16[3,768]{1,0:T(4,128)(2,1)} %param.6), channel_id=1, source_target_pairs={{0,4},{4,8},{8,12},{12,0},{1,5},{5,9},{9,13},{13,1},{2,6},{6,10},{... | collective-permute-start | bytes 13832 | tf_op jit(solution)/shard_map/ppermute | solution.py:13
  3.7 7.3 %collective-permute-start.2 = (bf16[3,768]{1,0:T(4,128)(2,1)}, bf16[3,768]{1,0:T(4,128)(2,1)S(1)}, u32[]{:S(2)}, u32[]{:S(2)}) collective-permute-start(bf16[3,768]{1,0:T(4,128)(2,1)} %param.6), channel_id=1, source_target_pairs={{0,12},{4,0},{8,4},{12,8},{1,13},{5,1},{9,5},{13,9},{2,14},{6,2},{... | collective-permute-start | bytes 13832 | tf_op jit(solution)/shard_map/ppermute | solution.py:13
  5.8 28.3 %collective-permute-start.1 = (bf16[2,768,64]{1,2,0:T(8,128)(2,1)}, bf16[2,768,64]{1,2,0:T(8,128)(2,1)S(1)}, u32[]{:S(2)}, u32[]{:S(2)}) collective-permute-start(bf16[2,768,64]{1,2,0:T(8,128)(2,1)} %param.8), channel_id=1, source_target_pairs={{0,4},{4,8},{8,12},{12,0},{1,5},{5,9},{9,13},{13,1},{2,6},{6,10},{... | collective-permute-start | bytes 589832 | tf_op jit(solution)/shard_map/ppermute | solution.py:13
  5.8 29.4 %collective-permute-start.3 = (bf16[2,768,64]{1,2,0:T(8,128)(2,1)}, bf16[2,768,64]{1,2,0:T(8,128)(2,1)S(1)}, u32[]{:S(2)}, u32[]{:S(2)}) collective-permute-start(bf16[2,768,64]{1,2,0:T(8,128)(2,1)} %param.8), channel_id=1, source_target_pairs={{0,12},{4,0},{8,4},{12,8},{1,13},{5,1},{9,5},{13,9},{2,14},{6,2},{... | collective-permute-start | bytes 589832 | tf_op jit(solution)/shard_map/ppermute | solution.py:13
  9.6 26.7 %collective-permute-start.5 = (bf16[2,768,64]{1,2,0:T(8,128)(2,1)}, bf16[2,768,64]{1,2,0:T(8,128)(2,1)S(1)}, u32[]{:S(2)}, u32[]{:S(2)}) collective-permute-start(bf16[2,768,64]{1,2,0:T(8,128)(2,1)} %param.8), channel_id=1, source_target_pairs={{0,8},{4,12},{8,0},{12,4},{1,9},{5,13},{9,1},{13,5},{2,10},{6,14},... | collective-permute-start | bytes 589832 | tf_op jit(solution)/shard_map/ppermute | solution.py:13
  9.7 13.2 %collective-permute-start.4 = (bf16[3,768]{1,0:T(4,128)(2,1)S(1)}, bf16[3,768]{1,0:T(4,128)(2,1)S(1)}, u32[]{:S(2)}, u32[]{:S(2)}) collective-permute-start(bf16[3,768]{1,0:T(4,128)(2,1)S(1)} %collective-permute-done), channel_id=1, source_target_pairs={{0,4},{4,8},{8,12},{12,0},{1,5},{5,9},{9,13},{13,1},{2,6},{6,10},{... | collective-permute-start | bytes 13832 | tf_op jit(solution)/shard_map/ppermute | solution.py:13
  24.8 15.1 %all-to-all-start = ((bf16[4,2,768,64]{2,3,1,0:T(8,128)(2,1)}), bf16[4,2,768,64]{2,3,1,0:T(8,128)(2,1)S(1)}, u32[]{:S(2)}, u32[]{:S(2)}) async-start(bf16[4,2,768,64]{2,3,1,0:T(8,128)(2,1)} %broadcast_in_dim.2), calls=%async_computation | async-start | bytes 1572864 | tf_op jit(solution)/shard_map/all_to_all | solution.py:71
  28.4 4.7 %copy-start.1 = (bf16[2,768,64]{1,2,0:T(8,128)(2,1)S(1)}, bf16[2,768,64]{1,2,0:T(8,128)(2,1)}, u32[]{:S(2)}) copy-start(bf16[2,768,64]{1,2,0:T(8,128)(2,1)} %param.8) | copy-start | bytes 589828
  36.4 3.5 %copy-start.4 = (bf16[2]{0:T(256)(128)(2,1)S(1)}, bf16[2]{0:T(256)(128)(2,1)}, u32[]{:S(2)}) copy-start(bf16[2]{0:T(256)(128)(2,1)} %constant.38.clone) | copy-start | bytes 16
  37.5 15.8 %copy-start.3 = (f32[64]{0:T(128)S(1)}, f32[64]{0:T(128)}, u32[]{:S(2)}) copy-start(f32[64]{0:T(128)} %param.10) | copy-start | bytes 772
  40.6 13.5 %collective-permute-start.6 = (f32[64,256]{1,0:T(8,128)S(1)}, f32[64,256]{1,0:T(8,128)S(1)}, u32[]{:S(2)}, u32[]{:S(2)}) collective-permute-start(f32[64,256]{1,0:T(8,128)S(1)} %reshape.16), channel_id=1, source_target_pairs={{0,12},{4,0},{8,4},{12,8},{1,13},{5,1},{9,5},{13,9},{2,14},{6,2},{... | collective-permute-start | bytes 196616 | tf_op jit(solution)/shard_map/ppermute | solution.py:13
  40.7 13.5 %collective-permute-start.7 = (f32[64,256]{1,0:T(8,128)S(1)}, f32[64,256]{1,0:T(8,128)S(1)}, u32[]{:S(2)}, u32[]{:S(2)}) collective-permute-start(f32[64,256]{1,0:T(8,128)S(1)} %reshape.16), channel_id=1, source_target_pairs={{0,4},{4,8},{8,12},{12,0},{1,5},{5,9},{9,13},{13,1},{2,6},{6,10},{... | collective-permute-start | bytes 196616 | tf_op jit(solution)/shard_map/ppermute | solution.py:13
  42.7 11.5 %collective-permute-start.8 = (f32[64,256]{1,0:T(8,128)S(1)}, f32[64,256]{1,0:T(8,128)S(1)}, u32[]{:S(2)}, u32[]{:S(2)}) collective-permute-start(f32[64,256]{1,0:T(8,128)S(1)} %reshape.16), channel_id=1, source_target_pairs={{0,8},{4,12},{8,0},{12,4},{1,9},{5,13},{9,1},{13,5},{2,10},{6,14},... | collective-permute-start | bytes 196616 | tf_op jit(solution)/shard_map/ppermute | solution.py:13

commit v23 on v14

--- a/solution.py
+++ b/solution.py
@@ -45,7 +45,8 @@
         peer_coords = [shift(coords, "dp", k, n_dp) for k in range(1, n_dp)]
         task_input = lax.optimization_barrier((vectors, peer_coords))[0]
         summed = block(coords, vectors)
-        for k in range(1, n_dp):
+        order = [1, 3, 2] if n_dp == 4 else list(range(1, n_dp))
+        for k in order:
             summed = summed + block(peer_coords[k - 1], moved[k - 1])
     else:
 

time: 43.7 us -> 44.3 us (1.014)
  waiting for transfers between devices: 2.37 us -> 3.77 us
  starting transfers between devices: 18.8 us -> 18 us
    ppermute x6, waiting for transfers between devices: 0.02 us -> 2.41 us  [shift(): return lax.ppermute(x, axis, [(i, (i + k) % n) for i in range(n)])]
    all_to_all x1, waiting for transfers between devices: 2.35 us -> 1.35 us  [per_device(): task_blocks = lax.all_to_all(copies, 'task', 0, 0, tiled=True)]
    ppermute x6, starting transfers between devices: 10.8 us -> 10.1 us  [shift(): return lax.ppermute(x, axis, [(i, (i + k) % n) for i in range(n)])]
  transfers between devices with their start and end apart: 10 -> 10, of which waited for: 1 -> 3; matrix products, arithmetic and copies ran while one was open for 29% -> 29% of each run, Pallas kernels for 0% -> 0%
where the time goes in v23:
time: 44.3 us; the launch traced here: 44.1 us
  starting transfers between devices  18 us (41%)
  blocking collectives  7.45 us (17%)
  other arithmetic  6.12 us (14%)
  matrix products  5.83 us (13%)
  waiting for transfers between devices  3.77 us (9%)
  local copies, waits for them, and re-layouts  2.13 us (5%)
  between operations  0.73 us (2%)
    ppermute x6, starting transfers between devices, shift(): return lax.ppermute(x, axis, [(i, (i + k) % n) for i in range(n)])  10.1 us
    all_gather x1, blocking collectives, per_device(): lax.all_gather(jnp.transpose(gather_input, (2, 0, 1)), 'task', axis=0, ti...  7.45 us
    reduce_sum x1, other arithmetic, kernel_tile(): return jnp.exp(0.1 - jnp.sqrt(jnp.sum(diff * diff, axis=0) + 0.01))  4.65 us
    ppermute x3, starting transfers between devices, sum_over(): lax.ppermute(x, axis, [(i, i ^ k) for i in range(n)])  4.43 us
    unnamed x4, matrix products  4.38 us
    all_to_all x1, starting transfers between devices, per_device(): task_blocks = lax.all_to_all(copies, 'task', 0, 0, tiled=True)  3.49 us
    ppermute x6, waiting for transfers between devices, shift(): return lax.ppermute(x, axis, [(i, (i + k) % n) for i in range(n)])  2.41 us
    broadcast_in_dim x1, local copies, waits for them, and re-layouts, per_device(): copies = jnp.broadcast_to(task_input[None], (n_task,) + vectors.shape)  1.87 us
  transfers between devices with their start and end apart: 10, of which 3 were waited for; matrix products, arithmetic and copies ran while one was open for 29% of the time, Pallas kernels for 0%

profile of v23, /device:TPU:0, one launch (start us, length us, event | category | flops | bytes accessed | tf_op | source)
XLA Modules:
  0.0 44.1 jit_solution(18187066724206249752)
XLA Ops:
  0.7 3.1 %collective-permute-start = (bf16[3,768]{1,0:T(4,128)(2,1)}, bf16[3,768]{1,0:T(4,128)(2,1)S(1)}, u32[]{:S(2)}, u32[]{:S(2)}) collective-permute-start(bf16[3,768]{1,0:T(4,128)(2,1)} %param.6), channel_id=1, source_target_pairs={{0,4},{4,8},{8,12},{12,0},{1,5},{5,9},{9,13},{13,1},{2,6},{6,10},{... | collective-permute-start | bytes 13832 | tf_op jit(solution)/shard_map/ppermute | solution.py:13
  3.7 2.1 %collective-permute-start.2 = (bf16[3,768]{1,0:T(4,128)(2,1)}, bf16[3,768]{1,0:T(4,128)(2,1)S(1)}, u32[]{:S(2)}, u32[]{:S(2)}) collective-permute-start(bf16[3,768]{1,0:T(4,128)(2,1)} %param.6), channel_id=1, source_target_pairs={{0,12},{4,0},{8,4},{12,8},{1,13},{5,1},{9,5},{13,9},{2,14},{6,2},{... | collective-permute-start | bytes 13832 | tf_op jit(solution)/shard_map/ppermute | solution.py:13
  5.8 0.9 %collective-permute-start.4 = (bf16[3,768]{1,0:T(4,128)(2,1)}, bf16[3,768]{1,0:T(4,128)(2,1)S(1)}, u32[]{:S(2)}, u32[]{:S(2)}) collective-permute-start(bf16[3,768]{1,0:T(4,128)(2,1)} %param.6), channel_id=1, source_target_pairs={{0,8},{4,12},{8,0},{12,4},{1,9},{5,13},{9,1},{13,5},{2,10},{6,14},... | collective-permute-start | bytes 13832 | tf_op jit(solution)/shard_map/ppermute | solution.py:13
  6.8 1.6 %collective-permute-start.1 = (bf16[2,768,64]{1,2,0:T(8,128)(2,1)}, bf16[2,768,64]{1,2,0:T(8,128)(2,1)S(1)}, u32[]{:S(2)}, u32[]{:S(2)}) collective-permute-start(bf16[2,768,64]{1,2,0:T(8,128)(2,1)} %param.8), channel_id=1, source_target_pairs={{0,4},{4,8},{8,12},{12,0},{1,5},{5,9},{9,13},{13,1},{2,6},{6,10},{... | collective-permute-start | bytes 589832 | tf_op jit(solution)/shard_map/ppermute | solution.py:13
  8.3 2.2 %collective-permute-start.3 = (bf16[2,768,64]{1,2,0:T(8,128)(2,1)}, bf16[2,768,64]{1,2,0:T(8,128)(2,1)S(1)}, u32[]{:S(2)}, u32[]{:S(2)}) collective-permute-start(bf16[2,768,64]{1,2,0:T(8,128)(2,1)} %param.8), channel_id=1, source_target_pairs={{0,12},{4,0},{8,4},{12,8},{1,13},{5,1},{9,5},{13,9},{2,14},{6,2},{... | collective-permute-start | bytes 589832 | tf_op jit(solution)/shard_map/ppermute | solution.py:13
  10.6 0.7 %broadcast_divide_fusion = f32[3]{0:T(128)S(1)} fusion(f32[3]{0:T(128)} %param.7), kind=kLoop, calls=%fused_computation.28 | loop fusion | flops 3 | bytes 24 | tf_op jit(solution)/shard_map/div | solution.py:34
  11.3 0.2 collective-permute-start.5
  11.4 1.4 %collective-permute-done.4 = bf16[3,768]{1,0:T(4,128)(2,1)S(1)} collective-permute-done((bf16[3,768]{1,0:T(4,128)(2,1)}, bf16[3,768]{1,0:T(4,128)(2,1)S(1)}, u32[]{:S(2)}, u32[]{:S(2)}) %collective-permute-start.4) | collective-permute-done | bytes 4640 | tf_op jit(solution)/shard_map/ppermute | solution.py:13
  12.8 1.9 %broadcast_in_dim.2 = bf16[4,2,768,64]{2,3,1,0:T(8,128)(2,1)} broadcast(bf16[2,768,64]{1,2,0:T(8,128)(2,1)} %param.8), dimensions={1,2,3} | broadcast | bytes 983040 | tf_op jit(solution)/shard_map/broadcast_in_dim | solution.py:63
  14.7 3.5 %all-to-all-start = ((bf16[4,2,768,64]{2,3,1,0:T(8,128)(2,1)}), bf16[4,2,768,64]{2,3,1,0:T(8,128)(2,1)S(1)}, u32[]{:S(2)}, u32[]{:S(2)}) async-start(bf16[4,2,768,64]{2,3,1,0:T(8,128)(2,1)} %broadcast_in_dim.2), calls=%async_computation | async-start | bytes 1572864 | tf_op jit(solution)/shard_map/all_to_all | solution.py:64
  18.3 4.7 %multiply_reduce_fusion.2 = (f32[768,768]{1,0:T(8,128)S(1)}, f32[768,768]{1,0:T(8,128)S(1)}, f32[768,768]{1,0:T(8,128)S(1)}, f32[768,768]{1,0:T(8,128)S(1)}) fusion(f32[3,768]{1,0:T(4,128)S(1)} %get-tuple-element.11, f32[3,768]{1,0:T(4,128)S(1)} %get-tuple-element.13, f32[3,768]{1,0:T(4,128)S(1)} %get-tuple-element.12, f32[3,768]{1,0:T(4,128)S(1)} %get-tuple-element.10), kind=kLoop, calls=%fused_computation.2 | loop fusion | flops 18874368 | bytes 9474048 | tf_op jit(solution)/shard_map/reduce_sum | solution.py:9
  23.0 1.1 %fusion = f32[768,128]{0,1:S(1)} fusion(bf16[768,128]{0,1:T(8,128)(2,1)S(1)} %bitcast.35, f32[768,768]{1,0:T(8,128)S(1)} %get-tuple-element.9), kind=kOutput, calls=%fused_computation.9 | convolution fusion | flops 152764416 | bytes 2949120
  24.1 1.1 %fusion.1 = f32[768,128]{0,1:S(1)} fusion(bf16[768,128]{0,1:T(8,128)(2,1)S(1)} %bitcast.41, f32[768,768]{1,0:T(8,128)S(1)} %get-tuple-element.6), kind=kOutput, calls=%fused_computation.10 | convolution fusion | flops 152764416 | bytes 2949120
  25.2 1.1 %fusion.2 = f32[768,128]{0,1:S(1)} fusion(bf16[768,128]{0,1:T(8,128)(2,1)S(1)} %bitcast.40, f32[768,768]{1,0:T(8,128)S(1)} %get-tuple-element.7), kind=kOutput, calls=%fused_computation.11 | convolution fusion | flops 152764416 | bytes 2949120
  26.3 1.0 %collective-permute-done.5 = bf16[2,768,64]{1,2,0:T(8,128)(2,1)S(1)} collective-permute-done((bf16[2,768,64]{1,2,0:T(8,128)(2,1)}, bf16[2,768,64]{1,2,0:T(8,128)(2,1)S(1)}, u32[]{:S(2)}, u32[]{:S(2)}) %collective-permute-start.5) | collective-permute-done | bytes 196640 | tf_op jit(solution)/shard_map/ppermute | solution.py:13
  27.3 1.1 %fusion.3 = f32[768,128]{0,1:S(1)} fusion(bf16[768,128]{0,1:T(8,128)(2,1)S(1)} %bitcast.42, f32[768,768]{1,0:T(8,128)S(1)} %get-tuple-element.8), kind=kOutput, calls=%fused_computation.12 | convolution fusion | flops 152764416 | bytes 2949120
  28.5 1.3 %all-to-all-done = bf16[4,2,768,64]{2,3,1,0:T(8,128)(2,1)S(1)} async-done(((bf16[4,2,768,64]{2,3,1,0:T(8,128)(2,1)}), bf16[4,2,768,64]{2,3,1,0:T(8,128)(2,1)S(1)}, u32[]{:S(2)}, u32[]{:S(2)}) %all-to-all-start) | async-done | bytes 786464 | tf_op jit(solution)/shard_map/all_to_all | solution.py:64
  29.8 0.5 %convolution_bitcast_fusion = f32[64,4,64]{2,0,1:T(8,128)S(1)} fusion(bf16[4,2,768,64]{2,3,1,0:T(8,128)(2,1)S(1)} %all-to-all-done, bf16[2,768,64]{1,2,0:T(8,128)(2,1)S(1)} %fusion.5, bf16[2]{0:T(256)(128)(2,1)S(1)} %copy-done.4), kind=kOutput, calls=%fused_computation.14 | convolution fusion | flops 50724864 | bytes 1048580 | tf_op jit(solution)/shard_map/sna,ksnb->akb/dot_general | solution.py:68
  30.4 0.1 reshape.16
  30.6 1.5 %collective-permute-start.7 = (f32[64,256]{1,0:T(8,128)S(1)}, f32[64,256]{1,0:T(8,128)S(1)}, u32[]{:S(2)}, u32[]{:S(2)}) collective-permute-start(f32[64,256]{1,0:T(8,128)S(1)} %reshape.16), channel_id=1, source_target_pairs={{0,8},{4,12},{8,0},{12,4},{1,9},{5,13},{9,1},{13,5},{2,10},{6,14},... | collective-permute-start | bytes 196616 | tf_op jit(solution)/shard_map/ppermute | solution.py:18
  32.1 2.9 %collective-permute-start.8 = (f32[64,256]{1,0:T(8,128)S(1)}, f32[64,256]{1,0:T(8,128)S(1)}, u32[]{:S(2)}, u32[]{:S(2)}) collective-permute-start(f32[64,256]{1,0:T(8,128)S(1)} %reshape.16), channel_id=1, source_target_pairs={{0,12},{4,8},{8,4},{12,0},{1,13},{5,9},{9,5},{13,1},{2,14},{6,10},... | collective-permute-start | bytes 196616 | tf_op jit(solution)/shard_map/ppermute | solution.py:18
  35.0 7.5 %all_gather.3 = bf16[256,2,768]{2,0,1:T(8,128)(2,1)S(1)} all-gather(bf16[64,2,768]{2,0,1:T(8,128)(2,1)S(1)} %bitcast.34), channel_id=1, replica_groups=mesh['groups'=2,'dp'=4,'task'=4] {'task'}, dimensions={0}, use_global_device_ids=true | all-gather | bytes 983040 | tf_op jit(solution)/shard_map/all_gather | solution.py:73
  42.5 0.9 %fusion.4 = bf16[2,768,64]{1,2,0:T(8,128)(2,1)} fusion(bf16[256,2,768]{2,0,1:T(8,128)(2,1)S(1)} %all_gather.3, bf16[2,768,64]{1,2,0:T(8,128)(2,1)S(1)} %copy-done.1, f32[64]{0:T(128)S(1)} %copy-done.3, bf16[256,256]{1,0:T(8,128)(2,1)S(1)} %copy-done, s32[]{:T(128)S(6)} %select_n.3), kind=kOutput, calls=%fused_computation.13 | convolution fusion | flops 50724864 | bytes 1212932 | tf_op jit(solution)/shard_map/asn,ca->snc/dot_general | solution.py:75
  43.4 0.6 %add_multiply_fusion = f32[64,256]{1,0:T(8,128)} fusion(f32[64,256]{1,0:T(8,128)S(1)} %collective-permute-done.7, f32[64,256]{1,0:T(8,128)S(1)} %collective-permute-done.8, f32[64,256]{1,0:T(8,128)S(1)} %reshape.16, f32[64,256]{1,0:T(8,128)S(1)} %collective-permute-done.6), kind=kLoop, calls=%fused_computation.20 | loop fusion | flops 65536 | bytes 327680 | tf_op jit(solution)/shard_map/div | solution.py:77
  (21 shorter events, 0.4 us)
Async XLA Ops:
  0.6 41.8 %copy-start = (bf16[256,256]{1,0:T(8,128)(2,1)S(1)}, bf16[256,256]{1,0:T(8,128)(2,1)}, u32[]{:S(2)}) copy-start(bf16[256,256]{1,0:T(8,128)(2,1)} %param.9) | copy-start | bytes 393220
  0.6 17.6 %copy-start.2 = (bf16[3,768]{1,0:T(4,128)(2,1)S(1)}, bf16[3,768]{1,0:T(4,128)(2,1)}, u32[]{:S(2)}) copy-start(bf16[3,768]{1,0:T(4,128)(2,1)} %param.6) | copy-start | bytes 13828
  0.7 10.6 %collective-permute-start = (bf16[3,768]{1,0:T(4,128)(2,1)}, bf16[3,768]{1,0:T(4,128)(2,1)S(1)}, u32[]{:S(2)}, u32[]{:S(2)}) collective-permute-start(bf16[3,768]{1,0:T(4,128)(2,1)} %param.6), channel_id=1, source_target_pairs={{0,4},{4,8},{8,12},{12,0},{1,5},{5,9},{9,13},{13,1},{2,6},{6,10},{... | collective-permute-start | bytes 13832 | tf_op jit(solution)/shard_map/ppermute | solution.py:13
  3.7 7.7 %collective-permute-start.2 = (bf16[3,768]{1,0:T(4,128)(2,1)}, bf16[3,768]{1,0:T(4,128)(2,1)S(1)}, u32[]{:S(2)}, u32[]{:S(2)}) collective-permute-start(bf16[3,768]{1,0:T(4,128)(2,1)} %param.6), channel_id=1, source_target_pairs={{0,12},{4,0},{8,4},{12,8},{1,13},{5,1},{9,5},{13,9},{2,14},{6,2},{... | collective-permute-start | bytes 13832 | tf_op jit(solution)/shard_map/ppermute | solution.py:13
  5.8 7.0 %collective-permute-start.4 = (bf16[3,768]{1,0:T(4,128)(2,1)}, bf16[3,768]{1,0:T(4,128)(2,1)S(1)}, u32[]{:S(2)}, u32[]{:S(2)}) collective-permute-start(bf16[3,768]{1,0:T(4,128)(2,1)} %param.6), channel_id=1, source_target_pairs={{0,8},{4,12},{8,0},{12,4},{1,9},{5,13},{9,1},{13,5},{2,10},{6,14},... | collective-permute-start | bytes 13832 | tf_op jit(solution)/shard_map/ppermute | solution.py:13
  6.8 17.3 %collective-permute-start.1 = (bf16[2,768,64]{1,2,0:T(8,128)(2,1)}, bf16[2,768,64]{1,2,0:T(8,128)(2,1)S(1)}, u32[]{:S(2)}, u32[]{:S(2)}) collective-permute-start(bf16[2,768,64]{1,2,0:T(8,128)(2,1)} %param.8), channel_id=1, source_target_pairs={{0,4},{4,8},{8,12},{12,0},{1,5},{5,9},{9,13},{13,1},{2,6},{6,10},{... | collective-permute-start | bytes 589832 | tf_op jit(solution)/shard_map/ppermute | solution.py:13
  8.3 16.8 %collective-permute-start.3 = (bf16[2,768,64]{1,2,0:T(8,128)(2,1)}, bf16[2,768,64]{1,2,0:T(8,128)(2,1)S(1)}, u32[]{:S(2)}, u32[]{:S(2)}) collective-permute-start(bf16[2,768,64]{1,2,0:T(8,128)(2,1)} %param.8), channel_id=1, source_target_pairs={{0,12},{4,0},{8,4},{12,8},{1,13},{5,1},{9,5},{13,9},{2,14},{6,2},{... | collective-permute-start | bytes 589832 | tf_op jit(solution)/shard_map/ppermute | solution.py:13
  11.3 16.0 %collective-permute-start.5 = (bf16[2,768,64]{1,2,0:T(8,128)(2,1)}, bf16[2,768,64]{1,2,0:T(8,128)(2,1)S(1)}, u32[]{:S(2)}, u32[]{:S(2)}) collective-permute-start(bf16[2,768,64]{1,2,0:T(8,128)(2,1)} %param.8), channel_id=1, source_target_pairs={{0,8},{4,12},{8,0},{12,4},{1,9},{5,13},{9,1},{13,5},{2,10},{6,14},... | collective-permute-start | bytes 589832 | tf_op jit(solution)/shard_map/ppermute | solution.py:13
  14.7 15.1 %all-to-all-start = ((bf16[4,2,768,64]{2,3,1,0:T(8,128)(2,1)}), bf16[4,2,768,64]{2,3,1,0:T(8,128)(2,1)S(1)}, u32[]{:S(2)}, u32[]{:S(2)}) async-start(bf16[4,2,768,64]{2,3,1,0:T(8,128)(2,1)} %broadcast_in_dim.2), calls=%async_computation | async-start | bytes 1572864 | tf_op jit(solution)/shard_map/all_to_all | solution.py:64
  18.3 4.7 %copy-start.1 = (bf16[2,768,64]{1,2,0:T(8,128)(2,1)S(1)}, bf16[2,768,64]{1,2,0:T(8,128)(2,1)}, u32[]{:S(2)}) copy-start(bf16[2,768,64]{1,2,0:T(8,128)(2,1)} %param.8) | copy-start | bytes 589828
  27.3 2.5 %copy-start.4 = (bf16[2]{0:T(256)(128)(2,1)S(1)}, bf16[2]{0:T(256)(128)(2,1)}, u32[]{:S(2)}) copy-start(bf16[2]{0:T(256)(128)(2,1)} %constant.23.clone) | copy-start | bytes 16
  28.4 14.1 %copy-start.3 = (f32[64]{0:T(128)S(1)}, f32[64]{0:T(128)}, u32[]{:S(2)}) copy-start(f32[64]{0:T(128)} %param.10) | copy-start | bytes 772
  30.6 12.8 %collective-permute-start.6 = (f32[64,256]{1,0:T(8,128)S(1)}, f32[64,256]{1,0:T(8,128)S(1)}, u32[]{:S(2)}, u32[]{:S(2)}) collective-permute-start(f32[64,256]{1,0:T(8,128)S(1)} %reshape.16), channel_id=1, source_target_pairs={{0,4},{4,0},{8,12},{12,8},{1,5},{5,1},{9,13},{13,9},{2,6},{6,2},{1... | collective-permute-start | bytes 196616 | tf_op jit(solution)/shard_map/ppermute | solution.py:18
  30.6 12.8 %collective-permute-start.7 = (f32[64,256]{1,0:T(8,128)S(1)}, f32[64,256]{1,0:T(8,128)S(1)}, u32[]{:S(2)}, u32[]{:S(2)}) collective-permute-start(f32[64,256]{1,0:T(8,128)S(1)} %reshape.16), channel_id=1, source_target_pairs={{0,8},{4,12},{8,0},{12,4},{1,9},{5,13},{9,1},{13,5},{2,10},{6,14},... | collective-permute-start | bytes 196616 | tf_op jit(solution)/shard_map/ppermute | solution.py:18
  32.1 11.3 %collective-permute-start.8 = (f32[64,256]{1,0:T(8,128)S(1)}, f32[64,256]{1,0:T(8,128)S(1)}, u32[]{:S(2)}, u32[]{:S(2)}) collective-permute-start(f32[64,256]{1,0:T(8,128)S(1)} %reshape.16), channel_id=1, source_target_pairs={{0,12},{4,8},{8,4},{12,0},{1,13},{5,9},{9,5},{13,1},{2,14},{6,10},... | collective-permute-start | bytes 196616 | tf_op jit(solution)/shard_map/ppermute | solution.py:18

commit v24 on v21

--- a/solution.py
+++ b/solution.py
@@ -48,7 +48,7 @@
         peer_coords = [shift(coords, "dp", k, n_dp) for k in range(1, n_dp)]
         task_input = lax.optimization_barrier((vectors, peer_coords))[0]
         summed = block(coords, vectors)
-        order = [1, 3, 2] if n_dp == 4 else list(range(1, n_dp))
+        order = [3, 1, 2] if n_dp == 4 else list(range(1, n_dp))
         for k in order:
             summed = summed + block(peer_coords[k - 1], moved[k - 1])
     else:

time: 43.3 us -> 45.3 us (1.046)
  the two profiles are of different devices: /device:TPU:0 before, /device:TPU:11 now
where the time goes in v24:
time: 45.3 us; the launch traced here: 45.1 us
  starting transfers between devices  19.7 us (43%)
  blocking collectives  10 us (22%)
  other arithmetic  6.12 us (14%)
  matrix products  5.84 us (13%)
  local copies, waits for them, and re-layouts  2.16 us (5%)
  between operations  0.72 us (2%)
  waiting for transfers between devices  0.51 us (1%)
    ppermute x9, starting transfers between devices, shift(): return lax.ppermute(x, axis, [(i, (i + k) % n) for i in range(n)])  14 us
    all_gather x1, blocking collectives, per_device(): lax.all_gather(jnp.transpose(gather_input, (2, 0, 1)), 'task', axis=0, ti...  10 us
    all_to_all x1, starting transfers between devices, per_device(): task_blocks = lax.all_to_all(copies, 'task', 0, 0, tiled=True)  5.71 us
    reduce_sum x1, other arithmetic, kernel_tile(): return jnp.exp(0.1 - jnp.sqrt(jnp.sum(diff * diff, axis=0) + 0.01))  4.65 us
    unnamed x4, matrix products  4.39 us
    broadcast_in_dim x1, local copies, waits for them, and re-layouts, per_device(): copies = jnp.broadcast_to(task_input[None], (n_task,) + vectors.shape)  1.9 us
    dot_general x1, matrix products, per_device(): jnp.einsum('asn,ca->snc', whole_images, own_rows, preferred_element_type=...  0.94 us
  transfers between devices with their start and end apart: 10, of which 1 were waited for; matrix products, arithmetic and copies ran while one was open for 28% of the time, Pallas kernels for 0%

profile of v24, /device:TPU:11, one launch (start us, length us, event | category | flops | bytes accessed | tf_op | source)
XLA Modules:
  0.0 45.1 jit_solution(14653625490817026132)
XLA Ops:
  0.7 0.2 collective-permute-start
  0.9 1.3 %collective-permute-start.2 = (bf16[3,768]{1,0:T(4,128)(2,1)}, bf16[3,768]{1,0:T(4,128)(2,1)S(1)}, u32[]{:S(2)}, u32[]{:S(2)}) collective-permute-start(bf16[3,768]{1,0:T(4,128)(2,1)} %param.6), channel_id=1, source_target_pairs={{0,4},{4,8},{8,12},{12,0},{1,5},{5,9},{9,13},{13,1},{2,6},{6,10},{... | collective-permute-start | bytes 13832 | tf_op jit(solution)/shard_map/ppermute | solution.py:13
  2.2 4.1 %collective-permute-start.4 = (bf16[3,768]{1,0:T(4,128)(2,1)}, bf16[3,768]{1,0:T(4,128)(2,1)S(1)}, u32[]{:S(2)}, u32[]{:S(2)}) collective-permute-start(bf16[3,768]{1,0:T(4,128)(2,1)} %param.6), channel_id=1, source_target_pairs={{0,8},{4,12},{8,0},{12,4},{1,9},{5,13},{9,1},{13,5},{2,10},{6,14},... | collective-permute-start | bytes 13832 | tf_op jit(solution)/shard_map/ppermute | solution.py:13
  6.3 1.5 %collective-permute-start.3 = (bf16[2,768,64]{1,2,0:T(8,128)(2,1)}, bf16[2,768,64]{1,2,0:T(8,128)(2,1)S(1)}, u32[]{:S(2)}, u32[]{:S(2)}) collective-permute-start(bf16[2,768,64]{1,2,0:T(8,128)(2,1)} %param.8), channel_id=1, source_target_pairs={{0,4},{4,8},{8,12},{12,0},{1,5},{5,9},{9,13},{13,1},{2,6},{6,10},{... | collective-permute-start | bytes 589832 | tf_op jit(solution)/shard_map/ppermute | solution.py:13
  7.7 0.7 %broadcast_divide_fusion = f32[3]{0:T(128)S(1)} fusion(f32[3]{0:T(128)} %param.7), kind=kLoop, calls=%fused_computation.28 | loop fusion | flops 3 | bytes 24 | tf_op jit(solution)/shard_map/div | solution.py:37
  8.4 1.8 %collective-permute-start.5 = (bf16[2,768,64]{1,2,0:T(8,128)(2,1)}, bf16[2,768,64]{1,2,0:T(8,128)(2,1)S(1)}, u32[]{:S(2)}, u32[]{:S(2)}) collective-permute-start(bf16[2,768,64]{1,2,0:T(8,128)(2,1)} %param.8), channel_id=1, source_target_pairs={{0,8},{4,12},{8,0},{12,4},{1,9},{5,13},{9,1},{13,5},{2,10},{6,14},... | collective-permute-start | bytes 589832 | tf_op jit(solution)/shard_map/ppermute | solution.py:13
  10.2 1.9 %broadcast_in_dim.2 = bf16[4,2,768,64]{2,3,1,0:T(8,128)(2,1)} broadcast(bf16[2,768,64]{1,2,0:T(8,128)(2,1)} %param.8), dimensions={1,2,3} | broadcast | bytes 983040 | tf_op jit(solution)/shard_map/broadcast_in_dim | solution.py:66
  12.1 5.7 %all-to-all-start = ((bf16[4,2,768,64]{2,3,1,0:T(8,128)(2,1)}), bf16[4,2,768,64]{2,3,1,0:T(8,128)(2,1)S(1)}, u32[]{:S(2)}, u32[]{:S(2)}) async-start(bf16[4,2,768,64]{2,3,1,0:T(8,128)(2,1)} %broadcast_in_dim.2), calls=%async_computation | async-start | bytes 1572864 | tf_op jit(solution)/shard_map/all_to_all | solution.py:67
  17.8 0.1 convert_multiply_fusion
  17.9 4.7 %multiply_reduce_fusion.2 = (f32[768,768]{1,0:T(8,128)S(1)}, f32[768,768]{1,0:T(8,128)S(1)}, f32[768,768]{1,0:T(8,128)S(1)}, f32[768,768]{1,0:T(8,128)S(1)}) fusion(f32[3,768]{1,0:T(4,128)S(1)} %get-tuple-element.11, f32[3,768]{1,0:T(4,128)S(1)} %get-tuple-element.13, f32[3,768]{1,0:T(4,128)S(1)} %get-tuple-element.12, f32[3,768]{1,0:T(4,128)S(1)} %get-tuple-element.10), kind=kLoop, calls=%fused_computation.2 | loop fusion | flops 18874368 | bytes 9474048 | tf_op jit(solution)/shard_map/reduce_sum | solution.py:9
  22.6 1.1 %fusion = f32[768,128]{0,1:S(1)} fusion(bf16[768,128]{0,1:T(8,128)(2,1)S(1)} %bitcast.35, f32[768,768]{1,0:T(8,128)S(1)} %get-tuple-element.9), kind=kOutput, calls=%fused_computation.9 | convolution fusion | flops 152764416 | bytes 2949120
  23.7 1.1 %fusion.1 = f32[768,128]{0,1:S(1)} fusion(bf16[768,128]{0,1:T(8,128)(2,1)S(1)} %bitcast.41, f32[768,768]{1,0:T(8,128)S(1)} %get-tuple-element.6), kind=kOutput, calls=%fused_computation.10 | convolution fusion | flops 152764416 | bytes 2949120
  24.8 1.1 %fusion.2 = f32[768,128]{0,1:S(1)} fusion(bf16[768,128]{0,1:T(8,128)(2,1)S(1)} %bitcast.40, f32[768,768]{1,0:T(8,128)S(1)} %get-tuple-element.7), kind=kOutput, calls=%fused_computation.11 | convolution fusion | flops 152764416 | bytes 2949120
  25.9 1.1 %fusion.3 = f32[768,128]{0,1:S(1)} fusion(bf16[768,128]{0,1:T(8,128)(2,1)S(1)} %bitcast.42, f32[768,768]{1,0:T(8,128)S(1)} %get-tuple-element.8), kind=kOutput, calls=%fused_computation.12 | convolution fusion | flops 152764416 | bytes 2949120
  27.0 0.1 fusion.5
  27.1 0.5 %all-to-all-done = bf16[4,2,768,64]{2,3,1,0:T(8,128)(2,1)S(1)} async-done(((bf16[4,2,768,64]{2,3,1,0:T(8,128)(2,1)}), bf16[4,2,768,64]{2,3,1,0:T(8,128)(2,1)S(1)}, u32[]{:S(2)}, u32[]{:S(2)}) %all-to-all-start) | async-done | bytes 786464 | tf_op jit(solution)/shard_map/all_to_all | solution.py:67
  27.6 0.5 %convolution_bitcast_fusion = f32[64,4,64]{2,0,1:T(8,128)S(1)} fusion(bf16[4,2,768,64]{2,3,1,0:T(8,128)(2,1)S(1)} %all-to-all-done, bf16[2,768,64]{1,2,0:T(8,128)(2,1)S(1)} %fusion.5, bf16[2]{0:T(256)(128)(2,1)S(1)} %copy-done.4), kind=kOutput, calls=%fused_computation.14 | convolution fusion | flops 50724864 | bytes 1048580 | tf_op jit(solution)/shard_map/sna,ksnb->akb/dot_general | solution.py:71
  28.1 0.1 copy.9
  28.2 0.1 reshape.16
  28.4 1.5 %collective-permute-start.7 = (f32[64,256]{1,0:T(8,128)S(1)}, f32[64,256]{1,0:T(8,128)S(1)}, u32[]{:S(2)}, u32[]{:S(2)}) collective-permute-start(f32[64,256]{1,0:T(8,128)S(1)} %reshape.16), channel_id=1, source_target_pairs={{0,4},{4,8},{8,12},{12,0},{1,5},{5,9},{9,13},{13,1},{2,6},{6,10},{... | collective-permute-start | bytes 196616 | tf_op jit(solution)/shard_map/ppermute | solution.py:13
  29.8 3.6 %collective-permute-start.8 = (f32[64,256]{1,0:T(8,128)S(1)}, f32[64,256]{1,0:T(8,128)S(1)}, u32[]{:S(2)}, u32[]{:S(2)}) collective-permute-start(f32[64,256]{1,0:T(8,128)S(1)} %reshape.16), channel_id=1, source_target_pairs={{0,8},{4,12},{8,0},{12,4},{1,9},{5,13},{9,1},{13,5},{2,10},{6,14},... | collective-permute-start | bytes 196616 | tf_op jit(solution)/shard_map/ppermute | solution.py:13
  33.5 10.0 %all_gather.3 = bf16[256,2,768]{2,0,1:T(8,128)(2,1)S(1)} all-gather(bf16[64,2,768]{2,0,1:T(8,128)(2,1)S(1)} %bitcast.34), channel_id=1, replica_groups=mesh['groups'=2,'dp'=4,'task'=4] {'task'}, dimensions={0}, use_global_device_ids=true | all-gather | bytes 983040 | tf_op jit(solution)/shard_map/all_gather | solution.py:76
  43.5 0.9 %fusion.4 = bf16[2,768,64]{1,2,0:T(8,128)(2,1)} fusion(bf16[256,2,768]{2,0,1:T(8,128)(2,1)S(1)} %all_gather.3, bf16[2,768,64]{1,2,0:T(8,128)(2,1)S(1)} %copy-done.1, f32[64]{0:T(128)S(1)} %copy-done.3, bf16[256,256]{1,0:T(8,128)(2,1)S(1)} %copy-done, s32[]{:T(128)S(6)} %select_n.22), kind=kOutput, calls=%fused_computation.13 | convolution fusion | flops 50724864 | bytes 1212932 | tf_op jit(solution)/shard_map/asn,ca->snc/dot_general | solution.py:78
  44.5 0.7 %add_multiply_fusion = f32[64,256]{1,0:T(8,128)} fusion(f32[64,256]{1,0:T(8,128)S(1)} %collective-permute-done.8, f32[64,256]{1,0:T(8,128)S(1)} %collective-permute-done.7, f32[64,256]{1,0:T(8,128)S(1)} %collective-permute-done.6, f32[64,256]{1,0:T(8,128)S(1)} %reshape.16, pred[]{:T(512)S(6)} %eq.5), kind=kLoop, calls=%fused_computation.20 | loop fusion | flops 98304 | bytes 327681 | tf_op jit(solution)/shard_map/div | solution.py:80
  (21 shorter events, 0.1 us)
Async XLA Ops:
  0.6 42.9 %copy-start = (bf16[256,256]{1,0:T(8,128)(2,1)S(1)}, bf16[256,256]{1,0:T(8,128)(2,1)}, u32[]{:S(2)}) copy-start(bf16[256,256]{1,0:T(8,128)(2,1)} %param.9) | copy-start | bytes 393220
  0.6 17.2 %copy-start.2 = (bf16[3,768]{1,0:T(4,128)(2,1)S(1)}, bf16[3,768]{1,0:T(4,128)(2,1)}, u32[]{:S(2)}) copy-start(bf16[3,768]{1,0:T(4,128)(2,1)} %param.6) | copy-start | bytes 13828
  0.7 7.8 %collective-permute-start = (bf16[3,768]{1,0:T(4,128)(2,1)}, bf16[3,768]{1,0:T(4,128)(2,1)S(1)}, u32[]{:S(2)}, u32[]{:S(2)}) collective-permute-start(bf16[3,768]{1,0:T(4,128)(2,1)} %param.6), channel_id=1, source_target_pairs={{0,12},{4,0},{8,4},{12,8},{1,13},{5,1},{9,5},{13,9},{2,14},{6,2},{... | collective-permute-start | bytes 13832 | tf_op jit(solution)/shard_map/ppermute | solution.py:13
  0.9 9.3 %collective-permute-start.2 = (bf16[3,768]{1,0:T(4,128)(2,1)}, bf16[3,768]{1,0:T(4,128)(2,1)S(1)}, u32[]{:S(2)}, u32[]{:S(2)}) collective-permute-start(bf16[3,768]{1,0:T(4,128)(2,1)} %param.6), channel_id=1, source_target_pairs={{0,4},{4,8},{8,12},{12,0},{1,5},{5,9},{9,13},{13,1},{2,6},{6,10},{... | collective-permute-start | bytes 13832 | tf_op jit(solution)/shard_map/ppermute | solution.py:13
  2.2 8.0 %collective-permute-start.4 = (bf16[3,768]{1,0:T(4,128)(2,1)}, bf16[3,768]{1,0:T(4,128)(2,1)S(1)}, u32[]{:S(2)}, u32[]{:S(2)}) collective-permute-start(bf16[3,768]{1,0:T(4,128)(2,1)} %param.6), channel_id=1, source_target_pairs={{0,8},{4,12},{8,0},{12,4},{1,9},{5,13},{9,1},{13,5},{2,10},{6,14},... | collective-permute-start | bytes 13832 | tf_op jit(solution)/shard_map/ppermute | solution.py:13
  6.3 17.4 %collective-permute-start.1 = (bf16[2,768,64]{1,2,0:T(8,128)(2,1)}, bf16[2,768,64]{1,2,0:T(8,128)(2,1)S(1)}, u32[]{:S(2)}, u32[]{:S(2)}) collective-permute-start(bf16[2,768,64]{1,2,0:T(8,128)(2,1)} %param.8), channel_id=1, source_target_pairs={{0,12},{4,0},{8,4},{12,8},{1,13},{5,1},{9,5},{13,9},{2,14},{6,2},{... | collective-permute-start | bytes 589832 | tf_op jit(solution)/shard_map/ppermute | solution.py:13
  6.3 18.5 %collective-permute-start.3 = (bf16[2,768,64]{1,2,0:T(8,128)(2,1)}, bf16[2,768,64]{1,2,0:T(8,128)(2,1)S(1)}, u32[]{:S(2)}, u32[]{:S(2)}) collective-permute-start(bf16[2,768,64]{1,2,0:T(8,128)(2,1)} %param.8), channel_id=1, source_target_pairs={{0,4},{4,8},{8,12},{12,0},{1,5},{5,9},{9,13},{13,1},{2,6},{6,10},{... | collective-permute-start | bytes 589832 | tf_op jit(solution)/shard_map/ppermute | solution.py:13
  8.4 17.5 %collective-permute-start.5 = (bf16[2,768,64]{1,2,0:T(8,128)(2,1)}, bf16[2,768,64]{1,2,0:T(8,128)(2,1)S(1)}, u32[]{:S(2)}, u32[]{:S(2)}) collective-permute-start(bf16[2,768,64]{1,2,0:T(8,128)(2,1)} %param.8), channel_id=1, source_target_pairs={{0,8},{4,12},{8,0},{12,4},{1,9},{5,13},{9,1},{13,5},{2,10},{6,14},... | collective-permute-start | bytes 589832 | tf_op jit(solution)/shard_map/ppermute | solution.py:13
  12.1 15.5 %all-to-all-start = ((bf16[4,2,768,64]{2,3,1,0:T(8,128)(2,1)}), bf16[4,2,768,64]{2,3,1,0:T(8,128)(2,1)S(1)}, u32[]{:S(2)}, u32[]{:S(2)}) async-start(bf16[4,2,768,64]{2,3,1,0:T(8,128)(2,1)} %broadcast_in_dim.2), calls=%async_computation | async-start | bytes 1572864 | tf_op jit(solution)/shard_map/all_to_all | solution.py:67
  17.9 4.7 %copy-start.1 = (bf16[2,768,64]{1,2,0:T(8,128)(2,1)S(1)}, bf16[2,768,64]{1,2,0:T(8,128)(2,1)}, u32[]{:S(2)}) copy-start(bf16[2,768,64]{1,2,0:T(8,128)(2,1)} %param.8) | copy-start | bytes 589828
  25.9 1.7 %copy-start.4 = (bf16[2]{0:T(256)(128)(2,1)S(1)}, bf16[2]{0:T(256)(128)(2,1)}, u32[]{:S(2)}) copy-start(bf16[2]{0:T(256)(128)(2,1)} %constant.38.clone) | copy-start | bytes 16
  27.0 16.5 %copy-start.3 = (f32[64]{0:T(128)S(1)}, f32[64]{0:T(128)}, u32[]{:S(2)}) copy-start(f32[64]{0:T(128)} %param.10) | copy-start | bytes 772
  28.3 16.1 %collective-permute-start.6 = (f32[64,256]{1,0:T(8,128)S(1)}, f32[64,256]{1,0:T(8,128)S(1)}, u32[]{:S(2)}, u32[]{:S(2)}) collective-permute-start(f32[64,256]{1,0:T(8,128)S(1)} %reshape.16), channel_id=1, source_target_pairs={{0,12},{4,0},{8,4},{12,8},{1,13},{5,1},{9,5},{13,9},{2,14},{6,2},{... | collective-permute-start | bytes 196616 | tf_op jit(solution)/shard_map/ppermute | solution.py:13
  28.4 16.1 %collective-permute-start.7 = (f32[64,256]{1,0:T(8,128)S(1)}, f32[64,256]{1,0:T(8,128)S(1)}, u32[]{:S(2)}, u32[]{:S(2)}) collective-permute-start(f32[64,256]{1,0:T(8,128)S(1)} %reshape.16), channel_id=1, source_target_pairs={{0,4},{4,8},{8,12},{12,0},{1,5},{5,9},{9,13},{13,1},{2,6},{6,10},{... | collective-permute-start | bytes 196616 | tf_op jit(solution)/shard_map/ppermute | solution.py:13
  29.8 14.6 %collective-permute-start.8 = (f32[64,256]{1,0:T(8,128)S(1)}, f32[64,256]{1,0:T(8,128)S(1)}, u32[]{:S(2)}, u32[]{:S(2)}) collective-permute-start(f32[64,256]{1,0:T(8,128)S(1)} %reshape.16), channel_id=1, source_target_pairs={{0,8},{4,12},{8,0},{12,4},{1,9},{5,13},{9,1},{13,5},{2,10},{6,14},... | collective-permute-start | bytes 196616 | tf_op jit(solution)/shard_map/ppermute | solution.py:13
